TPU v7x, 128 devices: a whole 4x4x4 slice. The times are simulated.
128 devices in a mesh: dp: 8 (over z, y_lo), slab: 16 (over y_hi, x, core).
Axes of the slice: x: 4, y: 4 (y_hi: 2, y_lo: 2; y = y_hi * 2 + y_lo), z: 4, core: 2. Of those that a mesh axis runs over, the one named last changes fastest.
Arguments:
- sensitivity: bfloat16 [8192, 128, 256], P('dp', 'slab'), may hold values from -6 to 6
- cell_class: int32 [128, 256], P('slab'), may hold values from 0 to 7
- class_rate: float32 [8], replicated, may hold values from 0.28 to 0.4
- panel_owner: int32 [8], replicated, may hold values from 0 to 7, each once
Outputs:
- smoothed: float32 [8192, 128, 256], P('dp', 'slab')
- gram: float32 [8192, 3, 256], P(('dp', 'slab'))
Inputs may be any that keep to these rules, and one draw needn't show every extreme that they name: `panel_owner`: each dp index appears exactly once.
All inputs are finite; a program needn't handle non-finite values.
Results may differ from a plain program's by a relative error of at most 0.002.
Values may be sent and summed in bfloat16 or wider, within the bound.
No kernel may reach another device: no remote copies, remote signals or barrier semaphores. Data moves between devices by JAX's collectives and lax.ppermute only.
A program may use at most 128 MiB of HBM per device.

v0:
```python
import jax
import jax.numpy as jnp
from jax import lax
from jax.sharding import PartitionSpec as P

LX = 16
PASSES = 4
PANELS = 3
PANEL = 256


lateral_weight = 0.125


def padded_2(shard, sides, width):
    for axis, dim in sides:
        size, length = (lax.axis_size(axis), shard.shape[dim])
        up = [(i, (i + 1) % size) for i in range(size - 1)]
        down = [(j, i) for i, j in up]
        last = lax.slice_in_dim(shard, length - width, length, axis=dim)
        leading = lax.slice_in_dim(shard, 0, width, axis=dim)
        before = lax.ppermute(last, axis, up)
        after = lax.ppermute(leading, axis, down)
        shard = jnp.concatenate([before, shard, after], axis=dim)
    return shard


def from_root(value, axis, source):
    kept = jnp.where(lax.axis_index(axis) == source, value, 0).astype(value.dtype)
    return lax.psum(kept, axis)


def shift_last(v, s):
    zeros = jnp.zeros(v.shape[:-1] + (abs(s),), v.dtype)
    if s > 0:
        return jnp.concatenate([zeros, v[..., :-s]], axis=-1)
    return jnp.concatenate([v[..., -s:], zeros], axis=-1)


def lateral_sum(v, side):
    column = jnp.arange(v.shape[-1]) % side
    low_mask = (column != 0).astype(jnp.float32)
    high_mask = (column != side - 1).astype(jnp.float32)
    total = shift_last(v, side) + shift_last(v, -side)
    return total + low_mask * shift_last(v, 1) + high_mask * shift_last(v, -1)


def update(field, padded, rate):
    depth_sum = padded[:, 2:] + padded[:, :-2]
    return (
        field
        + rate * (depth_sum - 2.0 * field)
        + lateral_weight * rate * (lateral_sum(field, LX) - 4.0 * field)
    )


def body(sensitivity, cell_class, class_rate, panel_owner):
    rows, depth, lat = sensitivity.shape
    onehot = (cell_class[..., None] == jnp.arange(class_rate.shape[0])[None, None, :]).astype(
        jnp.float32
    )
    kappa = jnp.sum(onehot * class_rate[None, None, :], axis=-1)
    field = sensitivity.astype(jnp.float32)
    for step in range(PASSES):
        padded = padded_2(field, (("slab", 1),), 1)
        field = update(field, padded, kappa)
    cells = depth * lat * lax.axis_size("slab")
    flat = sensitivity.reshape(rows, depth * lat)
    partials = []
    for p in range(PANELS):
        piece = field[p * PANEL : (p + 1) * PANEL].reshape(PANEL, depth * lat).astype(jnp.bfloat16)
        received = from_root(piece, "dp", panel_owner[p])
        term = (
            lax.dot_general(
                flat, received, (((1,), (1,)), ((), ())), preferred_element_type=jnp.float32
            )
            / cells
        )
        partials.append(lax.psum_scatter(term, "slab", scatter_dimension=0, tiled=True))
    gram = jnp.stack(partials, axis=1)
    return (field, gram)


def solution(mesh):
    placed = (P("dp", "slab", None), P("slab", None), P(), P())
    return jax.shard_map(
        body,
        mesh=mesh,
        in_specs=placed,
        out_specs=(P("dp", "slab", None), P(("dp", "slab"), None, None)),
        check_vma=False,
    )
```

profile of v0, /device:TPU:0, one launch (start us, length us, event | category | flops | bytes accessed | tf_op | source)
XLA Modules:
  0.0 638.0 jit_solution(18162034326145226816)
XLA Ops:
  7.2 6.7 %copy.29 = bf16[1024,8,256]{0,2,1:T(8,128)(2,1)} copy(bf16[1024,8,256]{2,1,0:T(8,128)(2,1)} %param.4) | data formatting | bytes 8388608 | tf_op args[0]
  13.9 1.4 fusion.36
  15.7 1.3 collective-permute-start
  17.0 1.3 copy.32
  18.3 4.3 collective-permute-start.1
  22.6 10.8 %fusion.34 = (f32[1024,8,240]{0,2,1:T(8,128)}, f32[1024,8,240]{0,2,1:T(8,128)}) fusion(bf16[1024,8,256]{0,2,1:T(8,128)(2,1)} %copy.29), kind=kLoop, calls=%fused_computation.54 | loop fusion | bytes 31457280 | tf_op jit(solution)/shard_map/slice | solution.py:36
  33.4 4.4 convert_element_type.46
  40.5 11.6 %fusion.35 = (f32[1024,8,255]{0,2,1:T(8,128)}, f32[1024,8,255]{0,2,1:T(8,128)}) fusion(bf16[1024,8,256]{0,2,1:T(8,128)(2,1)} %copy.29), kind=kLoop, calls=%fused_computation.55 | loop fusion | bytes 33423360 | tf_op jit(solution)/shard_map/slice | solution.py:36
  52.4 1.6 copy.33
  54.0 19.2 %fusion.19 = f32[1024,8,256]{0,2,1:T(8,128)S(1)} fusion(f32[1024,8,256]{0,2,1:T(8,128)} %convert_element_type.46, f32[1024,1,256]{0,2,1:T(8,128)S(1)} %copy.33, f32[1024,1,256]{0,2,1:T(8,128)S(1)} %copy.31, f32[1024,8,255]{0,2,1:T(8,128)} %get-tuple-element.39, f32[1024,8,255]{0,2,1:T(8,128)} %get-tuple-element.38, f32[1024,8,240]{0,2,1:T(8,128)} %get-tuple-element.37, ...), kind=kLoop, calls=%fused_computation.26 | loop fusion | flops 33554432 | bytes 51333120 | tf_op jit(solution)/shard_map/add | solution.py:51
  73.2 3.4 copy-done.2
  77.0 1.3 collective-permute-start.2
  78.3 1.3 copy.36
  79.7 4.0 collective-permute-start.3
  83.7 14.5 %fusion.31 = (f32[1024,8,240]{0,2,1:T(8,128)}, f32[1024,8,240]{0,2,1:T(8,128)}) fusion(f32[1024,8,256]{0,2,1:T(8,128)} %copy-done.2), kind=kLoop, calls=%fused_computation.51 | loop fusion | bytes 31457280 | tf_op jit(solution)/shard_map/slice | solution.py:36
  98.2 13.4 %fusion.32 = (f32[1024,8,255]{0,2,1:T(8,128)}, f32[1024,8,255]{0,2,1:T(8,128)}) fusion(f32[1024,8,256]{0,2,1:T(8,128)} %copy-done.2), kind=kLoop, calls=%fused_computation.52 | loop fusion | bytes 33423360 | tf_op jit(solution)/shard_map/slice | solution.py:36
  111.9 1.6 copy.37
  113.5 19.2 %fusion.14 = f32[1024,8,256]{0,2,1:T(8,128)S(1)} fusion(f32[1024,8,256]{0,2,1:T(8,128)} %copy-done.2, f32[1024,1,256]{0,2,1:T(8,128)S(1)} %copy.37, f32[1024,1,256]{0,2,1:T(8,128)S(1)} %copy.35, f32[1024,8,255]{0,2,1:T(8,128)} %get-tuple-element.30, f32[1024,8,255]{0,2,1:T(8,128)} %get-tuple-element.29, f32[1024,8,240]{0,2,1:T(8,128)} %get-tuple-element.28, ...), kind=kLoop, calls=%fused_computation.19 | loop fusion | flops 33554432 | bytes 51333120 | tf_op jit(solution)/shard_map/add | solution.py:51
  132.7 3.4 copy-done.3
  136.6 1.3 collective-permute-start.4
  137.9 1.3 copy.40
  139.2 4.2 collective-permute-start.5
  143.4 14.5 %fusion.28 = (f32[1024,8,240]{0,2,1:T(8,128)}, f32[1024,8,240]{0,2,1:T(8,128)}) fusion(f32[1024,8,256]{0,2,1:T(8,128)} %copy-done.3), kind=kLoop, calls=%fused_computation.48 | loop fusion | bytes 31457280 | tf_op jit(solution)/shard_map/slice | solution.py:36
  157.9 13.4 %fusion.29 = (f32[1024,8,255]{0,2,1:T(8,128)}, f32[1024,8,255]{0,2,1:T(8,128)}) fusion(f32[1024,8,256]{0,2,1:T(8,128)} %copy-done.3), kind=kLoop, calls=%fused_computation.49 | loop fusion | bytes 33423360 | tf_op jit(solution)/shard_map/slice | solution.py:36
  171.6 1.6 copy.41
  173.2 19.2 %fusion.9 = f32[1024,8,256]{0,2,1:T(8,128)S(1)} fusion(f32[1024,8,256]{0,2,1:T(8,128)} %copy-done.3, f32[1024,1,256]{0,2,1:T(8,128)S(1)} %copy.41, f32[1024,1,256]{0,2,1:T(8,128)S(1)} %copy.39, f32[1024,8,255]{0,2,1:T(8,128)} %get-tuple-element.24, f32[1024,8,255]{0,2,1:T(8,128)} %get-tuple-element.23, f32[1024,8,240]{0,2,1:T(8,128)} %get-tuple-element.22, ...), kind=kLoop, calls=%fused_computation.12 | loop fusion | flops 33554432 | bytes 51333120 | tf_op jit(solution)/shard_map/add | solution.py:51
  192.4 3.4 copy-done.1
  196.2 1.3 collective-permute-start.6
  197.6 1.3 copy.44
  198.9 4.3 collective-permute-start.7
  203.1 14.4 %fusion.26 = (f32[1024,8,240]{0,2,1:T(8,128)}, f32[1024,8,240]{0,2,1:T(8,128)}) fusion(f32[1024,8,256]{0,2,1:T(8,128)} %copy-done.1), kind=kLoop, calls=%fused_computation.46 | loop fusion | bytes 31457280 | tf_op jit(solution)/shard_map/slice | solution.py:36
  217.6 13.5 %fusion.27 = (f32[1024,8,255]{0,2,1:T(8,128)}, f32[1024,8,255]{0,2,1:T(8,128)}) fusion(f32[1024,8,256]{0,2,1:T(8,128)} %copy-done.1), kind=kLoop, calls=%fused_computation.47 | loop fusion | bytes 33423360 | tf_op jit(solution)/shard_map/slice | solution.py:36
  231.4 1.6 copy.45
  233.0 22.4 %fusion.23 = (bf16[1024,8,256]{0,2,1:T(8,128)(2,1)S(1)}, f32[1024,8,256]{0,2,1:T(8,128)}) fusion(f32[1024,8,256]{0,2,1:T(8,128)} %copy-done.1, f32[1024,8,255]{0,2,1:T(8,128)} %get-tuple-element.20, f32[256]{0:T(256)S(1)} %get-tuple-element.45, f32[1024,8,255]{0,2,1:T(8,128)} %get-tuple-element.19, f32[256]{0:T(256)S(1)} %get-tuple-element.46, ...), kind=kLoop, calls=%fused_computation.44 | loop fusion | flops 35651584 | bytes 55527424 | tf_op jit(solution)/shard_map/convert.2
  255.4 1.8 slice_select_fusion.2
  257.3 5.7 copy.54
  263.0 155.2 %all-reduce.19.cloned.1.call-done = (bf16[256,2048]{0,1:T(8,128)(2,1)}, bf16[256,2048]{0,1:T(8,128)(2,1)}, bf16[256,2048]{0,1:T(8,128)(2,1)}) async-done(((bf16[256,2048]{0,1:T(8,128)(2,1)}, bf16[256,2048]{0,1:T(8,128)(2,1)}, bf16[256,2048]{0,1:T(8,128)(2,1)}), (bf16[256,2048]{0,1:T(8,128)(2,1)}, bf16[256,2048]{0,1:T(8,128)(2,1)}, bf16[256,2048]{0,1:T(8,128)(2,1)})) %all-reduce.19.cloned.1.call-update) | async-done | bytes 3145744 | tf_op jit(solution)/shard_map/psum | solution.py:30
  418.2 3.9 fusion.20
  422.1 1.3 copy.52
  423.6 3.5 fusion.22
  427.1 1.3 copy.48
  428.5 3.5 fusion.21
  432.0 1.4 copy.50
  433.4 9.3 %copy.46 = f32[1024,8,256]{2,1,0:T(8,128)} copy(f32[1024,8,256]{0,2,1:T(8,128)} %get-tuple-element.14) | data formatting | bytes 16777216
  442.7 47.3 %reduce-scatter.14.cloned.1.call-done = f32[64,256]{1,0:T(8,128)} async-done(((f32[1024,256]{1,0:T(8,128)}), f32[64,256]{1,0:T(8,128)}) %reduce-scatter.14.cloned.1.call-update) | async-done | bytes 65552
  489.9 0.9 copy.53
  490.9 69.3 %reduce-scatter.10.cloned.1.call-done = f32[64,256]{1,0:T(8,128)} async-done(((f32[1024,256]{1,0:T(8,128)}), f32[64,256]{1,0:T(8,128)}) %reduce-scatter.10.cloned.1.call-update) | async-done | bytes 65552
  561.1 68.6 %reduce-scatter.12.cloned.1.call-done = f32[64,256]{1,0:T(8,128)} async-done(((f32[1024,256]{1,0:T(8,128)}), f32[64,256]{1,0:T(8,128)}) %reduce-scatter.12.cloned.1.call-update) | async-done | bytes 65552
  (50 shorter events, 6.8 us)
Async XLA Ops:
  7.2 411.1 %all-reduce.19.cloned.1.call-start = ((), (), s32[]{:S(2)}) async-start(), calls=%async_computation.6 | async-start | bytes 6291456 | tf_op jit(solution)/shard_map/psum | solution.py:30
  15.7 36.4 %collective-permute-start = (f32[1024,1,256]{2,0,1:T(8,128)S(1)}, f32[1024,1,256]{2,0,1:T(8,128)S(1)}, u32[]{:S(2)}, u32[]{:S(2)}) collective-permute-start(f32[1024,1,256]{2,0,1:T(8,128)S(1)} %copy.30), channel_id=1, source_target_pairs={{1,0},{2,1},{3,2},{4,3},{5,4},{6,5},{7,6},{8,7},{9,8},{10,9},{11,1... | collective-permute-start | bytes 3145736 | tf_op jit(solution)/shard_map/ppermute | solution.py:23
  18.3 15.1 %copy-start = (bf16[1024,8,256]{0,2,1:T(8,128)(2,1)S(1)}, bf16[1024,8,256]{0,2,1:T(8,128)(2,1)}, u32[]{:S(2)}) copy-start(bf16[1024,8,256]{0,2,1:T(8,128)(2,1)} %copy.29) | copy-start | bytes 12582916
  18.3 34.1 %collective-permute-start.1 = (f32[1024,1,256]{2,0,1:T(8,128)}, f32[1024,1,256]{2,0,1:T(8,128)}, u32[]{:S(2)}, u32[]{:S(2)}) collective-permute-start(f32[1024,1,256]{2,0,1:T(8,128)} %copy.32), channel_id=1, source_target_pairs={{0,1},{1,2},{2,3},{3,4},{4,5},{5,6},{6,7},{7,8},{8,9},{9,10},{10,1... | collective-permute-start | bytes 3145736 | tf_op jit(solution)/shard_map/ppermute | solution.py:22
  33.4 4.4 copy-start.5
  33.4 7.0 %copy-start.4 = (s32[8,256]{1,0:T(8,128)S(1)}, s32[8,256]{1,0:T(8,128)}, u32[]{:S(2)}) copy-start(s32[8,256]{1,0:T(8,128)} %param.5) | copy-start | bytes 24580
  33.4 7.0 %copy-start.6 = (f32[8]{0:T(128)S(1)}, f32[8]{0:T(128)}, u32[]{:S(2)}) copy-start(f32[8]{0:T(128)} %param.6) | copy-start | bytes 100
  73.2 3.4 copy-start.2
  77.0 34.6 %collective-permute-start.2 = (f32[1024,1,256]{2,0,1:T(8,128)S(1)}, f32[1024,1,256]{2,0,1:T(8,128)S(1)}, u32[]{:S(2)}, u32[]{:S(2)}) collective-permute-start(f32[1024,1,256]{2,0,1:T(8,128)S(1)} %copy.34), channel_id=1, source_target_pairs={{1,0},{2,1},{3,2},{4,3},{5,4},{6,5},{7,6},{8,7},{9,8},{10,9},{11,1... | collective-permute-start | bytes 3145736 | tf_op jit(solution)/shard_map/ppermute | solution.py:23
  79.7 32.3 %collective-permute-start.3 = (f32[1024,1,256]{2,0,1:T(8,128)}, f32[1024,1,256]{2,0,1:T(8,128)}, u32[]{:S(2)}, u32[]{:S(2)}) collective-permute-start(f32[1024,1,256]{2,0,1:T(8,128)} %copy.36), channel_id=1, source_target_pairs={{0,1},{1,2},{2,3},{3,4},{4,5},{5,6},{6,7},{7,8},{8,9},{9,10},{10,1... | collective-permute-start | bytes 3145736 | tf_op jit(solution)/shard_map/ppermute | solution.py:22
  132.7 3.4 copy-start.3
  136.6 34.7 %collective-permute-start.4 = (f32[1024,1,256]{2,0,1:T(8,128)S(1)}, f32[1024,1,256]{2,0,1:T(8,128)S(1)}, u32[]{:S(2)}, u32[]{:S(2)}) collective-permute-start(f32[1024,1,256]{2,0,1:T(8,128)S(1)} %copy.38), channel_id=1, source_target_pairs={{1,0},{2,1},{3,2},{4,3},{5,4},{6,5},{7,6},{8,7},{9,8},{10,9},{11,1... | collective-permute-start | bytes 3145736 | tf_op jit(solution)/shard_map/ppermute | solution.py:23
  139.2 32.4 %collective-permute-start.5 = (f32[1024,1,256]{2,0,1:T(8,128)}, f32[1024,1,256]{2,0,1:T(8,128)}, u32[]{:S(2)}, u32[]{:S(2)}) collective-permute-start(f32[1024,1,256]{2,0,1:T(8,128)} %copy.40), channel_id=1, source_target_pairs={{0,1},{1,2},{2,3},{3,4},{4,5},{5,6},{6,7},{7,8},{8,9},{9,10},{10,1... | collective-permute-start | bytes 3145736 | tf_op jit(solution)/shard_map/ppermute | solution.py:22
  192.4 3.4 copy-start.1
  196.2 34.8 %collective-permute-start.6 = (f32[1024,1,256]{2,0,1:T(8,128)S(1)}, f32[1024,1,256]{2,0,1:T(8,128)S(1)}, u32[]{:S(2)}, u32[]{:S(2)}) collective-permute-start(f32[1024,1,256]{2,0,1:T(8,128)S(1)} %copy.42), channel_id=1, source_target_pairs={{1,0},{2,1},{3,2},{4,3},{5,4},{6,5},{7,6},{8,7},{9,8},{10,9},{11,1... | collective-permute-start | bytes 3145736 | tf_op jit(solution)/shard_map/ppermute | solution.py:23
  198.9 32.5 %collective-permute-start.7 = (f32[1024,1,256]{2,0,1:T(8,128)}, f32[1024,1,256]{2,0,1:T(8,128)}, u32[]{:S(2)}, u32[]{:S(2)}) collective-permute-start(f32[1024,1,256]{2,0,1:T(8,128)} %copy.44), channel_id=1, source_target_pairs={{0,1},{1,2},{2,3},{3,4},{4,5},{5,6},{6,7},{7,8},{8,9},{9,10},{10,1... | collective-permute-start | bytes 3145736 | tf_op jit(solution)/shard_map/ppermute | solution.py:22
  257.2 232.7 %reduce-scatter.14.cloned.1.call-start = ((), (), s32[]{:S(2)}) async-start(), calls=%async_computation.5 | async-start | bytes 1114112
  418.2 5.3 copy-start.8
  422.1 6.3 copy-start.7
  423.5 136.6 %reduce-scatter.10.cloned.1.call-start = ((), (), s32[]{:S(2)}) async-start(), calls=%async_computation.3 | async-start | bytes 1114112
  428.4 201.2 %reduce-scatter.12.cloned.1.call-start = ((), (), s32[]{:S(2)}) async-start(), calls=%async_computation.4 | async-start | bytes 1114112
Sparse Core Ops, SparseCore 0:
  257.4 160.8 all-reduce.18
  423.6 66.2 reduce-scatter.13
  494.2 65.8 reduce-scatter.9
  563.8 65.8 reduce-scatter.11
where the time goes:
time: 639 us; the launch traced here: 638 us
  waiting for transfers between devices  340 us (53%)
  local copies, waits for them, and re-layouts  162 us (25%)
  other arithmetic  86.3 us (14%)
  starting transfers between devices  22.1 us (3%)
  between operations  16 us (3%)
  matrix products  10.9 us (2%)
    unnamed x7, waiting for transfers between devices  185 us
    psum x1, waiting for transfers between devices, from_root(): return lax.psum(kept, axis)  155 us
    slice x8, local copies, waits for them, and re-layouts, shift_last(): return jnp.concatenate([zeros, v[..., :-s]], axis=-1)  106 us
    add x3, other arithmetic, update(): field + rate * (depth_sum - 2.0 * field)  57.5 us
    unnamed x28, local copies, waits for them, and re-layouts  39.5 us
    another operation x1, other arithmetic  22.4 us
    ppermute x4, starting transfers between devices, padded_2(): before = lax.ppermute(last, axis, up)  16.7 us
  transfers between devices with their start and end apart: 12, of which 4 were waited for; matrix products, arithmetic and copies ran while one was open for 23% of the time, Pallas kernels for 0%

commit v1 on v0

v1 whole, which is shorter than its diff:
```python
import functools

import jax
import jax.numpy as jnp
from jax import lax
from jax.experimental import pallas as pl
from jax.experimental.pallas import tpu as pltpu
from jax.sharding import PartitionSpec as P

LX = 16
PASSES = 4
PANELS = 3
PANEL = 256
HALO = 4

lateral_weight = 0.125


def from_root(value, axis, source):
    kept = jnp.where(lax.axis_index(axis) == source, value, 0).astype(value.dtype)
    return lax.psum(kept, axis)


def halo_of(shard, axis, dim):
    size, length = lax.axis_size(axis), shard.shape[dim]
    up = [(i, i + 1) for i in range(size - 1)]
    down = [(j, i) for i, j in up]
    top = lax.slice_in_dim(shard, length - HALO, length, axis=dim)
    bottom = lax.slice_in_dim(shard, 0, HALO, axis=dim)
    below = lax.ppermute(top, axis, up)
    above = lax.ppermute(bottom, axis, down)
    return jnp.concatenate([below, above], axis=dim)


def smooth_kernel(ka_ref, kb_ref, a_ref, b_ref, o_ref, *, sub):
    depth, lat = ka_ref.shape
    shape = (sub, depth, lat)
    lane = lax.broadcasted_iota(jnp.int32, shape, 2)
    row = lax.broadcasted_iota(jnp.int32, shape, 1)
    col = lane % LX
    ka = jnp.broadcast_to(ka_ref[...][None], shape)
    kb = jnp.broadcast_to(kb_ref[...][None], shape)

    def coeffs(k):
        k8 = lateral_weight * k
        return (
            k,
            1.0 - 2.0 * k - 4.0 * k8,
            jnp.where(lane >= LX, k8, 0.0),
            jnp.where(lane < lat - LX, k8, 0.0),
            jnp.where(col != 0, k8, 0.0),
            jnp.where(col != LX - 1, k8, 0.0),
        )

    ca, cb = coeffs(ka), coeffs(kb)
    first_a, last_a = row == 0, row == depth - 1
    first_b, last_b = row == HALO, row == HALO - 1

    def step(v, down, up, c):
        k, cself, c_xm, c_xp, c_ym, c_yp = c
        lateral = (
            c_xm * pltpu.roll(v, LX, 2)
            + c_xp * pltpu.roll(v, lat - LX, 2)
            + c_ym * pltpu.roll(v, 1, 2)
            + c_yp * pltpu.roll(v, lat - 1, 2)
        )
        return cself * v + k * (down + up) + lateral

    def body(i, carry):
        r = pl.multiple_of(i * sub, sub)
        a = a_ref[pl.ds(r, sub)].astype(jnp.float32)
        b = b_ref[pl.ds(r, sub)].astype(jnp.float32)
        for _ in range(PASSES):
            a_dn = jnp.where(first_a, pltpu.roll(b, depth - HALO + 1, 1), pltpu.roll(a, 1, 1))
            a_up = jnp.where(last_a, pltpu.roll(b, HALO - 1, 1), pltpu.roll(a, depth - 1, 1))
            b_dn = jnp.where(first_b, pltpu.roll(a, depth - HALO + 1, 1), pltpu.roll(b, 1, 1))
            b_up = jnp.where(last_b, pltpu.roll(a, HALO - 1, 1), pltpu.roll(b, depth - 1, 1))
            a, b = step(a, a_dn, a_up, ca), step(b, b_dn, b_up, cb)
        o_ref[pl.ds(r, sub)] = a
        return carry

    lax.fori_loop(0, a_ref.shape[0] // sub, body, 0)


def smooth(sensitivity, halo, kappa, kappa_halo, block=128, sub=2):
    rows, depth, lat = sensitivity.shape
    kernel = functools.partial(smooth_kernel, sub=sub)
    return pl.pallas_call(
        kernel,
        grid=(rows // block,),
        in_specs=[
            pl.BlockSpec((depth, lat), lambda i: (0, 0)),
            pl.BlockSpec((depth, lat), lambda i: (0, 0)),
            pl.BlockSpec((block, depth, lat), lambda i: (i, 0, 0)),
            pl.BlockSpec((block, depth, lat), lambda i: (i, 0, 0)),
        ],
        out_specs=pl.BlockSpec((block, depth, lat), lambda i: (i, 0, 0)),
        out_shape=jax.ShapeDtypeStruct((rows, depth, lat), jnp.float32),
    )(kappa, kappa_halo, sensitivity, halo)


def body(sensitivity, cell_class, class_rate, panel_owner):
    rows, depth, lat = sensitivity.shape
    onehot = (cell_class[..., None] == jnp.arange(class_rate.shape[0])[None, None, :]).astype(
        jnp.float32
    )
    kappa = jnp.sum(onehot * class_rate[None, None, :], axis=-1)
    halo = halo_of(sensitivity, "slab", 1)
    kappa_halo = halo_of(kappa, "slab", 0)
    field = smooth(sensitivity, halo, kappa, kappa_halo)
    cells = depth * lat * lax.axis_size("slab")
    flat = sensitivity.reshape(rows, depth * lat)
    partials = []
    for p in range(PANELS):
        piece = field[p * PANEL : (p + 1) * PANEL].reshape(PANEL, depth * lat).astype(jnp.bfloat16)
        received = from_root(piece, "dp", panel_owner[p])
        term = (
            lax.dot_general(
                flat, received, (((1,), (1,)), ((), ())), preferred_element_type=jnp.float32
            )
            / cells
        )
        partials.append(lax.psum_scatter(term, "slab", scatter_dimension=0, tiled=True))
    gram = jnp.stack(partials, axis=1)
    return (field, gram)


def solution(mesh):
    placed = (P("dp", "slab", None), P("slab", None), P(), P())
    return jax.shard_map(
        body,
        mesh=mesh,
        in_specs=placed,
        out_specs=(P("dp", "slab", None), P(("dp", "slab"), None, None)),
        check_vma=False,
    )
```

time: 639 us -> 605 us (0.947)
  Pallas kernels: 0 us -> 177 us
  local copies, waits for them, and re-layouts: 162 us -> 23.9 us
  other arithmetic: 86.3 us -> 9.3 us
  waiting for transfers between devices: 340 us -> 359 us
  starting transfers between devices: 22.1 us -> 8.87 us
    pallas_call x0 -> x1, Pallas kernels: none -> 177 us  [smooth(): pl.pallas_call(kernel, grid=(rows // block,), in_specs=[pl.BlockSpec((dep...]
    slice x20 -> x2, local copies, waits for them, and re-layouts: 115 us -> 6.09 us  [halo_of(): top = lax.slice_in_dim(shard, length - HALO, length, axis=dim)]
    add x3 -> x0, other arithmetic: 57.5 us -> none  [update(): field + rate * (depth_sum - 2.0 * field)]
    unnamed x28 -> x23, local copies, waits for them, and re-layouts: 39.5 us -> 17.2 us
    another operation x1, other arithmetic: 22.4 us -> 3.79 us
    ppermute x8 -> x4, starting transfers between devices: 21.9 us -> 8.7 us  [the longest x2 6.12 us: halo_of(): below = lax.ppermute(top, axis, up)]
    unnamed x7, waiting for transfers between devices: 185 us -> 194 us
    psum x1, waiting for transfers between devices: 155 us -> 164 us  [from_root(): return lax.psum(kept, axis)]
  transfers between devices with their start and end apart: 12 -> 8, of which waited for: 4 -> 5; matrix products, arithmetic and copies ran while one was open for 23% -> 3% of each run, Pallas kernels for 0% -> 0%
where the time goes in v1:
time: 605 us; the launch traced here: 604 us
  waiting for transfers between devices  359 us (59%)
  Pallas kernels  177 us (29%)
  local copies, waits for them, and re-layouts  23.9 us (4%)
  between operations  15.8 us (3%)
  matrix products  10.9 us (2%)
  other arithmetic  9.3 us (2%)
  starting transfers between devices  8.87 us (1%)
    unnamed x7, waiting for transfers between devices  194 us
    pallas_call x1, Pallas kernels, smooth(): pl.pallas_call(kernel, grid=(rows // block,), in_specs=[pl.BlockSpec((dep...  177 us
    psum x1, waiting for transfers between devices, from_root(): return lax.psum(kept, axis)  164 us
    unnamed x23, local copies, waits for them, and re-layouts  17.2 us
  transfers between devices with their start and end apart: 8, of which 5 were waited for; matrix products, arithmetic and copies ran while one was open for 3% of the time, Pallas kernels for 0%

profile of v1, /device:TPU:0, one launch (start us, length us, event | category | flops | bytes accessed | tf_op | source)
XLA Modules:
  0.0 604.4 jit_solution(12280993125169871492)
XLA Ops:
  7.2 0.0 copy-start.1
  7.2 0.0 copy-start.3
  7.2 0.0 copy-start.2
  7.2 0.0 all-reduce.3.cloned.1.call-start
  7.2 6.1 %fusion.3 = (bf16[1024,4,256]{2,1,0:T(4,128)(2,1)}, bf16[1024,4,256]{2,1,0:T(4,128)(2,1)}) fusion(bf16[1024,8,256]{2,1,0:T(8,128)(2,1)} %a_ref.1), kind=kLoop, calls=%fused_computation.14 | loop fusion | bytes 8388608 | tf_op jit(solution)/shard_map/slice | solution.py:28
  13.3 1.4 collective-permute-start.2
  14.7 1.3 collective-permute-start.3
  16.0 0.0 copy-done.1
  16.1 0.1 select_reduce_fusion.ka_ref
  16.2 0.0 copy-start
  16.2 4.7 collective-permute-start
  20.9 1.3 collective-permute-start.1
  22.2 0.0 copy-done.2
  22.2 0.6 fusion.5
  24.6 0.0 collective-permute-done
  24.6 0.6 collective-permute-done.1
  25.2 0.6 pad_maximum_fusion.2.kb_ref
  25.8 0.0 collective-permute-done.2
  25.8 0.0 collective-permute-done.3
  25.8 4.6 pad_maximum_fusion.b_ref
  30.4 177.0 %shard_map.59 = f32[1024,8,256]{2,1,0:T(8,128)} custom-call(f32[8,256]{1,0:T(8,128)} %copy-done, f32[8,256]{1,0:T(8,128)} %pad_maximum_fusion.2.kb_ref, bf16[1024,8,256]{2,1,0:T(8,128)(2,1)} %a_ref.1, bf16[1024,8,256]{2,1,0:T(8,128)(2,1)} %pad_maximum_fusion.b_ref), custom_call_target="tpu_custom_call" | custom-call | tf_op jit(solution)/shard_map/pallas_call | solution.py:88
  207.4 3.8 convert.5
  211.2 0.2 slice_select_fusion.2
  211.4 1.3 copy.15
  212.7 1.4 copy.17
  214.1 1.3 copy.18
  215.4 0.0 all-reduce.3.cloned.1.call-update
  215.4 0.0 reduce-scatter.10.cloned.1.call-start
  215.5 5.6 copy.16
  221.1 163.6 %all-reduce.3.cloned.1.call-done = (bf16[256,2048]{1,0:T(8,128)(2,1)}, bf16[256,2048]{1,0:T(8,128)(2,1)}, bf16[256,2048]{1,0:T(8,128)(2,1)}) async-done(((bf16[256,2048]{1,0:T(8,128)(2,1)}, bf16[256,2048]{1,0:T(8,128)(2,1)}, bf16[256,2048]{1,0:T(8,128)(2,1)}), (bf16[256,2048]{1,0:T(8,128)(2,1)}, bf16[256,2048]{1,0:T(8,128)(2,1)}, bf16[256,2048]{1,0:T(8,128)(2,1)})) %all-reduce.3.cloned.1.call-update) | async-done | bytes 3145744 | tf_op jit(solution)/shard_map/psum | solution.py:21
  384.7 3.9 fusion.2
  388.6 1.3 copy.9
  390.0 0.0 reduce-scatter.10.cloned.1.call-update
  390.0 0.0 reduce-scatter.12.cloned.1.call-start
  390.0 3.6 fusion.1
  393.6 1.3 copy.11
  395.0 0.0 reduce-scatter.12.cloned.1.call-update
  395.0 0.0 reduce-scatter.14.cloned.1.call-start
  395.0 3.5 fusion
  398.5 1.3 copy.13
  399.8 0.0 reduce-scatter.14.cloned.1.call-update
  399.8 56.5 %reduce-scatter.10.cloned.1.call-done = f32[64,256]{1,0:T(8,128)} async-done(((f32[1024,256]{1,0:T(8,128)}), f32[64,256]{1,0:T(8,128)}) %reduce-scatter.10.cloned.1.call-update) | async-done | bytes 65552
  456.4 0.9 copy.10
  457.3 69.3 %reduce-scatter.12.cloned.1.call-done = f32[64,256]{1,0:T(8,128)} async-done(((f32[1024,256]{1,0:T(8,128)}), f32[64,256]{1,0:T(8,128)}) %reduce-scatter.12.cloned.1.call-update) | async-done | bytes 65552
  526.6 0.9 copy.12
  527.5 68.6 %reduce-scatter.14.cloned.1.call-done = f32[64,256]{1,0:T(8,128)} async-done(((f32[1024,256]{1,0:T(8,128)}), f32[64,256]{1,0:T(8,128)}) %reduce-scatter.14.cloned.1.call-update) | async-done | bytes 65552
  596.1 0.9 copy.14
  597.1 0.8 copy.8
  (8 shorter events, 0.0 us)
Async XLA Ops:
  7.2 8.9 %copy-start.1 = (s32[8,256]{1,0:T(8,128)S(1)}, s32[8,256]{1,0:T(8,128)}, u32[]{:S(2)}) copy-start(s32[8,256]{1,0:T(8,128)} %param.5) | copy-start | bytes 24580
  7.2 8.9 %copy-start.3 = (f32[8]{0:T(128)S(1)}, f32[8]{0:T(128)}, u32[]{:S(2)}) copy-start(f32[8]{0:T(128)} %param.6) | copy-start | bytes 100
  7.2 15.0 %copy-start.2 = (s32[8]{0:T(128)S(1)}, s32[8]{0:T(128)}, u32[]{:S(2)}) copy-start(s32[8]{0:T(128)} %param.7) | copy-start | bytes 100
  7.2 377.5 %all-reduce.3.cloned.1.call-start = ((), (), s32[]{:S(2)}) async-start(), calls=%async_computation.6 | async-start | bytes 6291456 | tf_op jit(solution)/shard_map/psum | solution.py:21
  13.3 12.5 %collective-permute-start.2 = (bf16[1024,4,256]{2,1,0:T(4,128)(2,1)}, bf16[1024,4,256]{2,1,0:T(4,128)(2,1)S(1)}, u32[]{:S(2)}, u32[]{:S(2)}) collective-permute-start(bf16[1024,4,256]{2,1,0:T(4,128)(2,1)} %get-tuple-element.14), channel_id=1, source_target_pairs={{0,1},{1,2},{2,3},{3,4},{4,5},{5,6},{6,7},{7,8},{8,9},{9,10},{10,1... | collective-permute-start | bytes 6291464 | tf_op jit(solution)/shard_map/ppermute | solution.py:30
  14.7 11.1 %collective-permute-start.3 = (bf16[1024,4,256]{2,1,0:T(4,128)(2,1)}, bf16[1024,4,256]{2,1,0:T(4,128)(2,1)}, u32[]{:S(2)}, u32[]{:S(2)}) collective-permute-start(bf16[1024,4,256]{2,1,0:T(4,128)(2,1)} %get-tuple-element.15), channel_id=1, source_target_pairs={{1,0},{2,1},{3,2},{4,3},{5,4},{6,5},{7,6},{8,7},{9,8},{10,9},{11,1... | collective-permute-start | bytes 6291464 | tf_op jit(solution)/shard_map/ppermute | solution.py:31
  16.2 14.2 %copy-start = (f32[8,256]{1,0:T(8,128)}, f32[8,256]{1,0:T(8,128)S(1)}, u32[]{:S(2)}) copy-start(f32[8,256]{1,0:T(8,128)S(1)} %select_reduce_fusion.ka_ref) | copy-start | bytes 24580
  16.2 8.4 %collective-permute-start = (f32[4,256]{1,0:T(4,128)S(1)}, f32[4,256]{1,0:T(4,128)S(1)}, u32[]{:S(2)}, u32[]{:S(2)}) collective-permute-start(f32[4,256]{1,0:T(4,128)S(1)} %get-tuple-element.16), channel_id=1, source_target_pairs={{0,1},{1,2},{2,3},{3,4},{4,5},{5,6},{6,7},{7,8},{8,9},{9,10},{10,1... | collective-permute-start | bytes 12296 | tf_op jit(solution)/shard_map/ppermute | solution.py:30
  20.9 4.3 collective-permute-start.1
  215.4 240.9 %reduce-scatter.10.cloned.1.call-start = ((), (), s32[]{:S(2)}) async-start(), calls=%async_computation.3 | async-start | bytes 1114112
  384.7 5.3 copy-start.5
  390.0 136.6 %reduce-scatter.12.cloned.1.call-start = ((), (), s32[]{:S(2)}) async-start(), calls=%async_computation.4 | async-start | bytes 1114112
  390.0 5.0 copy-start.4
  395.0 201.1 %reduce-scatter.14.cloned.1.call-start = ((), (), s32[]{:S(2)}) async-start(), calls=%async_computation.5 | async-start | bytes 1114112
Sparse Core Ops, SparseCore 0:
  215.5 169.1 all-reduce.2
  390.1 66.2 reduce-scatter.9
  460.7 65.8 reduce-scatter.11
  530.2 65.8 reduce-scatter.13

commit v2 on v1

--- a/solution.py
+++ b/solution.py
@@ -16,9 +16,34 @@
 lateral_weight = 0.125
 
 
-def from_root(value, axis, source):
-    kept = jnp.where(lax.axis_index(axis) == source, value, 0).astype(value.dtype)
-    return lax.psum(kept, axis)
+def broadcast_dp(piece, owner, axis):
+    size = lax.axis_size(axis)
+    me = lax.axis_index(axis)
+    ring = size // 2
+    z, oz = me // 2, owner // 2
+    pair = lax.ppermute(piece, axis, [(i, i ^ 1) for i in range(size)])
+    val = jnp.where(me == owner, piece, pair)
+    from_below = lax.ppermute(val, axis, [(i, (i + 2) % size) for i in range(size)])
+    from_above = lax.ppermute(val, axis, [(i, (i - 2) % size) for i in range(size)])
+    val = jnp.where(z == oz, val, jnp.where(z == (oz + 1) % ring, from_below, from_above))
+    last = lax.ppermute(val, axis, [(i, (i + 2) % size) for i in range(size)])
+    return jnp.where(z == (oz + 2) % ring, last, val)
+
+
+def reduce_scatter_slab(term, axis):
+    size = lax.axis_size(axis)
+    me = lax.axis_index(axis)
+    rows = term.shape[0] // size
+    part = term.reshape((size, rows) + term.shape[1:])
+    bit = 1
+    while bit < size:
+        mine = (me // bit) % 2
+        halves = part.reshape((part.shape[0] // 2, 2) + part.shape[1:])
+        keep = lax.dynamic_index_in_dim(halves, mine, axis=1, keepdims=False)
+        send = lax.dynamic_index_in_dim(halves, 1 - mine, axis=1, keepdims=False)
+        part = keep + lax.ppermute(send, axis, [(i, i ^ bit) for i in range(size)])
+        bit *= 2
+    return part.reshape((rows,) + term.shape[1:])
 
 
 def halo_of(shard, axis, dim):
@@ -113,14 +138,14 @@
     partials = []
     for p in range(PANELS):
         piece = field[p * PANEL : (p + 1) * PANEL].reshape(PANEL, depth * lat).astype(jnp.bfloat16)
-        received = from_root(piece, "dp", panel_owner[p])
+        received = broadcast_dp(piece, panel_owner[p], "dp")
         term = (
             lax.dot_general(
                 flat, received, (((1,), (1,)), ((), ())), preferred_element_type=jnp.float32
             )
             / cells
         )
-        partials.append(lax.psum_scatter(term, "slab", scatter_dimension=0, tiled=True))
+        partials.append(reduce_scatter_slab(term, "slab"))
     gram = jnp.stack(partials, axis=1)
     return (field, gram)
 

time: 605 us -> 433 us (0.72)
  waiting for transfers between devices: 359 us -> 75 us
  starting transfers between devices: 8.87 us -> 125 us
    unnamed x7 -> x0, waiting for transfers between devices: 194 us -> none
    psum x1 -> x0, waiting for transfers between devices: 164 us -> none  [from_root(): return lax.psum(kept, axis)]
    ppermute x0 -> x24, starting transfers between devices: none -> 116 us  [the longest x12 96.9 us: reduce_scatter_slab(): part = keep + lax.ppermute(send, axis, [(i, i ^ bit) for i in range(size)])]
    ppermute x0 -> x24, waiting for transfers between devices: none -> 72 us  [the longest x3 22.7 us: broadcast_dp(): pair = lax.ppermute(piece, axis, [(i, i ^ 1) for i in range(size)])]
    unnamed x23 -> x14, local copies, waits for them, and re-layouts: 17.2 us -> 6.56 us
  transfers between devices with their start and end apart: 8 -> 28, of which waited for: 5 -> 12; matrix products, arithmetic and copies ran while one was open for 3% -> 7% of each run, Pallas kernels for 0% -> 0%
where the time goes in v2:
time: 433 us; the launch traced here: 432 us
  Pallas kernels  177 us (41%)
  starting transfers between devices  125 us (29%)
  waiting for transfers between devices  75 us (17%)
  local copies, waits for them, and re-layouts  18.8 us (4%)
  other arithmetic  14.5 us (3%)
  matrix products  11.5 us (3%)
  between operations  10.3 us (2%)
    pallas_call x1, Pallas kernels, smooth(): pl.pallas_call(kernel, grid=(rows // block,), in_specs=[pl.BlockSpec((dep...  177 us
    ppermute x12, starting transfers between devices, reduce_scatter_slab(): part = keep + lax.ppermute(send, axis, [(i, i ^ bit) for i in range(size)])  96.9 us
    ppermute x3, waiting for transfers between devices, broadcast_dp(): pair = lax.ppermute(piece, axis, [(i, i ^ 1) for i in range(size)])  22.7 us
    ppermute x3, waiting for transfers between devices, broadcast_dp(): last = lax.ppermute(val, axis, [(i, (i + 2) % size) for i in range(size)])  18.5 us
    ppermute x3, waiting for transfers between devices, broadcast_dp(): lax.ppermute(val, axis, [(i, (i + 2) % size) for i in range(size)])  18.5 us
    dot_general x3, matrix products, body(): lax.dot_general(flat, received, (((1,), (1,)), ((), ())), preferred_eleme...  11.5 us
    ppermute x12, waiting for transfers between devices, reduce_scatter_slab(): part = keep + lax.ppermute(send, axis, [(i, i ^ bit) for i in range(size)])  10.6 us
  transfers between devices with their start and end apart: 28, of which 12 were waited for; matrix products, arithmetic and copies ran while one was open for 7% of the time, Pallas kernels for 0%

profile of v2, /device:TPU:0, one launch (start us, length us, event | category | flops | bytes accessed | tf_op | source)
XLA Modules:
  0.0 432.1 jit_solution(15477830325618487961)
XLA Ops:
  0.6 4.8 %fusion.10 = (bf16[1024,4,256]{2,1,0:T(4,128)(2,1)S(1)}, bf16[1024,4,256]{2,1,0:T(4,128)(2,1)S(1)}) fusion(bf16[1024,8,256]{2,1,0:T(8,128)(2,1)} %a_ref.1), kind=kLoop, calls=%fused_computation.48 | loop fusion | bytes 8388608 | tf_op jit(solution)/shard_map/slice | solution.py:53
  5.5 1.4 collective-permute-start.2
  6.9 1.3 collective-permute-start.3
  8.3 4.7 %collective-permute-start = (f32[4,256]{1,0:T(4,128)S(1)}, f32[4,256]{1,0:T(4,128)S(1)}, u32[]{:S(2)}, u32[]{:S(2)}) collective-permute-start(f32[4,256]{1,0:T(4,128)S(1)} %get-tuple-element.7), channel_id=1, source_target_pairs={{0,1},{1,2},{2,3},{3,4},{4,5},{5,6},{6,7},{7,8},{8,9},{9,10},{10,1... | collective-permute-start | bytes 12296 | tf_op jit(solution)/shard_map/ppermute | solution.py:55
  13.0 1.3 collective-permute-start.1
  14.3 3.0 collective-permute-done.1
  17.9 3.4 pad_maximum_fusion.b_ref
  21.4 177.0 %shard_map.59 = f32[1024,8,256]{2,1,0:T(8,128)} custom-call(f32[8,256]{1,0:T(8,128)} %copy-done.1, f32[8,256]{1,0:T(8,128)} %pad_maximum_fusion.2.kb_ref, bf16[1024,8,256]{2,1,0:T(8,128)(2,1)} %a_ref.1, bf16[1024,8,256]{2,1,0:T(8,128)(2,1)} %pad_maximum_fusion.b_ref), custom_call_target="tpu_custom_call" | custom-call | tf_op jit(solution)/shard_map/pallas_call | solution.py:113
  198.4 3.8 convert.5
  202.7 1.7 collective-permute-start.4
  215.2 5.6 %copy.16 = bf16[128,8,8,256]{3,1,2,0:T(8,128)(2,1)} copy(bf16[128,8,8,256]{3,2,1,0:T(8,128)(2,1)} %bitcast.71) | data formatting | bytes 8388608
  221.1 1.7 collective-permute-start.20
  222.8 1.3 broadcast_select_fusion.2
  224.1 2.0 collective-permute-start.5
  226.1 1.3 collective-permute-start.6
  227.4 5.8 %collective-permute-done.12 = bf16[256,2048]{1,0:T(8,128)(2,1)} collective-permute-done((bf16[256,2048]{1,0:T(8,128)(2,1)S(1)}, bf16[256,2048]{1,0:T(8,128)(2,1)}, u32[]{:S(2)}, u32[]{:S(2)}) %collective-permute-start.12) | collective-permute-done | bytes 1048608 | tf_op jit(solution)/shard_map/ppermute | solution.py:24
  233.2 1.3 broadcast_select_fusion.1
  234.6 2.0 collective-permute-start.13
  236.5 2.2 collective-permute-start.14
  238.7 16.8 %collective-permute-done.20 = bf16[256,2048]{1,0:T(8,128)(2,1)S(1)} collective-permute-done((bf16[256,2048]{1,0:T(8,128)(2,1)S(1)}, bf16[256,2048]{1,0:T(8,128)(2,1)S(1)}, u32[]{:S(2)}, u32[]{:S(2)}) %collective-permute-start.20) | collective-permute-done | bytes 1048608 | tf_op jit(solution)/shard_map/ppermute | solution.py:24
  255.7 2.0 collective-permute-start.21
  257.7 2.2 collective-permute-start.22
  260.4 1.8 collective-permute-start.15
  262.2 18.5 %collective-permute-done.21 = bf16[256,2048]{1,0:T(8,128)(2,1)S(1)} collective-permute-done((bf16[256,2048]{1,0:T(8,128)(2,1)S(1)}, bf16[256,2048]{1,0:T(8,128)(2,1)S(1)}, u32[]{:S(2)}, u32[]{:S(2)}) %collective-permute-start.21) | collective-permute-done | bytes 1048608 | tf_op jit(solution)/shard_map/ppermute | solution.py:26
  280.7 1.7 collective-permute-done.22
  282.6 2.0 collective-permute-start.23
  284.6 18.5 %collective-permute-done.7 = bf16[256,2048]{1,0:T(8,128)(2,1)S(1)} collective-permute-done((bf16[256,2048]{1,0:T(8,128)(2,1)S(1)}, bf16[256,2048]{1,0:T(8,128)(2,1)S(1)}, u32[]{:S(2)}, u32[]{:S(2)}) %collective-permute-start.7) | collective-permute-done | bytes 1048608 | tf_op jit(solution)/shard_map/ppermute | solution.py:29
  303.2 2.2 fusion.2
  305.4 1.6 copy.12
  307.8 33.5 %collective-permute-start.8 = (f32[8,64,256]{2,1,0:T(8,128)}, f32[8,64,256]{2,1,0:T(8,128)}, u32[]{:S(2)}, u32[]{:S(2)}) collective-permute-start(f32[8,64,256]{2,1,0:T(8,128)} %dynamic-slice_bitcast_fusion.2), channel_id=1, source_target_pairs={{0,1},{1,0},{2,3},{3,2},{4,5},{5,4},{6,7},{7,6},{8,9},{9,8},{10,11... | collective-permute-start | bytes 1572872 | tf_op jit(solution)/shard_map/ppermute | solution.py:44
  341.3 4.8 %fusion.1 = f32[1024,256]{0,1:T(8,128)} fusion(bf16[1024,2048]{1,0:T(8,128)(2,1)} %bitcast.72, bf16[256,2048]{1,0:T(8,128)(2,1)} %collective-permute-done.15, bf16[256,2048]{1,0:T(8,128)(2,1)S(1)} %select_select_fusion.1, pred[]{:T(512)S(6)} %eq.75), kind=kOutput, calls=%fused_computation.4 | convolution fusion | flops 1074528256 | bytes 7340033 | tf_op jit(solution)/shard_map/dot_general | solution.py:143
  346.1 1.6 copy.13
  348.5 12.1 %collective-permute-start.16 = (f32[8,64,256]{2,1,0:T(8,128)}, f32[8,64,256]{2,1,0:T(8,128)}, u32[]{:S(2)}, u32[]{:S(2)}) collective-permute-start(f32[8,64,256]{2,1,0:T(8,128)} %dynamic-slice_bitcast_fusion.1), channel_id=1, source_target_pairs={{0,1},{1,0},{2,3},{3,2},{4,5},{5,4},{6,7},{7,6},{8,9},{9,8},{10,11... | collective-permute-start | bytes 1572872 | tf_op jit(solution)/shard_map/ppermute | solution.py:44
  360.6 4.5 %fusion = f32[1024,256]{0,1:T(8,128)} fusion(bf16[1024,2048]{1,0:T(8,128)(2,1)} %bitcast.73, bf16[256,2048]{1,0:T(8,128)(2,1)} %collective-permute-done.23, bf16[256,2048]{1,0:T(8,128)(2,1)S(1)} %select_select_fusion, pred[]{:T(512)S(6)} %eq.79), kind=kOutput, calls=%fused_computation.2 | convolution fusion | flops 1074528256 | bytes 7340033 | tf_op jit(solution)/shard_map/dot_general | solution.py:143
  365.1 1.6 copy.14
  366.7 4.2 collective-permute-start.24
  372.0 24.2 %collective-permute-start.9 = (f32[4,64,256]{2,1,0:T(8,128)S(1)}, f32[4,64,256]{2,1,0:T(8,128)S(1)}, u32[]{:S(2)}, u32[]{:S(2)}) collective-permute-start(f32[4,64,256]{2,1,0:T(8,128)S(1)} %dynamic-slice_bitcast_fusion.5), channel_id=1, source_target_pairs={{0,2},{1,3},{2,0},{3,1},{4,6},{5,7},{6,4},{7,5},{8,10},{9,11},{10,... | collective-permute-start | bytes 786440 | tf_op jit(solution)/shard_map/ppermute | solution.py:44
  397.5 2.1 collective-permute-start.25
  399.6 3.7 collective-permute-done.9
  403.3 4.1 collective-permute-start.10
  407.4 1.4 collective-permute-done.17
  409.0 4.1 collective-permute-start.18
  413.1 1.4 collective-permute-done.25
  414.6 4.1 collective-permute-start.26
  419.4 3.3 collective-permute-start.11
  422.7 2.8 collective-permute-start.19
  425.5 2.5 collective-permute-start.27
  428.6 2.8 collective-permute-done.27
  (68 shorter events, 10.3 us)
Async XLA Ops:
  0.6 7.6 %copy-start.2 = (s32[8,256]{1,0:T(8,128)S(1)}, s32[8,256]{1,0:T(8,128)}, u32[]{:S(2)}) copy-start(s32[8,256]{1,0:T(8,128)} %param.5) | copy-start | bytes 24580
  0.6 7.6 %copy-start.4 = (f32[8]{0:T(128)S(1)}, f32[8]{0:T(128)}, u32[]{:S(2)}) copy-start(f32[8]{0:T(128)} %param.6) | copy-start | bytes 100
  5.5 12.5 %collective-permute-start.2 = (bf16[1024,4,256]{2,1,0:T(4,128)(2,1)S(1)}, bf16[1024,4,256]{2,1,0:T(4,128)(2,1)S(1)}, u32[]{:S(2)}, u32[]{:S(2)}) collective-permute-start(bf16[1024,4,256]{2,1,0:T(4,128)(2,1)S(1)} %get-tuple-element.5), channel_id=1, source_target_pairs={{0,1},{1,2},{2,3},{3,4},{4,5},{5,6},{6,7},{7,8},{8,9},{9,10},{10,1... | collective-permute-start | bytes 6291464 | tf_op jit(solution)/shard_map/ppermute | solution.py:55
  6.9 11.1 %collective-permute-start.3 = (bf16[1024,4,256]{2,1,0:T(4,128)(2,1)S(1)}, bf16[1024,4,256]{2,1,0:T(4,128)(2,1)S(1)}, u32[]{:S(2)}, u32[]{:S(2)}) collective-permute-start(bf16[1024,4,256]{2,1,0:T(4,128)(2,1)S(1)} %get-tuple-element.6), channel_id=1, source_target_pairs={{1,0},{2,1},{3,2},{4,3},{5,4},{6,5},{7,6},{8,7},{9,8},{10,9},{11,1... | collective-permute-start | bytes 6291464 | tf_op jit(solution)/shard_map/ppermute | solution.py:56
  8.3 13.1 %copy-start.1 = (f32[8,256]{1,0:T(8,128)}, f32[8,256]{1,0:T(8,128)S(1)}, u32[]{:S(2)}) copy-start(f32[8,256]{1,0:T(8,128)S(1)} %select_reduce_fusion.ka_ref) | copy-start | bytes 24580
  8.3 6.0 %collective-permute-start = (f32[4,256]{1,0:T(4,128)S(1)}, f32[4,256]{1,0:T(4,128)S(1)}, u32[]{:S(2)}, u32[]{:S(2)}) collective-permute-start(f32[4,256]{1,0:T(4,128)S(1)} %get-tuple-element.7), channel_id=1, source_target_pairs={{0,1},{1,2},{2,3},{3,4},{4,5},{5,6},{6,7},{7,8},{8,9},{9,10},{10,1... | collective-permute-start | bytes 12296 | tf_op jit(solution)/shard_map/ppermute | solution.py:55
  13.0 4.3 collective-permute-start.1
  202.2 3.0 copy-start.3
  202.7 20.0 %collective-permute-start.4 = (bf16[256,2048]{1,0:T(8,128)(2,1)S(1)}, bf16[256,2048]{1,0:T(8,128)(2,1)}, u32[]{:S(2)}, u32[]{:S(2)}) collective-permute-start(bf16[256,2048]{1,0:T(8,128)(2,1)S(1)} %bitcast.77), channel_id=1, source_target_pairs={{0,16},{16,0},{32,48},{48,32},{64,80},{80,64},{96,112},{112,96},{1... | collective-permute-start | bytes 3145736 | tf_op jit(solution)/shard_map/ppermute | solution.py:24
  204.7 28.5 %collective-permute-start.12 = (bf16[256,2048]{1,0:T(8,128)(2,1)S(1)}, bf16[256,2048]{1,0:T(8,128)(2,1)}, u32[]{:S(2)}, u32[]{:S(2)}) collective-permute-start(bf16[256,2048]{1,0:T(8,128)(2,1)S(1)} %bitcast.75), channel_id=1, source_target_pairs={{0,16},{16,0},{32,48},{48,32},{64,80},{80,64},{96,112},{112,96},{1... | collective-permute-start | bytes 3145736 | tf_op jit(solution)/shard_map/ppermute | solution.py:24
  221.1 34.5 %collective-permute-start.20 = (bf16[256,2048]{1,0:T(8,128)(2,1)S(1)}, bf16[256,2048]{1,0:T(8,128)(2,1)S(1)}, u32[]{:S(2)}, u32[]{:S(2)}) collective-permute-start(bf16[256,2048]{1,0:T(8,128)(2,1)S(1)} %bitcast.81), channel_id=1, source_target_pairs={{0,16},{16,0},{32,48},{48,32},{64,80},{80,64},{96,112},{112,96},{1... | collective-permute-start | bytes 3145736 | tf_op jit(solution)/shard_map/ppermute | solution.py:24
  224.1 33.6 %collective-permute-start.5 = (bf16[256,2048]{1,0:T(8,128)(2,1)S(1)}, bf16[256,2048]{1,0:T(8,128)(2,1)S(1)}, u32[]{:S(2)}, u32[]{:S(2)}) collective-permute-start(bf16[256,2048]{1,0:T(8,128)(2,1)S(1)} %broadcast_select_fusion.2), channel_id=1, source_target_pairs={{0,32},{16,48},{32,64},{48,80},{64,96},{80,112},{96,0},{112,16},{1... | collective-permute-start | bytes 3145736 | tf_op jit(solution)/shard_map/ppermute | solution.py:26
  226.1 33.8 %collective-permute-start.6 = (bf16[256,2048]{1,0:T(8,128)(2,1)S(1)}, bf16[256,2048]{1,0:T(8,128)(2,1)S(1)}, u32[]{:S(2)}, u32[]{:S(2)}) collective-permute-start(bf16[256,2048]{1,0:T(8,128)(2,1)S(1)} %broadcast_select_fusion.2), channel_id=1, source_target_pairs={{0,96},{16,112},{32,0},{48,16},{64,32},{80,48},{96,64},{112,80},{1... | collective-permute-start | bytes 3145736 | tf_op jit(solution)/shard_map/ppermute | solution.py:27
  234.6 25.6 %collective-permute-start.13 = (bf16[256,2048]{1,0:T(8,128)(2,1)S(1)}, bf16[256,2048]{1,0:T(8,128)(2,1)S(1)}, u32[]{:S(2)}, u32[]{:S(2)}) collective-permute-start(bf16[256,2048]{1,0:T(8,128)(2,1)S(1)} %broadcast_select_fusion.1), channel_id=1, source_target_pairs={{0,32},{16,48},{32,64},{48,80},{64,96},{80,112},{96,0},{112,16},{1... | collective-permute-start | bytes 3145736 | tf_op jit(solution)/shard_map/ppermute | solution.py:26
  236.5 23.6 %collective-permute-start.14 = (bf16[256,2048]{1,0:T(8,128)(2,1)S(1)}, bf16[256,2048]{1,0:T(8,128)(2,1)S(1)}, u32[]{:S(2)}, u32[]{:S(2)}) collective-permute-start(bf16[256,2048]{1,0:T(8,128)(2,1)S(1)} %broadcast_select_fusion.1), channel_id=1, source_target_pairs={{0,96},{16,112},{32,0},{48,16},{64,32},{80,48},{96,64},{112,80},{1... | collective-permute-start | bytes 3145736 | tf_op jit(solution)/shard_map/ppermute | solution.py:27
  255.7 25.0 %collective-permute-start.21 = (bf16[256,2048]{1,0:T(8,128)(2,1)S(1)}, bf16[256,2048]{1,0:T(8,128)(2,1)S(1)}, u32[]{:S(2)}, u32[]{:S(2)}) collective-permute-start(bf16[256,2048]{1,0:T(8,128)(2,1)S(1)} %broadcast_select_fusion), channel_id=1, source_target_pairs={{0,32},{16,48},{32,64},{48,80},{64,96},{80,112},{96,0},{112,16},{1... | collective-permute-start | bytes 3145736 | tf_op jit(solution)/shard_map/ppermute | solution.py:26
  257.7 24.7 %collective-permute-start.22 = (bf16[256,2048]{1,0:T(8,128)(2,1)S(1)}, bf16[256,2048]{1,0:T(8,128)(2,1)S(1)}, u32[]{:S(2)}, u32[]{:S(2)}) collective-permute-start(bf16[256,2048]{1,0:T(8,128)(2,1)S(1)} %broadcast_select_fusion), channel_id=1, source_target_pairs={{0,96},{16,112},{32,0},{48,16},{64,32},{80,48},{96,64},{112,80},{1... | collective-permute-start | bytes 3145736 | tf_op jit(solution)/shard_map/ppermute | solution.py:27
  260.0 43.1 %copy-start = (bf16[128,8,8,256]{3,1,2,0:T(8,128)(2,1)S(1)}, bf16[128,8,8,256]{3,1,2,0:T(8,128)(2,1)}, u32[]{:S(2)}) copy-start(bf16[128,8,8,256]{3,1,2,0:T(8,128)(2,1)} %copy.16) | copy-start | bytes 12582916
  260.0 43.1 %collective-permute-start.7 = (bf16[256,2048]{1,0:T(8,128)(2,1)S(1)}, bf16[256,2048]{1,0:T(8,128)(2,1)S(1)}, u32[]{:S(2)}, u32[]{:S(2)}) collective-permute-start(bf16[256,2048]{1,0:T(8,128)(2,1)S(1)} %select_select_fusion.2), channel_id=1, source_target_pairs={{0,32},{16,48},{32,64},{48,80},{64,96},{80,112},{96,0},{112,16},{1... | collective-permute-start | bytes 3145736 | tf_op jit(solution)/shard_map/ppermute | solution.py:29
  260.4 80.9 %collective-permute-start.15 = (bf16[256,2048]{1,0:T(8,128)(2,1)S(1)}, bf16[256,2048]{1,0:T(8,128)(2,1)}, u32[]{:S(2)}, u32[]{:S(2)}) collective-permute-start(bf16[256,2048]{1,0:T(8,128)(2,1)S(1)} %select_select_fusion.1), channel_id=1, source_target_pairs={{0,32},{16,48},{32,64},{48,80},{64,96},{80,112},{96,0},{112,16},{1... | collective-permute-start | bytes 3145736 | tf_op jit(solution)/shard_map/ppermute | solution.py:29
  282.6 78.0 %collective-permute-start.23 = (bf16[256,2048]{1,0:T(8,128)(2,1)S(1)}, bf16[256,2048]{1,0:T(8,128)(2,1)}, u32[]{:S(2)}, u32[]{:S(2)}) collective-permute-start(bf16[256,2048]{1,0:T(8,128)(2,1)S(1)} %select_select_fusion), channel_id=1, source_target_pairs={{0,32},{16,48},{32,64},{48,80},{64,96},{80,112},{96,0},{112,16},{1... | collective-permute-start | bytes 3145736 | tf_op jit(solution)/shard_map/ppermute | solution.py:29
  307.8 63.0 %collective-permute-start.8 = (f32[8,64,256]{2,1,0:T(8,128)}, f32[8,64,256]{2,1,0:T(8,128)}, u32[]{:S(2)}, u32[]{:S(2)}) collective-permute-start(f32[8,64,256]{2,1,0:T(8,128)} %dynamic-slice_bitcast_fusion.2), channel_id=1, source_target_pairs={{0,1},{1,0},{2,3},{3,2},{4,5},{5,4},{6,7},{7,6},{8,9},{9,8},{10,11... | collective-permute-start | bytes 1572872 | tf_op jit(solution)/shard_map/ppermute | solution.py:44
  348.5 47.7 %collective-permute-start.16 = (f32[8,64,256]{2,1,0:T(8,128)}, f32[8,64,256]{2,1,0:T(8,128)}, u32[]{:S(2)}, u32[]{:S(2)}) collective-permute-start(f32[8,64,256]{2,1,0:T(8,128)} %dynamic-slice_bitcast_fusion.1), channel_id=1, source_target_pairs={{0,1},{1,0},{2,3},{3,2},{4,5},{5,4},{6,7},{7,6},{8,9},{9,8},{10,11... | collective-permute-start | bytes 1572872 | tf_op jit(solution)/shard_map/ppermute | solution.py:44
  366.7 30.7 %collective-permute-start.24 = (f32[8,64,256]{2,1,0:T(8,128)S(1)}, f32[8,64,256]{2,1,0:T(8,128)S(1)}, u32[]{:S(2)}, u32[]{:S(2)}) collective-permute-start(f32[8,64,256]{2,1,0:T(8,128)S(1)} %dynamic-slice_bitcast_fusion), channel_id=1, source_target_pairs={{0,1},{1,0},{2,3},{3,2},{4,5},{5,4},{6,7},{7,6},{8,9},{9,8},{10,11... | collective-permute-start | bytes 1572872 | tf_op jit(solution)/shard_map/ppermute | solution.py:44
  372.0 31.3 %collective-permute-start.9 = (f32[4,64,256]{2,1,0:T(8,128)S(1)}, f32[4,64,256]{2,1,0:T(8,128)S(1)}, u32[]{:S(2)}, u32[]{:S(2)}) collective-permute-start(f32[4,64,256]{2,1,0:T(8,128)S(1)} %dynamic-slice_bitcast_fusion.5), channel_id=1, source_target_pairs={{0,2},{1,3},{2,0},{3,1},{4,6},{5,7},{6,4},{7,5},{8,10},{9,11},{10,... | collective-permute-start | bytes 786440 | tf_op jit(solution)/shard_map/ppermute | solution.py:44
  397.3 11.6 %collective-permute-start.17 = (f32[4,64,256]{2,1,0:T(8,128)S(1)}, f32[4,64,256]{2,1,0:T(8,128)S(1)}, u32[]{:S(2)}, u32[]{:S(2)}) collective-permute-start(f32[4,64,256]{2,1,0:T(8,128)S(1)} %dynamic-slice_bitcast_fusion.4), channel_id=1, source_target_pairs={{0,2},{1,3},{2,0},{3,1},{4,6},{5,7},{6,4},{7,5},{8,10},{9,11},{10,... | collective-permute-start | bytes 786440 | tf_op jit(solution)/shard_map/ppermute | solution.py:44
  397.5 17.0 %collective-permute-start.25 = (f32[4,64,256]{2,1,0:T(8,128)S(1)}, f32[4,64,256]{2,1,0:T(8,128)S(1)}, u32[]{:S(2)}, u32[]{:S(2)}) collective-permute-start(f32[4,64,256]{2,1,0:T(8,128)S(1)} %dynamic-slice_bitcast_fusion.3), channel_id=1, source_target_pairs={{0,2},{1,3},{2,0},{3,1},{4,6},{5,7},{6,4},{7,5},{8,10},{9,11},{10,... | collective-permute-start | bytes 786440 | tf_op jit(solution)/shard_map/ppermute | solution.py:44
  403.3 16.0 %collective-permute-start.10 = (f32[2,64,256]{2,1,0:T(8,128)S(1)}, f32[2,64,256]{2,1,0:T(8,128)S(1)}, u32[]{:S(2)}, u32[]{:S(2)}) collective-permute-start(f32[2,64,256]{2,1,0:T(8,128)S(1)} %dynamic-slice_bitcast_fusion.8), channel_id=1, source_target_pairs={{0,4},{1,5},{2,6},{3,7},{4,0},{5,1},{6,2},{7,3},{8,12},{9,13},{10,... | collective-permute-start | bytes 393224 | tf_op jit(solution)/shard_map/ppermute | solution.py:44
  409.0 13.7 %collective-permute-start.18 = (f32[2,64,256]{2,1,0:T(8,128)S(1)}, f32[2,64,256]{2,1,0:T(8,128)S(1)}, u32[]{:S(2)}, u32[]{:S(2)}) collective-permute-start(f32[2,64,256]{2,1,0:T(8,128)S(1)} %dynamic-slice_bitcast_fusion.7), channel_id=1, source_target_pairs={{0,4},{1,5},{2,6},{3,7},{4,0},{5,1},{6,2},{7,3},{8,12},{9,13},{10,... | collective-permute-start | bytes 393224 | tf_op jit(solution)/shard_map/ppermute | solution.py:44
  414.6 10.9 %collective-permute-start.26 = (f32[2,64,256]{2,1,0:T(8,128)S(1)}, f32[2,64,256]{2,1,0:T(8,128)S(1)}, u32[]{:S(2)}, u32[]{:S(2)}) collective-permute-start(f32[2,64,256]{2,1,0:T(8,128)S(1)} %dynamic-slice_bitcast_fusion.6), channel_id=1, source_target_pairs={{0,4},{1,5},{2,6},{3,7},{4,0},{5,1},{6,2},{7,3},{8,12},{9,13},{10,... | collective-permute-start | bytes 393224 | tf_op jit(solution)/shard_map/ppermute | solution.py:44
  419.4 8.6 %collective-permute-start.11 = (f32[1,64,256]{2,1,0:T(8,128)S(1)}, f32[1,64,256]{2,1,0:T(8,128)S(1)}, u32[]{:S(2)}, u32[]{:S(2)}) collective-permute-start(f32[1,64,256]{2,1,0:T(8,128)S(1)} %constant_dynamic-slice_fusion.2), channel_id=1, source_target_pairs={{0,8},{1,9},{2,10},{3,11},{4,12},{5,13},{6,14},{7,15},{8,0},{9,1},... | collective-permute-start | bytes 196616 | tf_op jit(solution)/shard_map/ppermute | solution.py:44
  422.7 5.8 %collective-permute-start.19 = (f32[1,64,256]{2,1,0:T(8,128)S(1)}, f32[1,64,256]{2,1,0:T(8,128)S(1)}, u32[]{:S(2)}, u32[]{:S(2)}) collective-permute-start(f32[1,64,256]{2,1,0:T(8,128)S(1)} %constant_dynamic-slice_fusion.1), channel_id=1, source_target_pairs={{0,8},{1,9},{2,10},{3,11},{4,12},{5,13},{6,14},{7,15},{8,0},{9,1},... | collective-permute-start | bytes 196616 | tf_op jit(solution)/shard_map/ppermute | solution.py:44
  425.5 5.8 %collective-permute-start.27 = (f32[1,64,256]{2,1,0:T(8,128)S(1)}, f32[1,64,256]{2,1,0:T(8,128)S(1)}, u32[]{:S(2)}, u32[]{:S(2)}) collective-permute-start(f32[1,64,256]{2,1,0:T(8,128)S(1)} %constant_dynamic-slice_fusion), channel_id=1, source_target_pairs={{0,8},{1,9},{2,10},{3,11},{4,12},{5,13},{6,14},{7,15},{8,0},{9,1},... | collective-permute-start | bytes 196616 | tf_op jit(solution)/shard_map/ppermute | solution.py:44

commit v3 on v2

--- a/solution.py
+++ b/solution.py
@@ -57,71 +57,93 @@
     return jnp.concatenate([below, above], axis=dim)
 
 
-def smooth_kernel(ka_ref, kb_ref, a_ref, b_ref, o_ref, *, sub):
-    depth, lat = ka_ref.shape
-    shape = (sub, depth, lat)
+def smooth_kernel(coef_ref, a_ref, h_ref, o_ref, *, sub):
+    depth, lat = a_ref.shape[1], a_ref.shape[2]
+    half = lat // 2
+    shape = (sub, depth, half)
+    row = lax.broadcasted_iota(jnp.int32, shape, 1)
     lane = lax.broadcasted_iota(jnp.int32, shape, 2)
-    row = lax.broadcasted_iota(jnp.int32, shape, 1)
-    col = lane % LX
-    ka = jnp.broadcast_to(ka_ref[...][None], shape)
-    kb = jnp.broadcast_to(kb_ref[...][None], shape)
+    low_rows, first, last = row < HALO, row == 0, row == depth - 1
+    low_lanes, high_lanes = lane < LX, lane >= half - LX
 
-    def coeffs(k):
-        k8 = lateral_weight * k
-        return (
-            k,
-            1.0 - 2.0 * k - 4.0 * k8,
-            jnp.where(lane >= LX, k8, 0.0),
-            jnp.where(lane < lat - LX, k8, 0.0),
-            jnp.where(col != 0, k8, 0.0),
-            jnp.where(col != LX - 1, k8, 0.0),
-        )
-
-    ca, cb = coeffs(ka), coeffs(kb)
-    first_a, last_a = row == 0, row == depth - 1
-    first_b, last_b = row == HALO, row == HALO - 1
-
-    def step(v, down, up, c):
-        k, cself, c_xm, c_xp, c_ym, c_yp = c
-        lateral = (
-            c_xm * pltpu.roll(v, LX, 2)
-            + c_xp * pltpu.roll(v, lat - LX, 2)
-            + c_ym * pltpu.roll(v, 1, 2)
-            + c_yp * pltpu.roll(v, lat - 1, 2)
-        )
-        return cself * v + k * (down + up) + lateral
+    def coef(n, j, h):
+        return coef_ref[n, j * depth : (j + 1) * depth, h * half : (h + 1) * half][None]
 
     def body(i, carry):
         r = pl.multiple_of(i * sub, sub)
-        a = a_ref[pl.ds(r, sub)].astype(jnp.float32)
-        b = b_ref[pl.ds(r, sub)].astype(jnp.float32)
+        own = a_ref[pl.ds(r, sub)].astype(jnp.float32)
+        hal = h_ref[pl.ds(r, sub)].astype(jnp.float32)
+        own = [own[..., :half], own[..., half:]]
+        hal = [hal[..., :half], hal[..., half:]]
+        rot = [pltpu.roll(o, HALO, 1) for o in own]
+        x = [
+            [jnp.where(low_rows, hal[h], rot[h]) for h in range(2)],
+            [jnp.where(low_rows, rot[h], hal[h]) for h in range(2)],
+        ]
+        cf = [[[coef(n, j, h) for h in range(2)] for j in range(2)] for n in range(6)]
         for _ in range(PASSES):
-            a_dn = jnp.where(first_a, pltpu.roll(b, depth - HALO + 1, 1), pltpu.roll(a, 1, 1))
-            a_up = jnp.where(last_a, pltpu.roll(b, HALO - 1, 1), pltpu.roll(a, depth - 1, 1))
-            b_dn = jnp.where(first_b, pltpu.roll(a, depth - HALO + 1, 1), pltpu.roll(b, 1, 1))
-            b_up = jnp.where(last_b, pltpu.roll(a, HALO - 1, 1), pltpu.roll(b, depth - 1, 1))
-            a, b = step(a, a_dn, a_up, ca), step(b, b_dn, b_up, cb)
-        o_ref[pl.ds(r, sub)] = a
+            depth_sum = [[None, None], [None, None]]
+            for h in range(2):
+                d0, d1 = pltpu.roll(x[0][h], 1, 1), pltpu.roll(x[1][h], 1, 1)
+                u0, u1 = pltpu.roll(x[0][h], depth - 1, 1), pltpu.roll(x[1][h], depth - 1, 1)
+                depth_sum[0][h] = d0 + jnp.where(last, u1, u0)
+                depth_sum[1][h] = jnp.where(first, d0, d1) + u1
+            new = [[None, None], [None, None]]
+            for j in range(2):
+                a, b = x[j]
+                ra, rb = pltpu.roll(a, LX, 2), pltpu.roll(b, LX, 2)
+                sa, sb = pltpu.roll(a, half - LX, 2), pltpu.roll(b, half - LX, 2)
+                xm = [ra, jnp.where(low_lanes, ra, rb)]
+                xp = [jnp.where(high_lanes, sb, sa), sb]
+                for h, v in enumerate((a, b)):
+                    k, cself, c_xm, c_xp, c_ym, c_yp = (cf[n][j][h] for n in range(6))
+                    lateral = (
+                        c_xm * xm[h]
+                        + c_xp * xp[h]
+                        + c_ym * pltpu.roll(v, 1, 2)
+                        + c_yp * pltpu.roll(v, half - 1, 2)
+                    )
+                    new[j][h] = cself * v + k * depth_sum[j][h] + lateral
+            x = new
+        for h in range(2):
+            out = jnp.where(low_rows, pltpu.roll(x[0][h], HALO, 1), pltpu.roll(x[1][h], HALO, 1))
+            o_ref[pl.ds(r, sub), :, h * half : (h + 1) * half] = out
         return carry
 
     lax.fori_loop(0, a_ref.shape[0] // sub, body, 0)
 
 
-def smooth(sensitivity, halo, kappa, kappa_halo, block=128, sub=2):
+def coefficients(kappa_col, lat):
+    lane = jnp.arange(lat)[None, :]
+    col = lane % LX
+    k8 = lateral_weight * kappa_col
+    zero = jnp.zeros_like(kappa_col)
+    return jnp.stack(
+        [
+            kappa_col,
+            1.0 - 2.0 * kappa_col - 4.0 * k8,
+            jnp.where(lane >= LX, k8, zero),
+            jnp.where(lane < lat - LX, k8, zero),
+            jnp.where(col != 0, k8, zero),
+            jnp.where(col != LX - 1, k8, zero),
+        ]
+    )
+
+
+def smooth(sensitivity, halo, coef, block=128, sub=1):
     rows, depth, lat = sensitivity.shape
     kernel = functools.partial(smooth_kernel, sub=sub)
     return pl.pallas_call(
         kernel,
         grid=(rows // block,),
         in_specs=[
-            pl.BlockSpec((depth, lat), lambda i: (0, 0)),
-            pl.BlockSpec((depth, lat), lambda i: (0, 0)),
+            pl.BlockSpec(coef.shape, lambda i: (0, 0, 0)),
             pl.BlockSpec((block, depth, lat), lambda i: (i, 0, 0)),
             pl.BlockSpec((block, depth, lat), lambda i: (i, 0, 0)),
         ],
         out_specs=pl.BlockSpec((block, depth, lat), lambda i: (i, 0, 0)),
         out_shape=jax.ShapeDtypeStruct((rows, depth, lat), jnp.float32),
-    )(kappa, kappa_halo, sensitivity, halo)
+    )(coef, sensitivity, halo)
 
 
 def body(sensitivity, cell_class, class_rate, panel_owner):
@@ -132,7 +154,8 @@
     kappa = jnp.sum(onehot * class_rate[None, None, :], axis=-1)
     halo = halo_of(sensitivity, "slab", 1)
     kappa_halo = halo_of(kappa, "slab", 0)
-    field = smooth(sensitivity, halo, kappa, kappa_halo)
+    kappa_col = jnp.concatenate([kappa_halo[:HALO], kappa, kappa_halo[HALO:]], axis=0)
+    field = smooth(sensitivity, halo, coefficients(kappa_col, lat))
     cells = depth * lat * lax.axis_size("slab")
     flat = sensitivity.reshape(rows, depth * lat)
     partials = []

time: 433 us -> 604 us (1.39)
  Pallas kernels: 177 us -> 348 us
    pallas_call x1, Pallas kernels: 177 us -> 348 us  [smooth(): pl.pallas_call(kernel, grid=(rows // block,), in_specs=[pl.BlockSpec(coef...]
  transfers between devices with their start and end apart: 28 -> 28, of which waited for: 12 -> 11; matrix products, arithmetic and copies ran while one was open for 7% -> 5% of each run, Pallas kernels for 0% -> 0%
where the time goes in v3:
time: 604 us; the launch traced here: 603 us
  Pallas kernels  348 us (58%)
  starting transfers between devices  125 us (21%)
  waiting for transfers between devices  76.6 us (13%)
  local copies, waits for them, and re-layouts  18.8 us (3%)
  other arithmetic  12.8 us (2%)
  matrix products  11.5 us (2%)
  between operations  10.4 us (2%)
    pallas_call x1, Pallas kernels, smooth(): pl.pallas_call(kernel, grid=(rows // block,), in_specs=[pl.BlockSpec(coef...  348 us
    ppermute x12, starting transfers between devices, reduce_scatter_slab(): part = keep + lax.ppermute(send, axis, [(i, i ^ bit) for i in range(size)])  94.8 us
    ppermute x3, waiting for transfers between devices, broadcast_dp(): pair = lax.ppermute(piece, axis, [(i, i ^ 1) for i in range(size)])  21.8 us
    ppermute x3, waiting for transfers between devices, broadcast_dp(): lax.ppermute(val, axis, [(i, (i + 2) % size) for i in range(size)])  20.7 us
    ppermute x3, waiting for transfers between devices, broadcast_dp(): last = lax.ppermute(val, axis, [(i, (i + 2) % size) for i in range(size)])  20.6 us
  transfers between devices with their start and end apart: 28, of which 11 were waited for; matrix products, arithmetic and copies ran while one was open for 5% of the time, Pallas kernels for 0%

profile of v3, /device:TPU:0, one launch (start us, length us, event | category | flops | bytes accessed | tf_op | source)
XLA Modules:
  0.0 603.0 jit_solution(5032216309227234696)
XLA Ops:
  0.6 4.8 fusion.11
  5.5 1.4 collective-permute-start.2
  6.9 1.3 collective-permute-start.3
  8.3 4.7 collective-permute-start
  13.0 1.3 collective-permute-start.1
  14.4 2.9 collective-permute-done.1
  17.5 3.5 pad_maximum_fusion.h_ref
  20.9 348.4 %shard_map.59 = f32[1024,8,256]{2,1,0:T(8,128)} custom-call(f32[6,16,256]{2,1,0:T(8,128)} %copy-done.1, bf16[1024,8,256]{2,1,0:T(8,128)(2,1)} %a_ref.1, bf16[1024,8,256]{2,1,0:T(8,128)(2,1)} %pad_maximum_fusion.h_ref), custom_call_target="tpu_custom_call" | custom-call | tf_op jit(solution)/shard_map/pallas_call | solution.py:136
  369.3 3.8 convert.5
  373.6 1.7 collective-permute-start.4
  386.0 5.6 copy.16
  392.0 1.7 collective-permute-start.20
  393.7 3.2 collective-permute-start.5
  397.0 2.2 collective-permute-start.6
  399.2 4.9 collective-permute-done.12
  404.1 1.3 broadcast_select_fusion.1
  405.4 2.0 collective-permute-start.13
  407.4 2.2 collective-permute-start.14
  409.6 16.8 %collective-permute-done.20 = bf16[256,2048]{1,0:T(8,128)(2,1)S(1)} collective-permute-done((bf16[256,2048]{1,0:T(8,128)(2,1)S(1)}, bf16[256,2048]{1,0:T(8,128)(2,1)S(1)}, u32[]{:S(2)}, u32[]{:S(2)}) %collective-permute-start.20) | collective-permute-done | bytes 1048608 | tf_op jit(solution)/shard_map/ppermute | solution.py:24
  426.6 2.0 collective-permute-start.21
  428.5 2.2 collective-permute-start.22
  431.3 1.8 collective-permute-start.15
  433.1 20.7 %collective-permute-done.21 = bf16[256,2048]{1,0:T(8,128)(2,1)S(1)} collective-permute-done((bf16[256,2048]{1,0:T(8,128)(2,1)S(1)}, bf16[256,2048]{1,0:T(8,128)(2,1)S(1)}, u32[]{:S(2)}, u32[]{:S(2)}) %collective-permute-start.21) | collective-permute-done | bytes 1048608 | tf_op jit(solution)/shard_map/ppermute | solution.py:26
  454.0 1.6 collective-permute-start.23
  455.7 20.6 %collective-permute-done.7 = bf16[256,2048]{1,0:T(8,128)(2,1)S(1)} collective-permute-done((bf16[256,2048]{1,0:T(8,128)(2,1)S(1)}, bf16[256,2048]{1,0:T(8,128)(2,1)S(1)}, u32[]{:S(2)}, u32[]{:S(2)}) %collective-permute-start.7) | collective-permute-done | bytes 1048608 | tf_op jit(solution)/shard_map/ppermute | solution.py:29
  476.2 2.2 fusion.2
  478.5 1.6 copy.12
  480.9 31.3 %collective-permute-start.8 = (f32[8,64,256]{2,1,0:T(8,128)}, f32[8,64,256]{2,1,0:T(8,128)}, u32[]{:S(2)}, u32[]{:S(2)}) collective-permute-start(f32[8,64,256]{2,1,0:T(8,128)} %dynamic-slice_bitcast_fusion.2), channel_id=1, source_target_pairs={{0,1},{1,0},{2,3},{3,2},{4,5},{5,4},{6,7},{7,6},{8,9},{9,8},{10,11... | collective-permute-start | bytes 1572872 | tf_op jit(solution)/shard_map/ppermute | solution.py:44
  512.2 4.8 fusion.1
  517.0 1.6 copy.13
  519.4 13.2 %collective-permute-start.16 = (f32[8,64,256]{2,1,0:T(8,128)}, f32[8,64,256]{2,1,0:T(8,128)}, u32[]{:S(2)}, u32[]{:S(2)}) collective-permute-start(f32[8,64,256]{2,1,0:T(8,128)} %dynamic-slice_bitcast_fusion.1), channel_id=1, source_target_pairs={{0,1},{1,0},{2,3},{3,2},{4,5},{5,4},{6,7},{7,6},{8,9},{9,8},{10,11... | collective-permute-start | bytes 1572872 | tf_op jit(solution)/shard_map/ppermute | solution.py:44
  532.6 4.5 fusion
  537.0 1.6 copy.14
  538.7 4.2 collective-permute-start.24
  542.8 1.1 bitcast_add_fusion.2
  544.0 23.1 %collective-permute-start.9 = (f32[4,64,256]{2,1,0:T(8,128)S(1)}, f32[4,64,256]{2,1,0:T(8,128)S(1)}, u32[]{:S(2)}, u32[]{:S(2)}) collective-permute-start(f32[4,64,256]{2,1,0:T(8,128)S(1)} %dynamic-slice_bitcast_fusion.5), channel_id=1, source_target_pairs={{0,2},{1,3},{2,0},{3,1},{4,6},{5,7},{6,4},{7,5},{8,10},{9,11},{10,... | collective-permute-start | bytes 786440 | tf_op jit(solution)/shard_map/ppermute | solution.py:44
  567.1 1.1 bitcast_add_fusion.1
  568.4 2.1 collective-permute-start.25
  570.5 3.7 collective-permute-done.9
  574.2 4.1 collective-permute-start.10
  578.3 1.4 collective-permute-done.17
  579.8 4.1 collective-permute-start.18
  583.9 1.4 collective-permute-done.25
  585.5 4.1 collective-permute-start.26
  590.3 3.3 collective-permute-start.11
  593.6 2.8 collective-permute-start.19
  596.4 2.5 collective-permute-start.27
  599.5 2.8 collective-permute-done.27
  (77 shorter events, 7.7 us)
Async XLA Ops:
  0.6 7.6 %copy-start.2 = (s32[8,256]{1,0:T(8,128)S(1)}, s32[8,256]{1,0:T(8,128)}, u32[]{:S(2)}) copy-start(s32[8,256]{1,0:T(8,128)} %param.5) | copy-start | bytes 24580
  0.6 7.6 %copy-start.4 = (f32[8]{0:T(128)S(1)}, f32[8]{0:T(128)}, u32[]{:S(2)}) copy-start(f32[8]{0:T(128)} %param.6) | copy-start | bytes 100
  5.5 12.0 %collective-permute-start.2 = (bf16[1024,4,256]{2,1,0:T(4,128)(2,1)S(1)}, bf16[1024,4,256]{2,1,0:T(4,128)(2,1)S(1)}, u32[]{:S(2)}, u32[]{:S(2)}) collective-permute-start(bf16[1024,4,256]{2,1,0:T(4,128)(2,1)S(1)} %get-tuple-element.5), channel_id=1, source_target_pairs={{0,1},{1,2},{2,3},{3,4},{4,5},{5,6},{6,7},{7,8},{8,9},{9,10},{10,1... | collective-permute-start | bytes 6291464 | tf_op jit(solution)/shard_map/ppermute | solution.py:55
  6.9 10.6 %collective-permute-start.3 = (bf16[1024,4,256]{2,1,0:T(4,128)(2,1)S(1)}, bf16[1024,4,256]{2,1,0:T(4,128)(2,1)S(1)}, u32[]{:S(2)}, u32[]{:S(2)}) collective-permute-start(bf16[1024,4,256]{2,1,0:T(4,128)(2,1)S(1)} %get-tuple-element.6), channel_id=1, source_target_pairs={{1,0},{2,1},{3,2},{4,3},{5,4},{6,5},{7,6},{8,7},{9,8},{10,9},{11,1... | collective-permute-start | bytes 6291464 | tf_op jit(solution)/shard_map/ppermute | solution.py:56
  8.3 6.1 %collective-permute-start = (f32[4,256]{1,0:T(4,128)S(1)}, f32[4,256]{1,0:T(4,128)S(1)}, u32[]{:S(2)}, u32[]{:S(2)}) collective-permute-start(f32[4,256]{1,0:T(4,128)S(1)} %get-tuple-element.7), channel_id=1, source_target_pairs={{0,1},{1,2},{2,3},{3,4},{4,5},{5,6},{6,7},{7,8},{8,9},{9,10},{10,1... | collective-permute-start | bytes 12296 | tf_op jit(solution)/shard_map/ppermute | solution.py:55
  13.0 4.3 collective-permute-start.1
  17.4 3.5 copy-start.1
  373.1 3.0 copy-start.3
  373.6 20.0 %collective-permute-start.4 = (bf16[256,2048]{1,0:T(8,128)(2,1)S(1)}, bf16[256,2048]{1,0:T(8,128)(2,1)}, u32[]{:S(2)}, u32[]{:S(2)}) collective-permute-start(bf16[256,2048]{1,0:T(8,128)(2,1)S(1)} %bitcast.84), channel_id=1, source_target_pairs={{0,16},{16,0},{32,48},{48,32},{64,80},{80,64},{96,112},{112,96},{1... | collective-permute-start | bytes 3145736 | tf_op jit(solution)/shard_map/ppermute | solution.py:24
  375.6 28.5 %collective-permute-start.12 = (bf16[256,2048]{1,0:T(8,128)(2,1)S(1)}, bf16[256,2048]{1,0:T(8,128)(2,1)}, u32[]{:S(2)}, u32[]{:S(2)}) collective-permute-start(bf16[256,2048]{1,0:T(8,128)(2,1)S(1)} %bitcast.82), channel_id=1, source_target_pairs={{0,16},{16,0},{32,48},{48,32},{64,80},{80,64},{96,112},{112,96},{1... | collective-permute-start | bytes 3145736 | tf_op jit(solution)/shard_map/ppermute | solution.py:24
  392.0 34.5 %collective-permute-start.20 = (bf16[256,2048]{1,0:T(8,128)(2,1)S(1)}, bf16[256,2048]{1,0:T(8,128)(2,1)S(1)}, u32[]{:S(2)}, u32[]{:S(2)}) collective-permute-start(bf16[256,2048]{1,0:T(8,128)(2,1)S(1)} %bitcast.88), channel_id=1, source_target_pairs={{0,16},{16,0},{32,48},{48,32},{64,80},{80,64},{96,112},{112,96},{1... | collective-permute-start | bytes 3145736 | tf_op jit(solution)/shard_map/ppermute | solution.py:24
  393.7 34.8 %collective-permute-start.5 = (bf16[256,2048]{1,0:T(8,128)(2,1)S(1)}, bf16[256,2048]{1,0:T(8,128)(2,1)S(1)}, u32[]{:S(2)}, u32[]{:S(2)}) collective-permute-start(bf16[256,2048]{1,0:T(8,128)(2,1)S(1)} %broadcast_select_fusion.2), channel_id=1, source_target_pairs={{0,32},{16,48},{32,64},{48,80},{64,96},{80,112},{96,0},{112,16},{1... | collective-permute-start | bytes 3145736 | tf_op jit(solution)/shard_map/ppermute | solution.py:26
  397.0 33.8 %collective-permute-start.6 = (bf16[256,2048]{1,0:T(8,128)(2,1)S(1)}, bf16[256,2048]{1,0:T(8,128)(2,1)S(1)}, u32[]{:S(2)}, u32[]{:S(2)}) collective-permute-start(bf16[256,2048]{1,0:T(8,128)(2,1)S(1)} %broadcast_select_fusion.2), channel_id=1, source_target_pairs={{0,96},{16,112},{32,0},{48,16},{64,32},{80,48},{96,64},{112,80},{1... | collective-permute-start | bytes 3145736 | tf_op jit(solution)/shard_map/ppermute | solution.py:27
  405.4 25.6 %collective-permute-start.13 = (bf16[256,2048]{1,0:T(8,128)(2,1)S(1)}, bf16[256,2048]{1,0:T(8,128)(2,1)S(1)}, u32[]{:S(2)}, u32[]{:S(2)}) collective-permute-start(bf16[256,2048]{1,0:T(8,128)(2,1)S(1)} %broadcast_select_fusion.1), channel_id=1, source_target_pairs={{0,32},{16,48},{32,64},{48,80},{64,96},{80,112},{96,0},{112,16},{1... | collective-permute-start | bytes 3145736 | tf_op jit(solution)/shard_map/ppermute | solution.py:26
  407.4 23.6 %collective-permute-start.14 = (bf16[256,2048]{1,0:T(8,128)(2,1)S(1)}, bf16[256,2048]{1,0:T(8,128)(2,1)S(1)}, u32[]{:S(2)}, u32[]{:S(2)}) collective-permute-start(bf16[256,2048]{1,0:T(8,128)(2,1)S(1)} %broadcast_select_fusion.1), channel_id=1, source_target_pairs={{0,96},{16,112},{32,0},{48,16},{64,32},{80,48},{96,64},{112,80},{1... | collective-permute-start | bytes 3145736 | tf_op jit(solution)/shard_map/ppermute | solution.py:27
  426.6 27.2 %collective-permute-start.21 = (bf16[256,2048]{1,0:T(8,128)(2,1)S(1)}, bf16[256,2048]{1,0:T(8,128)(2,1)S(1)}, u32[]{:S(2)}, u32[]{:S(2)}) collective-permute-start(bf16[256,2048]{1,0:T(8,128)(2,1)S(1)} %broadcast_select_fusion), channel_id=1, source_target_pairs={{0,32},{16,48},{32,64},{48,80},{64,96},{80,112},{96,0},{112,16},{1... | collective-permute-start | bytes 3145736 | tf_op jit(solution)/shard_map/ppermute | solution.py:26
  428.5 25.2 %collective-permute-start.22 = (bf16[256,2048]{1,0:T(8,128)(2,1)S(1)}, bf16[256,2048]{1,0:T(8,128)(2,1)S(1)}, u32[]{:S(2)}, u32[]{:S(2)}) collective-permute-start(bf16[256,2048]{1,0:T(8,128)(2,1)S(1)} %broadcast_select_fusion), channel_id=1, source_target_pairs={{0,96},{16,112},{32,0},{48,16},{64,32},{80,48},{96,64},{112,80},{1... | collective-permute-start | bytes 3145736 | tf_op jit(solution)/shard_map/ppermute | solution.py:27
  430.9 45.3 %copy-start = (bf16[128,8,8,256]{3,1,2,0:T(8,128)(2,1)S(1)}, bf16[128,8,8,256]{3,1,2,0:T(8,128)(2,1)}, u32[]{:S(2)}) copy-start(bf16[128,8,8,256]{3,1,2,0:T(8,128)(2,1)} %copy.16) | copy-start | bytes 12582916
  430.9 45.3 %collective-permute-start.7 = (bf16[256,2048]{1,0:T(8,128)(2,1)S(1)}, bf16[256,2048]{1,0:T(8,128)(2,1)S(1)}, u32[]{:S(2)}, u32[]{:S(2)}) collective-permute-start(bf16[256,2048]{1,0:T(8,128)(2,1)S(1)} %select_select_fusion.2), channel_id=1, source_target_pairs={{0,32},{16,48},{32,64},{48,80},{64,96},{80,112},{96,0},{112,16},{1... | collective-permute-start | bytes 3145736 | tf_op jit(solution)/shard_map/ppermute | solution.py:29
  431.3 80.9 %collective-permute-start.15 = (bf16[256,2048]{1,0:T(8,128)(2,1)S(1)}, bf16[256,2048]{1,0:T(8,128)(2,1)}, u32[]{:S(2)}, u32[]{:S(2)}) collective-permute-start(bf16[256,2048]{1,0:T(8,128)(2,1)S(1)} %select_select_fusion.1), channel_id=1, source_target_pairs={{0,32},{16,48},{32,64},{48,80},{64,96},{80,112},{96,0},{112,16},{1... | collective-permute-start | bytes 3145736 | tf_op jit(solution)/shard_map/ppermute | solution.py:29
  454.0 78.5 %collective-permute-start.23 = (bf16[256,2048]{1,0:T(8,128)(2,1)S(1)}, bf16[256,2048]{1,0:T(8,128)(2,1)}, u32[]{:S(2)}, u32[]{:S(2)}) collective-permute-start(bf16[256,2048]{1,0:T(8,128)(2,1)S(1)} %select_select_fusion), channel_id=1, source_target_pairs={{0,32},{16,48},{32,64},{48,80},{64,96},{80,112},{96,0},{112,16},{1... | collective-permute-start | bytes 3145736 | tf_op jit(solution)/shard_map/ppermute | solution.py:29
  480.9 61.9 %collective-permute-start.8 = (f32[8,64,256]{2,1,0:T(8,128)}, f32[8,64,256]{2,1,0:T(8,128)}, u32[]{:S(2)}, u32[]{:S(2)}) collective-permute-start(f32[8,64,256]{2,1,0:T(8,128)} %dynamic-slice_bitcast_fusion.2), channel_id=1, source_target_pairs={{0,1},{1,0},{2,3},{3,2},{4,5},{5,4},{6,7},{7,6},{8,9},{9,8},{10,11... | collective-permute-start | bytes 1572872 | tf_op jit(solution)/shard_map/ppermute | solution.py:44
  519.4 47.7 %collective-permute-start.16 = (f32[8,64,256]{2,1,0:T(8,128)}, f32[8,64,256]{2,1,0:T(8,128)}, u32[]{:S(2)}, u32[]{:S(2)}) collective-permute-start(f32[8,64,256]{2,1,0:T(8,128)} %dynamic-slice_bitcast_fusion.1), channel_id=1, source_target_pairs={{0,1},{1,0},{2,3},{3,2},{4,5},{5,4},{6,7},{7,6},{8,9},{9,8},{10,11... | collective-permute-start | bytes 1572872 | tf_op jit(solution)/shard_map/ppermute | solution.py:44
  538.7 29.7 %collective-permute-start.24 = (f32[8,64,256]{2,1,0:T(8,128)S(1)}, f32[8,64,256]{2,1,0:T(8,128)S(1)}, u32[]{:S(2)}, u32[]{:S(2)}) collective-permute-start(f32[8,64,256]{2,1,0:T(8,128)S(1)} %dynamic-slice_bitcast_fusion), channel_id=1, source_target_pairs={{0,1},{1,0},{2,3},{3,2},{4,5},{5,4},{6,7},{7,6},{8,9},{9,8},{10,11... | collective-permute-start | bytes 1572872 | tf_op jit(solution)/shard_map/ppermute | solution.py:44
  544.0 30.2 %collective-permute-start.9 = (f32[4,64,256]{2,1,0:T(8,128)S(1)}, f32[4,64,256]{2,1,0:T(8,128)S(1)}, u32[]{:S(2)}, u32[]{:S(2)}) collective-permute-start(f32[4,64,256]{2,1,0:T(8,128)S(1)} %dynamic-slice_bitcast_fusion.5), channel_id=1, source_target_pairs={{0,2},{1,3},{2,0},{3,1},{4,6},{5,7},{6,4},{7,5},{8,10},{9,11},{10,... | collective-permute-start | bytes 786440 | tf_op jit(solution)/shard_map/ppermute | solution.py:44
  568.2 11.6 %collective-permute-start.17 = (f32[4,64,256]{2,1,0:T(8,128)S(1)}, f32[4,64,256]{2,1,0:T(8,128)S(1)}, u32[]{:S(2)}, u32[]{:S(2)}) collective-permute-start(f32[4,64,256]{2,1,0:T(8,128)S(1)} %dynamic-slice_bitcast_fusion.4), channel_id=1, source_target_pairs={{0,2},{1,3},{2,0},{3,1},{4,6},{5,7},{6,4},{7,5},{8,10},{9,11},{10,... | collective-permute-start | bytes 786440 | tf_op jit(solution)/shard_map/ppermute | solution.py:44
  568.4 17.0 %collective-permute-start.25 = (f32[4,64,256]{2,1,0:T(8,128)S(1)}, f32[4,64,256]{2,1,0:T(8,128)S(1)}, u32[]{:S(2)}, u32[]{:S(2)}) collective-permute-start(f32[4,64,256]{2,1,0:T(8,128)S(1)} %dynamic-slice_bitcast_fusion.3), channel_id=1, source_target_pairs={{0,2},{1,3},{2,0},{3,1},{4,6},{5,7},{6,4},{7,5},{8,10},{9,11},{10,... | collective-permute-start | bytes 786440 | tf_op jit(solution)/shard_map/ppermute | solution.py:44
  574.2 16.0 %collective-permute-start.10 = (f32[2,64,256]{2,1,0:T(8,128)S(1)}, f32[2,64,256]{2,1,0:T(8,128)S(1)}, u32[]{:S(2)}, u32[]{:S(2)}) collective-permute-start(f32[2,64,256]{2,1,0:T(8,128)S(1)} %dynamic-slice_bitcast_fusion.8), channel_id=1, source_target_pairs={{0,4},{1,5},{2,6},{3,7},{4,0},{5,1},{6,2},{7,3},{8,12},{9,13},{10,... | collective-permute-start | bytes 393224 | tf_op jit(solution)/shard_map/ppermute | solution.py:44
  579.8 13.7 %collective-permute-start.18 = (f32[2,64,256]{2,1,0:T(8,128)S(1)}, f32[2,64,256]{2,1,0:T(8,128)S(1)}, u32[]{:S(2)}, u32[]{:S(2)}) collective-permute-start(f32[2,64,256]{2,1,0:T(8,128)S(1)} %dynamic-slice_bitcast_fusion.7), channel_id=1, source_target_pairs={{0,4},{1,5},{2,6},{3,7},{4,0},{5,1},{6,2},{7,3},{8,12},{9,13},{10,... | collective-permute-start | bytes 393224 | tf_op jit(solution)/shard_map/ppermute | solution.py:44
  585.5 10.9 %collective-permute-start.26 = (f32[2,64,256]{2,1,0:T(8,128)S(1)}, f32[2,64,256]{2,1,0:T(8,128)S(1)}, u32[]{:S(2)}, u32[]{:S(2)}) collective-permute-start(f32[2,64,256]{2,1,0:T(8,128)S(1)} %dynamic-slice_bitcast_fusion.6), channel_id=1, source_target_pairs={{0,4},{1,5},{2,6},{3,7},{4,0},{5,1},{6,2},{7,3},{8,12},{9,13},{10,... | collective-permute-start | bytes 393224 | tf_op jit(solution)/shard_map/ppermute | solution.py:44
  590.3 8.6 %collective-permute-start.11 = (f32[1,64,256]{2,1,0:T(8,128)S(1)}, f32[1,64,256]{2,1,0:T(8,128)S(1)}, u32[]{:S(2)}, u32[]{:S(2)}) collective-permute-start(f32[1,64,256]{2,1,0:T(8,128)S(1)} %constant_dynamic-slice_fusion.2), channel_id=1, source_target_pairs={{0,8},{1,9},{2,10},{3,11},{4,12},{5,13},{6,14},{7,15},{8,0},{9,1},... | collective-permute-start | bytes 196616 | tf_op jit(solution)/shard_map/ppermute | solution.py:44
  593.6 5.8 collective-permute-start.19
  596.4 5.8 collective-permute-start.27

commit v4 on v3

--- a/solution.py
+++ b/solution.py
@@ -130,7 +130,7 @@
     )
 
 
-def smooth(sensitivity, halo, coef, block=128, sub=1):
+def smooth(sensitivity, halo, coef, block=128, sub=16):
     rows, depth, lat = sensitivity.shape
     kernel = functools.partial(smooth_kernel, sub=sub)
     return pl.pallas_call(

time: 604 us -> 327 us (0.54)
  Pallas kernels: 348 us -> 72.1 us
    pallas_call x1, Pallas kernels: 348 us -> 72.1 us  [smooth(): pl.pallas_call(kernel, grid=(rows // block,), in_specs=[pl.BlockSpec(coef...]
  transfers between devices with their start and end apart: 28 -> 28, of which waited for: 11 -> 11; matrix products, arithmetic and copies ran while one was open for 5% -> 9% of each run, Pallas kernels for 0% -> 0%
where the time goes in v4:
time: 327 us
  starting transfers between devices  124 us (38%)
  waiting for transfers between devices  76.7 us (23%)
  Pallas kernels  72.1 us (22%)
  local copies, waits for them, and re-layouts  18.8 us (6%)
  other arithmetic  14.1 us (4%)
  matrix products  11.1 us (3%)
  between operations  10.4 us (3%)
    ppermute x12, starting transfers between devices, reduce_scatter_slab(): part = keep + lax.ppermute(send, axis, [(i, i ^ bit) for i in range(size)])  95.1 us
    pallas_call x1, Pallas kernels, smooth(): pl.pallas_call(kernel, grid=(rows // block,), in_specs=[pl.BlockSpec(coef...  72.1 us
    ppermute x3, waiting for transfers between devices, broadcast_dp(): pair = lax.ppermute(piece, axis, [(i, i ^ 1) for i in range(size)])  21.8 us
    ppermute x3, waiting for transfers between devices, broadcast_dp(): last = lax.ppermute(val, axis, [(i, (i + 2) % size) for i in range(size)])  20.9 us
    ppermute x3, waiting for transfers between devices, broadcast_dp(): lax.ppermute(val, axis, [(i, (i + 2) % size) for i in range(size)])  20.5 us
    dot_general x3, matrix products, body(): lax.dot_general(flat, received, (((1,), (1,)), ((), ())), preferred_eleme...  11.1 us
    ppermute x12, waiting for transfers between devices, reduce_scatter_slab(): part = keep + lax.ppermute(send, axis, [(i, i ^ bit) for i in range(size)])  10.6 us
    ppermute x3, starting transfers between devices, broadcast_dp(): lax.ppermute(val, axis, [(i, (i - 2) % size) for i in range(size)])  6.61 us
  transfers between devices with their start and end apart: 28, of which 11 were waited for; matrix products, arithmetic and copies ran while one was open for 9% of the time, Pallas kernels for 0%

profile of v4, /device:TPU:0, one launch (start us, length us, event | category | flops | bytes accessed | tf_op | source)
XLA Modules:
  0.0 326.7 jit_solution(4441619078694375800)
XLA Ops:
  0.6 4.8 %fusion.11 = (bf16[1024,4,256]{2,1,0:T(4,128)(2,1)S(1)}, bf16[1024,4,256]{2,1,0:T(4,128)(2,1)S(1)}) fusion(bf16[1024,8,256]{2,1,0:T(8,128)(2,1)} %a_ref.1), kind=kLoop, calls=%fused_computation.60 | loop fusion | bytes 8388608 | tf_op jit(solution)/shard_map/slice | solution.py:53
  5.5 1.4 collective-permute-start.2
  6.9 1.3 collective-permute-start.3
  8.3 4.7 %collective-permute-start = (f32[4,256]{1,0:T(4,128)S(1)}, f32[4,256]{1,0:T(4,128)S(1)}, u32[]{:S(2)}, u32[]{:S(2)}) collective-permute-start(f32[4,256]{1,0:T(4,128)S(1)} %get-tuple-element.7), channel_id=1, source_target_pairs={{0,1},{1,2},{2,3},{3,4},{4,5},{5,6},{6,7},{7,8},{8,9},{9,10},{10,1... | collective-permute-start | bytes 12296 | tf_op jit(solution)/shard_map/ppermute | solution.py:55
  13.0 1.3 collective-permute-start.1
  14.4 2.9 collective-permute-done.1
  17.5 3.5 %pad_maximum_fusion.h_ref = bf16[1024,8,256]{2,1,0:T(8,128)(2,1)} fusion(bf16[1024,4,256]{2,1,0:T(4,128)(2,1)S(1)} %collective-permute-done.3, bf16[1024,4,256]{2,1,0:T(4,128)(2,1)S(1)} %collective-permute-done.2), kind=kLoop, calls=%fused_computation | loop fusion | flops 8388608 | bytes 8388608 | tf_op jit(solution)/shard_map/concatenate | solution.py:57
  20.9 72.1 %shard_map.59 = f32[1024,8,256]{2,1,0:T(8,128)} custom-call(f32[6,16,256]{2,1,0:T(8,128)} %copy-done.1, bf16[1024,8,256]{2,1,0:T(8,128)(2,1)} %a_ref.1, bf16[1024,8,256]{2,1,0:T(8,128)(2,1)} %pad_maximum_fusion.h_ref), custom_call_target="tpu_custom_call" | custom-call | tf_op jit(solution)/shard_map/pallas_call | solution.py:136
  93.0 3.8 %convert.5 = bf16[1024,8,256]{2,1,0:T(8,128)(2,1)S(1)} convert(f32[1024,8,256]{2,1,0:T(8,128)} %shard_map.59) | non-fusion elementwise | flops 2097152 | bytes 12582912 | tf_op jit(solution)/shard_map/convert.2
  97.3 1.7 collective-permute-start.4
  109.7 5.6 %copy.16 = bf16[128,8,8,256]{3,1,2,0:T(8,128)(2,1)} copy(bf16[128,8,8,256]{3,2,1,0:T(8,128)(2,1)} %bitcast.78) | data formatting | bytes 8388608
  115.7 1.7 collective-permute-start.20
  117.3 1.3 broadcast_select_fusion.2
  118.7 2.0 collective-permute-start.5
  120.7 2.2 collective-permute-start.6
  122.9 4.9 %collective-permute-done.12 = bf16[256,2048]{1,0:T(8,128)(2,1)} collective-permute-done((bf16[256,2048]{1,0:T(8,128)(2,1)S(1)}, bf16[256,2048]{1,0:T(8,128)(2,1)}, u32[]{:S(2)}, u32[]{:S(2)}) %collective-permute-start.12) | collective-permute-done | bytes 1048608 | tf_op jit(solution)/shard_map/ppermute | solution.py:24
  127.8 1.3 broadcast_select_fusion.1
  129.1 2.0 collective-permute-start.13
  131.1 2.2 collective-permute-start.14
  133.3 16.8 %collective-permute-done.20 = bf16[256,2048]{1,0:T(8,128)(2,1)S(1)} collective-permute-done((bf16[256,2048]{1,0:T(8,128)(2,1)S(1)}, bf16[256,2048]{1,0:T(8,128)(2,1)S(1)}, u32[]{:S(2)}, u32[]{:S(2)}) %collective-permute-start.20) | collective-permute-done | bytes 1048608 | tf_op jit(solution)/shard_map/ppermute | solution.py:24
  150.3 2.0 collective-permute-start.21
  152.2 2.2 collective-permute-start.22
  155.0 2.0 collective-permute-start.15
  156.9 20.5 %collective-permute-done.21 = bf16[256,2048]{1,0:T(8,128)(2,1)S(1)} collective-permute-done((bf16[256,2048]{1,0:T(8,128)(2,1)S(1)}, bf16[256,2048]{1,0:T(8,128)(2,1)S(1)}, u32[]{:S(2)}, u32[]{:S(2)}) %collective-permute-start.21) | collective-permute-done | bytes 1048608 | tf_op jit(solution)/shard_map/ppermute | solution.py:26
  177.7 1.3 collective-permute-start.23
  179.1 20.9 %collective-permute-done.7 = bf16[256,2048]{1,0:T(8,128)(2,1)S(1)} collective-permute-done((bf16[256,2048]{1,0:T(8,128)(2,1)S(1)}, bf16[256,2048]{1,0:T(8,128)(2,1)S(1)}, u32[]{:S(2)}, u32[]{:S(2)}) %collective-permute-start.7) | collective-permute-done | bytes 1048608 | tf_op jit(solution)/shard_map/ppermute | solution.py:29
  199.9 2.2 fusion.2
  202.2 1.6 copy.12
  204.6 31.3 %collective-permute-start.8 = (f32[8,64,256]{2,1,0:T(8,128)}, f32[8,64,256]{2,1,0:T(8,128)}, u32[]{:S(2)}, u32[]{:S(2)}) collective-permute-start(f32[8,64,256]{2,1,0:T(8,128)} %dynamic-slice_bitcast_fusion.2), channel_id=1, source_target_pairs={{0,1},{1,0},{2,3},{3,2},{4,5},{5,4},{6,7},{7,6},{8,9},{9,8},{10,11... | collective-permute-start | bytes 1572872 | tf_op jit(solution)/shard_map/ppermute | solution.py:44
  235.9 4.4 %fusion.1 = f32[1024,256]{0,1:T(8,128)} fusion(bf16[1024,2048]{1,0:T(8,128)(2,1)} %bitcast.79, bf16[256,2048]{1,0:T(8,128)(2,1)} %collective-permute-done.15, bf16[256,2048]{1,0:T(8,128)(2,1)S(1)} %select_select_fusion.1, pred[]{:T(512)S(6)} %eq.77), kind=kOutput, calls=%fused_computation.4 | convolution fusion | flops 1074528256 | bytes 7340033 | tf_op jit(solution)/shard_map/dot_general | solution.py:166
  240.4 1.6 copy.13
  242.8 13.2 %collective-permute-start.16 = (f32[8,64,256]{2,1,0:T(8,128)}, f32[8,64,256]{2,1,0:T(8,128)}, u32[]{:S(2)}, u32[]{:S(2)}) collective-permute-start(f32[8,64,256]{2,1,0:T(8,128)} %dynamic-slice_bitcast_fusion.1), channel_id=1, source_target_pairs={{0,1},{1,0},{2,3},{3,2},{4,5},{5,4},{6,7},{7,6},{8,9},{9,8},{10,11... | collective-permute-start | bytes 1572872 | tf_op jit(solution)/shard_map/ppermute | solution.py:44
  256.0 4.5 %fusion = f32[1024,256]{0,1:T(8,128)} fusion(bf16[1024,2048]{1,0:T(8,128)(2,1)} %bitcast.80, bf16[256,2048]{1,0:T(8,128)(2,1)} %collective-permute-done.23, bf16[256,2048]{1,0:T(8,128)(2,1)S(1)} %select_select_fusion, pred[]{:T(512)S(6)} %eq.81), kind=kOutput, calls=%fused_computation.2 | convolution fusion | flops 1074528256 | bytes 7340033 | tf_op jit(solution)/shard_map/dot_general | solution.py:166
  260.4 1.6 copy.14
  262.0 4.5 %collective-permute-start.24 = (f32[8,64,256]{2,1,0:T(8,128)S(1)}, f32[8,64,256]{2,1,0:T(8,128)S(1)}, u32[]{:S(2)}, u32[]{:S(2)}) collective-permute-start(f32[8,64,256]{2,1,0:T(8,128)S(1)} %dynamic-slice_bitcast_fusion), channel_id=1, source_target_pairs={{0,1},{1,0},{2,3},{3,2},{4,5},{5,4},{6,7},{7,6},{8,9},{9,8},{10,11... | collective-permute-start | bytes 1572872 | tf_op jit(solution)/shard_map/ppermute | solution.py:44
  266.5 1.1 bitcast_add_fusion.2
  267.7 23.1 %collective-permute-start.9 = (f32[4,64,256]{2,1,0:T(8,128)S(1)}, f32[4,64,256]{2,1,0:T(8,128)S(1)}, u32[]{:S(2)}, u32[]{:S(2)}) collective-permute-start(f32[4,64,256]{2,1,0:T(8,128)S(1)} %dynamic-slice_bitcast_fusion.5), channel_id=1, source_target_pairs={{0,2},{1,3},{2,0},{3,1},{4,6},{5,7},{6,4},{7,5},{8,10},{9,11},{10,... | collective-permute-start | bytes 786440 | tf_op jit(solution)/shard_map/ppermute | solution.py:44
  292.1 2.1 collective-permute-start.25
  294.2 3.7 %collective-permute-done.9 = f32[4,64,256]{2,1,0:T(8,128)S(1)} collective-permute-done((f32[4,64,256]{2,1,0:T(8,128)S(1)}, f32[4,64,256]{2,1,0:T(8,128)S(1)}, u32[]{:S(2)}, u32[]{:S(2)}) %collective-permute-start.9) | collective-permute-done | bytes 262176 | tf_op jit(solution)/shard_map/ppermute | solution.py:44
  297.9 4.1 %collective-permute-start.10 = (f32[2,64,256]{2,1,0:T(8,128)S(1)}, f32[2,64,256]{2,1,0:T(8,128)S(1)}, u32[]{:S(2)}, u32[]{:S(2)}) collective-permute-start(f32[2,64,256]{2,1,0:T(8,128)S(1)} %dynamic-slice_bitcast_fusion.8), channel_id=1, source_target_pairs={{0,4},{1,5},{2,6},{3,7},{4,0},{5,1},{6,2},{7,3},{8,12},{9,13},{10,... | collective-permute-start | bytes 393224 | tf_op jit(solution)/shard_map/ppermute | solution.py:44
  302.0 1.4 collective-permute-done.17
  303.5 4.1 %collective-permute-start.18 = (f32[2,64,256]{2,1,0:T(8,128)S(1)}, f32[2,64,256]{2,1,0:T(8,128)S(1)}, u32[]{:S(2)}, u32[]{:S(2)}) collective-permute-start(f32[2,64,256]{2,1,0:T(8,128)S(1)} %dynamic-slice_bitcast_fusion.7), channel_id=1, source_target_pairs={{0,4},{1,5},{2,6},{3,7},{4,0},{5,1},{6,2},{7,3},{8,12},{9,13},{10,... | collective-permute-start | bytes 393224 | tf_op jit(solution)/shard_map/ppermute | solution.py:44
  307.7 1.4 collective-permute-done.25
  309.2 4.1 %collective-permute-start.26 = (f32[2,64,256]{2,1,0:T(8,128)S(1)}, f32[2,64,256]{2,1,0:T(8,128)S(1)}, u32[]{:S(2)}, u32[]{:S(2)}) collective-permute-start(f32[2,64,256]{2,1,0:T(8,128)S(1)} %dynamic-slice_bitcast_fusion.6), channel_id=1, source_target_pairs={{0,4},{1,5},{2,6},{3,7},{4,0},{5,1},{6,2},{7,3},{8,12},{9,13},{10,... | collective-permute-start | bytes 393224 | tf_op jit(solution)/shard_map/ppermute | solution.py:44
  314.0 3.3 %collective-permute-start.11 = (f32[1,64,256]{2,1,0:T(8,128)S(1)}, f32[1,64,256]{2,1,0:T(8,128)S(1)}, u32[]{:S(2)}, u32[]{:S(2)}) collective-permute-start(f32[1,64,256]{2,1,0:T(8,128)S(1)} %constant_dynamic-slice_fusion.2), channel_id=1, source_target_pairs={{0,8},{1,9},{2,10},{3,11},{4,12},{5,13},{6,14},{7,15},{8,0},{9,1},... | collective-permute-start | bytes 196616 | tf_op jit(solution)/shard_map/ppermute | solution.py:44
  317.3 2.8 collective-permute-start.19
  320.1 2.5 collective-permute-start.27
  323.2 2.8 collective-permute-done.27
  (77 shorter events, 8.7 us)
Async XLA Ops:
  0.6 7.6 %copy-start.2 = (s32[8,256]{1,0:T(8,128)S(1)}, s32[8,256]{1,0:T(8,128)}, u32[]{:S(2)}) copy-start(s32[8,256]{1,0:T(8,128)} %param.5) | copy-start | bytes 24580
  0.6 7.6 %copy-start.4 = (f32[8]{0:T(128)S(1)}, f32[8]{0:T(128)}, u32[]{:S(2)}) copy-start(f32[8]{0:T(128)} %param.6) | copy-start | bytes 100
  5.5 12.0 %collective-permute-start.2 = (bf16[1024,4,256]{2,1,0:T(4,128)(2,1)S(1)}, bf16[1024,4,256]{2,1,0:T(4,128)(2,1)S(1)}, u32[]{:S(2)}, u32[]{:S(2)}) collective-permute-start(bf16[1024,4,256]{2,1,0:T(4,128)(2,1)S(1)} %get-tuple-element.5), channel_id=1, source_target_pairs={{0,1},{1,2},{2,3},{3,4},{4,5},{5,6},{6,7},{7,8},{8,9},{9,10},{10,1... | collective-permute-start | bytes 6291464 | tf_op jit(solution)/shard_map/ppermute | solution.py:55
  6.9 10.6 %collective-permute-start.3 = (bf16[1024,4,256]{2,1,0:T(4,128)(2,1)S(1)}, bf16[1024,4,256]{2,1,0:T(4,128)(2,1)S(1)}, u32[]{:S(2)}, u32[]{:S(2)}) collective-permute-start(bf16[1024,4,256]{2,1,0:T(4,128)(2,1)S(1)} %get-tuple-element.6), channel_id=1, source_target_pairs={{1,0},{2,1},{3,2},{4,3},{5,4},{6,5},{7,6},{8,7},{9,8},{10,9},{11,1... | collective-permute-start | bytes 6291464 | tf_op jit(solution)/shard_map/ppermute | solution.py:56
  8.3 6.1 %collective-permute-start = (f32[4,256]{1,0:T(4,128)S(1)}, f32[4,256]{1,0:T(4,128)S(1)}, u32[]{:S(2)}, u32[]{:S(2)}) collective-permute-start(f32[4,256]{1,0:T(4,128)S(1)} %get-tuple-element.7), channel_id=1, source_target_pairs={{0,1},{1,2},{2,3},{3,4},{4,5},{5,6},{6,7},{7,8},{8,9},{9,10},{10,1... | collective-permute-start | bytes 12296 | tf_op jit(solution)/shard_map/ppermute | solution.py:55
  13.0 4.3 %collective-permute-start.1 = (f32[4,256]{1,0:T(4,128)S(1)}, f32[4,256]{1,0:T(4,128)S(1)}, u32[]{:S(2)}, u32[]{:S(2)}) collective-permute-start(f32[4,256]{1,0:T(4,128)S(1)} %get-tuple-element.8), channel_id=1, source_target_pairs={{1,0},{2,1},{3,2},{4,3},{5,4},{6,5},{7,6},{8,7},{9,8},{10,9},{11,1... | collective-permute-start | bytes 12296 | tf_op jit(solution)/shard_map/ppermute | solution.py:56
  17.4 3.5 %copy-start.1 = (f32[6,16,256]{2,1,0:T(8,128)}, f32[6,16,256]{2,1,0:T(8,128)S(1)}, u32[]{:S(2)}) copy-start(f32[6,16,256]{2,1,0:T(8,128)S(1)} %select_dynamic-update-slice_fusion.coef_ref) | copy-start | bytes 294916
  96.8 3.0 copy-start.3
  97.3 20.0 %collective-permute-start.4 = (bf16[256,2048]{1,0:T(8,128)(2,1)S(1)}, bf16[256,2048]{1,0:T(8,128)(2,1)}, u32[]{:S(2)}, u32[]{:S(2)}) collective-permute-start(bf16[256,2048]{1,0:T(8,128)(2,1)S(1)} %bitcast.84), channel_id=1, source_target_pairs={{0,16},{16,0},{32,48},{48,32},{64,80},{80,64},{96,112},{112,96},{1... | collective-permute-start | bytes 3145736 | tf_op jit(solution)/shard_map/ppermute | solution.py:24
  99.3 28.5 %collective-permute-start.12 = (bf16[256,2048]{1,0:T(8,128)(2,1)S(1)}, bf16[256,2048]{1,0:T(8,128)(2,1)}, u32[]{:S(2)}, u32[]{:S(2)}) collective-permute-start(bf16[256,2048]{1,0:T(8,128)(2,1)S(1)} %bitcast.82), channel_id=1, source_target_pairs={{0,16},{16,0},{32,48},{48,32},{64,80},{80,64},{96,112},{112,96},{1... | collective-permute-start | bytes 3145736 | tf_op jit(solution)/shard_map/ppermute | solution.py:24
  115.7 34.5 %collective-permute-start.20 = (bf16[256,2048]{1,0:T(8,128)(2,1)S(1)}, bf16[256,2048]{1,0:T(8,128)(2,1)S(1)}, u32[]{:S(2)}, u32[]{:S(2)}) collective-permute-start(bf16[256,2048]{1,0:T(8,128)(2,1)S(1)} %bitcast.88), channel_id=1, source_target_pairs={{0,16},{16,0},{32,48},{48,32},{64,80},{80,64},{96,112},{112,96},{1... | collective-permute-start | bytes 3145736 | tf_op jit(solution)/shard_map/ppermute | solution.py:24
  118.7 33.6 %collective-permute-start.5 = (bf16[256,2048]{1,0:T(8,128)(2,1)S(1)}, bf16[256,2048]{1,0:T(8,128)(2,1)S(1)}, u32[]{:S(2)}, u32[]{:S(2)}) collective-permute-start(bf16[256,2048]{1,0:T(8,128)(2,1)S(1)} %broadcast_select_fusion.2), channel_id=1, source_target_pairs={{0,32},{16,48},{32,64},{48,80},{64,96},{80,112},{96,0},{112,16},{1... | collective-permute-start | bytes 3145736 | tf_op jit(solution)/shard_map/ppermute | solution.py:26
  120.7 33.8 %collective-permute-start.6 = (bf16[256,2048]{1,0:T(8,128)(2,1)S(1)}, bf16[256,2048]{1,0:T(8,128)(2,1)S(1)}, u32[]{:S(2)}, u32[]{:S(2)}) collective-permute-start(bf16[256,2048]{1,0:T(8,128)(2,1)S(1)} %broadcast_select_fusion.2), channel_id=1, source_target_pairs={{0,96},{16,112},{32,0},{48,16},{64,32},{80,48},{96,64},{112,80},{1... | collective-permute-start | bytes 3145736 | tf_op jit(solution)/shard_map/ppermute | solution.py:27
  129.1 25.6 %collective-permute-start.13 = (bf16[256,2048]{1,0:T(8,128)(2,1)S(1)}, bf16[256,2048]{1,0:T(8,128)(2,1)S(1)}, u32[]{:S(2)}, u32[]{:S(2)}) collective-permute-start(bf16[256,2048]{1,0:T(8,128)(2,1)S(1)} %broadcast_select_fusion.1), channel_id=1, source_target_pairs={{0,32},{16,48},{32,64},{48,80},{64,96},{80,112},{96,0},{112,16},{1... | collective-permute-start | bytes 3145736 | tf_op jit(solution)/shard_map/ppermute | solution.py:26
  131.1 23.6 %collective-permute-start.14 = (bf16[256,2048]{1,0:T(8,128)(2,1)S(1)}, bf16[256,2048]{1,0:T(8,128)(2,1)S(1)}, u32[]{:S(2)}, u32[]{:S(2)}) collective-permute-start(bf16[256,2048]{1,0:T(8,128)(2,1)S(1)} %broadcast_select_fusion.1), channel_id=1, source_target_pairs={{0,96},{16,112},{32,0},{48,16},{64,32},{80,48},{96,64},{112,80},{1... | collective-permute-start | bytes 3145736 | tf_op jit(solution)/shard_map/ppermute | solution.py:27
  150.3 27.2 %collective-permute-start.21 = (bf16[256,2048]{1,0:T(8,128)(2,1)S(1)}, bf16[256,2048]{1,0:T(8,128)(2,1)S(1)}, u32[]{:S(2)}, u32[]{:S(2)}) collective-permute-start(bf16[256,2048]{1,0:T(8,128)(2,1)S(1)} %broadcast_select_fusion), channel_id=1, source_target_pairs={{0,32},{16,48},{32,64},{48,80},{64,96},{80,112},{96,0},{112,16},{1... | collective-permute-start | bytes 3145736 | tf_op jit(solution)/shard_map/ppermute | solution.py:26
  152.2 25.2 %collective-permute-start.22 = (bf16[256,2048]{1,0:T(8,128)(2,1)S(1)}, bf16[256,2048]{1,0:T(8,128)(2,1)S(1)}, u32[]{:S(2)}, u32[]{:S(2)}) collective-permute-start(bf16[256,2048]{1,0:T(8,128)(2,1)S(1)} %broadcast_select_fusion), channel_id=1, source_target_pairs={{0,96},{16,112},{32,0},{48,16},{64,32},{80,48},{96,64},{112,80},{1... | collective-permute-start | bytes 3145736 | tf_op jit(solution)/shard_map/ppermute | solution.py:27
  154.6 45.3 %copy-start = (bf16[128,8,8,256]{3,1,2,0:T(8,128)(2,1)S(1)}, bf16[128,8,8,256]{3,1,2,0:T(8,128)(2,1)}, u32[]{:S(2)}) copy-start(bf16[128,8,8,256]{3,1,2,0:T(8,128)(2,1)} %copy.16) | copy-start | bytes 12582916
  154.6 45.3 %collective-permute-start.7 = (bf16[256,2048]{1,0:T(8,128)(2,1)S(1)}, bf16[256,2048]{1,0:T(8,128)(2,1)S(1)}, u32[]{:S(2)}, u32[]{:S(2)}) collective-permute-start(bf16[256,2048]{1,0:T(8,128)(2,1)S(1)} %select_select_fusion.2), channel_id=1, source_target_pairs={{0,32},{16,48},{32,64},{48,80},{64,96},{80,112},{96,0},{112,16},{1... | collective-permute-start | bytes 3145736 | tf_op jit(solution)/shard_map/ppermute | solution.py:29
  155.0 80.9 %collective-permute-start.15 = (bf16[256,2048]{1,0:T(8,128)(2,1)S(1)}, bf16[256,2048]{1,0:T(8,128)(2,1)}, u32[]{:S(2)}, u32[]{:S(2)}) collective-permute-start(bf16[256,2048]{1,0:T(8,128)(2,1)S(1)} %select_select_fusion.1), channel_id=1, source_target_pairs={{0,32},{16,48},{32,64},{48,80},{64,96},{80,112},{96,0},{112,16},{1... | collective-permute-start | bytes 3145736 | tf_op jit(solution)/shard_map/ppermute | solution.py:29
  177.7 78.2 %collective-permute-start.23 = (bf16[256,2048]{1,0:T(8,128)(2,1)S(1)}, bf16[256,2048]{1,0:T(8,128)(2,1)}, u32[]{:S(2)}, u32[]{:S(2)}) collective-permute-start(bf16[256,2048]{1,0:T(8,128)(2,1)S(1)} %select_select_fusion), channel_id=1, source_target_pairs={{0,32},{16,48},{32,64},{48,80},{64,96},{80,112},{96,0},{112,16},{1... | collective-permute-start | bytes 3145736 | tf_op jit(solution)/shard_map/ppermute | solution.py:29
  204.6 61.9 %collective-permute-start.8 = (f32[8,64,256]{2,1,0:T(8,128)}, f32[8,64,256]{2,1,0:T(8,128)}, u32[]{:S(2)}, u32[]{:S(2)}) collective-permute-start(f32[8,64,256]{2,1,0:T(8,128)} %dynamic-slice_bitcast_fusion.2), channel_id=1, source_target_pairs={{0,1},{1,0},{2,3},{3,2},{4,5},{5,4},{6,7},{7,6},{8,9},{9,8},{10,11... | collective-permute-start | bytes 1572872 | tf_op jit(solution)/shard_map/ppermute | solution.py:44
  242.8 48.0 %collective-permute-start.16 = (f32[8,64,256]{2,1,0:T(8,128)}, f32[8,64,256]{2,1,0:T(8,128)}, u32[]{:S(2)}, u32[]{:S(2)}) collective-permute-start(f32[8,64,256]{2,1,0:T(8,128)} %dynamic-slice_bitcast_fusion.1), channel_id=1, source_target_pairs={{0,1},{1,0},{2,3},{3,2},{4,5},{5,4},{6,7},{7,6},{8,9},{9,8},{10,11... | collective-permute-start | bytes 1572872 | tf_op jit(solution)/shard_map/ppermute | solution.py:44
  262.0 30.0 %collective-permute-start.24 = (f32[8,64,256]{2,1,0:T(8,128)S(1)}, f32[8,64,256]{2,1,0:T(8,128)S(1)}, u32[]{:S(2)}, u32[]{:S(2)}) collective-permute-start(f32[8,64,256]{2,1,0:T(8,128)S(1)} %dynamic-slice_bitcast_fusion), channel_id=1, source_target_pairs={{0,1},{1,0},{2,3},{3,2},{4,5},{5,4},{6,7},{7,6},{8,9},{9,8},{10,11... | collective-permute-start | bytes 1572872 | tf_op jit(solution)/shard_map/ppermute | solution.py:44
  267.7 30.2 %collective-permute-start.9 = (f32[4,64,256]{2,1,0:T(8,128)S(1)}, f32[4,64,256]{2,1,0:T(8,128)S(1)}, u32[]{:S(2)}, u32[]{:S(2)}) collective-permute-start(f32[4,64,256]{2,1,0:T(8,128)S(1)} %dynamic-slice_bitcast_fusion.5), channel_id=1, source_target_pairs={{0,2},{1,3},{2,0},{3,1},{4,6},{5,7},{6,4},{7,5},{8,10},{9,11},{10,... | collective-permute-start | bytes 786440 | tf_op jit(solution)/shard_map/ppermute | solution.py:44
  291.9 11.6 %collective-permute-start.17 = (f32[4,64,256]{2,1,0:T(8,128)S(1)}, f32[4,64,256]{2,1,0:T(8,128)S(1)}, u32[]{:S(2)}, u32[]{:S(2)}) collective-permute-start(f32[4,64,256]{2,1,0:T(8,128)S(1)} %dynamic-slice_bitcast_fusion.4), channel_id=1, source_target_pairs={{0,2},{1,3},{2,0},{3,1},{4,6},{5,7},{6,4},{7,5},{8,10},{9,11},{10,... | collective-permute-start | bytes 786440 | tf_op jit(solution)/shard_map/ppermute | solution.py:44
  292.1 17.0 %collective-permute-start.25 = (f32[4,64,256]{2,1,0:T(8,128)S(1)}, f32[4,64,256]{2,1,0:T(8,128)S(1)}, u32[]{:S(2)}, u32[]{:S(2)}) collective-permute-start(f32[4,64,256]{2,1,0:T(8,128)S(1)} %dynamic-slice_bitcast_fusion.3), channel_id=1, source_target_pairs={{0,2},{1,3},{2,0},{3,1},{4,6},{5,7},{6,4},{7,5},{8,10},{9,11},{10,... | collective-permute-start | bytes 786440 | tf_op jit(solution)/shard_map/ppermute | solution.py:44
  297.9 16.0 %collective-permute-start.10 = (f32[2,64,256]{2,1,0:T(8,128)S(1)}, f32[2,64,256]{2,1,0:T(8,128)S(1)}, u32[]{:S(2)}, u32[]{:S(2)}) collective-permute-start(f32[2,64,256]{2,1,0:T(8,128)S(1)} %dynamic-slice_bitcast_fusion.8), channel_id=1, source_target_pairs={{0,4},{1,5},{2,6},{3,7},{4,0},{5,1},{6,2},{7,3},{8,12},{9,13},{10,... | collective-permute-start | bytes 393224 | tf_op jit(solution)/shard_map/ppermute | solution.py:44
  303.5 13.7 %collective-permute-start.18 = (f32[2,64,256]{2,1,0:T(8,128)S(1)}, f32[2,64,256]{2,1,0:T(8,128)S(1)}, u32[]{:S(2)}, u32[]{:S(2)}) collective-permute-start(f32[2,64,256]{2,1,0:T(8,128)S(1)} %dynamic-slice_bitcast_fusion.7), channel_id=1, source_target_pairs={{0,4},{1,5},{2,6},{3,7},{4,0},{5,1},{6,2},{7,3},{8,12},{9,13},{10,... | collective-permute-start | bytes 393224 | tf_op jit(solution)/shard_map/ppermute | solution.py:44
  309.2 10.9 %collective-permute-start.26 = (f32[2,64,256]{2,1,0:T(8,128)S(1)}, f32[2,64,256]{2,1,0:T(8,128)S(1)}, u32[]{:S(2)}, u32[]{:S(2)}) collective-permute-start(f32[2,64,256]{2,1,0:T(8,128)S(1)} %dynamic-slice_bitcast_fusion.6), channel_id=1, source_target_pairs={{0,4},{1,5},{2,6},{3,7},{4,0},{5,1},{6,2},{7,3},{8,12},{9,13},{10,... | collective-permute-start | bytes 393224 | tf_op jit(solution)/shard_map/ppermute | solution.py:44
  314.0 8.6 %collective-permute-start.11 = (f32[1,64,256]{2,1,0:T(8,128)S(1)}, f32[1,64,256]{2,1,0:T(8,128)S(1)}, u32[]{:S(2)}, u32[]{:S(2)}) collective-permute-start(f32[1,64,256]{2,1,0:T(8,128)S(1)} %constant_dynamic-slice_fusion.2), channel_id=1, source_target_pairs={{0,8},{1,9},{2,10},{3,11},{4,12},{5,13},{6,14},{7,15},{8,0},{9,1},... | collective-permute-start | bytes 196616 | tf_op jit(solution)/shard_map/ppermute | solution.py:44
  317.3 5.8 %collective-permute-start.19 = (f32[1,64,256]{2,1,0:T(8,128)S(1)}, f32[1,64,256]{2,1,0:T(8,128)S(1)}, u32[]{:S(2)}, u32[]{:S(2)}) collective-permute-start(f32[1,64,256]{2,1,0:T(8,128)S(1)} %constant_dynamic-slice_fusion.1), channel_id=1, source_target_pairs={{0,8},{1,9},{2,10},{3,11},{4,12},{5,13},{6,14},{7,15},{8,0},{9,1},... | collective-permute-start | bytes 196616 | tf_op jit(solution)/shard_map/ppermute | solution.py:44
  320.1 5.8 %collective-permute-start.27 = (f32[1,64,256]{2,1,0:T(8,128)S(1)}, f32[1,64,256]{2,1,0:T(8,128)S(1)}, u32[]{:S(2)}, u32[]{:S(2)}) collective-permute-start(f32[1,64,256]{2,1,0:T(8,128)S(1)} %constant_dynamic-slice_fusion), channel_id=1, source_target_pairs={{0,8},{1,9},{2,10},{3,11},{4,12},{5,13},{6,14},{7,15},{8,0},{9,1},... | collective-permute-start | bytes 196616 | tf_op jit(solution)/shard_map/ppermute | solution.py:44

commit v5 on v4

--- a/solution.py
+++ b/solution.py
@@ -57,7 +57,10 @@
     return jnp.concatenate([below, above], axis=dim)
 
 
-def smooth_kernel(coef_ref, a_ref, h_ref, o_ref, *, sub):
+def smooth_kernel(coef_ref, a_ref, h_ref, *refs, sub, aliased):
+    if aliased:
+        refs = refs[1:]
+    o_ref, p_ref = refs
     depth, lat = a_ref.shape[1], a_ref.shape[2]
     half = lat // 2
     shape = (sub, depth, half)
@@ -108,6 +111,7 @@
         for h in range(2):
             out = jnp.where(low_rows, pltpu.roll(x[0][h], HALO, 1), pltpu.roll(x[1][h], HALO, 1))
             o_ref[pl.ds(r, sub), :, h * half : (h + 1) * half] = out
+            p_ref[pl.ds(r, sub), :, h * half : (h + 1) * half] = out.astype(p_ref.dtype)
         return carry
 
     lax.fori_loop(0, a_ref.shape[0] // sub, body, 0)
@@ -130,20 +134,35 @@
     )
 
 
-def smooth(sensitivity, halo, coef, block=128, sub=16):
+def smooth_chunk(field, sensitivity, halo, coef, chunk, size, block=128, sub=16):
     rows, depth, lat = sensitivity.shape
-    kernel = functools.partial(smooth_kernel, sub=sub)
+    steps = size // block
+    first = chunk * steps
+    aliased = field is not None
+    kernel = functools.partial(smooth_kernel, sub=sub, aliased=aliased)
+    in_specs = [
+        pl.BlockSpec(coef.shape, lambda i: (0, 0, 0)),
+        pl.BlockSpec((block, depth, lat), lambda i: (i + first, 0, 0)),
+        pl.BlockSpec((block, depth, lat), lambda i: (i + first, 0, 0)),
+    ]
+    args = [coef, sensitivity, halo]
+    if aliased:
+        in_specs.append(pl.BlockSpec(memory_space=pl.ANY))
+        args.append(field)
     return pl.pallas_call(
         kernel,
-        grid=(rows // block,),
-        in_specs=[
-            pl.BlockSpec(coef.shape, lambda i: (0, 0, 0)),
-            pl.BlockSpec((block, depth, lat), lambda i: (i, 0, 0)),
+        grid=(steps,),
+        in_specs=in_specs,
+        out_specs=[
+            pl.BlockSpec((block, depth, lat), lambda i: (i + first, 0, 0)),
             pl.BlockSpec((block, depth, lat), lambda i: (i, 0, 0)),
         ],
-        out_specs=pl.BlockSpec((block, depth, lat), lambda i: (i, 0, 0)),
-        out_shape=jax.ShapeDtypeStruct((rows, depth, lat), jnp.float32),
-    )(coef, sensitivity, halo)
+        out_shape=[
+            jax.ShapeDtypeStruct((rows, depth, lat), jnp.float32),
+            jax.ShapeDtypeStruct((size, depth, lat), jnp.bfloat16),
+        ],
+        input_output_aliases={3: 0} if aliased else {},
+    )(*args)
 
 
 def body(sensitivity, cell_class, class_rate, panel_owner):
@@ -155,12 +174,17 @@
     halo = halo_of(sensitivity, "slab", 1)
     kappa_halo = halo_of(kappa, "slab", 0)
     kappa_col = jnp.concatenate([kappa_halo[:HALO], kappa, kappa_halo[HALO:]], axis=0)
-    field = smooth(sensitivity, halo, coefficients(kappa_col, lat))
+    coef = coefficients(kappa_col, lat)
+    field = None
+    pieces = []
+    for chunk in range(rows // PANEL):
+        field, piece = smooth_chunk(field, sensitivity, halo, coef, chunk, PANEL)
+        pieces.append(piece)
     cells = depth * lat * lax.axis_size("slab")
     flat = sensitivity.reshape(rows, depth * lat)
     partials = []
     for p in range(PANELS):
-        piece = field[p * PANEL : (p + 1) * PANEL].reshape(PANEL, depth * lat).astype(jnp.bfloat16)
+        piece = pieces[p].reshape(PANEL, depth * lat)
         received = broadcast_dp(piece, panel_owner[p], "dp")
         term = (
             lax.dot_general(

time: 327 us -> 328 us (level)
  Pallas kernels: 72.1 us -> 79.7 us
  other arithmetic: 14.1 us -> 9.1 us
  starting transfers between devices: 124 us -> 119 us
    ppermute x3, waiting for transfers between devices: 21.8 us -> 9.55 us  [broadcast_dp(): pair = lax.ppermute(piece, axis, [(i, i ^ 1) for i in range(size)])]
    ppermute x3, waiting for transfers between devices: 20.5 us -> 31.7 us  [broadcast_dp(): lax.ppermute(val, axis, [(i, (i + 2) % size) for i in range(size)])]
    pallas_call x1 -> x4, Pallas kernels: 72.1 us -> 79.7 us  [smooth_chunk(): pl.pallas_call(kernel, grid=(steps,), in_specs=in_specs, out_specs=[pl.Bl...]
    ppermute x12, starting transfers between devices: 95.1 us -> 89 us  [reduce_scatter_slab(): part = keep + lax.ppermute(send, axis, [(i, i ^ bit) for i in range(size)])]
    ppermute x12, waiting for transfers between devices: 10.6 us -> 14.6 us  [reduce_scatter_slab(): part = keep + lax.ppermute(send, axis, [(i, i ^ bit) for i in range(size)])]
    another operation x1 -> x0, other arithmetic: 3.79 us -> none
    unnamed x14 -> x16, local copies, waits for them, and re-layouts: 6.56 us -> 9.03 us
  transfers between devices with their start and end apart: 28 -> 28, of which waited for: 11 -> 15; matrix products, arithmetic and copies ran while one was open for 9% -> 10% of each run, Pallas kernels for 0% -> 6%
where the time goes in v5:
time: 328 us; the launch traced here: 327 us
  starting transfers between devices  119 us (36%)
  Pallas kernels  79.7 us (24%)
  waiting for transfers between devices  76.6 us (23%)
  local copies, waits for them, and re-layouts  21.1 us (6%)
  matrix products  11.5 us (4%)
  between operations  10.3 us (3%)
  other arithmetic  9.1 us (3%)
    ppermute x12, starting transfers between devices, reduce_scatter_slab(): part = keep + lax.ppermute(send, axis, [(i, i ^ bit) for i in range(size)])  89 us
    pallas_call x4, Pallas kernels, smooth_chunk(): pl.pallas_call(kernel, grid=(steps,), in_specs=in_specs, out_specs=[pl.Bl...  79.7 us
    ppermute x3, waiting for transfers between devices, broadcast_dp(): lax.ppermute(val, axis, [(i, (i + 2) % size) for i in range(size)])  31.7 us
    ppermute x3, waiting for transfers between devices, broadcast_dp(): last = lax.ppermute(val, axis, [(i, (i + 2) % size) for i in range(size)])  19.8 us
    ppermute x12, waiting for transfers between devices, reduce_scatter_slab(): part = keep + lax.ppermute(send, axis, [(i, i ^ bit) for i in range(size)])  14.6 us
    dot_general x3, matrix products, body(): lax.dot_general(flat, received, (((1,), (1,)), ((), ())), preferred_eleme...  11.5 us
    ppermute x3, waiting for transfers between devices, broadcast_dp(): pair = lax.ppermute(piece, axis, [(i, i ^ 1) for i in range(size)])  9.55 us
    ppermute x3, starting transfers between devices, broadcast_dp(): lax.ppermute(val, axis, [(i, (i - 2) % size) for i in range(size)])  9.04 us
  transfers between devices with their start and end apart: 28, of which 15 were waited for; matrix products, arithmetic and copies ran while one was open for 10% of the time, Pallas kernels for 6%

profile of v5, /device:TPU:0, one launch (start us, length us, event | category | flops | bytes accessed | tf_op | source)
XLA Modules:
  0.0 327.1 jit_solution(10571130062687094798)
XLA Ops:
  0.6 4.8 %fusion.10 = (bf16[1024,4,256]{2,1,0:T(4,128)(2,1)S(1)}, bf16[1024,4,256]{2,1,0:T(4,128)(2,1)S(1)}) fusion(bf16[1024,8,256]{2,1,0:T(8,128)(2,1)} %a_ref.7), kind=kLoop, calls=%fused_computation.59 | loop fusion | bytes 8388608 | tf_op jit(solution)/shard_map/slice | solution.py:53
  5.5 1.3 collective-permute-start.3
  6.8 3.2 collective-permute-start.2
  10.1 1.3 collective-permute-start.1
  11.4 3.6 %collective-permute-start = (f32[4,256]{1,0:T(4,128)S(1)}, f32[4,256]{1,0:T(4,128)S(1)}, u32[]{:S(2)}, u32[]{:S(2)}) collective-permute-start(f32[4,256]{1,0:T(4,128)S(1)} %get-tuple-element.18), channel_id=1, source_target_pairs={{0,1},{1,2},{2,3},{3,4},{4,5},{5,6},{6,7},{7,8},{8,9},{9,10},{10,1... | collective-permute-start | bytes 12296 | tf_op jit(solution)/shard_map/ppermute | solution.py:55
  15.9 3.5 %pad_maximum_fusion.h_ref = bf16[1024,8,256]{2,1,0:T(8,128)(2,1)} fusion(bf16[1024,4,256]{2,1,0:T(4,128)(2,1)S(1)} %collective-permute-done.3, bf16[1024,4,256]{2,1,0:T(4,128)(2,1)S(1)} %collective-permute-done.2), kind=kLoop, calls=%fused_computation | loop fusion | flops 8388608 | bytes 8388608 | tf_op jit(solution)/shard_map/concatenate | solution.py:57
  19.4 19.9 %shard_map.59 = (f32[1024,8,256]{2,1,0:T(8,128)}, bf16[256,8,256]{2,1,0:T(8,128)(2,1)}) custom-call(f32[6,16,256]{2,1,0:T(8,128)} %copy-done.1, bf16[1024,8,256]{2,1,0:T(8,128)(2,1)} %a_ref.7, bf16[1024,8,256]{2,1,0:T(8,128)(2,1)} %pad_maximum_fusion.h_ref), custom_call_target="tpu_custom_call" | custom-call | tf_op jit(solution)/shard_map/pallas_call | solution.py:152
  39.3 19.9 %shard_map.60 = (f32[1024,8,256]{2,1,0:T(8,128)}, bf16[256,8,256]{2,1,0:T(8,128)(2,1)}) custom-call(f32[6,16,256]{2,1,0:T(8,128)} %copy-done.1, bf16[1024,8,256]{2,1,0:T(8,128)(2,1)} %a_ref.7, bf16[1024,8,256]{2,1,0:T(8,128)(2,1)} %pad_maximum_fusion.h_ref, f32[1024,8,256]{2,1,0:T(8,128)} %get-tuple-element.9.refs_0_), custom_call_target="tpu_custom_call", output_to_operand_aliasing={{0}: (3, {})} | custom-call | tf_op jit(solution)/shard_map/pallas_call | solution.py:152
  59.3 20.0 %shard_map.61 = (f32[1024,8,256]{2,1,0:T(8,128)}, bf16[256,8,256]{2,1,0:T(8,128)(2,1)}) custom-call(f32[6,16,256]{2,1,0:T(8,128)} %copy-done.1, bf16[1024,8,256]{2,1,0:T(8,128)(2,1)} %a_ref.7, bf16[1024,8,256]{2,1,0:T(8,128)(2,1)} %pad_maximum_fusion.h_ref, f32[1024,8,256]{2,1,0:T(8,128)} %get-tuple-element.10.refs_0_), custom_call_target="tpu_custom_call", output_to_operand_aliasing={{0}: (3, {})} | custom-call | tf_op jit(solution)/shard_map/pallas_call | solution.py:152
  79.3 1.5 copy.21
  80.8 1.7 collective-permute-start.20
  93.2 5.6 %copy.19 = bf16[128,8,8,256]{3,1,2,0:T(8,128)(2,1)} copy(bf16[128,8,8,256]{3,2,1,0:T(8,128)(2,1)} %bitcast.78) | data formatting | bytes 8388608
  98.9 19.9 %shard_map.62 = (f32[1024,8,256]{2,1,0:T(8,128)}, bf16[256,8,256]{2,1,0:T(8,128)(2,1)}) custom-call(f32[6,16,256]{2,1,0:T(8,128)} %copy-done.1, bf16[1024,8,256]{2,1,0:T(8,128)(2,1)} %a_ref.7, bf16[1024,8,256]{2,1,0:T(8,128)(2,1)} %pad_maximum_fusion.h_ref, f32[1024,8,256]{2,1,0:T(8,128)} %get-tuple-element.11.refs_0_), custom_call_target="tpu_custom_call", output_to_operand_aliasing={{0}: (3, {})} | custom-call | tf_op jit(solution)/shard_map/pallas_call | solution.py:152
  118.8 1.5 copy.18
  120.3 1.7 collective-permute-start.4
  122.0 1.3 broadcast_select_fusion
  124.1 3.6 %collective-permute-start.22 = (bf16[256,2048]{1,0:T(8,128)(2,1)S(1)}, bf16[256,2048]{1,0:T(8,128)(2,1)S(1)}, u32[]{:S(2)}, u32[]{:S(2)}) collective-permute-start(bf16[256,2048]{1,0:T(8,128)(2,1)S(1)} %broadcast_select_fusion), channel_id=1, source_target_pairs={{0,96},{16,112},{32,0},{48,16},{64,32},{80,48},{96,64},{112,80},{1... | collective-permute-start | bytes 3145736 | tf_op jit(solution)/shard_map/ppermute | solution.py:27
  127.9 3.2 collective-permute-start.14
  131.1 9.5 %collective-permute-done.4 = bf16[256,2048]{1,0:T(8,128)(2,1)S(1)} collective-permute-done((bf16[256,2048]{1,0:T(8,128)(2,1)S(1)}, bf16[256,2048]{1,0:T(8,128)(2,1)S(1)}, u32[]{:S(2)}, u32[]{:S(2)}) %collective-permute-start.4) | collective-permute-done | bytes 1048608 | tf_op jit(solution)/shard_map/ppermute | solution.py:24
  140.7 2.0 collective-permute-start.5
  142.7 2.2 collective-permute-start.6
  145.2 11.9 %collective-permute-done.13 = bf16[256,2048]{1,0:T(8,128)(2,1)S(1)} collective-permute-done((bf16[256,2048]{1,0:T(8,128)(2,1)S(1)}, bf16[256,2048]{1,0:T(8,128)(2,1)S(1)}, u32[]{:S(2)}, u32[]{:S(2)}) %collective-permute-start.13) | collective-permute-done | bytes 1048608 | tf_op jit(solution)/shard_map/ppermute | solution.py:26
  157.5 2.4 collective-permute-start.15
  159.8 19.8 %collective-permute-done.5 = bf16[256,2048]{1,0:T(8,128)(2,1)S(1)} collective-permute-done((bf16[256,2048]{1,0:T(8,128)(2,1)S(1)}, bf16[256,2048]{1,0:T(8,128)(2,1)S(1)}, u32[]{:S(2)}, u32[]{:S(2)}) %collective-permute-start.5) | collective-permute-done | bytes 1048608 | tf_op jit(solution)/shard_map/ppermute | solution.py:26
  179.9 2.4 collective-permute-start.7
  182.3 19.8 %collective-permute-done.23 = bf16[256,2048]{1,0:T(8,128)(2,1)S(1)} collective-permute-done((bf16[256,2048]{1,0:T(8,128)(2,1)S(1)}, bf16[256,2048]{1,0:T(8,128)(2,1)S(1)}, u32[]{:S(2)}, u32[]{:S(2)}) %collective-permute-start.23) | collective-permute-done | bytes 1048608 | tf_op jit(solution)/shard_map/ppermute | solution.py:29
  202.1 2.3 fusion
  204.3 1.6 copy.17
  206.8 33.8 %collective-permute-start.24 = (f32[8,64,256]{2,1,0:T(8,128)}, f32[8,64,256]{2,1,0:T(8,128)}, u32[]{:S(2)}, u32[]{:S(2)}) collective-permute-start(f32[8,64,256]{2,1,0:T(8,128)} %dynamic-slice_bitcast_fusion), channel_id=1, source_target_pairs={{0,1},{1,0},{2,3},{3,2},{4,5},{5,4},{6,7},{7,6},{8,9},{9,8},{10,11... | collective-permute-start | bytes 1572872 | tf_op jit(solution)/shard_map/ppermute | solution.py:44
  240.5 4.8 %fusion.1 = f32[1024,256]{0,1:T(8,128)} fusion(bf16[1024,2048]{1,0:T(8,128)(2,1)} %bitcast.79, bf16[256,2048]{1,0:T(8,128)(2,1)} %collective-permute-done.15, bf16[256,2048]{1,0:T(8,128)(2,1)S(1)} %select_select_fusion.1, pred[]{:T(512)S(6)} %eq.77), kind=kOutput, calls=%fused_computation.4 | convolution fusion | flops 1074528256 | bytes 7340033 | tf_op jit(solution)/shard_map/dot_general | solution.py:190
  245.3 1.6 copy.16
  247.7 11.9 %collective-permute-start.16 = (f32[8,64,256]{2,1,0:T(8,128)}, f32[8,64,256]{2,1,0:T(8,128)}, u32[]{:S(2)}, u32[]{:S(2)}) collective-permute-start(f32[8,64,256]{2,1,0:T(8,128)} %dynamic-slice_bitcast_fusion.1), channel_id=1, source_target_pairs={{0,1},{1,0},{2,3},{3,2},{4,5},{5,4},{6,7},{7,6},{8,9},{9,8},{10,11... | collective-permute-start | bytes 1572872 | tf_op jit(solution)/shard_map/ppermute | solution.py:44
  259.6 4.5 %fusion.2 = f32[1024,256]{0,1:T(8,128)} fusion(bf16[1024,2048]{1,0:T(8,128)(2,1)} %bitcast.80, bf16[256,2048]{1,0:T(8,128)(2,1)} %collective-permute-done.7, bf16[256,2048]{1,0:T(8,128)(2,1)S(1)} %select_select_fusion.2, pred[]{:T(512)S(6)} %eq.73), kind=kOutput, calls=%fused_computation.6 | convolution fusion | flops 1074528256 | bytes 7340033 | tf_op jit(solution)/shard_map/dot_general | solution.py:190
  264.1 1.6 copy.15
  265.7 4.1 %collective-permute-start.8 = (f32[8,64,256]{2,1,0:T(8,128)S(1)}, f32[8,64,256]{2,1,0:T(8,128)S(1)}, u32[]{:S(2)}, u32[]{:S(2)}) collective-permute-start(f32[8,64,256]{2,1,0:T(8,128)S(1)} %dynamic-slice_bitcast_fusion.2), channel_id=1, source_target_pairs={{0,1},{1,0},{2,3},{3,2},{4,5},{5,4},{6,7},{7,6},{8,9},{9,8},{10,11... | collective-permute-start | bytes 1572872 | tf_op jit(solution)/shard_map/ppermute | solution.py:44
  269.9 1.1 bitcast_add_fusion
  271.0 18.5 %collective-permute-start.25 = (f32[4,64,256]{2,1,0:T(8,128)S(1)}, f32[4,64,256]{2,1,0:T(8,128)S(1)}, u32[]{:S(2)}, u32[]{:S(2)}) collective-permute-start(f32[4,64,256]{2,1,0:T(8,128)S(1)} %dynamic-slice_bitcast_fusion.3), channel_id=1, source_target_pairs={{0,2},{1,3},{2,0},{3,1},{4,6},{5,7},{6,4},{7,5},{8,10},{9,11},{10,... | collective-permute-start | bytes 786440 | tf_op jit(solution)/shard_map/ppermute | solution.py:44
  289.5 1.1 bitcast_add_fusion.1
  290.9 2.1 collective-permute-start.9
  292.9 3.7 %collective-permute-done.25 = f32[4,64,256]{2,1,0:T(8,128)S(1)} collective-permute-done((f32[4,64,256]{2,1,0:T(8,128)S(1)}, f32[4,64,256]{2,1,0:T(8,128)S(1)}, u32[]{:S(2)}, u32[]{:S(2)}) %collective-permute-start.25) | collective-permute-done | bytes 262176 | tf_op jit(solution)/shard_map/ppermute | solution.py:44
  296.7 5.2 %collective-permute-start.26 = (f32[2,64,256]{2,1,0:T(8,128)S(1)}, f32[2,64,256]{2,1,0:T(8,128)S(1)}, u32[]{:S(2)}, u32[]{:S(2)}) collective-permute-start(f32[2,64,256]{2,1,0:T(8,128)S(1)} %dynamic-slice_bitcast_fusion.6), channel_id=1, source_target_pairs={{0,4},{1,5},{2,6},{3,7},{4,0},{5,1},{6,2},{7,3},{8,12},{9,13},{10,... | collective-permute-start | bytes 393224 | tf_op jit(solution)/shard_map/ppermute | solution.py:44
  302.3 5.2 %collective-permute-start.18 = (f32[2,64,256]{2,1,0:T(8,128)S(1)}, f32[2,64,256]{2,1,0:T(8,128)S(1)}, u32[]{:S(2)}, u32[]{:S(2)}) collective-permute-start(f32[2,64,256]{2,1,0:T(8,128)S(1)} %dynamic-slice_bitcast_fusion.7), channel_id=1, source_target_pairs={{0,4},{1,5},{2,6},{3,7},{4,0},{5,1},{6,2},{7,3},{8,12},{9,13},{10,... | collective-permute-start | bytes 393224 | tf_op jit(solution)/shard_map/ppermute | solution.py:44
  308.0 5.2 %collective-permute-start.10 = (f32[2,64,256]{2,1,0:T(8,128)S(1)}, f32[2,64,256]{2,1,0:T(8,128)S(1)}, u32[]{:S(2)}, u32[]{:S(2)}) collective-permute-start(f32[2,64,256]{2,1,0:T(8,128)S(1)} %dynamic-slice_bitcast_fusion.8), channel_id=1, source_target_pairs={{0,4},{1,5},{2,6},{3,7},{4,0},{5,1},{6,2},{7,3},{8,12},{9,13},{10,... | collective-permute-start | bytes 393224 | tf_op jit(solution)/shard_map/ppermute | solution.py:44
  313.2 2.7 collective-permute-done.26
  316.0 2.7 collective-permute-done.18
  320.6 1.9 collective-permute-start.11
  322.5 2.7 collective-permute-done.19
  325.2 1.2 collective-permute-done.11
  (80 shorter events, 10.0 us)
Async XLA Ops:
  0.6 9.3 %copy-start.5 = (f32[8]{0:T(128)S(1)}, f32[8]{0:T(128)}, u32[]{:S(2)}) copy-start(f32[8]{0:T(128)} %param.6) | copy-start | bytes 100
  0.6 9.3 %copy-start.3 = (s32[8,256]{1,0:T(8,128)S(1)}, s32[8,256]{1,0:T(8,128)}, u32[]{:S(2)}) copy-start(s32[8,256]{1,0:T(8,128)} %param.5) | copy-start | bytes 24580
  5.5 10.4 %collective-permute-start.3 = (bf16[1024,4,256]{2,1,0:T(4,128)(2,1)S(1)}, bf16[1024,4,256]{2,1,0:T(4,128)(2,1)S(1)}, u32[]{:S(2)}, u32[]{:S(2)}) collective-permute-start(bf16[1024,4,256]{2,1,0:T(4,128)(2,1)S(1)} %get-tuple-element.17), channel_id=1, source_target_pairs={{1,0},{2,1},{3,2},{4,3},{5,4},{6,5},{7,6},{8,7},{9,8},{10,9},{11,1... | collective-permute-start | bytes 6291464 | tf_op jit(solution)/shard_map/ppermute | solution.py:56
  6.8 9.1 %collective-permute-start.2 = (bf16[1024,4,256]{2,1,0:T(4,128)(2,1)S(1)}, bf16[1024,4,256]{2,1,0:T(4,128)(2,1)S(1)}, u32[]{:S(2)}, u32[]{:S(2)}) collective-permute-start(bf16[1024,4,256]{2,1,0:T(4,128)(2,1)S(1)} %get-tuple-element.16), channel_id=1, source_target_pairs={{0,1},{1,2},{2,3},{3,4},{4,5},{5,6},{6,7},{7,8},{8,9},{9,10},{10,1... | collective-permute-start | bytes 6291464 | tf_op jit(solution)/shard_map/ppermute | solution.py:55
  10.1 5.0 %collective-permute-start.1 = (f32[4,256]{1,0:T(4,128)S(1)}, f32[4,256]{1,0:T(4,128)S(1)}, u32[]{:S(2)}, u32[]{:S(2)}) collective-permute-start(f32[4,256]{1,0:T(4,128)S(1)} %get-tuple-element.19), channel_id=1, source_target_pairs={{1,0},{2,1},{3,2},{4,3},{5,4},{6,5},{7,6},{8,7},{9,8},{10,9},{11,1... | collective-permute-start | bytes 12296 | tf_op jit(solution)/shard_map/ppermute | solution.py:56
  11.4 4.4 %collective-permute-start = (f32[4,256]{1,0:T(4,128)S(1)}, f32[4,256]{1,0:T(4,128)S(1)}, u32[]{:S(2)}, u32[]{:S(2)}) collective-permute-start(f32[4,256]{1,0:T(4,128)S(1)} %get-tuple-element.18), channel_id=1, source_target_pairs={{0,1},{1,2},{2,3},{3,4},{4,5},{5,6},{6,7},{7,8},{8,9},{9,10},{10,1... | collective-permute-start | bytes 12296 | tf_op jit(solution)/shard_map/ppermute | solution.py:55
  15.9 3.6 %copy-start.1 = (f32[6,16,256]{2,1,0:T(8,128)}, f32[6,16,256]{2,1,0:T(8,128)S(1)}, u32[]{:S(2)}) copy-start(f32[6,16,256]{2,1,0:T(8,128)S(1)} %select_dynamic-update-slice_fusion.coef_ref) | copy-start | bytes 294916
  59.2 23.2 %copy-start.2 = (bf16[256,8,256]{2,1,0:T(8,128)(2,1)S(1)}, bf16[256,8,256]{2,1,0:T(8,128)(2,1)}, u32[]{:S(2)}) copy-start(bf16[256,8,256]{2,1,0:T(8,128)(2,1)} %get-tuple-element.14) | copy-start | bytes 3145732
  79.3 4.0 %copy-start.4 = (s32[8]{0:T(128)S(1)}, s32[8]{0:T(128)}, u32[]{:S(2)}) copy-start(s32[8]{0:T(128)} %param.7) | copy-start | bytes 100
  80.8 41.1 %collective-permute-start.20 = (bf16[256,2048]{1,0:T(8,128)(2,1)S(1)}, bf16[256,2048]{1,0:T(8,128)(2,1)}, u32[]{:S(2)}, u32[]{:S(2)}) collective-permute-start(bf16[256,2048]{1,0:T(8,128)(2,1)S(1)} %bitcast.84), channel_id=1, source_target_pairs={{0,16},{16,0},{32,48},{48,32},{64,80},{80,64},{96,112},{112,96},{1... | collective-permute-start | bytes 3145736 | tf_op jit(solution)/shard_map/ppermute | solution.py:24
  82.8 44.9 %collective-permute-start.12 = (bf16[256,2048]{1,0:T(8,128)(2,1)S(1)}, bf16[256,2048]{1,0:T(8,128)(2,1)S(1)}, u32[]{:S(2)}, u32[]{:S(2)}) collective-permute-start(bf16[256,2048]{1,0:T(8,128)(2,1)S(1)} %bitcast.82), channel_id=1, source_target_pairs={{0,16},{16,0},{32,48},{48,32},{64,80},{80,64},{96,112},{112,96},{1... | collective-permute-start | bytes 3145736 | tf_op jit(solution)/shard_map/ppermute | solution.py:24
  120.3 20.3 %collective-permute-start.4 = (bf16[256,2048]{1,0:T(8,128)(2,1)S(1)}, bf16[256,2048]{1,0:T(8,128)(2,1)S(1)}, u32[]{:S(2)}, u32[]{:S(2)}) collective-permute-start(bf16[256,2048]{1,0:T(8,128)(2,1)S(1)} %bitcast.88), channel_id=1, source_target_pairs={{0,16},{16,0},{32,48},{48,32},{64,80},{80,64},{96,112},{112,96},{1... | collective-permute-start | bytes 3145736 | tf_op jit(solution)/shard_map/ppermute | solution.py:24
  123.3 19.4 %collective-permute-start.21 = (bf16[256,2048]{1,0:T(8,128)(2,1)S(1)}, bf16[256,2048]{1,0:T(8,128)(2,1)S(1)}, u32[]{:S(2)}, u32[]{:S(2)}) collective-permute-start(bf16[256,2048]{1,0:T(8,128)(2,1)S(1)} %broadcast_select_fusion), channel_id=1, source_target_pairs={{0,32},{16,48},{32,64},{48,80},{64,96},{80,112},{96,0},{112,16},{1... | collective-permute-start | bytes 3145736 | tf_op jit(solution)/shard_map/ppermute | solution.py:26
  124.1 20.9 %collective-permute-start.22 = (bf16[256,2048]{1,0:T(8,128)(2,1)S(1)}, bf16[256,2048]{1,0:T(8,128)(2,1)S(1)}, u32[]{:S(2)}, u32[]{:S(2)}) collective-permute-start(bf16[256,2048]{1,0:T(8,128)(2,1)S(1)} %broadcast_select_fusion), channel_id=1, source_target_pairs={{0,96},{16,112},{32,0},{48,16},{64,32},{80,48},{96,64},{112,80},{1... | collective-permute-start | bytes 3145736 | tf_op jit(solution)/shard_map/ppermute | solution.py:27
  127.8 29.3 %collective-permute-start.13 = (bf16[256,2048]{1,0:T(8,128)(2,1)S(1)}, bf16[256,2048]{1,0:T(8,128)(2,1)S(1)}, u32[]{:S(2)}, u32[]{:S(2)}) collective-permute-start(bf16[256,2048]{1,0:T(8,128)(2,1)S(1)} %broadcast_select_fusion.1), channel_id=1, source_target_pairs={{0,32},{16,48},{32,64},{48,80},{64,96},{80,112},{96,0},{112,16},{1... | collective-permute-start | bytes 3145736 | tf_op jit(solution)/shard_map/ppermute | solution.py:26
  127.9 29.3 %collective-permute-start.14 = (bf16[256,2048]{1,0:T(8,128)(2,1)S(1)}, bf16[256,2048]{1,0:T(8,128)(2,1)S(1)}, u32[]{:S(2)}, u32[]{:S(2)}) collective-permute-start(bf16[256,2048]{1,0:T(8,128)(2,1)S(1)} %broadcast_select_fusion.1), channel_id=1, source_target_pairs={{0,96},{16,112},{32,0},{48,16},{64,32},{80,48},{96,64},{112,80},{1... | collective-permute-start | bytes 3145736 | tf_op jit(solution)/shard_map/ppermute | solution.py:27
  140.7 38.8 %collective-permute-start.5 = (bf16[256,2048]{1,0:T(8,128)(2,1)S(1)}, bf16[256,2048]{1,0:T(8,128)(2,1)S(1)}, u32[]{:S(2)}, u32[]{:S(2)}) collective-permute-start(bf16[256,2048]{1,0:T(8,128)(2,1)S(1)} %broadcast_select_fusion.2), channel_id=1, source_target_pairs={{0,32},{16,48},{32,64},{48,80},{64,96},{80,112},{96,0},{112,16},{1... | collective-permute-start | bytes 3145736 | tf_op jit(solution)/shard_map/ppermute | solution.py:26
  142.7 36.9 %collective-permute-start.6 = (bf16[256,2048]{1,0:T(8,128)(2,1)S(1)}, bf16[256,2048]{1,0:T(8,128)(2,1)S(1)}, u32[]{:S(2)}, u32[]{:S(2)}) collective-permute-start(bf16[256,2048]{1,0:T(8,128)(2,1)S(1)} %broadcast_select_fusion.2), channel_id=1, source_target_pairs={{0,96},{16,112},{32,0},{48,16},{64,32},{80,48},{96,64},{112,80},{1... | collective-permute-start | bytes 3145736 | tf_op jit(solution)/shard_map/ppermute | solution.py:27
  145.1 57.0 %copy-start = (bf16[128,8,8,256]{3,1,2,0:T(8,128)(2,1)S(1)}, bf16[128,8,8,256]{3,1,2,0:T(8,128)(2,1)}, u32[]{:S(2)}) copy-start(bf16[128,8,8,256]{3,1,2,0:T(8,128)(2,1)} %copy.19) | copy-start | bytes 12582916
  145.1 57.0 %collective-permute-start.23 = (bf16[256,2048]{1,0:T(8,128)(2,1)S(1)}, bf16[256,2048]{1,0:T(8,128)(2,1)S(1)}, u32[]{:S(2)}, u32[]{:S(2)}) collective-permute-start(bf16[256,2048]{1,0:T(8,128)(2,1)S(1)} %select_select_fusion), channel_id=1, source_target_pairs={{0,32},{16,48},{32,64},{48,80},{64,96},{80,112},{96,0},{112,16},{1... | collective-permute-start | bytes 3145736 | tf_op jit(solution)/shard_map/ppermute | solution.py:29
  157.5 83.1 %collective-permute-start.15 = (bf16[256,2048]{1,0:T(8,128)(2,1)S(1)}, bf16[256,2048]{1,0:T(8,128)(2,1)}, u32[]{:S(2)}, u32[]{:S(2)}) collective-permute-start(bf16[256,2048]{1,0:T(8,128)(2,1)S(1)} %select_select_fusion.1), channel_id=1, source_target_pairs={{0,32},{16,48},{32,64},{48,80},{64,96},{80,112},{96,0},{112,16},{1... | collective-permute-start | bytes 3145736 | tf_op jit(solution)/shard_map/ppermute | solution.py:29
  179.9 79.7 %collective-permute-start.7 = (bf16[256,2048]{1,0:T(8,128)(2,1)S(1)}, bf16[256,2048]{1,0:T(8,128)(2,1)}, u32[]{:S(2)}, u32[]{:S(2)}) collective-permute-start(bf16[256,2048]{1,0:T(8,128)(2,1)S(1)} %select_select_fusion.2), channel_id=1, source_target_pairs={{0,32},{16,48},{32,64},{48,80},{64,96},{80,112},{96,0},{112,16},{1... | collective-permute-start | bytes 3145736 | tf_op jit(solution)/shard_map/ppermute | solution.py:29
  206.8 63.1 %collective-permute-start.24 = (f32[8,64,256]{2,1,0:T(8,128)}, f32[8,64,256]{2,1,0:T(8,128)}, u32[]{:S(2)}, u32[]{:S(2)}) collective-permute-start(f32[8,64,256]{2,1,0:T(8,128)} %dynamic-slice_bitcast_fusion), channel_id=1, source_target_pairs={{0,1},{1,0},{2,3},{3,2},{4,5},{5,4},{6,7},{7,6},{8,9},{9,8},{10,11... | collective-permute-start | bytes 1572872 | tf_op jit(solution)/shard_map/ppermute | solution.py:44
  247.7 41.8 %collective-permute-start.16 = (f32[8,64,256]{2,1,0:T(8,128)}, f32[8,64,256]{2,1,0:T(8,128)}, u32[]{:S(2)}, u32[]{:S(2)}) collective-permute-start(f32[8,64,256]{2,1,0:T(8,128)} %dynamic-slice_bitcast_fusion.1), channel_id=1, source_target_pairs={{0,1},{1,0},{2,3},{3,2},{4,5},{5,4},{6,7},{7,6},{8,9},{9,8},{10,11... | collective-permute-start | bytes 1572872 | tf_op jit(solution)/shard_map/ppermute | solution.py:44
  265.7 25.0 %collective-permute-start.8 = (f32[8,64,256]{2,1,0:T(8,128)S(1)}, f32[8,64,256]{2,1,0:T(8,128)S(1)}, u32[]{:S(2)}, u32[]{:S(2)}) collective-permute-start(f32[8,64,256]{2,1,0:T(8,128)S(1)} %dynamic-slice_bitcast_fusion.2), channel_id=1, source_target_pairs={{0,1},{1,0},{2,3},{3,2},{4,5},{5,4},{6,7},{7,6},{8,9},{9,8},{10,11... | collective-permute-start | bytes 1572872 | tf_op jit(solution)/shard_map/ppermute | solution.py:44
  271.0 25.6 %collective-permute-start.25 = (f32[4,64,256]{2,1,0:T(8,128)S(1)}, f32[4,64,256]{2,1,0:T(8,128)S(1)}, u32[]{:S(2)}, u32[]{:S(2)}) collective-permute-start(f32[4,64,256]{2,1,0:T(8,128)S(1)} %dynamic-slice_bitcast_fusion.3), channel_id=1, source_target_pairs={{0,2},{1,3},{2,0},{3,1},{4,6},{5,7},{6,4},{7,5},{8,10},{9,11},{10,... | collective-permute-start | bytes 786440 | tf_op jit(solution)/shard_map/ppermute | solution.py:44
  290.6 11.6 %collective-permute-start.17 = (f32[4,64,256]{2,1,0:T(8,128)S(1)}, f32[4,64,256]{2,1,0:T(8,128)S(1)}, u32[]{:S(2)}, u32[]{:S(2)}) collective-permute-start(f32[4,64,256]{2,1,0:T(8,128)S(1)} %dynamic-slice_bitcast_fusion.4), channel_id=1, source_target_pairs={{0,2},{1,3},{2,0},{3,1},{4,6},{5,7},{6,4},{7,5},{8,10},{9,11},{10,... | collective-permute-start | bytes 786440 | tf_op jit(solution)/shard_map/ppermute | solution.py:44
  290.9 17.0 %collective-permute-start.9 = (f32[4,64,256]{2,1,0:T(8,128)S(1)}, f32[4,64,256]{2,1,0:T(8,128)S(1)}, u32[]{:S(2)}, u32[]{:S(2)}) collective-permute-start(f32[4,64,256]{2,1,0:T(8,128)S(1)} %dynamic-slice_bitcast_fusion.5), channel_id=1, source_target_pairs={{0,2},{1,3},{2,0},{3,1},{4,6},{5,7},{6,4},{7,5},{8,10},{9,11},{10,... | collective-permute-start | bytes 786440 | tf_op jit(solution)/shard_map/ppermute | solution.py:44
  296.7 19.2 %collective-permute-start.26 = (f32[2,64,256]{2,1,0:T(8,128)S(1)}, f32[2,64,256]{2,1,0:T(8,128)S(1)}, u32[]{:S(2)}, u32[]{:S(2)}) collective-permute-start(f32[2,64,256]{2,1,0:T(8,128)S(1)} %dynamic-slice_bitcast_fusion.6), channel_id=1, source_target_pairs={{0,4},{1,5},{2,6},{3,7},{4,0},{5,1},{6,2},{7,3},{8,12},{9,13},{10,... | collective-permute-start | bytes 393224 | tf_op jit(solution)/shard_map/ppermute | solution.py:44
  302.3 16.3 %collective-permute-start.18 = (f32[2,64,256]{2,1,0:T(8,128)S(1)}, f32[2,64,256]{2,1,0:T(8,128)S(1)}, u32[]{:S(2)}, u32[]{:S(2)}) collective-permute-start(f32[2,64,256]{2,1,0:T(8,128)S(1)} %dynamic-slice_bitcast_fusion.7), channel_id=1, source_target_pairs={{0,4},{1,5},{2,6},{3,7},{4,0},{5,1},{6,2},{7,3},{8,12},{9,13},{10,... | collective-permute-start | bytes 393224 | tf_op jit(solution)/shard_map/ppermute | solution.py:44
  308.0 12.6 %collective-permute-start.10 = (f32[2,64,256]{2,1,0:T(8,128)S(1)}, f32[2,64,256]{2,1,0:T(8,128)S(1)}, u32[]{:S(2)}, u32[]{:S(2)}) collective-permute-start(f32[2,64,256]{2,1,0:T(8,128)S(1)} %dynamic-slice_bitcast_fusion.8), channel_id=1, source_target_pairs={{0,4},{1,5},{2,6},{3,7},{4,0},{5,1},{6,2},{7,3},{8,12},{9,13},{10,... | collective-permute-start | bytes 393224 | tf_op jit(solution)/shard_map/ppermute | solution.py:44
  315.9 6.5 %collective-permute-start.27 = (f32[1,64,256]{2,1,0:T(8,128)S(1)}, f32[1,64,256]{2,1,0:T(8,128)S(1)}, u32[]{:S(2)}, u32[]{:S(2)}) collective-permute-start(f32[1,64,256]{2,1,0:T(8,128)S(1)} %constant_dynamic-slice_fusion), channel_id=1, source_target_pairs={{0,8},{1,9},{2,10},{3,11},{4,12},{5,13},{6,14},{7,15},{8,0},{9,1},... | collective-permute-start | bytes 196616 | tf_op jit(solution)/shard_map/ppermute | solution.py:44
  318.7 6.5 %collective-permute-start.19 = (f32[1,64,256]{2,1,0:T(8,128)S(1)}, f32[1,64,256]{2,1,0:T(8,128)S(1)}, u32[]{:S(2)}, u32[]{:S(2)}) collective-permute-start(f32[1,64,256]{2,1,0:T(8,128)S(1)} %constant_dynamic-slice_fusion.1), channel_id=1, source_target_pairs={{0,8},{1,9},{2,10},{3,11},{4,12},{5,13},{6,14},{7,15},{8,0},{9,1},... | collective-permute-start | bytes 196616 | tf_op jit(solution)/shard_map/ppermute | solution.py:44
  320.6 5.8 %collective-permute-start.11 = (f32[1,64,256]{2,1,0:T(8,128)S(1)}, f32[1,64,256]{2,1,0:T(8,128)S(1)}, u32[]{:S(2)}, u32[]{:S(2)}) collective-permute-start(f32[1,64,256]{2,1,0:T(8,128)S(1)} %constant_dynamic-slice_fusion.2), channel_id=1, source_target_pairs={{0,8},{1,9},{2,10},{3,11},{4,12},{5,13},{6,14},{7,15},{8,0},{9,1},... | collective-permute-start | bytes 196616 | tf_op jit(solution)/shard_map/ppermute | solution.py:44

commit v6 on v5

--- a/solution.py
+++ b/solution.py
@@ -182,18 +182,14 @@
         pieces.append(piece)
     cells = depth * lat * lax.axis_size("slab")
     flat = sensitivity.reshape(rows, depth * lat)
-    partials = []
-    for p in range(PANELS):
-        piece = pieces[p].reshape(PANEL, depth * lat)
-        received = broadcast_dp(piece, panel_owner[p], "dp")
-        term = (
-            lax.dot_general(
-                flat, received, (((1,), (1,)), ((), ())), preferred_element_type=jnp.float32
-            )
-            / cells
-        )
-        partials.append(reduce_scatter_slab(term, "slab"))
-    gram = jnp.stack(partials, axis=1)
+    stacked = jnp.stack([pieces[p].reshape(PANEL, depth * lat) for p in range(PANELS)])
+    owners = panel_owner[:PANELS].reshape(PANELS, 1, 1)
+    received = broadcast_dp(stacked, owners, "dp").reshape(PANELS * PANEL, depth * lat)
+    term = (
+        lax.dot_general(flat, received, (((1,), (1,)), ((), ())), preferred_element_type=jnp.float32)
+        / cells
+    )
+    gram = reduce_scatter_slab(term.reshape(rows, PANELS, PANEL), "slab")
     return (field, gram)
 
 

time: 328 us -> 408 us (1.24)
  waiting for transfers between devices: 76.6 us -> 196 us
  starting transfers between devices: 119 us -> 81 us
  local copies, waits for them, and re-layouts: 21.1 us -> 32.5 us
  between operations: 10.3 us -> 0.89 us
  matrix products: 11.5 us -> 5.13 us
    ppermute x3 -> x1, waiting for transfers between devices: 9.55 us -> 51.3 us  [broadcast_dp(): pair = lax.ppermute(piece, axis, [(i, i ^ 1) for i in range(size)])]
    ppermute x3 -> x1, waiting for transfers between devices: 19.8 us -> 59.8 us  [broadcast_dp(): last = lax.ppermute(val, axis, [(i, (i + 2) % size) for i in range(size)])]
    ppermute x12 -> x4, starting transfers between devices: 89 us -> 64.1 us  [reduce_scatter_slab(): part = keep + lax.ppermute(send, axis, [(i, i ^ bit) for i in range(size)])]
    ppermute x3 -> x1, waiting for transfers between devices: 31.7 us -> 51.2 us  [broadcast_dp(): lax.ppermute(val, axis, [(i, (i + 2) % size) for i in range(size)])]
    ppermute x12 -> x4, waiting for transfers between devices: 14.6 us -> 30.4 us  [reduce_scatter_slab(): part = keep + lax.ppermute(send, axis, [(i, i ^ bit) for i in range(size)])]
    another operation x0 -> x5, local copies, waits for them, and re-layouts: none -> 10.6 us  [the longest x4 7.29 us: body(): jnp.stack([pieces[p].reshape(PANEL, depth * lat) for p in range(PANELS)])]
    ppermute x3 -> x1, starting transfers between devices: 9.04 us -> 2.2 us  [broadcast_dp(): lax.ppermute(val, axis, [(i, (i - 2) % size) for i in range(size)])]
    dot_general x3 -> x1, matrix products: 11.5 us -> 5.13 us  [body(): lax.dot_general(flat, received, (((1,), (1,)), ((), ())), preferred_eleme...]
  transfers between devices with their start and end apart: 28 -> 12, of which waited for: 15 -> 8; matrix products, arithmetic and copies ran while one was open for 10% -> 1% of each run, Pallas kernels for 6% -> 5%
where the time goes in v6:
time: 408 us
  waiting for transfers between devices  196 us (48%)
  starting transfers between devices  81 us (20%)
  Pallas kernels  79.8 us (20%)
  local copies, waits for them, and re-layouts  32.5 us (8%)
  other arithmetic  12.6 us (3%)
  matrix products  5.13 us (1%)
    pallas_call x4, Pallas kernels, smooth_chunk(): pl.pallas_call(kernel, grid=(steps,), in_specs=in_specs, out_specs=[pl.Bl...  79.8 us
    ppermute x4, starting transfers between devices, reduce_scatter_slab(): part = keep + lax.ppermute(send, axis, [(i, i ^ bit) for i in range(size)])  64.1 us
    ppermute x1, waiting for transfers between devices, broadcast_dp(): last = lax.ppermute(val, axis, [(i, (i + 2) % size) for i in range(size)])  59.8 us
    ppermute x1, waiting for transfers between devices, broadcast_dp(): pair = lax.ppermute(piece, axis, [(i, i ^ 1) for i in range(size)])  51.3 us
    ppermute x1, waiting for transfers between devices, broadcast_dp(): lax.ppermute(val, axis, [(i, (i + 2) % size) for i in range(size)])  51.2 us
    ppermute x4, waiting for transfers between devices, reduce_scatter_slab(): part = keep + lax.ppermute(send, axis, [(i, i ^ bit) for i in range(size)])  30.4 us
    unnamed x17, local copies, waits for them, and re-layouts  10.2 us
  transfers between devices with their start and end apart: 12, of which 8 were waited for; matrix products, arithmetic and copies ran while one was open for 1% of the time, Pallas kernels for 5%

profile of v6, /device:TPU:0, one launch (start us, length us, event | category | flops | bytes accessed | tf_op | source)
XLA Modules:
  0.0 407.8 jit_solution(7253840078099825009)
XLA Ops:
  0.6 4.8 %fusion.4 = (bf16[1024,4,256]{2,1,0:T(4,128)(2,1)S(1)}, bf16[1024,4,256]{2,1,0:T(4,128)(2,1)S(1)}) fusion(bf16[1024,8,256]{2,1,0:T(8,128)(2,1)} %a_ref.7), kind=kLoop, calls=%fused_computation.49 | loop fusion | bytes 8388608 | tf_op jit(solution)/shard_map/slice | solution.py:53
  5.5 1.4 collective-permute-start.2
  6.9 1.3 collective-permute-start.3
  8.2 0.1 select_reduce_fusion
  8.3 4.7 %collective-permute-start = (f32[4,256]{1,0:T(4,128)S(1)}, f32[4,256]{1,0:T(4,128)S(1)}, u32[]{:S(2)}, u32[]{:S(2)}) collective-permute-start(f32[4,256]{1,0:T(4,128)S(1)} %get-tuple-element.22), channel_id=1, source_target_pairs={{0,1},{1,2},{2,3},{3,4},{4,5},{5,6},{6,7},{7,8},{8,9},{9,10},{10,1... | collective-permute-start | bytes 12296 | tf_op jit(solution)/shard_map/ppermute | solution.py:55
  13.0 1.3 collective-permute-start.1
  14.4 2.9 collective-permute-done.1
  17.5 3.4 pad_maximum_fusion.h_ref
  20.9 19.9 %shard_map.59 = (f32[1024,8,256]{2,1,0:T(8,128)}, bf16[256,8,256]{2,1,0:T(8,128)(2,1)}) custom-call(f32[6,16,256]{2,1,0:T(8,128)} %copy-done.2, bf16[1024,8,256]{2,1,0:T(8,128)(2,1)} %a_ref.7, bf16[1024,8,256]{2,1,0:T(8,128)(2,1)} %pad_maximum_fusion.h_ref), custom_call_target="tpu_custom_call" | custom-call | tf_op jit(solution)/shard_map/pallas_call | solution.py:152
  40.8 20.0 %shard_map.60 = (f32[1024,8,256]{2,1,0:T(8,128)}, bf16[256,8,256]{2,1,0:T(8,128)(2,1)}) custom-call(f32[6,16,256]{2,1,0:T(8,128)} %copy-done.2, bf16[1024,8,256]{2,1,0:T(8,128)(2,1)} %a_ref.7, bf16[1024,8,256]{2,1,0:T(8,128)(2,1)} %pad_maximum_fusion.h_ref, f32[1024,8,256]{2,1,0:T(8,128)} %get-tuple-element.9.refs_0_), custom_call_target="tpu_custom_call", output_to_operand_aliasing={{0}: (3, {})} | custom-call | tf_op jit(solution)/shard_map/pallas_call | solution.py:152
  60.8 2.3 stack_reshape.10
  63.2 1.3 stack_reshape.9
  64.5 1.3 constant_dynamic-update-slice_fusion.8
  65.8 19.9 %shard_map.61 = (f32[1024,8,256]{2,1,0:T(8,128)}, bf16[256,8,256]{2,1,0:T(8,128)(2,1)}) custom-call(f32[6,16,256]{2,1,0:T(8,128)} %copy-done.2, bf16[1024,8,256]{2,1,0:T(8,128)(2,1)} %a_ref.7, bf16[1024,8,256]{2,1,0:T(8,128)(2,1)} %pad_maximum_fusion.h_ref, f32[1024,8,256]{2,1,0:T(8,128)} %get-tuple-element.10.refs_0_), custom_call_target="tpu_custom_call", output_to_operand_aliasing={{0}: (3, {})} | custom-call | tf_op jit(solution)/shard_map/pallas_call | solution.py:152
  85.7 2.4 stack_reshape.11
  88.1 1.3 constant_dynamic-update-slice_fusion.7
  89.4 1.3 constant_dynamic-update-slice_fusion.6
  90.7 1.7 collective-permute-start.4
  92.3 51.3 %collective-permute-done.4 = bf16[3,256,2048]{2,1,0:T(8,128)(2,1)} collective-permute-done((bf16[3,256,2048]{2,1,0:T(8,128)(2,1)S(1)}, bf16[3,256,2048]{2,1,0:T(8,128)(2,1)}, u32[]{:S(2)}, u32[]{:S(2)}) %collective-permute-start.4) | collective-permute-done | bytes 3145760 | tf_op jit(solution)/shard_map/ppermute | solution.py:24
  143.6 2.3 broadcast_select_fusion
  145.9 2.0 collective-permute-start.5
  147.9 2.2 collective-permute-start.6
  150.1 51.2 %collective-permute-done.5 = bf16[3,256,2048]{2,1,0:T(8,128)(2,1)S(1)} collective-permute-done((bf16[3,256,2048]{2,1,0:T(8,128)(2,1)S(1)}, bf16[3,256,2048]{2,1,0:T(8,128)(2,1)S(1)}, u32[]{:S(2)}, u32[]{:S(2)}) %collective-permute-start.5) | collective-permute-done | bytes 3145760 | tf_op jit(solution)/shard_map/ppermute | solution.py:26
  201.3 0.3 collective-permute-done.6
  201.6 0.5 select_select_fusion
  202.1 2.3 collective-permute-start.7
  204.4 5.7 %copy.17 = bf16[128,8,8,256]{3,1,2,0:T(8,128)(2,1)} copy(bf16[128,8,8,256]{3,2,1,0:T(8,128)(2,1)} %bitcast.31) | data formatting | bytes 8388608
  210.1 59.8 %collective-permute-done.7 = bf16[3,256,2048]{2,1,0:T(8,128)(2,1)} collective-permute-done((bf16[3,256,2048]{2,1,0:T(8,128)(2,1)S(1)}, bf16[3,256,2048]{2,1,0:T(8,128)(2,1)}, u32[]{:S(2)}, u32[]{:S(2)}) %collective-permute-start.7) | collective-permute-done | bytes 3145760 | tf_op jit(solution)/shard_map/ppermute | solution.py:29
  269.9 2.4 broadcast_select_fusion.1
  272.4 0.7 copy-done.1
  273.1 5.1 %multiply_bitcast_fusion = f32[1024,768]{0,1:T(8,128)} fusion(bf16[768,2048]{1,0:T(8,128)(2,1)S(1)} %bitcast.37, bf16[1024,2048]{1,0:T(8,128)(2,1)S(1)} %bitcast.34), kind=kOutput, calls=%fused_computation.1 | convolution fusion | flops 3222011904 | bytes 10485760 | tf_op jit(solution)/shard_map/dot_general | solution.py:189
  278.2 2.4 copy.14
  280.6 3.3 reshape_reshape_reshape.3
  283.9 2.9 constant_dynamic-slice_fusion.2
  286.9 1.5 copy.20
  288.3 16.3 %collective-permute-start.8 = (f32[8,64,3,256]{3,1,2,0:T(8,128)}, f32[8,64,3,256]{3,1,2,0:T(8,128)}, u32[]{:S(2)}, u32[]{:S(2)}) collective-permute-start(f32[8,64,3,256]{3,1,2,0:T(8,128)} %bitcast.30), channel_id=1, source_target_pairs={{0,1},{1,0},{2,3},{3,2},{4,5},{5,4},{6,7},{7,6},{8,9},{9,8},{10,11... | collective-permute-start | bytes 4718600 | tf_op jit(solution)/shard_map/ppermute | solution.py:44
  304.7 3.4 collective-permute-done.8
  308.0 1.8 bitcast_add_fusion
  309.8 1.2 copy-done
  311.0 0.1 dynamic-slice_bitcast_fusion
  311.1 41.4 %collective-permute-start.9 = (f32[4,64,3,256]{3,1,2,0:T(8,128)S(1)}, f32[4,64,3,256]{3,1,2,0:T(8,128)S(1)}, u32[]{:S(2)}, u32[]{:S(2)}) collective-permute-start(f32[4,64,3,256]{3,1,2,0:T(8,128)S(1)} %dynamic-slice_bitcast_fusion), channel_id=1, source_target_pairs={{0,2},{1,3},{2,0},{3,1},{4,6},{5,7},{6,4},{7,5},{8,10},{9,11},{10,... | collective-permute-start | bytes 2359304 | tf_op jit(solution)/shard_map/ppermute | solution.py:44
  352.5 17.8 %collective-permute-done.9 = f32[4,64,3,256]{3,1,2,0:T(8,128)S(1)} collective-permute-done((f32[4,64,3,256]{3,1,2,0:T(8,128)S(1)}, f32[4,64,3,256]{3,1,2,0:T(8,128)S(1)}, u32[]{:S(2)}, u32[]{:S(2)}) %collective-permute-start.9) | collective-permute-done | bytes 786464 | tf_op jit(solution)/shard_map/ppermute | solution.py:44
  370.3 1.2 bitcast_add_fusion.1
  371.6 3.1 collective-permute-start.10
  374.7 9.1 %collective-permute-done.10 = f32[2,64,3,256]{3,1,2,0:T(8,128)S(1)} collective-permute-done((f32[2,64,3,256]{3,1,2,0:T(8,128)S(1)}, f32[2,64,3,256]{3,1,2,0:T(8,128)S(1)}, u32[]{:S(2)}, u32[]{:S(2)}) %collective-permute-start.10) | collective-permute-done | bytes 393248 | tf_op jit(solution)/shard_map/ppermute | solution.py:44
  383.9 3.3 collective-permute-start.11
  387.2 19.9 %shard_map.62 = (f32[1024,8,256]{2,1,0:T(8,128)}, bf16[256,8,256]{2,1,0:T(8,128)(2,1)}) custom-call(f32[6,16,256]{2,1,0:T(8,128)} %copy-done.2, bf16[1024,8,256]{2,1,0:T(8,128)(2,1)} %a_ref.7, bf16[1024,8,256]{2,1,0:T(8,128)(2,1)} %pad_maximum_fusion.h_ref, f32[1024,8,256]{2,1,0:T(8,128)} %get-tuple-element.11.refs_0_), custom_call_target="tpu_custom_call", output_to_operand_aliasing={{0}: (3, {})} | custom-call | tf_op jit(solution)/shard_map/pallas_call | solution.py:152
  407.1 0.7 add_bitcast_fusion
  (32 shorter events, 0.3 us)
Async XLA Ops:
  0.6 7.6 %copy-start.4 = (s32[8,256]{1,0:T(8,128)S(1)}, s32[8,256]{1,0:T(8,128)}, u32[]{:S(2)}) copy-start(s32[8,256]{1,0:T(8,128)} %param.5) | copy-start | bytes 24580
  0.6 7.6 %copy-start.5 = (f32[8]{0:T(128)S(1)}, f32[8]{0:T(128)}, u32[]{:S(2)}) copy-start(f32[8]{0:T(128)} %param.6) | copy-start | bytes 100
  5.5 12.0 %collective-permute-start.2 = (bf16[1024,4,256]{2,1,0:T(4,128)(2,1)S(1)}, bf16[1024,4,256]{2,1,0:T(4,128)(2,1)S(1)}, u32[]{:S(2)}, u32[]{:S(2)}) collective-permute-start(bf16[1024,4,256]{2,1,0:T(4,128)(2,1)S(1)} %get-tuple-element.20), channel_id=1, source_target_pairs={{0,1},{1,2},{2,3},{3,4},{4,5},{5,6},{6,7},{7,8},{8,9},{9,10},{10,1... | collective-permute-start | bytes 6291464 | tf_op jit(solution)/shard_map/ppermute | solution.py:55
  6.9 10.6 %collective-permute-start.3 = (bf16[1024,4,256]{2,1,0:T(4,128)(2,1)S(1)}, bf16[1024,4,256]{2,1,0:T(4,128)(2,1)S(1)}, u32[]{:S(2)}, u32[]{:S(2)}) collective-permute-start(bf16[1024,4,256]{2,1,0:T(4,128)(2,1)S(1)} %get-tuple-element.21), channel_id=1, source_target_pairs={{1,0},{2,1},{3,2},{4,3},{5,4},{6,5},{7,6},{8,7},{9,8},{10,9},{11,1... | collective-permute-start | bytes 6291464 | tf_op jit(solution)/shard_map/ppermute | solution.py:56
  8.3 6.1 %collective-permute-start = (f32[4,256]{1,0:T(4,128)S(1)}, f32[4,256]{1,0:T(4,128)S(1)}, u32[]{:S(2)}, u32[]{:S(2)}) collective-permute-start(f32[4,256]{1,0:T(4,128)S(1)} %get-tuple-element.22), channel_id=1, source_target_pairs={{0,1},{1,2},{2,3},{3,4},{4,5},{5,6},{6,7},{7,8},{8,9},{9,10},{10,1... | collective-permute-start | bytes 12296 | tf_op jit(solution)/shard_map/ppermute | solution.py:55
  13.0 4.3 %collective-permute-start.1 = (f32[4,256]{1,0:T(4,128)S(1)}, f32[4,256]{1,0:T(4,128)S(1)}, u32[]{:S(2)}, u32[]{:S(2)}) collective-permute-start(f32[4,256]{1,0:T(4,128)S(1)} %get-tuple-element.23), channel_id=1, source_target_pairs={{1,0},{2,1},{3,2},{4,3},{5,4},{6,5},{7,6},{8,7},{9,8},{10,9},{11,1... | collective-permute-start | bytes 12296 | tf_op jit(solution)/shard_map/ppermute | solution.py:56
  17.4 3.5 copy-start.2
  40.8 22.4 %copy-start.3 = (bf16[256,8,256]{2,1,0:T(8,128)(2,1)S(1)}, bf16[256,8,256]{2,1,0:T(8,128)(2,1)}, u32[]{:S(2)}) copy-start(bf16[256,8,256]{2,1,0:T(8,128)(2,1)} %get-tuple-element.13) | copy-start | bytes 3145732
  85.7 6.6 %copy-start.6 = (s32[8]{0:T(128)S(1)}, s32[8]{0:T(128)}, u32[]{:S(2)}) copy-start(s32[8]{0:T(128)} %param.7) | copy-start | bytes 100
  90.7 52.9 %collective-permute-start.4 = (bf16[3,256,2048]{2,1,0:T(8,128)(2,1)S(1)}, bf16[3,256,2048]{2,1,0:T(8,128)(2,1)}, u32[]{:S(2)}, u32[]{:S(2)}) collective-permute-start(bf16[3,256,2048]{2,1,0:T(8,128)(2,1)S(1)} %constant_dynamic-update-slice_fusion.6), channel_id=1, source_target_pairs={{0,16},{16,0},{32,48},{48,32},{64,80},{80,64},{96,112},{112,96},{1... | collective-permute-start | bytes 9437192 | tf_op jit(solution)/shard_map/ppermute | solution.py:24
  145.9 55.4 %collective-permute-start.5 = (bf16[3,256,2048]{2,1,0:T(8,128)(2,1)S(1)}, bf16[3,256,2048]{2,1,0:T(8,128)(2,1)S(1)}, u32[]{:S(2)}, u32[]{:S(2)}) collective-permute-start(bf16[3,256,2048]{2,1,0:T(8,128)(2,1)S(1)} %broadcast_select_fusion), channel_id=1, source_target_pairs={{0,32},{16,48},{32,64},{48,80},{64,96},{80,112},{96,0},{112,16},{1... | collective-permute-start | bytes 9437192 | tf_op jit(solution)/shard_map/ppermute | solution.py:26
  147.9 53.7 %collective-permute-start.6 = (bf16[3,256,2048]{2,1,0:T(8,128)(2,1)S(1)}, bf16[3,256,2048]{2,1,0:T(8,128)(2,1)S(1)}, u32[]{:S(2)}, u32[]{:S(2)}) collective-permute-start(bf16[3,256,2048]{2,1,0:T(8,128)(2,1)S(1)} %broadcast_select_fusion), channel_id=1, source_target_pairs={{0,96},{16,112},{32,0},{48,16},{64,32},{80,48},{96,64},{112,80},{1... | collective-permute-start | bytes 9437192 | tf_op jit(solution)/shard_map/ppermute | solution.py:27
  202.1 67.9 %collective-permute-start.7 = (bf16[3,256,2048]{2,1,0:T(8,128)(2,1)S(1)}, bf16[3,256,2048]{2,1,0:T(8,128)(2,1)}, u32[]{:S(2)}, u32[]{:S(2)}) collective-permute-start(bf16[3,256,2048]{2,1,0:T(8,128)(2,1)S(1)} %select_select_fusion), channel_id=1, source_target_pairs={{0,32},{16,48},{32,64},{48,80},{64,96},{80,112},{96,0},{112,16},{1... | collective-permute-start | bytes 9437192 | tf_op jit(solution)/shard_map/ppermute | solution.py:29
  269.9 3.1 copy-start.1
  288.3 19.7 %collective-permute-start.8 = (f32[8,64,3,256]{3,1,2,0:T(8,128)}, f32[8,64,3,256]{3,1,2,0:T(8,128)}, u32[]{:S(2)}, u32[]{:S(2)}) collective-permute-start(f32[8,64,3,256]{3,1,2,0:T(8,128)} %bitcast.30), channel_id=1, source_target_pairs={{0,1},{1,0},{2,3},{3,2},{4,5},{5,4},{6,7},{7,6},{8,9},{9,8},{10,11... | collective-permute-start | bytes 4718600 | tf_op jit(solution)/shard_map/ppermute | solution.py:44
  309.8 1.2 copy-start
  311.1 59.2 %collective-permute-start.9 = (f32[4,64,3,256]{3,1,2,0:T(8,128)S(1)}, f32[4,64,3,256]{3,1,2,0:T(8,128)S(1)}, u32[]{:S(2)}, u32[]{:S(2)}) collective-permute-start(f32[4,64,3,256]{3,1,2,0:T(8,128)S(1)} %dynamic-slice_bitcast_fusion), channel_id=1, source_target_pairs={{0,2},{1,3},{2,0},{3,1},{4,6},{5,7},{6,4},{7,5},{8,10},{9,11},{10,... | collective-permute-start | bytes 2359304 | tf_op jit(solution)/shard_map/ppermute | solution.py:44
  371.6 12.2 %collective-permute-start.10 = (f32[2,64,3,256]{3,1,2,0:T(8,128)S(1)}, f32[2,64,3,256]{3,1,2,0:T(8,128)S(1)}, u32[]{:S(2)}, u32[]{:S(2)}) collective-permute-start(f32[2,64,3,256]{3,1,2,0:T(8,128)S(1)} %dynamic-slice_bitcast_fusion.1), channel_id=1, source_target_pairs={{0,4},{1,5},{2,6},{3,7},{4,0},{5,1},{6,2},{7,3},{8,12},{9,13},{10,... | collective-permute-start | bytes 1179656 | tf_op jit(solution)/shard_map/ppermute | solution.py:44
  383.9 23.2 %collective-permute-start.11 = (f32[1,64,3,256]{3,1,2,0:T(8,128)S(1)}, f32[1,64,3,256]{3,1,2,0:T(8,128)S(1)}, u32[]{:S(2)}, u32[]{:S(2)}) collective-permute-start(f32[1,64,3,256]{3,1,2,0:T(8,128)S(1)} %constant_dynamic-slice_fusion), channel_id=1, source_target_pairs={{0,8},{1,9},{2,10},{3,11},{4,12},{5,13},{6,14},{7,15},{8,0},{9,1},... | collective-permute-start | bytes 589832 | tf_op jit(solution)/shard_map/ppermute | solution.py:44

commit v7 on v4

--- a/solution.py
+++ b/solution.py
@@ -26,7 +26,13 @@
     from_below = lax.ppermute(val, axis, [(i, (i + 2) % size) for i in range(size)])
     from_above = lax.ppermute(val, axis, [(i, (i - 2) % size) for i in range(size)])
     val = jnp.where(z == oz, val, jnp.where(z == (oz + 1) % ring, from_below, from_above))
-    last = lax.ppermute(val, axis, [(i, (i + 2) % size) for i in range(size)])
+    rows = val.shape[0] // 2
+    last = jnp.concatenate(
+        [
+            lax.ppermute(val[:rows], axis, [(i, (i + 2) % size) for i in range(size)]),
+            lax.ppermute(val[rows:], axis, [(i, (i - 2) % size) for i in range(size)]),
+        ]
+    )
     return jnp.where(z == (oz + 2) % ring, last, val)
 
 

time: 327 us -> 294 us (0.90)
  starting transfers between devices: 124 us -> 105 us
  waiting for transfers between devices: 76.7 us -> 58.7 us
    ppermute x12, starting transfers between devices: 95.1 us -> 72.6 us  [reduce_scatter_slab(): part = keep + lax.ppermute(send, axis, [(i, i ^ bit) for i in range(size)])]
    ppermute x3 -> x6, waiting for transfers between devices: 20.9 us -> 6.8 us  [the longest x3 6.58 us: broadcast_dp(): lax.ppermute(val[:rows], axis, [(i, (i + 2) % size) for i in range(size)])]
    ppermute x3 -> x6, starting transfers between devices: 3.35 us -> 7.97 us  [the longest x3 6.15 us: broadcast_dp(): lax.ppermute(val[rows:], axis, [(i, (i - 2) % size) for i in range(size)])]
    ppermute x3, waiting for transfers between devices: 20.5 us -> 15.9 us  [broadcast_dp(): lax.ppermute(val, axis, [(i, (i + 2) % size) for i in range(size)])]
  transfers between devices with their start and end apart: 28 -> 31, of which waited for: 11 -> 13; matrix products, arithmetic and copies ran while one was open for 9% -> 11% of each run, Pallas kernels for 0% -> 0%
where the time goes in v7:
time: 294 us; the launch traced here: 293 us
  starting transfers between devices  105 us (36%)
  Pallas kernels  72.1 us (25%)
  waiting for transfers between devices  58.7 us (20%)
  local copies, waits for them, and re-layouts  21.1 us (7%)
  other arithmetic  13.9 us (5%)
  matrix products  11.9 us (4%)
  between operations  10.8 us (4%)
    ppermute x12, starting transfers between devices, reduce_scatter_slab(): part = keep + lax.ppermute(send, axis, [(i, i ^ bit) for i in range(size)])  72.6 us
    pallas_call x1, Pallas kernels, smooth(): pl.pallas_call(kernel, grid=(rows // block,), in_specs=[pl.BlockSpec(coef...  72.1 us
    ppermute x3, waiting for transfers between devices, broadcast_dp(): pair = lax.ppermute(piece, axis, [(i, i ^ 1) for i in range(size)])  22.1 us
    ppermute x3, waiting for transfers between devices, broadcast_dp(): lax.ppermute(val, axis, [(i, (i + 2) % size) for i in range(size)])  15.9 us
    dot_general x3, matrix products, body(): lax.dot_general(flat, received, (((1,), (1,)), ((), ())), preferred_eleme...  11.9 us
    ppermute x12, waiting for transfers between devices, reduce_scatter_slab(): part = keep + lax.ppermute(send, axis, [(i, i ^ bit) for i in range(size)])  10.7 us
    ppermute x3, waiting for transfers between devices, broadcast_dp(): lax.ppermute(val[:rows], axis, [(i, (i + 2) % size) for i in range(size)])  6.58 us
    unnamed x14, local copies, waits for them, and re-layouts  6.58 us
  transfers between devices with their start and end apart: 31, of which 13 were waited for; matrix products, arithmetic and copies ran while one was open for 11% of the time, Pallas kernels for 0%

profile of v7, /device:TPU:0, one launch (start us, length us, event | category | flops | bytes accessed | tf_op | source)
XLA Modules:
  0.0 293.3 jit_solution(2476008939082837969)
XLA Ops:
  0.6 4.8 %fusion.17 = (bf16[1024,4,256]{2,1,0:T(4,128)(2,1)S(1)}, bf16[1024,4,256]{2,1,0:T(4,128)(2,1)S(1)}) fusion(bf16[1024,8,256]{2,1,0:T(8,128)(2,1)} %a_ref.1), kind=kLoop, calls=%fused_computation.69 | loop fusion | bytes 8388608 | tf_op jit(solution)/shard_map/slice | solution.py:59
  5.5 1.4 collective-permute-start.2
  6.9 1.3 collective-permute-start.3
  8.3 4.7 %collective-permute-start = (f32[4,256]{1,0:T(4,128)S(1)}, f32[4,256]{1,0:T(4,128)S(1)}, u32[]{:S(2)}, u32[]{:S(2)}) collective-permute-start(f32[4,256]{1,0:T(4,128)S(1)} %get-tuple-element.13), channel_id=1, source_target_pairs={{0,1},{1,2},{2,3},{3,4},{4,5},{5,6},{6,7},{7,8},{8,9},{9,10},{10,1... | collective-permute-start | bytes 12296 | tf_op jit(solution)/shard_map/ppermute | solution.py:61
  13.0 1.3 collective-permute-start.1
  14.4 2.9 %collective-permute-done.1 = f32[4,256]{1,0:T(4,128)S(1)} collective-permute-done((f32[4,256]{1,0:T(4,128)S(1)}, f32[4,256]{1,0:T(4,128)S(1)}, u32[]{:S(2)}, u32[]{:S(2)}) %collective-permute-start.1) | collective-permute-done | bytes 4128 | tf_op jit(solution)/shard_map/ppermute | solution.py:62
  17.5 3.5 %pad_maximum_fusion.h_ref = bf16[1024,8,256]{2,1,0:T(8,128)(2,1)} fusion(bf16[1024,4,256]{2,1,0:T(4,128)(2,1)S(1)} %collective-permute-done.3, bf16[1024,4,256]{2,1,0:T(4,128)(2,1)S(1)} %collective-permute-done.2), kind=kLoop, calls=%fused_computation | loop fusion | flops 8388608 | bytes 8388608 | tf_op jit(solution)/shard_map/concatenate | solution.py:63
  20.9 72.1 %shard_map.59 = f32[1024,8,256]{2,1,0:T(8,128)} custom-call(f32[6,16,256]{2,1,0:T(8,128)} %copy-done.1, bf16[1024,8,256]{2,1,0:T(8,128)(2,1)} %a_ref.1, bf16[1024,8,256]{2,1,0:T(8,128)(2,1)} %pad_maximum_fusion.h_ref), custom_call_target="tpu_custom_call" | custom-call | tf_op jit(solution)/shard_map/pallas_call | solution.py:142
  93.0 3.8 %convert.5 = bf16[1024,8,256]{2,1,0:T(8,128)(2,1)S(1)} convert(f32[1024,8,256]{2,1,0:T(8,128)} %shard_map.59) | non-fusion elementwise | flops 2097152 | bytes 12582912 | tf_op jit(solution)/shard_map/convert.2
  97.3 1.7 collective-permute-start.4
  110.2 5.7 %copy.16 = bf16[128,8,8,256]{3,1,2,0:T(8,128)(2,1)} copy(bf16[128,8,8,256]{3,2,1,0:T(8,128)(2,1)} %bitcast.78) | data formatting | bytes 8388608
  116.2 1.7 collective-permute-start.22
  117.8 1.3 broadcast_select_fusion.2
  119.2 2.0 collective-permute-start.5
  121.2 1.3 collective-permute-start.6
  122.5 5.3 %collective-permute-done.13 = bf16[256,2048]{1,0:T(8,128)(2,1)} collective-permute-done((bf16[256,2048]{1,0:T(8,128)(2,1)S(1)}, bf16[256,2048]{1,0:T(8,128)(2,1)}, u32[]{:S(2)}, u32[]{:S(2)}) %collective-permute-start.13) | collective-permute-done | bytes 1048608 | tf_op jit(solution)/shard_map/ppermute | solution.py:24
  127.8 1.3 broadcast_select_fusion.1
  129.1 2.0 collective-permute-start.14
  131.1 2.2 collective-permute-start.15
  133.3 16.8 %collective-permute-done.22 = bf16[256,2048]{1,0:T(8,128)(2,1)S(1)} collective-permute-done((bf16[256,2048]{1,0:T(8,128)(2,1)S(1)}, bf16[256,2048]{1,0:T(8,128)(2,1)S(1)}, u32[]{:S(2)}, u32[]{:S(2)}) %collective-permute-start.22) | collective-permute-done | bytes 1048608 | tf_op jit(solution)/shard_map/ppermute | solution.py:24
  150.3 2.0 collective-permute-start.23
  152.3 2.2 collective-permute-start.24
  154.8 3.2 %collective-permute-start.8 = (bf16[128,2048]{1,0:T(8,128)(2,1)S(1)}, bf16[128,2048]{1,0:T(8,128)(2,1)S(1)}, u32[]{:S(2)}, u32[]{:S(2)}) collective-permute-start(bf16[128,2048]{1,0:T(8,128)(2,1)S(1)} %get-tuple-element.8), channel_id=1, source_target_pairs={{0,96},{16,112},{32,0},{48,16},{64,32},{80,48},{96,64},{112,80},{1... | collective-permute-start | bytes 1572872 | tf_op jit(solution)/shard_map/ppermute | solution.py:33
  159.4 15.9 %collective-permute-done.23 = bf16[256,2048]{1,0:T(8,128)(2,1)S(1)} collective-permute-done((bf16[256,2048]{1,0:T(8,128)(2,1)S(1)}, bf16[256,2048]{1,0:T(8,128)(2,1)S(1)}, u32[]{:S(2)}, u32[]{:S(2)}) %collective-permute-start.23) | collective-permute-done | bytes 1048608 | tf_op jit(solution)/shard_map/ppermute | solution.py:26
  175.3 1.5 collective-permute-start.17
  178.2 1.7 collective-permute-start.25
  180.0 6.6 %collective-permute-done.7 = bf16[128,2048]{1,0:T(8,128)(2,1)S(1)} collective-permute-done((bf16[128,2048]{1,0:T(8,128)(2,1)S(1)}, bf16[128,2048]{1,0:T(8,128)(2,1)S(1)}, u32[]{:S(2)}, u32[]{:S(2)}) %collective-permute-start.7) | collective-permute-done | bytes 524320 | tf_op jit(solution)/shard_map/ppermute | solution.py:32
  186.5 1.5 collective-permute-start.26
  188.2 2.3 fusion.2
  190.5 1.6 copy.12
  192.9 27.3 %collective-permute-start.9 = (f32[8,64,256]{2,1,0:T(8,128)}, f32[8,64,256]{2,1,0:T(8,128)}, u32[]{:S(2)}, u32[]{:S(2)}) collective-permute-start(f32[8,64,256]{2,1,0:T(8,128)} %dynamic-slice_bitcast_fusion.2), channel_id=1, source_target_pairs={{0,1},{1,0},{2,3},{3,2},{4,5},{5,4},{6,7},{7,6},{8,9},{9,8},{10,11... | collective-permute-start | bytes 1572872 | tf_op jit(solution)/shard_map/ppermute | solution.py:50
  220.2 4.8 %fusion.1 = f32[1024,256]{0,1:T(8,128)} fusion(bf16[1024,2048]{1,0:T(8,128)(2,1)} %bitcast.79, bf16[256,2048]{1,0:T(8,128)(2,1)S(1)} %select_select_fusion.1, bf16[128,2048]{1,0:T(8,128)(2,1)} %collective-permute-done.17, bf16[128,2048]{1,0:T(8,128)(2,1)} %collective-permute-done.16, pred[]{:T(512)S(6)} %eq.77), kind=kOutput, calls=%fused_computation.4 | convolution fusion | flops 1076625408 | bytes 7340033 | tf_op jit(solution)/shard_map/dot_general | solution.py:172
  225.0 1.6 copy.13
  227.8 4.8 %fusion = f32[1024,256]{0,1:T(8,128)} fusion(bf16[1024,2048]{1,0:T(8,128)(2,1)} %bitcast.80, bf16[256,2048]{1,0:T(8,128)(2,1)S(1)} %select_select_fusion, bf16[128,2048]{1,0:T(8,128)(2,1)} %collective-permute-done.26, bf16[128,2048]{1,0:T(8,128)(2,1)} %collective-permute-done.25, pred[]{:T(512)S(6)} %eq.81), kind=kOutput, calls=%fused_computation.2 | convolution fusion | flops 1076625408 | bytes 7340033 | tf_op jit(solution)/shard_map/dot_general | solution.py:172
  232.6 1.6 copy.14
  235.7 21.7 %collective-permute-start.10 = (f32[4,64,256]{2,1,0:T(8,128)S(1)}, f32[4,64,256]{2,1,0:T(8,128)S(1)}, u32[]{:S(2)}, u32[]{:S(2)}) collective-permute-start(f32[4,64,256]{2,1,0:T(8,128)S(1)} %dynamic-slice_bitcast_fusion.5), channel_id=1, source_target_pairs={{0,2},{1,3},{2,0},{3,1},{4,6},{5,7},{6,4},{7,5},{8,10},{9,11},{10,... | collective-permute-start | bytes 786440 | tf_op jit(solution)/shard_map/ppermute | solution.py:50
  257.4 1.1 bitcast_add_fusion.1
  258.8 2.1 collective-permute-start.28
  260.8 3.6 %collective-permute-done.10 = f32[4,64,256]{2,1,0:T(8,128)S(1)} collective-permute-done((f32[4,64,256]{2,1,0:T(8,128)S(1)}, f32[4,64,256]{2,1,0:T(8,128)S(1)}, u32[]{:S(2)}, u32[]{:S(2)}) %collective-permute-start.10) | collective-permute-done | bytes 262176 | tf_op jit(solution)/shard_map/ppermute | solution.py:50
  264.5 4.1 %collective-permute-start.11 = (f32[2,64,256]{2,1,0:T(8,128)S(1)}, f32[2,64,256]{2,1,0:T(8,128)S(1)}, u32[]{:S(2)}, u32[]{:S(2)}) collective-permute-start(f32[2,64,256]{2,1,0:T(8,128)S(1)} %dynamic-slice_bitcast_fusion.8), channel_id=1, source_target_pairs={{0,4},{1,5},{2,6},{3,7},{4,0},{5,1},{6,2},{7,3},{8,12},{9,13},{10,... | collective-permute-start | bytes 393224 | tf_op jit(solution)/shard_map/ppermute | solution.py:50
  268.6 1.5 collective-permute-done.19
  270.2 4.1 %collective-permute-start.20 = (f32[2,64,256]{2,1,0:T(8,128)S(1)}, f32[2,64,256]{2,1,0:T(8,128)S(1)}, u32[]{:S(2)}, u32[]{:S(2)}) collective-permute-start(f32[2,64,256]{2,1,0:T(8,128)S(1)} %dynamic-slice_bitcast_fusion.7), channel_id=1, source_target_pairs={{0,4},{1,5},{2,6},{3,7},{4,0},{5,1},{6,2},{7,3},{8,12},{9,13},{10,... | collective-permute-start | bytes 393224 | tf_op jit(solution)/shard_map/ppermute | solution.py:50
  274.2 1.5 collective-permute-done.28
  275.8 4.1 %collective-permute-start.29 = (f32[2,64,256]{2,1,0:T(8,128)S(1)}, f32[2,64,256]{2,1,0:T(8,128)S(1)}, u32[]{:S(2)}, u32[]{:S(2)}) collective-permute-start(f32[2,64,256]{2,1,0:T(8,128)S(1)} %dynamic-slice_bitcast_fusion.6), channel_id=1, source_target_pairs={{0,4},{1,5},{2,6},{3,7},{4,0},{5,1},{6,2},{7,3},{8,12},{9,13},{10,... | collective-permute-start | bytes 393224 | tf_op jit(solution)/shard_map/ppermute | solution.py:50
  280.6 3.3 %collective-permute-start.12 = (f32[1,64,256]{2,1,0:T(8,128)S(1)}, f32[1,64,256]{2,1,0:T(8,128)S(1)}, u32[]{:S(2)}, u32[]{:S(2)}) collective-permute-start(f32[1,64,256]{2,1,0:T(8,128)S(1)} %constant_dynamic-slice_fusion.2), channel_id=1, source_target_pairs={{0,8},{1,9},{2,10},{3,11},{4,12},{5,13},{6,14},{7,15},{8,0},{9,1},... | collective-permute-start | bytes 196616 | tf_op jit(solution)/shard_map/ppermute | solution.py:50
  283.9 2.8 collective-permute-start.21
  286.7 2.5 collective-permute-start.30
  289.8 2.8 collective-permute-done.30
  (86 shorter events, 11.9 us)
Async XLA Ops:
  0.6 7.6 %copy-start.2 = (s32[8,256]{1,0:T(8,128)S(1)}, s32[8,256]{1,0:T(8,128)}, u32[]{:S(2)}) copy-start(s32[8,256]{1,0:T(8,128)} %param.5) | copy-start | bytes 24580
  0.6 7.6 %copy-start.4 = (f32[8]{0:T(128)S(1)}, f32[8]{0:T(128)}, u32[]{:S(2)}) copy-start(f32[8]{0:T(128)} %param.6) | copy-start | bytes 100
  5.5 12.0 %collective-permute-start.2 = (bf16[1024,4,256]{2,1,0:T(4,128)(2,1)S(1)}, bf16[1024,4,256]{2,1,0:T(4,128)(2,1)S(1)}, u32[]{:S(2)}, u32[]{:S(2)}) collective-permute-start(bf16[1024,4,256]{2,1,0:T(4,128)(2,1)S(1)} %get-tuple-element.5), channel_id=1, source_target_pairs={{0,1},{1,2},{2,3},{3,4},{4,5},{5,6},{6,7},{7,8},{8,9},{9,10},{10,1... | collective-permute-start | bytes 6291464 | tf_op jit(solution)/shard_map/ppermute | solution.py:61
  6.9 10.6 %collective-permute-start.3 = (bf16[1024,4,256]{2,1,0:T(4,128)(2,1)S(1)}, bf16[1024,4,256]{2,1,0:T(4,128)(2,1)S(1)}, u32[]{:S(2)}, u32[]{:S(2)}) collective-permute-start(bf16[1024,4,256]{2,1,0:T(4,128)(2,1)S(1)} %get-tuple-element.6), channel_id=1, source_target_pairs={{1,0},{2,1},{3,2},{4,3},{5,4},{6,5},{7,6},{8,7},{9,8},{10,9},{11,1... | collective-permute-start | bytes 6291464 | tf_op jit(solution)/shard_map/ppermute | solution.py:62
  8.3 6.1 %collective-permute-start = (f32[4,256]{1,0:T(4,128)S(1)}, f32[4,256]{1,0:T(4,128)S(1)}, u32[]{:S(2)}, u32[]{:S(2)}) collective-permute-start(f32[4,256]{1,0:T(4,128)S(1)} %get-tuple-element.13), channel_id=1, source_target_pairs={{0,1},{1,2},{2,3},{3,4},{4,5},{5,6},{6,7},{7,8},{8,9},{9,10},{10,1... | collective-permute-start | bytes 12296 | tf_op jit(solution)/shard_map/ppermute | solution.py:61
  13.0 4.3 %collective-permute-start.1 = (f32[4,256]{1,0:T(4,128)S(1)}, f32[4,256]{1,0:T(4,128)S(1)}, u32[]{:S(2)}, u32[]{:S(2)}) collective-permute-start(f32[4,256]{1,0:T(4,128)S(1)} %get-tuple-element.14), channel_id=1, source_target_pairs={{1,0},{2,1},{3,2},{4,3},{5,4},{6,5},{7,6},{8,7},{9,8},{10,9},{11,1... | collective-permute-start | bytes 12296 | tf_op jit(solution)/shard_map/ppermute | solution.py:62
  17.4 3.5 %copy-start.1 = (f32[6,16,256]{2,1,0:T(8,128)}, f32[6,16,256]{2,1,0:T(8,128)S(1)}, u32[]{:S(2)}) copy-start(f32[6,16,256]{2,1,0:T(8,128)S(1)} %select_dynamic-update-slice_fusion.coef_ref) | copy-start | bytes 294916
  96.8 3.0 %copy-start.3 = (s32[8]{0:T(128)S(1)}, s32[8]{0:T(128)}, u32[]{:S(2)}) copy-start(s32[8]{0:T(128)} %param.7) | copy-start | bytes 100
  97.3 20.5 %collective-permute-start.4 = (bf16[256,2048]{1,0:T(8,128)(2,1)S(1)}, bf16[256,2048]{1,0:T(8,128)(2,1)}, u32[]{:S(2)}, u32[]{:S(2)}) collective-permute-start(bf16[256,2048]{1,0:T(8,128)(2,1)S(1)} %bitcast.84), channel_id=1, source_target_pairs={{0,16},{16,0},{32,48},{48,32},{64,80},{80,64},{96,112},{112,96},{1... | collective-permute-start | bytes 3145736 | tf_op jit(solution)/shard_map/ppermute | solution.py:24
  99.3 28.5 %collective-permute-start.13 = (bf16[256,2048]{1,0:T(8,128)(2,1)S(1)}, bf16[256,2048]{1,0:T(8,128)(2,1)}, u32[]{:S(2)}, u32[]{:S(2)}) collective-permute-start(bf16[256,2048]{1,0:T(8,128)(2,1)S(1)} %bitcast.82), channel_id=1, source_target_pairs={{0,16},{16,0},{32,48},{48,32},{64,80},{80,64},{96,112},{112,96},{1... | collective-permute-start | bytes 3145736 | tf_op jit(solution)/shard_map/ppermute | solution.py:24
  116.2 34.0 %collective-permute-start.22 = (bf16[256,2048]{1,0:T(8,128)(2,1)S(1)}, bf16[256,2048]{1,0:T(8,128)(2,1)S(1)}, u32[]{:S(2)}, u32[]{:S(2)}) collective-permute-start(bf16[256,2048]{1,0:T(8,128)(2,1)S(1)} %bitcast.90), channel_id=1, source_target_pairs={{0,16},{16,0},{32,48},{48,32},{64,80},{80,64},{96,112},{112,96},{1... | collective-permute-start | bytes 3145736 | tf_op jit(solution)/shard_map/ppermute | solution.py:24
  119.2 33.1 %collective-permute-start.5 = (bf16[256,2048]{1,0:T(8,128)(2,1)S(1)}, bf16[256,2048]{1,0:T(8,128)(2,1)S(1)}, u32[]{:S(2)}, u32[]{:S(2)}) collective-permute-start(bf16[256,2048]{1,0:T(8,128)(2,1)S(1)} %broadcast_select_fusion.2), channel_id=1, source_target_pairs={{0,32},{16,48},{32,64},{48,80},{64,96},{80,112},{96,0},{112,16},{1... | collective-permute-start | bytes 3145736 | tf_op jit(solution)/shard_map/ppermute | solution.py:26
  121.2 33.3 %collective-permute-start.6 = (bf16[256,2048]{1,0:T(8,128)(2,1)S(1)}, bf16[256,2048]{1,0:T(8,128)(2,1)S(1)}, u32[]{:S(2)}, u32[]{:S(2)}) collective-permute-start(bf16[256,2048]{1,0:T(8,128)(2,1)S(1)} %broadcast_select_fusion.2), channel_id=1, source_target_pairs={{0,96},{16,112},{32,0},{48,16},{64,32},{80,48},{96,64},{112,80},{1... | collective-permute-start | bytes 3145736 | tf_op jit(solution)/shard_map/ppermute | solution.py:27
  129.1 25.6 %collective-permute-start.14 = (bf16[256,2048]{1,0:T(8,128)(2,1)S(1)}, bf16[256,2048]{1,0:T(8,128)(2,1)S(1)}, u32[]{:S(2)}, u32[]{:S(2)}) collective-permute-start(bf16[256,2048]{1,0:T(8,128)(2,1)S(1)} %broadcast_select_fusion.1), channel_id=1, source_target_pairs={{0,32},{16,48},{32,64},{48,80},{64,96},{80,112},{96,0},{112,16},{1... | collective-permute-start | bytes 3145736 | tf_op jit(solution)/shard_map/ppermute | solution.py:26
  131.1 26.9 %collective-permute-start.15 = (bf16[256,2048]{1,0:T(8,128)(2,1)S(1)}, bf16[256,2048]{1,0:T(8,128)(2,1)S(1)}, u32[]{:S(2)}, u32[]{:S(2)}) collective-permute-start(bf16[256,2048]{1,0:T(8,128)(2,1)S(1)} %broadcast_select_fusion.1), channel_id=1, source_target_pairs={{0,96},{16,112},{32,0},{48,16},{64,32},{80,48},{96,64},{112,80},{1... | collective-permute-start | bytes 3145736 | tf_op jit(solution)/shard_map/ppermute | solution.py:27
  150.3 25.0 %collective-permute-start.23 = (bf16[256,2048]{1,0:T(8,128)(2,1)S(1)}, bf16[256,2048]{1,0:T(8,128)(2,1)S(1)}, u32[]{:S(2)}, u32[]{:S(2)}) collective-permute-start(bf16[256,2048]{1,0:T(8,128)(2,1)S(1)} %broadcast_select_fusion), channel_id=1, source_target_pairs={{0,32},{16,48},{32,64},{48,80},{64,96},{80,112},{96,0},{112,16},{1... | collective-permute-start | bytes 3145736 | tf_op jit(solution)/shard_map/ppermute | solution.py:26
  152.3 24.7 %collective-permute-start.24 = (bf16[256,2048]{1,0:T(8,128)(2,1)S(1)}, bf16[256,2048]{1,0:T(8,128)(2,1)S(1)}, u32[]{:S(2)}, u32[]{:S(2)}) collective-permute-start(bf16[256,2048]{1,0:T(8,128)(2,1)S(1)} %broadcast_select_fusion), channel_id=1, source_target_pairs={{0,96},{16,112},{32,0},{48,16},{64,32},{80,48},{96,64},{112,80},{1... | collective-permute-start | bytes 3145736 | tf_op jit(solution)/shard_map/ppermute | solution.py:27
  154.7 31.8 %collective-permute-start.7 = (bf16[128,2048]{1,0:T(8,128)(2,1)S(1)}, bf16[128,2048]{1,0:T(8,128)(2,1)S(1)}, u32[]{:S(2)}, u32[]{:S(2)}) collective-permute-start(bf16[128,2048]{1,0:T(8,128)(2,1)S(1)} %get-tuple-element.7), channel_id=1, source_target_pairs={{0,32},{16,48},{32,64},{48,80},{64,96},{80,112},{96,0},{112,16},{1... | collective-permute-start | bytes 1572872 | tf_op jit(solution)/shard_map/ppermute | solution.py:32
  154.8 33.4 %collective-permute-start.8 = (bf16[128,2048]{1,0:T(8,128)(2,1)S(1)}, bf16[128,2048]{1,0:T(8,128)(2,1)S(1)}, u32[]{:S(2)}, u32[]{:S(2)}) collective-permute-start(bf16[128,2048]{1,0:T(8,128)(2,1)S(1)} %get-tuple-element.8), channel_id=1, source_target_pairs={{0,96},{16,112},{32,0},{48,16},{64,32},{80,48},{96,64},{112,80},{1... | collective-permute-start | bytes 1572872 | tf_op jit(solution)/shard_map/ppermute | solution.py:33
  158.3 30.0 %copy-start = (bf16[128,8,8,256]{3,1,2,0:T(8,128)(2,1)S(1)}, bf16[128,8,8,256]{3,1,2,0:T(8,128)(2,1)}, u32[]{:S(2)}) copy-start(bf16[128,8,8,256]{3,1,2,0:T(8,128)(2,1)} %copy.16) | copy-start | bytes 12582916
  159.4 60.9 %collective-permute-start.16 = (bf16[128,2048]{1,0:T(8,128)(2,1)}, bf16[128,2048]{1,0:T(8,128)(2,1)}, u32[]{:S(2)}, u32[]{:S(2)}) collective-permute-start(bf16[128,2048]{1,0:T(8,128)(2,1)} %get-tuple-element.9), channel_id=1, source_target_pairs={{0,32},{16,48},{32,64},{48,80},{64,96},{80,112},{96,0},{112,16},{1... | collective-permute-start | bytes 1572872 | tf_op jit(solution)/shard_map/ppermute | solution.py:32
  175.3 44.9 %collective-permute-start.17 = (bf16[128,2048]{1,0:T(8,128)(2,1)}, bf16[128,2048]{1,0:T(8,128)(2,1)}, u32[]{:S(2)}, u32[]{:S(2)}) collective-permute-start(bf16[128,2048]{1,0:T(8,128)(2,1)} %get-tuple-element.10), channel_id=1, source_target_pairs={{0,96},{16,112},{32,0},{48,16},{64,32},{80,48},{96,64},{112,80},{1... | collective-permute-start | bytes 1572872 | tf_op jit(solution)/shard_map/ppermute | solution.py:33
  178.2 49.6 %collective-permute-start.25 = (bf16[128,2048]{1,0:T(8,128)(2,1)}, bf16[128,2048]{1,0:T(8,128)(2,1)}, u32[]{:S(2)}, u32[]{:S(2)}) collective-permute-start(bf16[128,2048]{1,0:T(8,128)(2,1)} %get-tuple-element.11), channel_id=1, source_target_pairs={{0,32},{16,48},{32,64},{48,80},{64,96},{80,112},{96,0},{112,16},{1... | collective-permute-start | bytes 1572872 | tf_op jit(solution)/shard_map/ppermute | solution.py:32
  186.5 41.3 %collective-permute-start.26 = (bf16[128,2048]{1,0:T(8,128)(2,1)}, bf16[128,2048]{1,0:T(8,128)(2,1)}, u32[]{:S(2)}, u32[]{:S(2)}) collective-permute-start(bf16[128,2048]{1,0:T(8,128)(2,1)} %get-tuple-element.12), channel_id=1, source_target_pairs={{0,96},{16,112},{32,0},{48,16},{64,32},{80,48},{96,64},{112,80},{1... | collective-permute-start | bytes 1572872 | tf_op jit(solution)/shard_map/ppermute | solution.py:33
  192.9 41.6 %collective-permute-start.9 = (f32[8,64,256]{2,1,0:T(8,128)}, f32[8,64,256]{2,1,0:T(8,128)}, u32[]{:S(2)}, u32[]{:S(2)}) collective-permute-start(f32[8,64,256]{2,1,0:T(8,128)} %dynamic-slice_bitcast_fusion.2), channel_id=1, source_target_pairs={{0,1},{1,0},{2,3},{3,2},{4,5},{5,4},{6,7},{7,6},{8,9},{9,8},{10,11... | collective-permute-start | bytes 1572872 | tf_op jit(solution)/shard_map/ppermute | solution.py:50
  227.5 29.9 %collective-permute-start.18 = (f32[8,64,256]{2,1,0:T(8,128)}, f32[8,64,256]{2,1,0:T(8,128)}, u32[]{:S(2)}, u32[]{:S(2)}) collective-permute-start(f32[8,64,256]{2,1,0:T(8,128)} %dynamic-slice_bitcast_fusion.1), channel_id=1, source_target_pairs={{0,1},{1,0},{2,3},{3,2},{4,5},{5,4},{6,7},{7,6},{8,9},{9,8},{10,11... | collective-permute-start | bytes 1572872 | tf_op jit(solution)/shard_map/ppermute | solution.py:50
  234.2 24.4 %collective-permute-start.27 = (f32[8,64,256]{2,1,0:T(8,128)S(1)}, f32[8,64,256]{2,1,0:T(8,128)S(1)}, u32[]{:S(2)}, u32[]{:S(2)}) collective-permute-start(f32[8,64,256]{2,1,0:T(8,128)S(1)} %dynamic-slice_bitcast_fusion), channel_id=1, source_target_pairs={{0,1},{1,0},{2,3},{3,2},{4,5},{5,4},{6,7},{7,6},{8,9},{9,8},{10,11... | collective-permute-start | bytes 1572872 | tf_op jit(solution)/shard_map/ppermute | solution.py:50
  235.7 28.8 %collective-permute-start.10 = (f32[4,64,256]{2,1,0:T(8,128)S(1)}, f32[4,64,256]{2,1,0:T(8,128)S(1)}, u32[]{:S(2)}, u32[]{:S(2)}) collective-permute-start(f32[4,64,256]{2,1,0:T(8,128)S(1)} %dynamic-slice_bitcast_fusion.5), channel_id=1, source_target_pairs={{0,2},{1,3},{2,0},{3,1},{4,6},{5,7},{6,4},{7,5},{8,10},{9,11},{10,... | collective-permute-start | bytes 786440 | tf_op jit(solution)/shard_map/ppermute | solution.py:50
  258.5 11.6 %collective-permute-start.19 = (f32[4,64,256]{2,1,0:T(8,128)S(1)}, f32[4,64,256]{2,1,0:T(8,128)S(1)}, u32[]{:S(2)}, u32[]{:S(2)}) collective-permute-start(f32[4,64,256]{2,1,0:T(8,128)S(1)} %dynamic-slice_bitcast_fusion.4), channel_id=1, source_target_pairs={{0,2},{1,3},{2,0},{3,1},{4,6},{5,7},{6,4},{7,5},{8,10},{9,11},{10,... | collective-permute-start | bytes 786440 | tf_op jit(solution)/shard_map/ppermute | solution.py:50
  258.8 17.0 %collective-permute-start.28 = (f32[4,64,256]{2,1,0:T(8,128)S(1)}, f32[4,64,256]{2,1,0:T(8,128)S(1)}, u32[]{:S(2)}, u32[]{:S(2)}) collective-permute-start(f32[4,64,256]{2,1,0:T(8,128)S(1)} %dynamic-slice_bitcast_fusion.3), channel_id=1, source_target_pairs={{0,2},{1,3},{2,0},{3,1},{4,6},{5,7},{6,4},{7,5},{8,10},{9,11},{10,... | collective-permute-start | bytes 786440 | tf_op jit(solution)/shard_map/ppermute | solution.py:50
  264.5 16.0 %collective-permute-start.11 = (f32[2,64,256]{2,1,0:T(8,128)S(1)}, f32[2,64,256]{2,1,0:T(8,128)S(1)}, u32[]{:S(2)}, u32[]{:S(2)}) collective-permute-start(f32[2,64,256]{2,1,0:T(8,128)S(1)} %dynamic-slice_bitcast_fusion.8), channel_id=1, source_target_pairs={{0,4},{1,5},{2,6},{3,7},{4,0},{5,1},{6,2},{7,3},{8,12},{9,13},{10,... | collective-permute-start | bytes 393224 | tf_op jit(solution)/shard_map/ppermute | solution.py:50
  270.2 13.7 %collective-permute-start.20 = (f32[2,64,256]{2,1,0:T(8,128)S(1)}, f32[2,64,256]{2,1,0:T(8,128)S(1)}, u32[]{:S(2)}, u32[]{:S(2)}) collective-permute-start(f32[2,64,256]{2,1,0:T(8,128)S(1)} %dynamic-slice_bitcast_fusion.7), channel_id=1, source_target_pairs={{0,4},{1,5},{2,6},{3,7},{4,0},{5,1},{6,2},{7,3},{8,12},{9,13},{10,... | collective-permute-start | bytes 393224 | tf_op jit(solution)/shard_map/ppermute | solution.py:50
  275.8 10.9 %collective-permute-start.29 = (f32[2,64,256]{2,1,0:T(8,128)S(1)}, f32[2,64,256]{2,1,0:T(8,128)S(1)}, u32[]{:S(2)}, u32[]{:S(2)}) collective-permute-start(f32[2,64,256]{2,1,0:T(8,128)S(1)} %dynamic-slice_bitcast_fusion.6), channel_id=1, source_target_pairs={{0,4},{1,5},{2,6},{3,7},{4,0},{5,1},{6,2},{7,3},{8,12},{9,13},{10,... | collective-permute-start | bytes 393224 | tf_op jit(solution)/shard_map/ppermute | solution.py:50
  280.6 8.6 %collective-permute-start.12 = (f32[1,64,256]{2,1,0:T(8,128)S(1)}, f32[1,64,256]{2,1,0:T(8,128)S(1)}, u32[]{:S(2)}, u32[]{:S(2)}) collective-permute-start(f32[1,64,256]{2,1,0:T(8,128)S(1)} %constant_dynamic-slice_fusion.2), channel_id=1, source_target_pairs={{0,8},{1,9},{2,10},{3,11},{4,12},{5,13},{6,14},{7,15},{8,0},{9,1},... | collective-permute-start | bytes 196616 | tf_op jit(solution)/shard_map/ppermute | solution.py:50
  283.9 5.8 %collective-permute-start.21 = (f32[1,64,256]{2,1,0:T(8,128)S(1)}, f32[1,64,256]{2,1,0:T(8,128)S(1)}, u32[]{:S(2)}, u32[]{:S(2)}) collective-permute-start(f32[1,64,256]{2,1,0:T(8,128)S(1)} %constant_dynamic-slice_fusion.1), channel_id=1, source_target_pairs={{0,8},{1,9},{2,10},{3,11},{4,12},{5,13},{6,14},{7,15},{8,0},{9,1},... | collective-permute-start | bytes 196616 | tf_op jit(solution)/shard_map/ppermute | solution.py:50
  286.7 5.8 %collective-permute-start.30 = (f32[1,64,256]{2,1,0:T(8,128)S(1)}, f32[1,64,256]{2,1,0:T(8,128)S(1)}, u32[]{:S(2)}, u32[]{:S(2)}) collective-permute-start(f32[1,64,256]{2,1,0:T(8,128)S(1)} %constant_dynamic-slice_fusion), channel_id=1, source_target_pairs={{0,8},{1,9},{2,10},{3,11},{4,12},{5,13},{6,14},{7,15},{8,0},{9,1},... | collective-permute-start | bytes 196616 | tf_op jit(solution)/shard_map/ppermute | solution.py:50

commit v8 on v4

--- a/solution.py
+++ b/solution.py
@@ -21,13 +21,21 @@
     me = lax.axis_index(axis)
     ring = size // 2
     z, oz = me // 2, owner // 2
-    pair = lax.ppermute(piece, axis, [(i, i ^ 1) for i in range(size)])
-    val = jnp.where(me == owner, piece, pair)
-    from_below = lax.ppermute(val, axis, [(i, (i + 2) % size) for i in range(size)])
-    from_above = lax.ppermute(val, axis, [(i, (i - 2) % size) for i in range(size)])
+    mine = me % 2 == owner % 2
+    half = piece.shape[0] // 2
+
+    def shift(v, step):
+        return lax.ppermute(v, axis, [(i, (i + step) % size) for i in range(size)])
+
+    pair = lax.ppermute(piece[half:], axis, [(i, i ^ 1) for i in range(size)])
+    val = jnp.where(mine, piece[:half], pair)
+    from_below, from_above = shift(val, 2), shift(val, -2)
     val = jnp.where(z == oz, val, jnp.where(z == (oz + 1) % ring, from_below, from_above))
-    last = lax.ppermute(val, axis, [(i, (i + 2) % size) for i in range(size)])
-    return jnp.where(z == (oz + 2) % ring, last, val)
+    quarter = half // 2
+    last = jnp.concatenate([shift(val[:quarter], 2), shift(val[quarter:], -2)])
+    val = jnp.where(z == (oz + 2) % ring, last, val)
+    other = lax.ppermute(val, axis, [(i, i ^ 1) for i in range(size)])
+    return jnp.where(mine, jnp.concatenate([val, other]), jnp.concatenate([other, val]))
 
 
 def reduce_scatter_slab(term, axis):

time: 327 us -> 262 us (0.80)
  waiting for transfers between devices: 76.7 us -> 32.4 us
  starting transfers between devices: 124 us -> 108 us
    ppermute x12 -> x18, waiting for transfers between devices: 63.2 us -> 16.5 us  [the longest x12 12.5 us: shift(): return lax.ppermute(v, axis, [(i, (i + step) % size) for i in range(size)])]
    ppermute x12, starting transfers between devices: 95.1 us -> 71.8 us  [reduce_scatter_slab(): part = keep + lax.ppermute(send, axis, [(i, i ^ bit) for i in range(size)])]
    ppermute x12 -> x18, starting transfers between devices: 19.8 us -> 27.7 us  [the longest x12 18.8 us: shift(): return lax.ppermute(v, axis, [(i, (i + step) % size) for i in range(size)])]
    unnamed x14 -> x19, local copies, waits for them, and re-layouts: 6.56 us -> 7.13 us
  transfers between devices with their start and end apart: 28 -> 34, of which waited for: 11 -> 15; matrix products, arithmetic and copies ran while one was open for 9% -> 10% of each run, Pallas kernels for 0% -> 0%
where the time goes in v8:
time: 262 us
  starting transfers between devices  108 us (41%)
  Pallas kernels  72.1 us (28%)
  waiting for transfers between devices  32.4 us (12%)
  local copies, waits for them, and re-layouts  17.1 us (7%)
  other arithmetic  12.1 us (5%)
  matrix products  10.6 us (4%)
  between operations  9.2 us (4%)
    pallas_call x1, Pallas kernels, smooth(): pl.pallas_call(kernel, grid=(rows // block,), in_specs=[pl.BlockSpec(coef...  72.1 us
    ppermute x12, starting transfers between devices, reduce_scatter_slab(): part = keep + lax.ppermute(send, axis, [(i, i ^ bit) for i in range(size)])  71.8 us
    ppermute x12, starting transfers between devices, shift(): return lax.ppermute(v, axis, [(i, (i + step) % size) for i in range(size)])  18.8 us
    ppermute x12, waiting for transfers between devices, reduce_scatter_slab(): part = keep + lax.ppermute(send, axis, [(i, i ^ bit) for i in range(size)])  12.9 us
    ppermute x12, waiting for transfers between devices, shift(): return lax.ppermute(v, axis, [(i, (i + step) % size) for i in range(size)])  12.5 us
    dot_general x3, matrix products, body(): lax.dot_general(flat, received, (((1,), (1,)), ((), ())), preferred_eleme...  10.6 us
    unnamed x19, local copies, waits for them, and re-layouts  7.13 us
    ppermute x2, starting transfers between devices, halo_of(): below = lax.ppermute(top, axis, up)  6.13 us
  transfers between devices with their start and end apart: 34, of which 15 were waited for; matrix products, arithmetic and copies ran while one was open for 10% of the time, Pallas kernels for 0%

profile of v8, /device:TPU:0, one launch (start us, length us, event | category | flops | bytes accessed | tf_op | source)
XLA Modules:
  0.0 261.6 jit_solution(8236838662025049225)
XLA Ops:
  0.6 4.8 %fusion.26 = (bf16[1024,4,256]{2,1,0:T(4,128)(2,1)S(1)}, bf16[1024,4,256]{2,1,0:T(4,128)(2,1)S(1)}) fusion(bf16[1024,8,256]{2,1,0:T(8,128)(2,1)} %a_ref.1), kind=kLoop, calls=%fused_computation.81 | loop fusion | bytes 8388608 | tf_op jit(solution)/shard_map/slice | solution.py:61
  5.5 1.4 collective-permute-start.2
  6.9 1.3 collective-permute-start.3
  8.3 4.7 %collective-permute-start = (f32[4,256]{1,0:T(4,128)S(1)}, f32[4,256]{1,0:T(4,128)S(1)}, u32[]{:S(2)}, u32[]{:S(2)}) collective-permute-start(f32[4,256]{1,0:T(4,128)S(1)} %get-tuple-element.16), channel_id=1, source_target_pairs={{0,1},{1,2},{2,3},{3,4},{4,5},{5,6},{6,7},{7,8},{8,9},{9,10},{10,1... | collective-permute-start | bytes 12296 | tf_op jit(solution)/shard_map/ppermute | solution.py:63
  13.0 1.3 collective-permute-start.1
  14.4 2.9 %collective-permute-done.1 = f32[4,256]{1,0:T(4,128)S(1)} collective-permute-done((f32[4,256]{1,0:T(4,128)S(1)}, f32[4,256]{1,0:T(4,128)S(1)}, u32[]{:S(2)}, u32[]{:S(2)}) %collective-permute-start.1) | collective-permute-done | bytes 4128 | tf_op jit(solution)/shard_map/ppermute | solution.py:64
  17.5 3.4 %pad_maximum_fusion.h_ref = bf16[1024,8,256]{2,1,0:T(8,128)(2,1)} fusion(bf16[1024,4,256]{2,1,0:T(4,128)(2,1)S(1)} %collective-permute-done.3, bf16[1024,4,256]{2,1,0:T(4,128)(2,1)S(1)} %collective-permute-done.2), kind=kLoop, calls=%fused_computation | loop fusion | flops 8388608 | bytes 8388608 | tf_op jit(solution)/shard_map/concatenate | solution.py:65
  20.9 72.1 %shard_map.59 = f32[1024,8,256]{2,1,0:T(8,128)} custom-call(f32[6,16,256]{2,1,0:T(8,128)} %copy-done.2, bf16[1024,8,256]{2,1,0:T(8,128)(2,1)} %a_ref.1, bf16[1024,8,256]{2,1,0:T(8,128)(2,1)} %pad_maximum_fusion.h_ref), custom_call_target="tpu_custom_call" | custom-call | tf_op jit(solution)/shard_map/pallas_call | solution.py:144
  93.0 3.8 %convert.5 = bf16[1024,8,256]{2,1,0:T(8,128)(2,1)S(1)} convert(f32[1024,8,256]{2,1,0:T(8,128)} %shard_map.59) | non-fusion elementwise | flops 2097152 | bytes 12582912 | tf_op jit(solution)/shard_map/convert.2
  97.9 1.6 collective-permute-start.4
  108.8 5.6 %copy.17 = bf16[128,8,8,256]{3,1,2,0:T(8,128)(2,1)} copy(bf16[128,8,8,256]{3,2,1,0:T(8,128)(2,1)} %bitcast.84) | data formatting | bytes 8388608
  114.8 1.7 collective-permute-start.24
  116.7 2.0 collective-permute-start.5
  118.7 2.2 collective-permute-start.6
  121.0 3.2 %collective-permute-start.16 = (bf16[128,2048]{1,0:T(8,128)(2,1)S(1)}, bf16[128,2048]{1,0:T(8,128)(2,1)S(1)}, u32[]{:S(2)}, u32[]{:S(2)}) collective-permute-start(bf16[128,2048]{1,0:T(8,128)(2,1)S(1)} %broadcast_select_fusion.1), channel_id=1, source_target_pairs={{0,96},{16,112},{32,0},{48,16},{64,32},{80,48},{96,64},{112,80},{1... | collective-permute-start | bytes 1572872 | tf_op jit(solution)/shard_map/ppermute | solution.py:28
  124.2 4.0 %collective-permute-done.24 = bf16[128,2048]{1,0:T(8,128)(2,1)S(1)} collective-permute-done((bf16[128,2048]{1,0:T(8,128)(2,1)S(1)}, bf16[128,2048]{1,0:T(8,128)(2,1)S(1)}, u32[]{:S(2)}, u32[]{:S(2)}) %collective-permute-start.24) | collective-permute-done | bytes 524320 | tf_op jit(solution)/shard_map/ppermute | solution.py:30
  128.3 2.0 collective-permute-start.25
  130.3 2.2 collective-permute-start.26
  133.6 2.4 collective-permute-start.8
  136.3 3.2 %collective-permute-done.25 = bf16[128,2048]{1,0:T(8,128)(2,1)S(1)} collective-permute-done((bf16[128,2048]{1,0:T(8,128)(2,1)S(1)}, bf16[128,2048]{1,0:T(8,128)(2,1)S(1)}, u32[]{:S(2)}, u32[]{:S(2)}) %collective-permute-start.25) | collective-permute-done | bytes 524320 | tf_op jit(solution)/shard_map/ppermute | solution.py:28
  139.6 2.0 collective-permute-start.18
  141.8 2.9 %collective-permute-done.7 = bf16[64,2048]{1,0:T(8,128)(2,1)S(1)} collective-permute-done((bf16[64,2048]{1,0:T(8,128)(2,1)S(1)}, bf16[64,2048]{1,0:T(8,128)(2,1)S(1)}, u32[]{:S(2)}, u32[]{:S(2)}) %collective-permute-start.7) | collective-permute-done | bytes 262176 | tf_op jit(solution)/shard_map/ppermute | solution.py:28
  144.8 2.3 collective-permute-start.28
  147.2 1.7 collective-permute-start.9
  148.9 1.4 collective-permute-done.17
  150.8 1.7 collective-permute-start.19
  152.6 3.4 %collective-permute-done.27 = bf16[64,2048]{1,0:T(8,128)(2,1)S(1)} collective-permute-done((bf16[64,2048]{1,0:T(8,128)(2,1)S(1)}, bf16[64,2048]{1,0:T(8,128)(2,1)S(1)}, u32[]{:S(2)}, u32[]{:S(2)}) %collective-permute-start.27) | collective-permute-done | bytes 262176 | tf_op jit(solution)/shard_map/ppermute | solution.py:28
  157.2 1.7 collective-permute-start.29
  158.9 1.3 fusion.2
  161.4 19.1 %collective-permute-start.10 = (f32[8,64,256]{2,1,0:T(8,128)}, f32[8,64,256]{2,1,0:T(8,128)}, u32[]{:S(2)}, u32[]{:S(2)}) collective-permute-start(f32[8,64,256]{2,1,0:T(8,128)} %dynamic-slice_bitcast_fusion.2), channel_id=1, source_target_pairs={{0,1},{1,0},{2,3},{3,2},{4,5},{5,4},{6,7},{7,6},{8,9},{9,8},{10,11... | collective-permute-start | bytes 1572872 | tf_op jit(solution)/shard_map/ppermute | solution.py:52
  180.4 4.1 %fusion.1 = f32[1024,256]{0,1:T(8,128)S(1)} fusion(bf16[1024,2048]{1,0:T(8,128)(2,1)} %bitcast.85, bf16[128,2048]{1,0:T(8,128)(2,1)} %collective-permute-done.19, bf16[128,2048]{1,0:T(8,128)(2,1)} %copy-done.1, pred[]{:T(512)S(6)} %eq.83), kind=kOutput, calls=%fused_computation.4 | convolution fusion | flops 1078722560 | bytes 6291457 | tf_op jit(solution)/shard_map/dot_general | solution.py:174
  185.8 3.2 %collective-permute-start.20 = (f32[8,64,256]{2,1,0:T(8,128)}, f32[8,64,256]{2,1,0:T(8,128)}, u32[]{:S(2)}, u32[]{:S(2)}) collective-permute-start(f32[8,64,256]{2,1,0:T(8,128)} %dynamic-slice_bitcast_fusion.1), channel_id=1, source_target_pairs={{0,1},{1,0},{2,3},{3,2},{4,5},{5,4},{6,7},{7,6},{8,9},{9,8},{10,11... | collective-permute-start | bytes 1572872 | tf_op jit(solution)/shard_map/ppermute | solution.py:52
  189.0 5.1 %fusion = f32[1024,256]{0,1:T(8,128)} fusion(bf16[1024,2048]{1,0:T(8,128)(2,1)} %bitcast.86, bf16[128,2048]{1,0:T(8,128)(2,1)} %collective-permute-done.29, bf16[128,2048]{1,0:T(8,128)(2,1)} %maximum_select_fusion.8, pred[]{:T(512)S(6)} %eq.87), kind=kOutput, calls=%fused_computation.2 | convolution fusion | flops 1078722560 | bytes 6291457 | tf_op jit(solution)/shard_map/dot_general | solution.py:174
  194.2 1.6 copy.14
  196.1 1.1 bitcast_add_fusion.2
  197.2 29.7 %collective-permute-start.11 = (f32[4,64,256]{2,1,0:T(8,128)S(1)}, f32[4,64,256]{2,1,0:T(8,128)S(1)}, u32[]{:S(2)}, u32[]{:S(2)}) collective-permute-start(f32[4,64,256]{2,1,0:T(8,128)S(1)} %dynamic-slice_bitcast_fusion.5), channel_id=1, source_target_pairs={{0,2},{1,3},{2,0},{3,1},{4,6},{5,7},{6,4},{7,5},{8,10},{9,11},{10,... | collective-permute-start | bytes 786440 | tf_op jit(solution)/shard_map/ppermute | solution.py:52
  227.0 1.1 bitcast_add_fusion.1
  228.3 2.1 collective-permute-start.31
  230.4 3.7 %collective-permute-done.11 = f32[4,64,256]{2,1,0:T(8,128)S(1)} collective-permute-done((f32[4,64,256]{2,1,0:T(8,128)S(1)}, f32[4,64,256]{2,1,0:T(8,128)S(1)}, u32[]{:S(2)}, u32[]{:S(2)}) %collective-permute-start.11) | collective-permute-done | bytes 262176 | tf_op jit(solution)/shard_map/ppermute | solution.py:52
  234.2 3.0 %collective-permute-start.12 = (f32[2,64,256]{2,1,0:T(8,128)S(1)}, f32[2,64,256]{2,1,0:T(8,128)S(1)}, u32[]{:S(2)}, u32[]{:S(2)}) collective-permute-start(f32[2,64,256]{2,1,0:T(8,128)S(1)} %dynamic-slice_bitcast_fusion.8), channel_id=1, source_target_pairs={{0,4},{1,5},{2,6},{3,7},{4,0},{5,1},{6,2},{7,3},{8,12},{9,13},{10,... | collective-permute-start | bytes 393224 | tf_op jit(solution)/shard_map/ppermute | solution.py:52
  237.2 2.6 collective-permute-done.21
  239.8 3.0 %collective-permute-start.22 = (f32[2,64,256]{2,1,0:T(8,128)S(1)}, f32[2,64,256]{2,1,0:T(8,128)S(1)}, u32[]{:S(2)}, u32[]{:S(2)}) collective-permute-start(f32[2,64,256]{2,1,0:T(8,128)S(1)} %dynamic-slice_bitcast_fusion.7), channel_id=1, source_target_pairs={{0,4},{1,5},{2,6},{3,7},{4,0},{5,1},{6,2},{7,3},{8,12},{9,13},{10,... | collective-permute-start | bytes 393224 | tf_op jit(solution)/shard_map/ppermute | solution.py:52
  242.8 2.6 collective-permute-done.31
  245.4 3.0 %collective-permute-start.32 = (f32[2,64,256]{2,1,0:T(8,128)S(1)}, f32[2,64,256]{2,1,0:T(8,128)S(1)}, u32[]{:S(2)}, u32[]{:S(2)}) collective-permute-start(f32[2,64,256]{2,1,0:T(8,128)S(1)} %dynamic-slice_bitcast_fusion.6), channel_id=1, source_target_pairs={{0,4},{1,5},{2,6},{3,7},{4,0},{5,1},{6,2},{7,3},{8,12},{9,13},{10,... | collective-permute-start | bytes 393224 | tf_op jit(solution)/shard_map/ppermute | solution.py:52
  249.2 3.0 %collective-permute-start.13 = (f32[1,64,256]{2,1,0:T(8,128)S(1)}, f32[1,64,256]{2,1,0:T(8,128)S(1)}, u32[]{:S(2)}, u32[]{:S(2)}) collective-permute-start(f32[1,64,256]{2,1,0:T(8,128)S(1)} %constant_dynamic-slice_fusion.2), channel_id=1, source_target_pairs={{0,8},{1,9},{2,10},{3,11},{4,12},{5,13},{6,14},{7,15},{8,0},{9,1},... | collective-permute-start | bytes 196616 | tf_op jit(solution)/shard_map/ppermute | solution.py:52
  252.2 2.8 %collective-permute-start.23 = (f32[1,64,256]{2,1,0:T(8,128)S(1)}, f32[1,64,256]{2,1,0:T(8,128)S(1)}, u32[]{:S(2)}, u32[]{:S(2)}) collective-permute-start(f32[1,64,256]{2,1,0:T(8,128)S(1)} %constant_dynamic-slice_fusion.1), channel_id=1, source_target_pairs={{0,8},{1,9},{2,10},{3,11},{4,12},{5,13},{6,14},{7,15},{8,0},{9,1},... | collective-permute-start | bytes 196616 | tf_op jit(solution)/shard_map/ppermute | solution.py:52
  255.0 2.6 collective-permute-start.33
  258.1 2.8 %collective-permute-done.33 = f32[1,64,256]{2,1,0:T(8,128)S(1)} collective-permute-done((f32[1,64,256]{2,1,0:T(8,128)S(1)}, f32[1,64,256]{2,1,0:T(8,128)S(1)}, u32[]{:S(2)}, u32[]{:S(2)}) %collective-permute-start.33) | collective-permute-done | bytes 65568 | tf_op jit(solution)/shard_map/ppermute | solution.py:52
  (100 shorter events, 11.9 us)
Async XLA Ops:
  0.6 7.6 %copy-start.3 = (s32[8,256]{1,0:T(8,128)S(1)}, s32[8,256]{1,0:T(8,128)}, u32[]{:S(2)}) copy-start(s32[8,256]{1,0:T(8,128)} %param.5) | copy-start | bytes 24580
  0.6 7.6 %copy-start.5 = (f32[8]{0:T(128)S(1)}, f32[8]{0:T(128)}, u32[]{:S(2)}) copy-start(f32[8]{0:T(128)} %param.6) | copy-start | bytes 100
  5.5 12.0 %collective-permute-start.2 = (bf16[1024,4,256]{2,1,0:T(4,128)(2,1)S(1)}, bf16[1024,4,256]{2,1,0:T(4,128)(2,1)S(1)}, u32[]{:S(2)}, u32[]{:S(2)}) collective-permute-start(bf16[1024,4,256]{2,1,0:T(4,128)(2,1)S(1)} %get-tuple-element.8), channel_id=1, source_target_pairs={{0,1},{1,2},{2,3},{3,4},{4,5},{5,6},{6,7},{7,8},{8,9},{9,10},{10,1... | collective-permute-start | bytes 6291464 | tf_op jit(solution)/shard_map/ppermute | solution.py:63
  6.9 10.6 %collective-permute-start.3 = (bf16[1024,4,256]{2,1,0:T(4,128)(2,1)S(1)}, bf16[1024,4,256]{2,1,0:T(4,128)(2,1)S(1)}, u32[]{:S(2)}, u32[]{:S(2)}) collective-permute-start(bf16[1024,4,256]{2,1,0:T(4,128)(2,1)S(1)} %get-tuple-element.9), channel_id=1, source_target_pairs={{1,0},{2,1},{3,2},{4,3},{5,4},{6,5},{7,6},{8,7},{9,8},{10,9},{11,1... | collective-permute-start | bytes 6291464 | tf_op jit(solution)/shard_map/ppermute | solution.py:64
  8.3 6.1 %collective-permute-start = (f32[4,256]{1,0:T(4,128)S(1)}, f32[4,256]{1,0:T(4,128)S(1)}, u32[]{:S(2)}, u32[]{:S(2)}) collective-permute-start(f32[4,256]{1,0:T(4,128)S(1)} %get-tuple-element.16), channel_id=1, source_target_pairs={{0,1},{1,2},{2,3},{3,4},{4,5},{5,6},{6,7},{7,8},{8,9},{9,10},{10,1... | collective-permute-start | bytes 12296 | tf_op jit(solution)/shard_map/ppermute | solution.py:63
  13.0 4.3 %collective-permute-start.1 = (f32[4,256]{1,0:T(4,128)S(1)}, f32[4,256]{1,0:T(4,128)S(1)}, u32[]{:S(2)}, u32[]{:S(2)}) collective-permute-start(f32[4,256]{1,0:T(4,128)S(1)} %get-tuple-element.17), channel_id=1, source_target_pairs={{1,0},{2,1},{3,2},{4,3},{5,4},{6,5},{7,6},{8,7},{9,8},{10,9},{11,1... | collective-permute-start | bytes 12296 | tf_op jit(solution)/shard_map/ppermute | solution.py:64
  17.4 3.5 %copy-start.2 = (f32[6,16,256]{2,1,0:T(8,128)}, f32[6,16,256]{2,1,0:T(8,128)S(1)}, u32[]{:S(2)}) copy-start(f32[6,16,256]{2,1,0:T(8,128)S(1)} %select_dynamic-update-slice_fusion.coef_ref) | copy-start | bytes 294916
  97.0 3.1 %copy-start.4 = (s32[8]{0:T(128)S(1)}, s32[8]{0:T(128)}, u32[]{:S(2)}) copy-start(s32[8]{0:T(128)} %param.7) | copy-start | bytes 100
  97.9 18.7 %collective-permute-start.4 = (bf16[128,2048]{1,0:T(8,128)(2,1)}, bf16[128,2048]{1,0:T(8,128)(2,1)}, u32[]{:S(2)}, u32[]{:S(2)}) collective-permute-start(bf16[128,2048]{1,0:T(8,128)(2,1)} %bitcast.43), channel_id=1, source_target_pairs={{0,16},{16,0},{32,48},{48,32},{64,80},{80,64},{96,112},{112,96},{1... | collective-permute-start | bytes 1572872 | tf_op jit(solution)/shard_map/ppermute | solution.py:30
  99.6 21.3 %collective-permute-start.14 = (bf16[128,2048]{1,0:T(8,128)(2,1)S(1)}, bf16[128,2048]{1,0:T(8,128)(2,1)S(1)}, u32[]{:S(2)}, u32[]{:S(2)}) collective-permute-start(bf16[128,2048]{1,0:T(8,128)(2,1)S(1)} %bitcast.115), channel_id=1, source_target_pairs={{0,16},{16,0},{32,48},{48,32},{64,80},{80,64},{96,112},{112,96},{1... | collective-permute-start | bytes 1572872 | tf_op jit(solution)/shard_map/ppermute | solution.py:30
  114.8 13.4 %collective-permute-start.24 = (bf16[128,2048]{1,0:T(8,128)(2,1)S(1)}, bf16[128,2048]{1,0:T(8,128)(2,1)S(1)}, u32[]{:S(2)}, u32[]{:S(2)}) collective-permute-start(bf16[128,2048]{1,0:T(8,128)(2,1)S(1)} %bitcast.116), channel_id=1, source_target_pairs={{0,16},{16,0},{32,48},{48,32},{64,80},{80,64},{96,112},{112,96},{1... | collective-permute-start | bytes 1572872 | tf_op jit(solution)/shard_map/ppermute | solution.py:30
  116.7 13.6 %collective-permute-start.5 = (bf16[128,2048]{1,0:T(8,128)(2,1)S(1)}, bf16[128,2048]{1,0:T(8,128)(2,1)S(1)}, u32[]{:S(2)}, u32[]{:S(2)}) collective-permute-start(bf16[128,2048]{1,0:T(8,128)(2,1)S(1)} %broadcast_select_fusion.2), channel_id=1, source_target_pairs={{0,32},{16,48},{32,64},{48,80},{64,96},{80,112},{96,0},{112,16},{1... | collective-permute-start | bytes 1572872 | tf_op jit(solution)/shard_map/ppermute | solution.py:28
  118.7 13.8 %collective-permute-start.6 = (bf16[128,2048]{1,0:T(8,128)(2,1)S(1)}, bf16[128,2048]{1,0:T(8,128)(2,1)S(1)}, u32[]{:S(2)}, u32[]{:S(2)}) collective-permute-start(bf16[128,2048]{1,0:T(8,128)(2,1)S(1)} %broadcast_select_fusion.2), channel_id=1, source_target_pairs={{0,96},{16,112},{32,0},{48,16},{64,32},{80,48},{96,64},{112,80},{1... | collective-permute-start | bytes 1572872 | tf_op jit(solution)/shard_map/ppermute | solution.py:28
  120.9 12.6 %collective-permute-start.15 = (bf16[128,2048]{1,0:T(8,128)(2,1)S(1)}, bf16[128,2048]{1,0:T(8,128)(2,1)S(1)}, u32[]{:S(2)}, u32[]{:S(2)}) collective-permute-start(bf16[128,2048]{1,0:T(8,128)(2,1)S(1)} %broadcast_select_fusion.1), channel_id=1, source_target_pairs={{0,32},{16,48},{32,64},{48,80},{64,96},{80,112},{96,0},{112,16},{1... | collective-permute-start | bytes 1572872 | tf_op jit(solution)/shard_map/ppermute | solution.py:28
  121.0 14.9 %collective-permute-start.16 = (bf16[128,2048]{1,0:T(8,128)(2,1)S(1)}, bf16[128,2048]{1,0:T(8,128)(2,1)S(1)}, u32[]{:S(2)}, u32[]{:S(2)}) collective-permute-start(bf16[128,2048]{1,0:T(8,128)(2,1)S(1)} %broadcast_select_fusion.1), channel_id=1, source_target_pairs={{0,96},{16,112},{32,0},{48,16},{64,32},{80,48},{96,64},{112,80},{1... | collective-permute-start | bytes 1572872 | tf_op jit(solution)/shard_map/ppermute | solution.py:28
  128.3 11.3 %collective-permute-start.25 = (bf16[128,2048]{1,0:T(8,128)(2,1)S(1)}, bf16[128,2048]{1,0:T(8,128)(2,1)S(1)}, u32[]{:S(2)}, u32[]{:S(2)}) collective-permute-start(bf16[128,2048]{1,0:T(8,128)(2,1)S(1)} %broadcast_select_fusion), channel_id=1, source_target_pairs={{0,32},{16,48},{32,64},{48,80},{64,96},{80,112},{96,0},{112,16},{1... | collective-permute-start | bytes 1572872 | tf_op jit(solution)/shard_map/ppermute | solution.py:28
  130.3 11.3 %collective-permute-start.26 = (bf16[128,2048]{1,0:T(8,128)(2,1)S(1)}, bf16[128,2048]{1,0:T(8,128)(2,1)S(1)}, u32[]{:S(2)}, u32[]{:S(2)}) collective-permute-start(bf16[128,2048]{1,0:T(8,128)(2,1)S(1)} %broadcast_select_fusion), channel_id=1, source_target_pairs={{0,96},{16,112},{32,0},{48,16},{64,32},{80,48},{96,64},{112,80},{1... | collective-permute-start | bytes 1572872 | tf_op jit(solution)/shard_map/ppermute | solution.py:28
  132.6 12.1 %collective-permute-start.7 = (bf16[64,2048]{1,0:T(8,128)(2,1)S(1)}, bf16[64,2048]{1,0:T(8,128)(2,1)S(1)}, u32[]{:S(2)}, u32[]{:S(2)}) collective-permute-start(bf16[64,2048]{1,0:T(8,128)(2,1)S(1)} %get-tuple-element.10), channel_id=1, source_target_pairs={{0,32},{16,48},{32,64},{48,80},{64,96},{80,112},{96,0},{112,16},{1... | collective-permute-start | bytes 786440 | tf_op jit(solution)/shard_map/ppermute | solution.py:28
  133.6 13.5 %collective-permute-start.8 = (bf16[64,2048]{1,0:T(8,128)(2,1)S(1)}, bf16[64,2048]{1,0:T(8,128)(2,1)S(1)}, u32[]{:S(2)}, u32[]{:S(2)}) collective-permute-start(bf16[64,2048]{1,0:T(8,128)(2,1)S(1)} %get-tuple-element.11), channel_id=1, source_target_pairs={{0,96},{16,112},{32,0},{48,16},{64,32},{80,48},{96,64},{112,80},{1... | collective-permute-start | bytes 786440 | tf_op jit(solution)/shard_map/ppermute | solution.py:28
  136.0 14.3 %collective-permute-start.17 = (bf16[64,2048]{1,0:T(8,128)(2,1)S(1)}, bf16[64,2048]{1,0:T(8,128)(2,1)S(1)}, u32[]{:S(2)}, u32[]{:S(2)}) collective-permute-start(bf16[64,2048]{1,0:T(8,128)(2,1)S(1)} %get-tuple-element.12), channel_id=1, source_target_pairs={{0,32},{16,48},{32,64},{48,80},{64,96},{80,112},{96,0},{112,16},{1... | collective-permute-start | bytes 786440 | tf_op jit(solution)/shard_map/ppermute | solution.py:28
  139.6 11.1 %collective-permute-start.18 = (bf16[64,2048]{1,0:T(8,128)(2,1)S(1)}, bf16[64,2048]{1,0:T(8,128)(2,1)S(1)}, u32[]{:S(2)}, u32[]{:S(2)}) collective-permute-start(bf16[64,2048]{1,0:T(8,128)(2,1)S(1)} %get-tuple-element.13), channel_id=1, source_target_pairs={{0,96},{16,112},{32,0},{48,16},{64,32},{80,48},{96,64},{112,80},{1... | collective-permute-start | bytes 786440 | tf_op jit(solution)/shard_map/ppermute | solution.py:28
  141.7 14.3 %collective-permute-start.27 = (bf16[64,2048]{1,0:T(8,128)(2,1)S(1)}, bf16[64,2048]{1,0:T(8,128)(2,1)S(1)}, u32[]{:S(2)}, u32[]{:S(2)}) collective-permute-start(bf16[64,2048]{1,0:T(8,128)(2,1)S(1)} %get-tuple-element.14), channel_id=1, source_target_pairs={{0,32},{16,48},{32,64},{48,80},{64,96},{80,112},{96,0},{112,16},{1... | collective-permute-start | bytes 786440 | tf_op jit(solution)/shard_map/ppermute | solution.py:28
  144.8 14.1 %copy-start = (bf16[128,8,8,256]{3,1,2,0:T(8,128)(2,1)S(1)}, bf16[128,8,8,256]{3,1,2,0:T(8,128)(2,1)}, u32[]{:S(2)}) copy-start(bf16[128,8,8,256]{3,1,2,0:T(8,128)(2,1)} %copy.17) | copy-start | bytes 12582916
  144.8 11.5 %collective-permute-start.28 = (bf16[64,2048]{1,0:T(8,128)(2,1)S(1)}, bf16[64,2048]{1,0:T(8,128)(2,1)S(1)}, u32[]{:S(2)}, u32[]{:S(2)}) collective-permute-start(bf16[64,2048]{1,0:T(8,128)(2,1)S(1)} %get-tuple-element.15), channel_id=1, source_target_pairs={{0,96},{16,112},{32,0},{48,16},{64,32},{80,48},{96,64},{112,80},{1... | collective-permute-start | bytes 786440 | tf_op jit(solution)/shard_map/ppermute | solution.py:28
  147.2 11.7 %collective-permute-start.9 = (bf16[128,2048]{1,0:T(8,128)(2,1)S(1)}, bf16[128,2048]{1,0:T(8,128)(2,1)S(1)}, u32[]{:S(2)}, u32[]{:S(2)}) collective-permute-start(bf16[128,2048]{1,0:T(8,128)(2,1)S(1)} %maximum_select_fusion.6), channel_id=1, source_target_pairs={{0,16},{16,0},{32,48},{48,32},{64,80},{80,64},{96,112},{112,96},{1... | collective-permute-start | bytes 1572872 | tf_op jit(solution)/shard_map/ppermute | solution.py:37
  150.8 9.4 %copy-start.1 = (bf16[128,2048]{1,0:T(8,128)(2,1)}, bf16[128,2048]{1,0:T(8,128)(2,1)S(1)}, u32[]{:S(2)}) copy-start(bf16[128,2048]{1,0:T(8,128)(2,1)S(1)} %maximum_select_fusion.7) | copy-start | bytes 1572868
  150.8 29.6 %collective-permute-start.19 = (bf16[128,2048]{1,0:T(8,128)(2,1)S(1)}, bf16[128,2048]{1,0:T(8,128)(2,1)}, u32[]{:S(2)}, u32[]{:S(2)}) collective-permute-start(bf16[128,2048]{1,0:T(8,128)(2,1)S(1)} %maximum_select_fusion.7), channel_id=1, source_target_pairs={{0,16},{16,0},{32,48},{48,32},{64,80},{80,64},{96,112},{112,96},{1... | collective-permute-start | bytes 1572872 | tf_op jit(solution)/shard_map/ppermute | solution.py:37
  157.2 31.8 %collective-permute-start.29 = (bf16[128,2048]{1,0:T(8,128)(2,1)}, bf16[128,2048]{1,0:T(8,128)(2,1)}, u32[]{:S(2)}, u32[]{:S(2)}) collective-permute-start(bf16[128,2048]{1,0:T(8,128)(2,1)} %maximum_select_fusion.8), channel_id=1, source_target_pairs={{0,16},{16,0},{32,48},{48,32},{64,80},{80,64},{96,112},{112,96},{1... | collective-permute-start | bytes 1572872 | tf_op jit(solution)/shard_map/ppermute | solution.py:37
  161.4 34.7 %collective-permute-start.10 = (f32[8,64,256]{2,1,0:T(8,128)}, f32[8,64,256]{2,1,0:T(8,128)}, u32[]{:S(2)}, u32[]{:S(2)}) collective-permute-start(f32[8,64,256]{2,1,0:T(8,128)} %dynamic-slice_bitcast_fusion.2), channel_id=1, source_target_pairs={{0,1},{1,0},{2,3},{3,2},{4,5},{5,4},{6,7},{7,6},{8,9},{9,8},{10,11... | collective-permute-start | bytes 1572872 | tf_op jit(solution)/shard_map/ppermute | solution.py:52
  185.8 41.2 %collective-permute-start.20 = (f32[8,64,256]{2,1,0:T(8,128)}, f32[8,64,256]{2,1,0:T(8,128)}, u32[]{:S(2)}, u32[]{:S(2)}) collective-permute-start(f32[8,64,256]{2,1,0:T(8,128)} %dynamic-slice_bitcast_fusion.1), channel_id=1, source_target_pairs={{0,1},{1,0},{2,3},{3,2},{4,5},{5,4},{6,7},{7,6},{8,9},{9,8},{10,11... | collective-permute-start | bytes 1572872 | tf_op jit(solution)/shard_map/ppermute | solution.py:52
  195.8 32.5 %collective-permute-start.30 = (f32[8,64,256]{2,1,0:T(8,128)S(1)}, f32[8,64,256]{2,1,0:T(8,128)S(1)}, u32[]{:S(2)}, u32[]{:S(2)}) collective-permute-start(f32[8,64,256]{2,1,0:T(8,128)S(1)} %dynamic-slice_bitcast_fusion), channel_id=1, source_target_pairs={{0,1},{1,0},{2,3},{3,2},{4,5},{5,4},{6,7},{7,6},{8,9},{9,8},{10,11... | collective-permute-start | bytes 1572872 | tf_op jit(solution)/shard_map/ppermute | solution.py:52
  197.2 36.9 %collective-permute-start.11 = (f32[4,64,256]{2,1,0:T(8,128)S(1)}, f32[4,64,256]{2,1,0:T(8,128)S(1)}, u32[]{:S(2)}, u32[]{:S(2)}) collective-permute-start(f32[4,64,256]{2,1,0:T(8,128)S(1)} %dynamic-slice_bitcast_fusion.5), channel_id=1, source_target_pairs={{0,2},{1,3},{2,0},{3,1},{4,6},{5,7},{6,4},{7,5},{8,10},{9,11},{10,... | collective-permute-start | bytes 786440 | tf_op jit(solution)/shard_map/ppermute | solution.py:52
  228.1 11.6 %collective-permute-start.21 = (f32[4,64,256]{2,1,0:T(8,128)S(1)}, f32[4,64,256]{2,1,0:T(8,128)S(1)}, u32[]{:S(2)}, u32[]{:S(2)}) collective-permute-start(f32[4,64,256]{2,1,0:T(8,128)S(1)} %dynamic-slice_bitcast_fusion.4), channel_id=1, source_target_pairs={{0,2},{1,3},{2,0},{3,1},{4,6},{5,7},{6,4},{7,5},{8,10},{9,11},{10,... | collective-permute-start | bytes 786440 | tf_op jit(solution)/shard_map/ppermute | solution.py:52
  228.3 17.0 %collective-permute-start.31 = (f32[4,64,256]{2,1,0:T(8,128)S(1)}, f32[4,64,256]{2,1,0:T(8,128)S(1)}, u32[]{:S(2)}, u32[]{:S(2)}) collective-permute-start(f32[4,64,256]{2,1,0:T(8,128)S(1)} %dynamic-slice_bitcast_fusion.3), channel_id=1, source_target_pairs={{0,2},{1,3},{2,0},{3,1},{4,6},{5,7},{6,4},{7,5},{8,10},{9,11},{10,... | collective-permute-start | bytes 786440 | tf_op jit(solution)/shard_map/ppermute | solution.py:52
  234.2 14.9 %collective-permute-start.12 = (f32[2,64,256]{2,1,0:T(8,128)S(1)}, f32[2,64,256]{2,1,0:T(8,128)S(1)}, u32[]{:S(2)}, u32[]{:S(2)}) collective-permute-start(f32[2,64,256]{2,1,0:T(8,128)S(1)} %dynamic-slice_bitcast_fusion.8), channel_id=1, source_target_pairs={{0,4},{1,5},{2,6},{3,7},{4,0},{5,1},{6,2},{7,3},{8,12},{9,13},{10,... | collective-permute-start | bytes 393224 | tf_op jit(solution)/shard_map/ppermute | solution.py:52
  239.8 12.4 %collective-permute-start.22 = (f32[2,64,256]{2,1,0:T(8,128)S(1)}, f32[2,64,256]{2,1,0:T(8,128)S(1)}, u32[]{:S(2)}, u32[]{:S(2)}) collective-permute-start(f32[2,64,256]{2,1,0:T(8,128)S(1)} %dynamic-slice_bitcast_fusion.7), channel_id=1, source_target_pairs={{0,4},{1,5},{2,6},{3,7},{4,0},{5,1},{6,2},{7,3},{8,12},{9,13},{10,... | collective-permute-start | bytes 393224 | tf_op jit(solution)/shard_map/ppermute | solution.py:52
  245.4 9.6 %collective-permute-start.32 = (f32[2,64,256]{2,1,0:T(8,128)S(1)}, f32[2,64,256]{2,1,0:T(8,128)S(1)}, u32[]{:S(2)}, u32[]{:S(2)}) collective-permute-start(f32[2,64,256]{2,1,0:T(8,128)S(1)} %dynamic-slice_bitcast_fusion.6), channel_id=1, source_target_pairs={{0,4},{1,5},{2,6},{3,7},{4,0},{5,1},{6,2},{7,3},{8,12},{9,13},{10,... | collective-permute-start | bytes 393224 | tf_op jit(solution)/shard_map/ppermute | solution.py:52
  249.2 8.4 %collective-permute-start.13 = (f32[1,64,256]{2,1,0:T(8,128)S(1)}, f32[1,64,256]{2,1,0:T(8,128)S(1)}, u32[]{:S(2)}, u32[]{:S(2)}) collective-permute-start(f32[1,64,256]{2,1,0:T(8,128)S(1)} %constant_dynamic-slice_fusion.2), channel_id=1, source_target_pairs={{0,8},{1,9},{2,10},{3,11},{4,12},{5,13},{6,14},{7,15},{8,0},{9,1},... | collective-permute-start | bytes 196616 | tf_op jit(solution)/shard_map/ppermute | solution.py:52
  252.2 5.8 %collective-permute-start.23 = (f32[1,64,256]{2,1,0:T(8,128)S(1)}, f32[1,64,256]{2,1,0:T(8,128)S(1)}, u32[]{:S(2)}, u32[]{:S(2)}) collective-permute-start(f32[1,64,256]{2,1,0:T(8,128)S(1)} %constant_dynamic-slice_fusion.1), channel_id=1, source_target_pairs={{0,8},{1,9},{2,10},{3,11},{4,12},{5,13},{6,14},{7,15},{8,0},{9,1},... | collective-permute-start | bytes 196616 | tf_op jit(solution)/shard_map/ppermute | solution.py:52
  255.0 5.8 %collective-permute-start.33 = (f32[1,64,256]{2,1,0:T(8,128)S(1)}, f32[1,64,256]{2,1,0:T(8,128)S(1)}, u32[]{:S(2)}, u32[]{:S(2)}) collective-permute-start(f32[1,64,256]{2,1,0:T(8,128)S(1)} %constant_dynamic-slice_fusion), channel_id=1, source_target_pairs={{0,8},{1,9},{2,10},{3,11},{4,12},{5,13},{6,14},{7,15},{8,0},{9,1},... | collective-permute-start | bytes 196616 | tf_op jit(solution)/shard_map/ppermute | solution.py:52

commit v9 on v5

--- a/solution.py
+++ b/solution.py
@@ -21,13 +21,21 @@
     me = lax.axis_index(axis)
     ring = size // 2
     z, oz = me // 2, owner // 2
-    pair = lax.ppermute(piece, axis, [(i, i ^ 1) for i in range(size)])
-    val = jnp.where(me == owner, piece, pair)
-    from_below = lax.ppermute(val, axis, [(i, (i + 2) % size) for i in range(size)])
-    from_above = lax.ppermute(val, axis, [(i, (i - 2) % size) for i in range(size)])
+    mine = me % 2 == owner % 2
+    half = piece.shape[0] // 2
+
+    def shift(v, step):
+        return lax.ppermute(v, axis, [(i, (i + step) % size) for i in range(size)])
+
+    pair = lax.ppermute(piece[half:], axis, [(i, i ^ 1) for i in range(size)])
+    val = jnp.where(mine, piece[:half], pair)
+    from_below, from_above = shift(val, 2), shift(val, -2)
     val = jnp.where(z == oz, val, jnp.where(z == (oz + 1) % ring, from_below, from_above))
-    last = lax.ppermute(val, axis, [(i, (i + 2) % size) for i in range(size)])
-    return jnp.where(z == (oz + 2) % ring, last, val)
+    quarter = half // 2
+    last = jnp.concatenate([shift(val[:quarter], 2), shift(val[quarter:], -2)])
+    val = jnp.where(z == (oz + 2) % ring, last, val)
+    other = lax.ppermute(val, axis, [(i, i ^ 1) for i in range(size)])
+    return jnp.where(mine, jnp.concatenate([val, other]), jnp.concatenate([other, val]))
 
 
 def reduce_scatter_slab(term, axis):
@@ -143,7 +151,7 @@
     in_specs = [
         pl.BlockSpec(coef.shape, lambda i: (0, 0, 0)),
         pl.BlockSpec((block, depth, lat), lambda i: (i + first, 0, 0)),
-        pl.BlockSpec((block, depth, lat), lambda i: (i + first, 0, 0)),
+        pl.BlockSpec((block, depth, lat), lambda i: (i, 0, 0)),
     ]
     args = [coef, sensitivity, halo]
     if aliased:
@@ -171,13 +179,13 @@
         jnp.float32
     )
     kappa = jnp.sum(onehot * class_rate[None, None, :], axis=-1)
-    halo = halo_of(sensitivity, "slab", 1)
     kappa_halo = halo_of(kappa, "slab", 0)
     kappa_col = jnp.concatenate([kappa_halo[:HALO], kappa, kappa_halo[HALO:]], axis=0)
     coef = coefficients(kappa_col, lat)
     field = None
     pieces = []
     for chunk in range(rows // PANEL):
+        halo = halo_of(sensitivity[chunk * PANEL : (chunk + 1) * PANEL], "slab", 1)
         field, piece = smooth_chunk(field, sensitivity, halo, coef, chunk, PANEL)
         pieces.append(piece)
     cells = depth * lat * lax.axis_size("slab")

time: 328 us -> 288 us (0.88)
  starting transfers between devices: 119 us -> 88.3 us
  waiting for transfers between devices: 76.6 us -> 61.3 us
  other arithmetic: 9.1 us -> 17.3 us
    ppermute x12, starting transfers between devices: 89 us -> 32.6 us  [reduce_scatter_slab(): part = keep + lax.ppermute(send, axis, [(i, i ^ bit) for i in range(size)])]
    ppermute x2 -> x5, starting transfers between devices: 6.76 us -> 25.1 us  [halo_of(): below = lax.ppermute(top, axis, up)]
    ppermute x12 -> x18, waiting for transfers between devices: 61.2 us -> 47.3 us  [the longest x12 32 us: shift(): return lax.ppermute(v, axis, [(i, (i + step) % size) for i in range(size)])]
    concatenate x1 -> x4, other arithmetic: 3.52 us -> 9.56 us  [halo_of(): return jnp.concatenate([below, above], axis=dim)]
    ppermute x2 -> x5, starting transfers between devices: 2.58 us -> 6.43 us  [halo_of(): above = lax.ppermute(bottom, axis, down)]
    ppermute x12 -> x18, starting transfers between devices: 20.5 us -> 24.2 us  [the longest x12 20.4 us: shift(): return lax.ppermute(v, axis, [(i, (i + step) % size) for i in range(size)])]
    unnamed x16 -> x19, local copies, waits for them, and re-layouts: 9.03 us -> 7.96 us
  transfers between devices with their start and end apart: 28 -> 40, of which waited for: 15 -> 17; matrix products, arithmetic and copies ran while one was open for 10% -> 16% of each run, Pallas kernels for 6% -> 28%
where the time goes in v9:
time: 288 us; the launch traced here: 287 us
  starting transfers between devices  88.3 us (31%)
  Pallas kernels  79.7 us (28%)
  waiting for transfers between devices  61.3 us (21%)
  local copies, waits for them, and re-layouts  20.3 us (7%)
  other arithmetic  17.3 us (6%)
  matrix products  10.6 us (4%)
  between operations  9.17 us (3%)
    pallas_call x4, Pallas kernels, smooth_chunk(): pl.pallas_call(kernel, grid=(steps,), in_specs=in_specs, out_specs=[pl.Bl...  79.7 us
    ppermute x12, starting transfers between devices, reduce_scatter_slab(): part = keep + lax.ppermute(send, axis, [(i, i ^ bit) for i in range(size)])  32.6 us
    ppermute x12, waiting for transfers between devices, shift(): return lax.ppermute(v, axis, [(i, (i + step) % size) for i in range(size)])  32 us
    ppermute x5, starting transfers between devices, halo_of(): below = lax.ppermute(top, axis, up)  25.1 us
    ppermute x12, starting transfers between devices, shift(): return lax.ppermute(v, axis, [(i, (i + step) % size) for i in range(size)])  20.4 us
    ppermute x3, waiting for transfers between devices, broadcast_dp(): other = lax.ppermute(val, axis, [(i, i ^ 1) for i in range(size)])  15.3 us
    ppermute x12, waiting for transfers between devices, reduce_scatter_slab(): part = keep + lax.ppermute(send, axis, [(i, i ^ bit) for i in range(size)])  14 us
    dot_general x3, matrix products, body(): lax.dot_general(flat, received, (((1,), (1,)), ((), ())), preferred_eleme...  10.6 us
  transfers between devices with their start and end apart: 40, of which 17 were waited for; matrix products, arithmetic and copies ran while one was open for 16% of the time, Pallas kernels for 28%

profile of v9, /device:TPU:0, one launch (start us, length us, event | category | flops | bytes accessed | tf_op | source)
XLA Modules:
  0.0 286.6 jit_solution(99081289946667811)
XLA Ops:
  1.4 1.3 collective-permute-start.1
  2.8 3.0 %collective-permute-start = (f32[4,256]{1,0:T(4,128)S(1)}, f32[4,256]{1,0:T(4,128)S(1)}, u32[]{:S(2)}, u32[]{:S(2)}) collective-permute-start(f32[4,256]{1,0:T(4,128)S(1)} %get-tuple-element.36), channel_id=1, source_target_pairs={{0,1},{1,2},{2,3},{3,4},{4,5},{5,6},{6,7},{7,8},{8,9},{9,10},{10,1... | collective-permute-start | bytes 12296 | tf_op jit(solution)/shard_map/ppermute | solution.py:63
  5.8 5.9 %fusion.25 = (bf16[256,4,256]{2,1,0:T(4,128)(2,1)}, bf16[256,4,256]{2,1,0:T(4,128)(2,1)}, bf16[256,4,256]{2,1,0:T(4,128)(2,1)}, bf16[256,4,256]{2,1,0:T(4,128)(2...) fusion(bf16[1024,8,256]{2,1,0:T(8,128)(2,1)} %a_ref.7), kind=kLoop, calls=%fused_computation.83 | loop fusion | bytes 8388608 | tf_op jit(solution)/shard_map/slice | solution.py:61
  13.0 4.6 %collective-permute-start.4 = (bf16[256,4,256]{2,1,0:T(4,128)(2,1)S(1)}, bf16[256,4,256]{2,1,0:T(4,128)(2,1)}, u32[]{:S(2)}, u32[]{:S(2)}) collective-permute-start(bf16[256,4,256]{2,1,0:T(4,128)(2,1)S(1)} %get-tuple-element.21), channel_id=1, source_target_pairs={{0,1},{1,2},{2,3},{3,4},{4,5},{5,6},{6,7},{7,8},{8,9},{9,10},{10,1... | collective-permute-start | bytes 1572872 | tf_op jit(solution)/shard_map/ppermute | solution.py:63
  27.5 5.7 %copy.20 = bf16[128,8,8,256]{3,1,2,0:T(8,128)(2,1)} copy(bf16[128,8,8,256]{3,2,1,0:T(8,128)(2,1)} %bitcast.84) | data formatting | bytes 8388608
  34.5 4.1 %collective-permute-start.8 = (bf16[256,4,256]{2,1,0:T(4,128)(2,1)}, bf16[256,4,256]{2,1,0:T(4,128)(2,1)S(1)}, u32[]{:S(2)}, u32[]{:S(2)}) collective-permute-start(bf16[256,4,256]{2,1,0:T(4,128)(2,1)} %get-tuple-element.16), channel_id=1, source_target_pairs={{0,1},{1,2},{2,3},{3,4},{4,5},{5,6},{6,7},{7,8},{8,9},{9,10},{10,1... | collective-permute-start | bytes 1572872 | tf_op jit(solution)/shard_map/ppermute | solution.py:63
  38.7 9.5 %collective-permute-start.6 = (bf16[256,4,256]{2,1,0:T(4,128)(2,1)S(1)}, bf16[256,4,256]{2,1,0:T(4,128)(2,1)}, u32[]{:S(2)}, u32[]{:S(2)}) collective-permute-start(bf16[256,4,256]{2,1,0:T(4,128)(2,1)S(1)} %get-tuple-element.19), channel_id=1, source_target_pairs={{0,1},{1,2},{2,3},{3,4},{4,5},{5,6},{6,7},{7,8},{8,9},{9,10},{10,1... | collective-permute-start | bytes 1572872 | tf_op jit(solution)/shard_map/ppermute | solution.py:63
  49.6 1.5 pad_maximum_fusion.3.h_ref
  51.0 19.9 %shard_map.59 = (f32[1024,8,256]{2,1,0:T(8,128)}, bf16[256,8,256]{2,1,0:T(8,128)(2,1)}) custom-call(f32[6,16,256]{2,1,0:T(8,128)} %copy-done.1, bf16[1024,8,256]{2,1,0:T(8,128)(2,1)} %a_ref.7, bf16[256,8,256]{2,1,0:T(8,128)(2,1)} %pad_maximum_fusion.3.h_ref), custom_call_target="tpu_custom_call" | custom-call | tf_op jit(solution)/shard_map/pallas_call | solution.py:160
  70.9 3.8 %collective-permute-start.2 = (bf16[256,4,256]{2,1,0:T(4,128)(2,1)S(1)}, bf16[256,4,256]{2,1,0:T(4,128)(2,1)}, u32[]{:S(2)}, u32[]{:S(2)}) collective-permute-start(bf16[256,4,256]{2,1,0:T(4,128)(2,1)S(1)} %get-tuple-element.23), channel_id=1, source_target_pairs={{0,1},{1,2},{2,3},{3,4},{4,5},{5,6},{6,7},{7,8},{8,9},{9,10},{10,1... | collective-permute-start | bytes 1572872 | tf_op jit(solution)/shard_map/ppermute | solution.py:63
  74.8 2.7 pad_maximum_fusion.2.h_ref
  77.4 20.0 %shard_map.60 = (f32[1024,8,256]{2,1,0:T(8,128)}, bf16[256,8,256]{2,1,0:T(8,128)(2,1)}) custom-call(f32[6,16,256]{2,1,0:T(8,128)} %copy-done.1, bf16[1024,8,256]{2,1,0:T(8,128)(2,1)} %a_ref.7, bf16[256,8,256]{2,1,0:T(8,128)(2,1)} %pad_maximum_fusion.2.h_ref, f32[1024,8,256]{2,1,0:T(8,128)} %get-tuple-element.9.refs_0_), custom_call_target="tpu_custom_call", output_to_operand_aliasing={{0}: (3, {})} | custom-call | tf_op jit(solution)/shard_map/pallas_call | solution.py:160
  97.4 2.7 pad_maximum_fusion.1.h_ref
  100.1 19.9 %shard_map.61 = (f32[1024,8,256]{2,1,0:T(8,128)}, bf16[256,8,256]{2,1,0:T(8,128)(2,1)}) custom-call(f32[6,16,256]{2,1,0:T(8,128)} %copy-done.1, bf16[1024,8,256]{2,1,0:T(8,128)(2,1)} %a_ref.7, bf16[256,8,256]{2,1,0:T(8,128)(2,1)} %pad_maximum_fusion.1.h_ref, f32[1024,8,256]{2,1,0:T(8,128)} %get-tuple-element.10.refs_0_), custom_call_target="tpu_custom_call", output_to_operand_aliasing={{0}: (3, {})} | custom-call | tf_op jit(solution)/shard_map/pallas_call | solution.py:160
  120.0 1.4 fusion.28
  121.5 1.7 collective-permute-start.30
  125.9 1.6 collective-permute-start.10
  127.5 2.8 pad_maximum_fusion.h_ref
  130.3 19.9 %shard_map.62 = (f32[1024,8,256]{2,1,0:T(8,128)}, bf16[256,8,256]{2,1,0:T(8,128)(2,1)}) custom-call(f32[6,16,256]{2,1,0:T(8,128)} %copy-done.1, bf16[1024,8,256]{2,1,0:T(8,128)(2,1)} %a_ref.7, bf16[256,8,256]{2,1,0:T(8,128)(2,1)} %pad_maximum_fusion.h_ref, f32[1024,8,256]{2,1,0:T(8,128)} %get-tuple-element.11.refs_0_), custom_call_target="tpu_custom_call", output_to_operand_aliasing={{0}: (3, {})} | custom-call | tf_op jit(solution)/shard_map/pallas_call | solution.py:160
  151.3 2.0 collective-permute-start.31
  153.3 2.2 collective-permute-start.32
  155.7 3.2 %collective-permute-start.22 = (bf16[128,2048]{1,0:T(8,128)(2,1)S(1)}, bf16[128,2048]{1,0:T(8,128)(2,1)S(1)}, u32[]{:S(2)}, u32[]{:S(2)}) collective-permute-start(bf16[128,2048]{1,0:T(8,128)(2,1)S(1)} %broadcast_select_fusion.1), channel_id=1, source_target_pairs={{0,96},{16,112},{32,0},{48,16},{64,32},{80,48},{96,64},{112,80},{1... | collective-permute-start | bytes 1572872 | tf_op jit(solution)/shard_map/ppermute | solution.py:28
  160.8 7.5 %collective-permute-done.31 = bf16[128,2048]{1,0:T(8,128)(2,1)S(1)} collective-permute-done((bf16[128,2048]{1,0:T(8,128)(2,1)S(1)}, bf16[128,2048]{1,0:T(8,128)(2,1)S(1)}, u32[]{:S(2)}, u32[]{:S(2)}) %collective-permute-start.31) | collective-permute-done | bytes 524320 | tf_op jit(solution)/shard_map/ppermute | solution.py:28
  168.3 2.0 collective-permute-start.12
  170.4 1.4 collective-permute-start.34
  171.8 7.7 %collective-permute-done.21 = bf16[128,2048]{1,0:T(8,128)(2,1)S(1)} collective-permute-done((bf16[128,2048]{1,0:T(8,128)(2,1)S(1)}, bf16[128,2048]{1,0:T(8,128)(2,1)S(1)}, u32[]{:S(2)}, u32[]{:S(2)}) %collective-permute-start.21) | collective-permute-done | bytes 524320 | tf_op jit(solution)/shard_map/ppermute | solution.py:28
  179.6 3.4 %collective-permute-start.24 = (bf16[64,2048]{1,0:T(8,128)(2,1)S(1)}, bf16[64,2048]{1,0:T(8,128)(2,1)S(1)}, u32[]{:S(2)}, u32[]{:S(2)}) collective-permute-start(bf16[64,2048]{1,0:T(8,128)(2,1)S(1)} %get-tuple-element.33), channel_id=1, source_target_pairs={{0,96},{16,112},{32,0},{48,16},{64,32},{80,48},{96,64},{112,80},{1... | collective-permute-start | bytes 786440 | tf_op jit(solution)/shard_map/ppermute | solution.py:28
  183.0 7.7 %collective-permute-done.11 = bf16[128,2048]{1,0:T(8,128)(2,1)S(1)} collective-permute-done((bf16[128,2048]{1,0:T(8,128)(2,1)S(1)}, bf16[128,2048]{1,0:T(8,128)(2,1)S(1)}, u32[]{:S(2)}, u32[]{:S(2)}) %collective-permute-start.11) | collective-permute-done | bytes 524320 | tf_op jit(solution)/shard_map/ppermute | solution.py:28
  190.9 3.4 %collective-permute-start.14 = (bf16[64,2048]{1,0:T(8,128)(2,1)S(1)}, bf16[64,2048]{1,0:T(8,128)(2,1)S(1)}, u32[]{:S(2)}, u32[]{:S(2)}) collective-permute-start(bf16[64,2048]{1,0:T(8,128)(2,1)S(1)} %get-tuple-element.31), channel_id=1, source_target_pairs={{0,96},{16,112},{32,0},{48,16},{64,32},{80,48},{96,64},{112,80},{1... | collective-permute-start | bytes 786440 | tf_op jit(solution)/shard_map/ppermute | solution.py:28
  194.3 2.0 collective-permute-done.34
  196.3 1.9 collective-permute-start.13
  198.4 3.5 %collective-permute-done.24 = bf16[64,2048]{1,0:T(8,128)(2,1)S(1)} collective-permute-done((bf16[64,2048]{1,0:T(8,128)(2,1)S(1)}, bf16[64,2048]{1,0:T(8,128)(2,1)S(1)}, u32[]{:S(2)}, u32[]{:S(2)}) %collective-permute-start.24) | collective-permute-done | bytes 262176 | tf_op jit(solution)/shard_map/ppermute | solution.py:28
  202.2 3.1 %collective-permute-done.14 = bf16[64,2048]{1,0:T(8,128)(2,1)S(1)} collective-permute-done((bf16[64,2048]{1,0:T(8,128)(2,1)S(1)}, bf16[64,2048]{1,0:T(8,128)(2,1)S(1)}, u32[]{:S(2)}, u32[]{:S(2)}) %collective-permute-start.14) | collective-permute-done | bytes 262176 | tf_op jit(solution)/shard_map/ppermute | solution.py:28
  206.7 6.6 %collective-permute-done.35 = bf16[128,2048]{1,0:T(8,128)(2,1)S(1)} collective-permute-done((bf16[128,2048]{1,0:T(8,128)(2,1)S(1)}, bf16[128,2048]{1,0:T(8,128)(2,1)S(1)}, u32[]{:S(2)}, u32[]{:S(2)}) %collective-permute-start.35) | collective-permute-done | bytes 524320 | tf_op jit(solution)/shard_map/ppermute | solution.py:37
  215.8 8.4 %collective-permute-done.25 = bf16[128,2048]{1,0:T(8,128)(2,1)} collective-permute-done((bf16[128,2048]{1,0:T(8,128)(2,1)S(1)}, bf16[128,2048]{1,0:T(8,128)(2,1)}, u32[]{:S(2)}, u32[]{:S(2)}) %collective-permute-start.25) | collective-permute-done | bytes 524320 | tf_op jit(solution)/shard_map/ppermute | solution.py:37
  224.2 4.1 %fusion.1 = f32[1024,256]{0,1:T(8,128)S(1)} fusion(bf16[1024,2048]{1,0:T(8,128)(2,1)} %bitcast.85, bf16[128,2048]{1,0:T(8,128)(2,1)} %collective-permute-done.25, bf16[128,2048]{1,0:T(8,128)(2,1)} %copy-done.4, pred[]{:T(512)S(6)} %eq.83), kind=kOutput, calls=%fused_computation.3 | convolution fusion | flops 1078722560 | bytes 6291457 | tf_op jit(solution)/shard_map/dot_general | solution.py:198
  229.8 5.2 %fusion.2 = f32[1024,256]{0,1:T(8,128)} fusion(bf16[1024,2048]{1,0:T(8,128)(2,1)} %bitcast.86, bf16[128,2048]{1,0:T(8,128)(2,1)} %collective-permute-done.15, bf16[128,2048]{1,0:T(8,128)(2,1)} %maximum_select_fusion.6, pred[]{:T(512)S(6)} %eq.79), kind=kOutput, calls=%fused_computation.5 | convolution fusion | flops 1078722560 | bytes 6291457 | tf_op jit(solution)/shard_map/dot_general | solution.py:198
  235.0 1.6 copy.15
  238.1 5.1 %collective-permute-start.37 = (f32[4,64,256]{2,1,0:T(8,128)S(1)}, f32[4,64,256]{2,1,0:T(8,128)S(1)}, u32[]{:S(2)}, u32[]{:S(2)}) collective-permute-start(f32[4,64,256]{2,1,0:T(8,128)S(1)} %dynamic-slice_bitcast_fusion.3), channel_id=1, source_target_pairs={{0,2},{1,3},{2,0},{3,1},{4,6},{5,7},{6,4},{7,5},{8,10},{9,11},{10,... | collective-permute-start | bytes 786440 | tf_op jit(solution)/shard_map/ppermute | solution.py:52
  244.6 2.1 collective-permute-start.17
  246.7 3.7 %collective-permute-done.37 = f32[4,64,256]{2,1,0:T(8,128)S(1)} collective-permute-done((f32[4,64,256]{2,1,0:T(8,128)S(1)}, f32[4,64,256]{2,1,0:T(8,128)S(1)}, u32[]{:S(2)}, u32[]{:S(2)}) %collective-permute-start.37) | collective-permute-done | bytes 262176 | tf_op jit(solution)/shard_map/ppermute | solution.py:52
  250.4 11.0 %collective-permute-start.38 = (f32[2,64,256]{2,1,0:T(8,128)S(1)}, f32[2,64,256]{2,1,0:T(8,128)S(1)}, u32[]{:S(2)}, u32[]{:S(2)}) collective-permute-start(f32[2,64,256]{2,1,0:T(8,128)S(1)} %dynamic-slice_bitcast_fusion.6), channel_id=1, source_target_pairs={{0,4},{1,5},{2,6},{3,7},{4,0},{5,1},{6,2},{7,3},{8,12},{9,13},{10,... | collective-permute-start | bytes 393224 | tf_op jit(solution)/shard_map/ppermute | solution.py:52
  261.5 5.5 %collective-permute-start.28 = (f32[2,64,256]{2,1,0:T(8,128)S(1)}, f32[2,64,256]{2,1,0:T(8,128)S(1)}, u32[]{:S(2)}, u32[]{:S(2)}) collective-permute-start(f32[2,64,256]{2,1,0:T(8,128)S(1)} %dynamic-slice_bitcast_fusion.7), channel_id=1, source_target_pairs={{0,4},{1,5},{2,6},{3,7},{4,0},{5,1},{6,2},{7,3},{8,12},{9,13},{10,... | collective-permute-start | bytes 393224 | tf_op jit(solution)/shard_map/ppermute | solution.py:52
  267.1 5.5 %collective-permute-start.18 = (f32[2,64,256]{2,1,0:T(8,128)S(1)}, f32[2,64,256]{2,1,0:T(8,128)S(1)}, u32[]{:S(2)}, u32[]{:S(2)}) collective-permute-start(f32[2,64,256]{2,1,0:T(8,128)S(1)} %dynamic-slice_bitcast_fusion.8), channel_id=1, source_target_pairs={{0,4},{1,5},{2,6},{3,7},{4,0},{5,1},{6,2},{7,3},{8,12},{9,13},{10,... | collective-permute-start | bytes 393224 | tf_op jit(solution)/shard_map/ppermute | solution.py:52
  272.7 2.7 collective-permute-done.38
  275.5 2.7 collective-permute-done.28
  280.1 1.9 collective-permute-start.19
  282.0 2.7 collective-permute-done.29
  (119 shorter events, 26.0 us)
Async XLA Ops:
  1.4 31.7 %collective-permute-start.1 = (f32[4,256]{1,0:T(4,128)S(1)}, f32[4,256]{1,0:T(4,128)S(1)}, u32[]{:S(2)}, u32[]{:S(2)}) collective-permute-start(f32[4,256]{1,0:T(4,128)S(1)} %get-tuple-element.37), channel_id=1, source_target_pairs={{1,0},{2,1},{3,2},{4,3},{5,4},{6,5},{7,6},{8,7},{9,8},{10,9},{11,1... | collective-permute-start | bytes 12296 | tf_op jit(solution)/shard_map/ppermute | solution.py:64
  2.7 16.1 %copy-start.5 = (s32[8]{0:T(128)S(1)}, s32[8]{0:T(128)}, u32[]{:S(2)}) copy-start(s32[8]{0:T(128)} %param.7) | copy-start | bytes 100
  2.8 31.7 %collective-permute-start = (f32[4,256]{1,0:T(4,128)S(1)}, f32[4,256]{1,0:T(4,128)S(1)}, u32[]{:S(2)}, u32[]{:S(2)}) collective-permute-start(f32[4,256]{1,0:T(4,128)S(1)} %get-tuple-element.36), channel_id=1, source_target_pairs={{0,1},{1,2},{2,3},{3,4},{4,5},{5,6},{6,7},{7,8},{8,9},{9,10},{10,1... | collective-permute-start | bytes 12296 | tf_op jit(solution)/shard_map/ppermute | solution.py:63
  11.7 85.7 %collective-permute-start.5 = (bf16[256,4,256]{2,1,0:T(4,128)(2,1)S(1)}, bf16[256,4,256]{2,1,0:T(4,128)(2,1)}, u32[]{:S(2)}, u32[]{:S(2)}) collective-permute-start(bf16[256,4,256]{2,1,0:T(4,128)(2,1)S(1)} %get-tuple-element.20), channel_id=1, source_target_pairs={{1,0},{2,1},{3,2},{4,3},{5,4},{6,5},{7,6},{8,7},{9,8},{10,9},{11,1... | collective-permute-start | bytes 1572872 | tf_op jit(solution)/shard_map/ppermute | solution.py:64
  13.0 84.4 %collective-permute-start.4 = (bf16[256,4,256]{2,1,0:T(4,128)(2,1)S(1)}, bf16[256,4,256]{2,1,0:T(4,128)(2,1)}, u32[]{:S(2)}, u32[]{:S(2)}) collective-permute-start(bf16[256,4,256]{2,1,0:T(4,128)(2,1)S(1)} %get-tuple-element.21), channel_id=1, source_target_pairs={{0,1},{1,2},{2,3},{3,4},{4,5},{5,6},{6,7},{7,8},{8,9},{9,10},{10,1... | collective-permute-start | bytes 1572872 | tf_op jit(solution)/shard_map/ppermute | solution.py:63
  17.5 53.4 %collective-permute-start.7 = (bf16[256,4,256]{2,1,0:T(4,128)(2,1)}, bf16[256,4,256]{2,1,0:T(4,128)(2,1)}, u32[]{:S(2)}, u32[]{:S(2)}) collective-permute-start(bf16[256,4,256]{2,1,0:T(4,128)(2,1)} %get-tuple-element.18), channel_id=1, source_target_pairs={{1,0},{2,1},{3,2},{4,3},{5,4},{6,5},{7,6},{8,7},{9,8},{10,9},{11,1... | collective-permute-start | bytes 1572872 | tf_op jit(solution)/shard_map/ppermute | solution.py:64
  33.2 5.5 %collective-permute-start.9 = (bf16[256,4,256]{2,1,0:T(4,128)(2,1)}, bf16[256,4,256]{2,1,0:T(4,128)(2,1)S(1)}, u32[]{:S(2)}, u32[]{:S(2)}) collective-permute-start(bf16[256,4,256]{2,1,0:T(4,128)(2,1)} %get-tuple-element.17), channel_id=1, source_target_pairs={{1,0},{2,1},{3,2},{4,3},{5,4},{6,5},{7,6},{8,7},{9,8},{10,9},{11,1... | collective-permute-start | bytes 1572872 | tf_op jit(solution)/shard_map/ppermute | solution.py:64
  34.5 13.8 %collective-permute-start.8 = (bf16[256,4,256]{2,1,0:T(4,128)(2,1)}, bf16[256,4,256]{2,1,0:T(4,128)(2,1)S(1)}, u32[]{:S(2)}, u32[]{:S(2)}) collective-permute-start(bf16[256,4,256]{2,1,0:T(4,128)(2,1)} %get-tuple-element.16), channel_id=1, source_target_pairs={{0,1},{1,2},{2,3},{3,4},{4,5},{5,6},{6,7},{7,8},{8,9},{9,10},{10,1... | collective-permute-start | bytes 1572872 | tf_op jit(solution)/shard_map/ppermute | solution.py:63
  38.7 36.1 %collective-permute-start.6 = (bf16[256,4,256]{2,1,0:T(4,128)(2,1)S(1)}, bf16[256,4,256]{2,1,0:T(4,128)(2,1)}, u32[]{:S(2)}, u32[]{:S(2)}) collective-permute-start(bf16[256,4,256]{2,1,0:T(4,128)(2,1)S(1)} %get-tuple-element.19), channel_id=1, source_target_pairs={{0,1},{1,2},{2,3},{3,4},{4,5},{5,6},{6,7},{7,8},{8,9},{9,10},{10,1... | collective-permute-start | bytes 1572872 | tf_op jit(solution)/shard_map/ppermute | solution.py:63
  48.2 2.8 copy-start.1
  48.3 79.3 %collective-permute-start.3 = (bf16[256,4,256]{2,1,0:T(4,128)(2,1)S(1)}, bf16[256,4,256]{2,1,0:T(4,128)(2,1)}, u32[]{:S(2)}, u32[]{:S(2)}) collective-permute-start(bf16[256,4,256]{2,1,0:T(4,128)(2,1)S(1)} %get-tuple-element.22), channel_id=1, source_target_pairs={{1,0},{2,1},{3,2},{4,3},{5,4},{6,5},{7,6},{8,7},{9,8},{10,9},{11,1... | collective-permute-start | bytes 1572872 | tf_op jit(solution)/shard_map/ppermute | solution.py:64
  70.9 56.6 %collective-permute-start.2 = (bf16[256,4,256]{2,1,0:T(4,128)(2,1)S(1)}, bf16[256,4,256]{2,1,0:T(4,128)(2,1)}, u32[]{:S(2)}, u32[]{:S(2)}) collective-permute-start(bf16[256,4,256]{2,1,0:T(4,128)(2,1)S(1)} %get-tuple-element.23), channel_id=1, source_target_pairs={{0,1},{1,2},{2,3},{3,4},{4,5},{5,6},{6,7},{7,8},{8,9},{9,10},{10,1... | collective-permute-start | bytes 1572872 | tf_op jit(solution)/shard_map/ppermute | solution.py:63
  120.0 3.1 %copy-start.3 = (bf16[256,8,256]{2,1,0:T(8,128)(2,1)S(1)}, bf16[256,8,256]{2,1,0:T(8,128)(2,1)}, u32[]{:S(2)}) copy-start(bf16[256,8,256]{2,1,0:T(8,128)(2,1)} %get-tuple-element.14) | copy-start | bytes 3145732
  121.5 28.7 %collective-permute-start.30 = (bf16[128,2048]{1,0:T(8,128)(2,1)S(1)}, bf16[128,2048]{1,0:T(8,128)(2,1)}, u32[]{:S(2)}, u32[]{:S(2)}) collective-permute-start(bf16[128,2048]{1,0:T(8,128)(2,1)S(1)} %bitcast.115), channel_id=1, source_target_pairs={{0,16},{16,0},{32,48},{48,32},{64,80},{80,64},{96,112},{112,96},{1... | collective-permute-start | bytes 1572872 | tf_op jit(solution)/shard_map/ppermute | solution.py:30
  123.2 1.6 copy-start.2
  124.4 31.1 %collective-permute-start.20 = (bf16[128,2048]{1,0:T(8,128)(2,1)}, bf16[128,2048]{1,0:T(8,128)(2,1)}, u32[]{:S(2)}, u32[]{:S(2)}) collective-permute-start(bf16[128,2048]{1,0:T(8,128)(2,1)} %bitcast.49), channel_id=1, source_target_pairs={{0,16},{16,0},{32,48},{48,32},{64,80},{80,64},{96,112},{112,96},{1... | collective-permute-start | bytes 1572872 | tf_op jit(solution)/shard_map/ppermute | solution.py:30
  125.9 32.9 %collective-permute-start.10 = (bf16[128,2048]{1,0:T(8,128)(2,1)}, bf16[128,2048]{1,0:T(8,128)(2,1)}, u32[]{:S(2)}, u32[]{:S(2)}) collective-permute-start(bf16[128,2048]{1,0:T(8,128)(2,1)} %bitcast.43), channel_id=1, source_target_pairs={{0,16},{16,0},{32,48},{48,32},{64,80},{80,64},{96,112},{112,96},{1... | collective-permute-start | bytes 1572872 | tf_op jit(solution)/shard_map/ppermute | solution.py:30
  151.3 16.9 %collective-permute-start.31 = (bf16[128,2048]{1,0:T(8,128)(2,1)S(1)}, bf16[128,2048]{1,0:T(8,128)(2,1)S(1)}, u32[]{:S(2)}, u32[]{:S(2)}) collective-permute-start(bf16[128,2048]{1,0:T(8,128)(2,1)S(1)} %broadcast_select_fusion), channel_id=1, source_target_pairs={{0,32},{16,48},{32,64},{48,80},{64,96},{80,112},{96,0},{112,16},{1... | collective-permute-start | bytes 1572872 | tf_op jit(solution)/shard_map/ppermute | solution.py:28
  153.3 17.0 %collective-permute-start.32 = (bf16[128,2048]{1,0:T(8,128)(2,1)S(1)}, bf16[128,2048]{1,0:T(8,128)(2,1)S(1)}, u32[]{:S(2)}, u32[]{:S(2)}) collective-permute-start(bf16[128,2048]{1,0:T(8,128)(2,1)S(1)} %broadcast_select_fusion), channel_id=1, source_target_pairs={{0,96},{16,112},{32,0},{48,16},{64,32},{80,48},{96,64},{112,80},{1... | collective-permute-start | bytes 1572872 | tf_op jit(solution)/shard_map/ppermute | solution.py:28
  155.6 23.9 %collective-permute-start.21 = (bf16[128,2048]{1,0:T(8,128)(2,1)S(1)}, bf16[128,2048]{1,0:T(8,128)(2,1)S(1)}, u32[]{:S(2)}, u32[]{:S(2)}) collective-permute-start(bf16[128,2048]{1,0:T(8,128)(2,1)S(1)} %broadcast_select_fusion.1), channel_id=1, source_target_pairs={{0,32},{16,48},{32,64},{48,80},{64,96},{80,112},{96,0},{112,16},{1... | collective-permute-start | bytes 1572872 | tf_op jit(solution)/shard_map/ppermute | solution.py:28
  155.7 23.8 %collective-permute-start.22 = (bf16[128,2048]{1,0:T(8,128)(2,1)S(1)}, bf16[128,2048]{1,0:T(8,128)(2,1)S(1)}, u32[]{:S(2)}, u32[]{:S(2)}) collective-permute-start(bf16[128,2048]{1,0:T(8,128)(2,1)S(1)} %broadcast_select_fusion.1), channel_id=1, source_target_pairs={{0,96},{16,112},{32,0},{48,16},{64,32},{80,48},{96,64},{112,80},{1... | collective-permute-start | bytes 1572872 | tf_op jit(solution)/shard_map/ppermute | solution.py:28
  160.0 30.7 %collective-permute-start.11 = (bf16[128,2048]{1,0:T(8,128)(2,1)S(1)}, bf16[128,2048]{1,0:T(8,128)(2,1)S(1)}, u32[]{:S(2)}, u32[]{:S(2)}) collective-permute-start(bf16[128,2048]{1,0:T(8,128)(2,1)S(1)} %broadcast_select_fusion.2), channel_id=1, source_target_pairs={{0,32},{16,48},{32,64},{48,80},{64,96},{80,112},{96,0},{112,16},{1... | collective-permute-start | bytes 1572872 | tf_op jit(solution)/shard_map/ppermute | solution.py:28
  168.3 22.5 %collective-permute-start.12 = (bf16[128,2048]{1,0:T(8,128)(2,1)S(1)}, bf16[128,2048]{1,0:T(8,128)(2,1)S(1)}, u32[]{:S(2)}, u32[]{:S(2)}) collective-permute-start(bf16[128,2048]{1,0:T(8,128)(2,1)S(1)} %broadcast_select_fusion.2), channel_id=1, source_target_pairs={{0,96},{16,112},{32,0},{48,16},{64,32},{80,48},{96,64},{112,80},{1... | collective-permute-start | bytes 1572872 | tf_op jit(solution)/shard_map/ppermute | solution.py:28
  170.4 25.8 %collective-permute-start.34 = (bf16[64,2048]{1,0:T(8,128)(2,1)S(1)}, bf16[64,2048]{1,0:T(8,128)(2,1)S(1)}, u32[]{:S(2)}, u32[]{:S(2)}) collective-permute-start(bf16[64,2048]{1,0:T(8,128)(2,1)S(1)} %get-tuple-element.35), channel_id=1, source_target_pairs={{0,96},{16,112},{32,0},{48,16},{64,32},{80,48},{96,64},{112,80},{1... | collective-permute-start | bytes 786440 | tf_op jit(solution)/shard_map/ppermute | solution.py:28
  179.5 18.7 %collective-permute-start.33 = (bf16[64,2048]{1,0:T(8,128)(2,1)S(1)}, bf16[64,2048]{1,0:T(8,128)(2,1)S(1)}, u32[]{:S(2)}, u32[]{:S(2)}) collective-permute-start(bf16[64,2048]{1,0:T(8,128)(2,1)S(1)} %get-tuple-element.34), channel_id=1, source_target_pairs={{0,32},{16,48},{32,64},{48,80},{64,96},{80,112},{96,0},{112,16},{1... | collective-permute-start | bytes 786440 | tf_op jit(solution)/shard_map/ppermute | solution.py:28
  179.6 22.2 %collective-permute-start.24 = (bf16[64,2048]{1,0:T(8,128)(2,1)S(1)}, bf16[64,2048]{1,0:T(8,128)(2,1)S(1)}, u32[]{:S(2)}, u32[]{:S(2)}) collective-permute-start(bf16[64,2048]{1,0:T(8,128)(2,1)S(1)} %get-tuple-element.33), channel_id=1, source_target_pairs={{0,96},{16,112},{32,0},{48,16},{64,32},{80,48},{96,64},{112,80},{1... | collective-permute-start | bytes 786440 | tf_op jit(solution)/shard_map/ppermute | solution.py:28
  190.7 11.2 %collective-permute-start.23 = (bf16[64,2048]{1,0:T(8,128)(2,1)S(1)}, bf16[64,2048]{1,0:T(8,128)(2,1)S(1)}, u32[]{:S(2)}, u32[]{:S(2)}) collective-permute-start(bf16[64,2048]{1,0:T(8,128)(2,1)S(1)} %get-tuple-element.32), channel_id=1, source_target_pairs={{0,32},{16,48},{32,64},{48,80},{64,96},{80,112},{96,0},{112,16},{1... | collective-permute-start | bytes 786440 | tf_op jit(solution)/shard_map/ppermute | solution.py:28
  190.9 14.4 %collective-permute-start.14 = (bf16[64,2048]{1,0:T(8,128)(2,1)S(1)}, bf16[64,2048]{1,0:T(8,128)(2,1)S(1)}, u32[]{:S(2)}, u32[]{:S(2)}) collective-permute-start(bf16[64,2048]{1,0:T(8,128)(2,1)S(1)} %get-tuple-element.31), channel_id=1, source_target_pairs={{0,96},{16,112},{32,0},{48,16},{64,32},{80,48},{96,64},{112,80},{1... | collective-permute-start | bytes 786440 | tf_op jit(solution)/shard_map/ppermute | solution.py:28
  196.3 17.0 %copy-start = (bf16[128,8,8,256]{3,1,2,0:T(8,128)(2,1)S(1)}, bf16[128,8,8,256]{3,1,2,0:T(8,128)(2,1)}, u32[]{:S(2)}) copy-start(bf16[128,8,8,256]{3,1,2,0:T(8,128)(2,1)} %copy.20) | copy-start | bytes 12582916
  196.3 9.5 %collective-permute-start.13 = (bf16[64,2048]{1,0:T(8,128)(2,1)S(1)}, bf16[64,2048]{1,0:T(8,128)(2,1)S(1)}, u32[]{:S(2)}, u32[]{:S(2)}) collective-permute-start(bf16[64,2048]{1,0:T(8,128)(2,1)S(1)} %get-tuple-element.30), channel_id=1, source_target_pairs={{0,32},{16,48},{32,64},{48,80},{64,96},{80,112},{96,0},{112,16},{1... | collective-permute-start | bytes 786440 | tf_op jit(solution)/shard_map/ppermute | solution.py:28
  198.3 14.9 %collective-permute-start.35 = (bf16[128,2048]{1,0:T(8,128)(2,1)S(1)}, bf16[128,2048]{1,0:T(8,128)(2,1)S(1)}, u32[]{:S(2)}, u32[]{:S(2)}) collective-permute-start(bf16[128,2048]{1,0:T(8,128)(2,1)S(1)} %maximum_select_fusion.8), channel_id=1, source_target_pairs={{0,16},{16,0},{32,48},{48,32},{64,80},{80,64},{96,112},{112,96},{1... | collective-permute-start | bytes 1572872 | tf_op jit(solution)/shard_map/ppermute | solution.py:37
  202.1 12.5 %copy-start.4 = (bf16[128,2048]{1,0:T(8,128)(2,1)}, bf16[128,2048]{1,0:T(8,128)(2,1)S(1)}, u32[]{:S(2)}) copy-start(bf16[128,2048]{1,0:T(8,128)(2,1)S(1)} %maximum_select_fusion.7) | copy-start | bytes 1572868
  202.1 22.1 %collective-permute-start.25 = (bf16[128,2048]{1,0:T(8,128)(2,1)S(1)}, bf16[128,2048]{1,0:T(8,128)(2,1)}, u32[]{:S(2)}, u32[]{:S(2)}) collective-permute-start(bf16[128,2048]{1,0:T(8,128)(2,1)S(1)} %maximum_select_fusion.7), channel_id=1, source_target_pairs={{0,16},{16,0},{32,48},{48,32},{64,80},{80,64},{96,112},{112,96},{1... | collective-permute-start | bytes 1572872 | tf_op jit(solution)/shard_map/ppermute | solution.py:37
  206.7 23.1 %collective-permute-start.15 = (bf16[128,2048]{1,0:T(8,128)(2,1)}, bf16[128,2048]{1,0:T(8,128)(2,1)}, u32[]{:S(2)}, u32[]{:S(2)}) collective-permute-start(bf16[128,2048]{1,0:T(8,128)(2,1)} %maximum_select_fusion.6), channel_id=1, source_target_pairs={{0,16},{16,0},{32,48},{48,32},{64,80},{80,64},{96,112},{112,96},{1... | collective-permute-start | bytes 1572872 | tf_op jit(solution)/shard_map/ppermute | solution.py:37
  215.8 21.1 %collective-permute-start.36 = (f32[8,64,256]{2,1,0:T(8,128)}, f32[8,64,256]{2,1,0:T(8,128)}, u32[]{:S(2)}, u32[]{:S(2)}) collective-permute-start(f32[8,64,256]{2,1,0:T(8,128)} %dynamic-slice_bitcast_fusion), channel_id=1, source_target_pairs={{0,1},{1,0},{2,3},{3,2},{4,5},{5,4},{6,7},{7,6},{8,9},{9,8},{10,11... | collective-permute-start | bytes 1572872 | tf_op jit(solution)/shard_map/ppermute | solution.py:52
  229.5 13.7 %collective-permute-start.26 = (f32[8,64,256]{2,1,0:T(8,128)}, f32[8,64,256]{2,1,0:T(8,128)}, u32[]{:S(2)}, u32[]{:S(2)}) collective-permute-start(f32[8,64,256]{2,1,0:T(8,128)} %dynamic-slice_bitcast_fusion.1), channel_id=1, source_target_pairs={{0,1},{1,0},{2,3},{3,2},{4,5},{5,4},{6,7},{7,6},{8,9},{9,8},{10,11... | collective-permute-start | bytes 1572872 | tf_op jit(solution)/shard_map/ppermute | solution.py:52
  236.6 7.8 %collective-permute-start.16 = (f32[8,64,256]{2,1,0:T(8,128)S(1)}, f32[8,64,256]{2,1,0:T(8,128)S(1)}, u32[]{:S(2)}, u32[]{:S(2)}) collective-permute-start(f32[8,64,256]{2,1,0:T(8,128)S(1)} %dynamic-slice_bitcast_fusion.2), channel_id=1, source_target_pairs={{0,1},{1,0},{2,3},{3,2},{4,5},{5,4},{6,7},{7,6},{8,9},{9,8},{10,11... | collective-permute-start | bytes 1572872 | tf_op jit(solution)/shard_map/ppermute | solution.py:52
  238.1 12.3 %collective-permute-start.37 = (f32[4,64,256]{2,1,0:T(8,128)S(1)}, f32[4,64,256]{2,1,0:T(8,128)S(1)}, u32[]{:S(2)}, u32[]{:S(2)}) collective-permute-start(f32[4,64,256]{2,1,0:T(8,128)S(1)} %dynamic-slice_bitcast_fusion.3), channel_id=1, source_target_pairs={{0,2},{1,3},{2,0},{3,1},{4,6},{5,7},{6,4},{7,5},{8,10},{9,11},{10,... | collective-permute-start | bytes 786440 | tf_op jit(solution)/shard_map/ppermute | solution.py:52
  244.4 17.1 %collective-permute-start.27 = (f32[4,64,256]{2,1,0:T(8,128)S(1)}, f32[4,64,256]{2,1,0:T(8,128)S(1)}, u32[]{:S(2)}, u32[]{:S(2)}) collective-permute-start(f32[4,64,256]{2,1,0:T(8,128)S(1)} %dynamic-slice_bitcast_fusion.4), channel_id=1, source_target_pairs={{0,2},{1,3},{2,0},{3,1},{4,6},{5,7},{6,4},{7,5},{8,10},{9,11},{10,... | collective-permute-start | bytes 786440 | tf_op jit(solution)/shard_map/ppermute | solution.py:52
  244.6 22.5 %collective-permute-start.17 = (f32[4,64,256]{2,1,0:T(8,128)S(1)}, f32[4,64,256]{2,1,0:T(8,128)S(1)}, u32[]{:S(2)}, u32[]{:S(2)}) collective-permute-start(f32[4,64,256]{2,1,0:T(8,128)S(1)} %dynamic-slice_bitcast_fusion.5), channel_id=1, source_target_pairs={{0,2},{1,3},{2,0},{3,1},{4,6},{5,7},{6,4},{7,5},{8,10},{9,11},{10,... | collective-permute-start | bytes 786440 | tf_op jit(solution)/shard_map/ppermute | solution.py:52
  250.4 24.9 %collective-permute-start.38 = (f32[2,64,256]{2,1,0:T(8,128)S(1)}, f32[2,64,256]{2,1,0:T(8,128)S(1)}, u32[]{:S(2)}, u32[]{:S(2)}) collective-permute-start(f32[2,64,256]{2,1,0:T(8,128)S(1)} %dynamic-slice_bitcast_fusion.6), channel_id=1, source_target_pairs={{0,4},{1,5},{2,6},{3,7},{4,0},{5,1},{6,2},{7,3},{8,12},{9,13},{10,... | collective-permute-start | bytes 393224 | tf_op jit(solution)/shard_map/ppermute | solution.py:52
  261.5 16.7 %collective-permute-start.28 = (f32[2,64,256]{2,1,0:T(8,128)S(1)}, f32[2,64,256]{2,1,0:T(8,128)S(1)}, u32[]{:S(2)}, u32[]{:S(2)}) collective-permute-start(f32[2,64,256]{2,1,0:T(8,128)S(1)} %dynamic-slice_bitcast_fusion.7), channel_id=1, source_target_pairs={{0,4},{1,5},{2,6},{3,7},{4,0},{5,1},{6,2},{7,3},{8,12},{9,13},{10,... | collective-permute-start | bytes 393224 | tf_op jit(solution)/shard_map/ppermute | solution.py:52
  267.1 12.9 %collective-permute-start.18 = (f32[2,64,256]{2,1,0:T(8,128)S(1)}, f32[2,64,256]{2,1,0:T(8,128)S(1)}, u32[]{:S(2)}, u32[]{:S(2)}) collective-permute-start(f32[2,64,256]{2,1,0:T(8,128)S(1)} %dynamic-slice_bitcast_fusion.8), channel_id=1, source_target_pairs={{0,4},{1,5},{2,6},{3,7},{4,0},{5,1},{6,2},{7,3},{8,12},{9,13},{10,... | collective-permute-start | bytes 393224 | tf_op jit(solution)/shard_map/ppermute | solution.py:52
  275.4 6.5 %collective-permute-start.39 = (f32[1,64,256]{2,1,0:T(8,128)S(1)}, f32[1,64,256]{2,1,0:T(8,128)S(1)}, u32[]{:S(2)}, u32[]{:S(2)}) collective-permute-start(f32[1,64,256]{2,1,0:T(8,128)S(1)} %constant_dynamic-slice_fusion), channel_id=1, source_target_pairs={{0,8},{1,9},{2,10},{3,11},{4,12},{5,13},{6,14},{7,15},{8,0},{9,1},... | collective-permute-start | bytes 196616 | tf_op jit(solution)/shard_map/ppermute | solution.py:52
  278.2 6.5 %collective-permute-start.29 = (f32[1,64,256]{2,1,0:T(8,128)S(1)}, f32[1,64,256]{2,1,0:T(8,128)S(1)}, u32[]{:S(2)}, u32[]{:S(2)}) collective-permute-start(f32[1,64,256]{2,1,0:T(8,128)S(1)} %constant_dynamic-slice_fusion.1), channel_id=1, source_target_pairs={{0,8},{1,9},{2,10},{3,11},{4,12},{5,13},{6,14},{7,15},{8,0},{9,1},... | collective-permute-start | bytes 196616 | tf_op jit(solution)/shard_map/ppermute | solution.py:52
  280.1 5.8 %collective-permute-start.19 = (f32[1,64,256]{2,1,0:T(8,128)S(1)}, f32[1,64,256]{2,1,0:T(8,128)S(1)}, u32[]{:S(2)}, u32[]{:S(2)}) collective-permute-start(f32[1,64,256]{2,1,0:T(8,128)S(1)} %constant_dynamic-slice_fusion.2), channel_id=1, source_target_pairs={{0,8},{1,9},{2,10},{3,11},{4,12},{5,13},{6,14},{7,15},{8,0},{9,1},... | collective-permute-start | bytes 196616 | tf_op jit(solution)/shard_map/ppermute | solution.py:52

commit v10 on v8

--- a/solution.py
+++ b/solution.py
@@ -176,8 +176,10 @@
             )
             / cells
         )
-        partials.append(reduce_scatter_slab(term, "slab"))
-    gram = jnp.stack(partials, axis=1)
+        partials.append(term)
+    size = lax.axis_size("slab")
+    blocks = jnp.stack(partials, axis=1).reshape(size, rows // size, PANELS, PANEL)
+    gram = jnp.sum(lax.all_to_all(blocks, "slab", 0, 0, tiled=True), axis=0)
     return (field, gram)
 
 

time: 262 us -> 274 us (1.046)
  blocking collectives: 0 us -> 96.8 us
  starting transfers between devices: 108 us -> 36.4 us
  waiting for transfers between devices: 32.4 us -> 21.4 us
    all_to_all x0 -> x1, blocking collectives: none -> 96.8 us  [body(): gram = jnp.sum(lax.all_to_all(blocks, 'slab', 0, 0, tiled=True), axis=0)]
    ppermute x12 -> x0, starting transfers between devices: 71.8 us -> none  [reduce_scatter_slab(): part = keep + lax.ppermute(send, axis, [(i, i ^ bit) for i in range(size)])]
    ppermute x12 -> x0, waiting for transfers between devices: 12.9 us -> none  [reduce_scatter_slab(): part = keep + lax.ppermute(send, axis, [(i, i ^ bit) for i in range(size)])]
  transfers between devices with their start and end apart: 34 -> 22, of which waited for: 15 -> 11; matrix products, arithmetic and copies ran while one was open for 10% -> 6% of each run, Pallas kernels for 0% -> 0%
where the time goes in v10:
time: 274 us; the launch traced here: 273 us
  blocking collectives  96.8 us (35%)
  Pallas kernels  72.1 us (26%)
  starting transfers between devices  36.4 us (13%)
  waiting for transfers between devices  21.4 us (8%)
  local copies, waits for them, and re-layouts  15.4 us (6%)
  other arithmetic  11.2 us (4%)
  matrix products  10.5 us (4%)
  between operations  8.81 us (3%)
    all_to_all x1, blocking collectives, body(): gram = jnp.sum(lax.all_to_all(blocks, 'slab', 0, 0, tiled=True), axis=0)  96.8 us
    pallas_call x1, Pallas kernels, smooth(): pl.pallas_call(kernel, grid=(rows // block,), in_specs=[pl.BlockSpec(coef...  72.1 us
    ppermute x12, starting transfers between devices, shift(): return lax.ppermute(v, axis, [(i, (i + step) % size) for i in range(size)])  18.4 us
    ppermute x12, waiting for transfers between devices, shift(): return lax.ppermute(v, axis, [(i, (i + step) % size) for i in range(size)])  13.2 us
    dot_general x3, matrix products, body(): lax.dot_general(flat, received, (((1,), (1,)), ((), ())), preferred_eleme...  10.5 us
    unnamed x19, local copies, waits for them, and re-layouts  7.13 us
    ppermute x2, starting transfers between devices, halo_of(): below = lax.ppermute(top, axis, up)  6.13 us
    ppermute x3, starting transfers between devices, broadcast_dp(): other = lax.ppermute(val, axis, [(i, i ^ 1) for i in range(size)])  5.55 us
  transfers between devices with their start and end apart: 22, of which 11 were waited for; matrix products, arithmetic and copies ran while one was open for 6% of the time, Pallas kernels for 0%

profile of v10, /device:TPU:0, one launch (start us, length us, event | category | flops | bytes accessed | tf_op | source)
XLA Modules:
  0.0 272.8 jit_solution(3742537238317981190)
XLA Ops:
  0.6 4.8 %fusion.26 = (bf16[1024,4,256]{2,1,0:T(4,128)(2,1)S(1)}, bf16[1024,4,256]{2,1,0:T(4,128)(2,1)S(1)}) fusion(bf16[1024,8,256]{2,1,0:T(8,128)(2,1)} %a_ref.1), kind=kLoop, calls=%fused_computation.57 | loop fusion | bytes 8388608 | tf_op jit(solution)/shard_map/slice | solution.py:61
  5.5 1.4 collective-permute-start.2
  6.9 1.3 collective-permute-start.3
  8.3 4.7 %collective-permute-start = (f32[4,256]{1,0:T(4,128)S(1)}, f32[4,256]{1,0:T(4,128)S(1)}, u32[]{:S(2)}, u32[]{:S(2)}) collective-permute-start(f32[4,256]{1,0:T(4,128)S(1)} %get-tuple-element.16), channel_id=1, source_target_pairs={{0,1},{1,2},{2,3},{3,4},{4,5},{5,6},{6,7},{7,8},{8,9},{9,10},{10,1... | collective-permute-start | bytes 12296 | tf_op jit(solution)/shard_map/ppermute | solution.py:63
  13.0 1.3 collective-permute-start.1
  14.4 2.9 %collective-permute-done.1 = f32[4,256]{1,0:T(4,128)S(1)} collective-permute-done((f32[4,256]{1,0:T(4,128)S(1)}, f32[4,256]{1,0:T(4,128)S(1)}, u32[]{:S(2)}, u32[]{:S(2)}) %collective-permute-start.1) | collective-permute-done | bytes 4128 | tf_op jit(solution)/shard_map/ppermute | solution.py:64
  17.5 3.4 %pad_maximum_fusion.h_ref = bf16[1024,8,256]{2,1,0:T(8,128)(2,1)} fusion(bf16[1024,4,256]{2,1,0:T(4,128)(2,1)S(1)} %collective-permute-done.3, bf16[1024,4,256]{2,1,0:T(4,128)(2,1)S(1)} %collective-permute-done.2), kind=kLoop, calls=%fused_computation | loop fusion | flops 8388608 | bytes 8388608 | tf_op jit(solution)/shard_map/concatenate | solution.py:65
  20.9 72.1 %shard_map.59 = f32[1024,8,256]{2,1,0:T(8,128)} custom-call(f32[6,16,256]{2,1,0:T(8,128)} %copy-done.2, bf16[1024,8,256]{2,1,0:T(8,128)(2,1)} %a_ref.1, bf16[1024,8,256]{2,1,0:T(8,128)(2,1)} %pad_maximum_fusion.h_ref), custom_call_target="tpu_custom_call" | custom-call | tf_op jit(solution)/shard_map/pallas_call | solution.py:144
  93.0 3.8 %convert.5 = bf16[1024,8,256]{2,1,0:T(8,128)(2,1)S(1)} convert(f32[1024,8,256]{2,1,0:T(8,128)} %shard_map.59) | non-fusion elementwise | flops 2097152 | bytes 12582912 | tf_op jit(solution)/shard_map/convert.2
  97.0 0.9 copy.18
  97.9 1.6 collective-permute-start.4
  99.6 0.5 collective-permute-start.10
  100.1 0.6 fusion.31
  108.5 5.6 %copy.19 = bf16[128,8,8,256]{3,1,2,0:T(8,128)(2,1)} copy(bf16[128,8,8,256]{3,2,1,0:T(8,128)(2,1)} %bitcast.36) | data formatting | bytes 8388608
  114.5 1.7 collective-permute-start.16
  116.3 1.1 broadcast_select_fusion.2
  117.4 2.0 collective-permute-start.5
  119.4 2.2 collective-permute-start.6
  121.7 3.2 %collective-permute-start.12 = (bf16[128,2048]{1,0:T(8,128)(2,1)S(1)}, bf16[128,2048]{1,0:T(8,128)(2,1)S(1)}, u32[]{:S(2)}, u32[]{:S(2)}) collective-permute-start(bf16[128,2048]{1,0:T(8,128)(2,1)S(1)} %broadcast_select_fusion.1), channel_id=1, source_target_pairs={{0,96},{16,112},{32,0},{48,16},{64,32},{80,48},{96,64},{112,80},{1... | collective-permute-start | bytes 1572872 | tf_op jit(solution)/shard_map/ppermute | solution.py:28
  124.9 2.6 collective-permute-done.16
  127.6 2.0 collective-permute-start.17
  129.6 2.2 collective-permute-start.18
  132.1 2.2 collective-permute-done.11
  134.3 2.0 collective-permute-start.8
  136.7 3.2 %collective-permute-done.17 = bf16[128,2048]{1,0:T(8,128)(2,1)S(1)} collective-permute-done((bf16[128,2048]{1,0:T(8,128)(2,1)S(1)}, bf16[128,2048]{1,0:T(8,128)(2,1)S(1)}, u32[]{:S(2)}, u32[]{:S(2)}) %collective-permute-start.17) | collective-permute-done | bytes 524320 | tf_op jit(solution)/shard_map/ppermute | solution.py:28
  139.9 2.0 collective-permute-start.14
  142.1 2.6 collective-permute-done.7
  144.7 2.3 collective-permute-start.20
  147.1 1.9 collective-permute-start.9
  149.0 1.3 collective-permute-done.13
  150.3 0.3 collective-permute-done.14
  150.7 1.9 collective-permute-start.15
  152.6 3.3 %collective-permute-done.19 = bf16[64,2048]{1,0:T(8,128)(2,1)S(1)} collective-permute-done((bf16[64,2048]{1,0:T(8,128)(2,1)S(1)}, bf16[64,2048]{1,0:T(8,128)(2,1)S(1)}, u32[]{:S(2)}, u32[]{:S(2)}) %collective-permute-start.19) | collective-permute-done | bytes 262176 | tf_op jit(solution)/shard_map/ppermute | solution.py:28
  155.9 0.3 collective-permute-done.20
  156.2 0.9 maximum_select_fusion.8
  157.1 1.8 collective-permute-start.21
  158.9 1.3 fusion.2
  160.2 0.3 copy.13
  160.6 1.5 collective-permute-done.15
  162.1 4.1 %fusion.1 = f32[1024,256]{0,1:T(8,128)S(1)} fusion(bf16[1024,2048]{1,0:T(8,128)(2,1)} %bitcast.37, bf16[128,2048]{1,0:T(8,128)(2,1)} %collective-permute-done.15, bf16[128,2048]{1,0:T(8,128)(2,1)} %copy-done.1, pred[]{:T(512)S(6)} %eq.71), kind=kOutput, calls=%fused_computation.5 | convolution fusion | flops 1078722560 | bytes 6291457 | tf_op jit(solution)/shard_map/dot_general | solution.py:174
  166.2 0.3 copy.14
  166.6 1.1 collective-permute-done.21
  167.7 5.1 %fusion = f32[1024,256]{0,1:T(8,128)} fusion(bf16[1024,2048]{1,0:T(8,128)(2,1)} %bitcast.38, bf16[128,2048]{1,0:T(8,128)(2,1)} %collective-permute-done.21, bf16[128,2048]{1,0:T(8,128)(2,1)} %maximum_select_fusion.8, pred[]{:T(512)S(6)} %eq.75), kind=kOutput, calls=%fused_computation.3 | convolution fusion | flops 1078722560 | bytes 6291457 | tf_op jit(solution)/shard_map/dot_general | solution.py:174
  172.9 1.6 copy.15
  174.4 0.4 pad_maximum_fusion.1
  174.8 0.3 copy.16
  175.1 96.8 %all_to_all.5 = f32[16,64,3,256]{3,1,2,0:T(8,128)S(1)} all-to-all(f32[16,64,3,256]{3,1,2,0:T(8,128)S(1)} %copy.16), channel_id=1, replica_groups=mesh['dp'=8,'slab'=16] {'slab'}, dimensions={0} | all-to-all | bytes 6291456 | tf_op jit(solution)/shard_map/all_to_all | solution.py:182
  271.9 0.9 reduce_sum.19
  (55 shorter events, 2.2 us)
Async XLA Ops:
  0.6 7.6 %copy-start.3 = (s32[8,256]{1,0:T(8,128)S(1)}, s32[8,256]{1,0:T(8,128)}, u32[]{:S(2)}) copy-start(s32[8,256]{1,0:T(8,128)} %param.5) | copy-start | bytes 24580
  0.6 7.6 %copy-start.5 = (f32[8]{0:T(128)S(1)}, f32[8]{0:T(128)}, u32[]{:S(2)}) copy-start(f32[8]{0:T(128)} %param.6) | copy-start | bytes 100
  5.5 12.0 %collective-permute-start.2 = (bf16[1024,4,256]{2,1,0:T(4,128)(2,1)S(1)}, bf16[1024,4,256]{2,1,0:T(4,128)(2,1)S(1)}, u32[]{:S(2)}, u32[]{:S(2)}) collective-permute-start(bf16[1024,4,256]{2,1,0:T(4,128)(2,1)S(1)} %get-tuple-element.8), channel_id=1, source_target_pairs={{0,1},{1,2},{2,3},{3,4},{4,5},{5,6},{6,7},{7,8},{8,9},{9,10},{10,1... | collective-permute-start | bytes 6291464 | tf_op jit(solution)/shard_map/ppermute | solution.py:63
  6.9 10.6 %collective-permute-start.3 = (bf16[1024,4,256]{2,1,0:T(4,128)(2,1)S(1)}, bf16[1024,4,256]{2,1,0:T(4,128)(2,1)S(1)}, u32[]{:S(2)}, u32[]{:S(2)}) collective-permute-start(bf16[1024,4,256]{2,1,0:T(4,128)(2,1)S(1)} %get-tuple-element.9), channel_id=1, source_target_pairs={{1,0},{2,1},{3,2},{4,3},{5,4},{6,5},{7,6},{8,7},{9,8},{10,9},{11,1... | collective-permute-start | bytes 6291464 | tf_op jit(solution)/shard_map/ppermute | solution.py:64
  8.3 6.1 %collective-permute-start = (f32[4,256]{1,0:T(4,128)S(1)}, f32[4,256]{1,0:T(4,128)S(1)}, u32[]{:S(2)}, u32[]{:S(2)}) collective-permute-start(f32[4,256]{1,0:T(4,128)S(1)} %get-tuple-element.16), channel_id=1, source_target_pairs={{0,1},{1,2},{2,3},{3,4},{4,5},{5,6},{6,7},{7,8},{8,9},{9,10},{10,1... | collective-permute-start | bytes 12296 | tf_op jit(solution)/shard_map/ppermute | solution.py:63
  13.0 4.3 %collective-permute-start.1 = (f32[4,256]{1,0:T(4,128)S(1)}, f32[4,256]{1,0:T(4,128)S(1)}, u32[]{:S(2)}, u32[]{:S(2)}) collective-permute-start(f32[4,256]{1,0:T(4,128)S(1)} %get-tuple-element.17), channel_id=1, source_target_pairs={{1,0},{2,1},{3,2},{4,3},{5,4},{6,5},{7,6},{8,7},{9,8},{10,9},{11,1... | collective-permute-start | bytes 12296 | tf_op jit(solution)/shard_map/ppermute | solution.py:64
  17.4 3.5 %copy-start.2 = (f32[6,16,256]{2,1,0:T(8,128)}, f32[6,16,256]{2,1,0:T(8,128)S(1)}, u32[]{:S(2)}) copy-start(f32[6,16,256]{2,1,0:T(8,128)S(1)} %select_dynamic-update-slice_fusion.coef_ref) | copy-start | bytes 294916
  96.8 3.4 %copy-start.4 = (s32[8]{0:T(128)S(1)}, s32[8]{0:T(128)}, u32[]{:S(2)}) copy-start(s32[8]{0:T(128)} %param.7) | copy-start | bytes 100
  97.9 18.4 %collective-permute-start.4 = (bf16[128,2048]{1,0:T(8,128)(2,1)}, bf16[128,2048]{1,0:T(8,128)(2,1)}, u32[]{:S(2)}, u32[]{:S(2)}) collective-permute-start(bf16[128,2048]{1,0:T(8,128)(2,1)} %bitcast.16), channel_id=1, source_target_pairs={{0,16},{16,0},{32,48},{48,32},{64,80},{80,64},{96,112},{112,96},{1... | collective-permute-start | bytes 1572872 | tf_op jit(solution)/shard_map/ppermute | solution.py:30
  99.6 22.0 %collective-permute-start.10 = (bf16[128,2048]{1,0:T(8,128)(2,1)S(1)}, bf16[128,2048]{1,0:T(8,128)(2,1)S(1)}, u32[]{:S(2)}, u32[]{:S(2)}) collective-permute-start(bf16[128,2048]{1,0:T(8,128)(2,1)S(1)} %bitcast.52), channel_id=1, source_target_pairs={{0,16},{16,0},{32,48},{48,32},{64,80},{80,64},{96,112},{112,96},{1... | collective-permute-start | bytes 1572872 | tf_op jit(solution)/shard_map/ppermute | solution.py:30
  114.5 13.1 %collective-permute-start.16 = (bf16[128,2048]{1,0:T(8,128)(2,1)S(1)}, bf16[128,2048]{1,0:T(8,128)(2,1)S(1)}, u32[]{:S(2)}, u32[]{:S(2)}) collective-permute-start(bf16[128,2048]{1,0:T(8,128)(2,1)S(1)} %bitcast.53), channel_id=1, source_target_pairs={{0,16},{16,0},{32,48},{48,32},{64,80},{80,64},{96,112},{112,96},{1... | collective-permute-start | bytes 1572872 | tf_op jit(solution)/shard_map/ppermute | solution.py:30
  117.4 12.3 %collective-permute-start.5 = (bf16[128,2048]{1,0:T(8,128)(2,1)S(1)}, bf16[128,2048]{1,0:T(8,128)(2,1)S(1)}, u32[]{:S(2)}, u32[]{:S(2)}) collective-permute-start(bf16[128,2048]{1,0:T(8,128)(2,1)S(1)} %broadcast_select_fusion.2), channel_id=1, source_target_pairs={{0,32},{16,48},{32,64},{48,80},{64,96},{80,112},{96,0},{112,16},{1... | collective-permute-start | bytes 1572872 | tf_op jit(solution)/shard_map/ppermute | solution.py:28
  119.4 12.5 %collective-permute-start.6 = (bf16[128,2048]{1,0:T(8,128)(2,1)S(1)}, bf16[128,2048]{1,0:T(8,128)(2,1)S(1)}, u32[]{:S(2)}, u32[]{:S(2)}) collective-permute-start(bf16[128,2048]{1,0:T(8,128)(2,1)S(1)} %broadcast_select_fusion.2), channel_id=1, source_target_pairs={{0,96},{16,112},{32,0},{48,16},{64,32},{80,48},{96,64},{112,80},{1... | collective-permute-start | bytes 1572872 | tf_op jit(solution)/shard_map/ppermute | solution.py:28
  121.6 12.6 %collective-permute-start.11 = (bf16[128,2048]{1,0:T(8,128)(2,1)S(1)}, bf16[128,2048]{1,0:T(8,128)(2,1)S(1)}, u32[]{:S(2)}, u32[]{:S(2)}) collective-permute-start(bf16[128,2048]{1,0:T(8,128)(2,1)S(1)} %broadcast_select_fusion.1), channel_id=1, source_target_pairs={{0,32},{16,48},{32,64},{48,80},{64,96},{80,112},{96,0},{112,16},{1... | collective-permute-start | bytes 1572872 | tf_op jit(solution)/shard_map/ppermute | solution.py:28
  121.7 14.6 %collective-permute-start.12 = (bf16[128,2048]{1,0:T(8,128)(2,1)S(1)}, bf16[128,2048]{1,0:T(8,128)(2,1)S(1)}, u32[]{:S(2)}, u32[]{:S(2)}) collective-permute-start(bf16[128,2048]{1,0:T(8,128)(2,1)S(1)} %broadcast_select_fusion.1), channel_id=1, source_target_pairs={{0,96},{16,112},{32,0},{48,16},{64,32},{80,48},{96,64},{112,80},{1... | collective-permute-start | bytes 1572872 | tf_op jit(solution)/shard_map/ppermute | solution.py:28
  127.6 12.2 %collective-permute-start.17 = (bf16[128,2048]{1,0:T(8,128)(2,1)S(1)}, bf16[128,2048]{1,0:T(8,128)(2,1)S(1)}, u32[]{:S(2)}, u32[]{:S(2)}) collective-permute-start(bf16[128,2048]{1,0:T(8,128)(2,1)S(1)} %broadcast_select_fusion), channel_id=1, source_target_pairs={{0,32},{16,48},{32,64},{48,80},{64,96},{80,112},{96,0},{112,16},{1... | collective-permute-start | bytes 1572872 | tf_op jit(solution)/shard_map/ppermute | solution.py:28
  129.6 12.3 %collective-permute-start.18 = (bf16[128,2048]{1,0:T(8,128)(2,1)S(1)}, bf16[128,2048]{1,0:T(8,128)(2,1)S(1)}, u32[]{:S(2)}, u32[]{:S(2)}) collective-permute-start(bf16[128,2048]{1,0:T(8,128)(2,1)S(1)} %broadcast_select_fusion), channel_id=1, source_target_pairs={{0,96},{16,112},{32,0},{48,16},{64,32},{80,48},{96,64},{112,80},{1... | collective-permute-start | bytes 1572872 | tf_op jit(solution)/shard_map/ppermute | solution.py:28
  132.0 12.7 %collective-permute-start.7 = (bf16[64,2048]{1,0:T(8,128)(2,1)S(1)}, bf16[64,2048]{1,0:T(8,128)(2,1)S(1)}, u32[]{:S(2)}, u32[]{:S(2)}) collective-permute-start(bf16[64,2048]{1,0:T(8,128)(2,1)S(1)} %get-tuple-element.10), channel_id=1, source_target_pairs={{0,32},{16,48},{32,64},{48,80},{64,96},{80,112},{96,0},{112,16},{1... | collective-permute-start | bytes 786440 | tf_op jit(solution)/shard_map/ppermute | solution.py:28
  134.3 12.7 %collective-permute-start.8 = (bf16[64,2048]{1,0:T(8,128)(2,1)S(1)}, bf16[64,2048]{1,0:T(8,128)(2,1)S(1)}, u32[]{:S(2)}, u32[]{:S(2)}) collective-permute-start(bf16[64,2048]{1,0:T(8,128)(2,1)S(1)} %get-tuple-element.11), channel_id=1, source_target_pairs={{0,96},{16,112},{32,0},{48,16},{64,32},{80,48},{96,64},{112,80},{1... | collective-permute-start | bytes 786440 | tf_op jit(solution)/shard_map/ppermute | solution.py:28
  136.4 13.9 %collective-permute-start.13 = (bf16[64,2048]{1,0:T(8,128)(2,1)S(1)}, bf16[64,2048]{1,0:T(8,128)(2,1)S(1)}, u32[]{:S(2)}, u32[]{:S(2)}) collective-permute-start(bf16[64,2048]{1,0:T(8,128)(2,1)S(1)} %get-tuple-element.12), channel_id=1, source_target_pairs={{0,32},{16,48},{32,64},{48,80},{64,96},{80,112},{96,0},{112,16},{1... | collective-permute-start | bytes 786440 | tf_op jit(solution)/shard_map/ppermute | solution.py:28
  139.9 10.7 %collective-permute-start.14 = (bf16[64,2048]{1,0:T(8,128)(2,1)S(1)}, bf16[64,2048]{1,0:T(8,128)(2,1)S(1)}, u32[]{:S(2)}, u32[]{:S(2)}) collective-permute-start(bf16[64,2048]{1,0:T(8,128)(2,1)S(1)} %get-tuple-element.13), channel_id=1, source_target_pairs={{0,96},{16,112},{32,0},{48,16},{64,32},{80,48},{96,64},{112,80},{1... | collective-permute-start | bytes 786440 | tf_op jit(solution)/shard_map/ppermute | solution.py:28
  142.0 17.0 %copy-start = (bf16[128,8,8,256]{3,1,2,0:T(8,128)(2,1)S(1)}, bf16[128,8,8,256]{3,1,2,0:T(8,128)(2,1)}, u32[]{:S(2)}) copy-start(bf16[128,8,8,256]{3,1,2,0:T(8,128)(2,1)} %copy.19) | copy-start | bytes 12582916
  142.0 13.9 %collective-permute-start.19 = (bf16[64,2048]{1,0:T(8,128)(2,1)S(1)}, bf16[64,2048]{1,0:T(8,128)(2,1)S(1)}, u32[]{:S(2)}, u32[]{:S(2)}) collective-permute-start(bf16[64,2048]{1,0:T(8,128)(2,1)S(1)} %get-tuple-element.14), channel_id=1, source_target_pairs={{0,32},{16,48},{32,64},{48,80},{64,96},{80,112},{96,0},{112,16},{1... | collective-permute-start | bytes 786440 | tf_op jit(solution)/shard_map/ppermute | solution.py:28
  144.7 11.5 %collective-permute-start.20 = (bf16[64,2048]{1,0:T(8,128)(2,1)S(1)}, bf16[64,2048]{1,0:T(8,128)(2,1)S(1)}, u32[]{:S(2)}, u32[]{:S(2)}) collective-permute-start(bf16[64,2048]{1,0:T(8,128)(2,1)S(1)} %get-tuple-element.15), channel_id=1, source_target_pairs={{0,96},{16,112},{32,0},{48,16},{64,32},{80,48},{96,64},{112,80},{1... | collective-permute-start | bytes 786440 | tf_op jit(solution)/shard_map/ppermute | solution.py:28
  147.1 11.8 %collective-permute-start.9 = (bf16[128,2048]{1,0:T(8,128)(2,1)S(1)}, bf16[128,2048]{1,0:T(8,128)(2,1)S(1)}, u32[]{:S(2)}, u32[]{:S(2)}) collective-permute-start(bf16[128,2048]{1,0:T(8,128)(2,1)S(1)} %maximum_select_fusion.6), channel_id=1, source_target_pairs={{0,16},{16,0},{32,48},{48,32},{64,80},{80,64},{96,112},{112,96},{1... | collective-permute-start | bytes 1572872 | tf_op jit(solution)/shard_map/ppermute | solution.py:37
  150.7 9.5 %copy-start.1 = (bf16[128,2048]{1,0:T(8,128)(2,1)}, bf16[128,2048]{1,0:T(8,128)(2,1)S(1)}, u32[]{:S(2)}) copy-start(bf16[128,2048]{1,0:T(8,128)(2,1)S(1)} %maximum_select_fusion.7) | copy-start | bytes 1572868
  150.7 11.4 %collective-permute-start.15 = (bf16[128,2048]{1,0:T(8,128)(2,1)S(1)}, bf16[128,2048]{1,0:T(8,128)(2,1)}, u32[]{:S(2)}, u32[]{:S(2)}) collective-permute-start(bf16[128,2048]{1,0:T(8,128)(2,1)S(1)} %maximum_select_fusion.7), channel_id=1, source_target_pairs={{0,16},{16,0},{32,48},{48,32},{64,80},{80,64},{96,112},{112,96},{1... | collective-permute-start | bytes 1572872 | tf_op jit(solution)/shard_map/ppermute | solution.py:37
  157.1 10.6 %collective-permute-start.21 = (bf16[128,2048]{1,0:T(8,128)(2,1)}, bf16[128,2048]{1,0:T(8,128)(2,1)}, u32[]{:S(2)}, u32[]{:S(2)}) collective-permute-start(bf16[128,2048]{1,0:T(8,128)(2,1)} %maximum_select_fusion.8), channel_id=1, source_target_pairs={{0,16},{16,0},{32,48},{48,32},{64,80},{80,64},{96,112},{112,96},{1... | collective-permute-start | bytes 1572872 | tf_op jit(solution)/shard_map/ppermute | solution.py:37

commit v11 on v8

--- a/solution.py
+++ b/solution.py
@@ -65,7 +65,7 @@
     return jnp.concatenate([below, above], axis=dim)
 
 
-def smooth_kernel(coef_ref, a_ref, h_ref, o_ref, *, sub):
+def smooth_kernel(coef_ref, a_ref, h_ref, o_ref, p_ref, *, sub):
     depth, lat = a_ref.shape[1], a_ref.shape[2]
     half = lat // 2
     shape = (sub, depth, half)
@@ -116,6 +116,7 @@
         for h in range(2):
             out = jnp.where(low_rows, pltpu.roll(x[0][h], HALO, 1), pltpu.roll(x[1][h], HALO, 1))
             o_ref[pl.ds(r, sub), :, h * half : (h + 1) * half] = out
+            p_ref[pl.ds(r, sub), :, h * half : (h + 1) * half] = out.astype(p_ref.dtype)
         return carry
 
     lax.fori_loop(0, a_ref.shape[0] // sub, body, 0)
@@ -149,8 +150,14 @@
             pl.BlockSpec((block, depth, lat), lambda i: (i, 0, 0)),
             pl.BlockSpec((block, depth, lat), lambda i: (i, 0, 0)),
         ],
-        out_specs=pl.BlockSpec((block, depth, lat), lambda i: (i, 0, 0)),
-        out_shape=jax.ShapeDtypeStruct((rows, depth, lat), jnp.float32),
+        out_specs=[
+            pl.BlockSpec((block, depth, lat), lambda i: (i, 0, 0)),
+            pl.BlockSpec((block, depth, lat), lambda i: (i, 0, 0)),
+        ],
+        out_shape=[
+            jax.ShapeDtypeStruct((rows, depth, lat), jnp.float32),
+            jax.ShapeDtypeStruct((rows, depth, lat), jnp.bfloat16),
+        ],
     )(coef, sensitivity, halo)
 
 
@@ -163,16 +170,15 @@
     halo = halo_of(sensitivity, "slab", 1)
     kappa_halo = halo_of(kappa, "slab", 0)
     kappa_col = jnp.concatenate([kappa_halo[:HALO], kappa, kappa_halo[HALO:]], axis=0)
-    field = smooth(sensitivity, halo, coefficients(kappa_col, lat))
+    field, rounded = smooth(sensitivity, halo, coefficients(kappa_col, lat))
     cells = depth * lat * lax.axis_size("slab")
-    flat = sensitivity.reshape(rows, depth * lat)
     partials = []
     for p in range(PANELS):
-        piece = field[p * PANEL : (p + 1) * PANEL].reshape(PANEL, depth * lat).astype(jnp.bfloat16)
+        piece = rounded[p * PANEL : (p + 1) * PANEL]
         received = broadcast_dp(piece, panel_owner[p], "dp")
         term = (
             lax.dot_general(
-                flat, received, (((1,), (1,)), ((), ())), preferred_element_type=jnp.float32
+                sensitivity, received, (((1, 2), (1, 2)), ((), ())), preferred_element_type=jnp.float32
             )
             / cells
         )

time: 262 us -> 269 us (1.027)
  waiting for transfers between devices: 32.4 us -> 53.1 us
  starting transfers between devices: 108 us -> 99.1 us
  local copies, waits for them, and re-layouts: 17.1 us -> 11 us
  other arithmetic: 12.1 us -> 17.4 us
  matrix products: 10.6 us -> 5.35 us
    ppermute x3, waiting for transfers between devices: 4.01 us -> 13.9 us  [broadcast_dp(): pair = lax.ppermute(piece[half:], axis, [(i, i ^ 1) for i in range(size)])]
    ppermute x12, waiting for transfers between devices: 12.5 us -> 21.8 us  [shift(): return lax.ppermute(v, axis, [(i, (i + step) % size) for i in range(size)])]
    ppermute x12, starting transfers between devices: 71.8 us -> 63.1 us  [reduce_scatter_slab(): part = keep + lax.ppermute(send, axis, [(i, i ^ bit) for i in range(size)])]
    unnamed x19 -> x14, local copies, waits for them, and re-layouts: 7.13 us -> 0.03 us
    dot_general x3, matrix products: 10.6 us -> 5.35 us  [body(): lax.dot_general(sensitivity, received, (((1, 2), (1, 2)), ((), ())), pref...]
    another operation x1 -> x0, other arithmetic: 3.79 us -> none
    ppermute x12, waiting for transfers between devices: 12.9 us -> 16.6 us  [reduce_scatter_slab(): part = keep + lax.ppermute(send, axis, [(i, i ^ bit) for i in range(size)])]
    ppermute x2, waiting for transfers between devices: 2.94 us -> 0.01 us  [halo_of(): above = lax.ppermute(bottom, axis, down)]
  transfers between devices with their start and end apart: 34 -> 34, of which waited for: 15 -> 16; matrix products, arithmetic and copies ran while one was open for 10% -> 8% of each run, Pallas kernels for 0% -> 0%
where the time goes in v11:
time: 269 us; the launch traced here: 268 us
  starting transfers between devices  99.1 us (37%)
  Pallas kernels  72.6 us (27%)
  waiting for transfers between devices  53.1 us (20%)
  other arithmetic  17.4 us (6%)
  local copies, waits for them, and re-layouts  11 us (4%)
  between operations  8.98 us (3%)
  matrix products  5.35 us (2%)
    pallas_call x1, Pallas kernels, smooth(): pl.pallas_call(kernel, grid=(rows // block,), in_specs=[pl.BlockSpec(coef...  72.6 us
    ppermute x12, starting transfers between devices, reduce_scatter_slab(): part = keep + lax.ppermute(send, axis, [(i, i ^ bit) for i in range(size)])  63.1 us
    ppermute x12, waiting for transfers between devices, shift(): return lax.ppermute(v, axis, [(i, (i + step) % size) for i in range(size)])  21.8 us
    ppermute x12, starting transfers between devices, shift(): return lax.ppermute(v, axis, [(i, (i + step) % size) for i in range(size)])  17.9 us
    ppermute x12, waiting for transfers between devices, reduce_scatter_slab(): part = keep + lax.ppermute(send, axis, [(i, i ^ bit) for i in range(size)])  16.6 us
    ppermute x3, waiting for transfers between devices, broadcast_dp(): pair = lax.ppermute(piece[half:], axis, [(i, i ^ 1) for i in range(size)])  13.9 us
    ppermute x2, starting transfers between devices, halo_of(): below = lax.ppermute(top, axis, up)  6.76 us
  transfers between devices with their start and end apart: 34, of which 16 were waited for; matrix products, arithmetic and copies ran while one was open for 8% of the time, Pallas kernels for 0%

profile of v11, /device:TPU:0, one launch (start us, length us, event | category | flops | bytes accessed | tf_op | source)
XLA Modules:
  0.0 267.6 jit_solution(13597462401084208021)
XLA Ops:
  0.6 4.8 %fusion.37 = (bf16[1024,4,256]{2,1,0:T(4,128)(2,1)S(1)}, bf16[1024,4,256]{2,1,0:T(4,128)(2,1)S(1)}) fusion(bf16[1024,8,256]{2,1,0:T(8,128)(2,1)} %a_ref.1), kind=kLoop, calls=%fused_computation.71 | loop fusion | bytes 8388608 | tf_op jit(solution)/shard_map/slice | solution.py:61
  5.5 1.3 collective-permute-start.3
  6.8 3.2 %collective-permute-start.2 = (bf16[1024,4,256]{2,1,0:T(4,128)(2,1)S(1)}, bf16[1024,4,256]{2,1,0:T(4,128)(2,1)S(1)}, u32[]{:S(2)}, u32[]{:S(2)}) collective-permute-start(bf16[1024,4,256]{2,1,0:T(4,128)(2,1)S(1)} %get-tuple-element.11), channel_id=1, source_target_pairs={{0,1},{1,2},{2,3},{3,4},{4,5},{5,6},{6,7},{7,8},{8,9},{9,10},{10,1... | collective-permute-start | bytes 6291464 | tf_op jit(solution)/shard_map/ppermute | solution.py:63
  10.1 1.3 collective-permute-start.1
  11.4 3.6 %collective-permute-start = (f32[4,256]{1,0:T(4,128)S(1)}, f32[4,256]{1,0:T(4,128)S(1)}, u32[]{:S(2)}, u32[]{:S(2)}) collective-permute-start(f32[4,256]{1,0:T(4,128)S(1)} %get-tuple-element.19), channel_id=1, source_target_pairs={{0,1},{1,2},{2,3},{3,4},{4,5},{5,6},{6,7},{7,8},{8,9},{9,10},{10,1... | collective-permute-start | bytes 12296 | tf_op jit(solution)/shard_map/ppermute | solution.py:63
  15.9 3.5 %pad_maximum_fusion.h_ref = bf16[1024,8,256]{2,1,0:T(8,128)(2,1)} fusion(bf16[1024,4,256]{2,1,0:T(4,128)(2,1)S(1)} %collective-permute-done.3, bf16[1024,4,256]{2,1,0:T(4,128)(2,1)S(1)} %collective-permute-done.2), kind=kLoop, calls=%fused_computation | loop fusion | flops 8388608 | bytes 8388608 | tf_op jit(solution)/shard_map/concatenate | solution.py:65
  19.4 72.6 %shard_map.59 = (f32[1024,8,256]{2,1,0:T(8,128)}, bf16[1024,8,256]{2,1,0:T(8,128)(2,1)}) custom-call(f32[6,16,256]{2,1,0:T(8,128)} %copy-done.3, bf16[1024,8,256]{2,1,0:T(8,128)(2,1)} %a_ref.1, bf16[1024,8,256]{2,1,0:T(8,128)(2,1)} %pad_maximum_fusion.h_ref), custom_call_target="tpu_custom_call" | custom-call | tf_op jit(solution)/shard_map/pallas_call | solution.py:145
  93.1 1.7 collective-permute-start.4
  97.4 5.0 %collective-permute-done.4 = bf16[128,8,256]{2,1,0:T(8,128)(2,1)S(1)} collective-permute-done((bf16[128,8,256]{2,1,0:T(8,128)(2,1)S(1)}, bf16[128,8,256]{2,1,0:T(8,128)(2,1)S(1)}, u32[]{:S(2)}, u32[]{:S(2)}) %collective-permute-start.4) | collective-permute-done | bytes 524320 | tf_op jit(solution)/shard_map/ppermute | solution.py:30
  102.4 1.5 slice_select_fusion.2
  103.9 1.7 collective-permute-start.14
  106.0 1.9 collective-permute-start.5
  107.9 2.1 collective-permute-start.6
  114.5 8.9 %collective-permute-done.24 = bf16[128,8,256]{2,1,0:T(8,128)(2,1)S(1)} collective-permute-done((bf16[128,8,256]{2,1,0:T(8,128)(2,1)S(1)}, bf16[128,8,256]{2,1,0:T(8,128)(2,1)S(1)}, u32[]{:S(2)}, u32[]{:S(2)}) %collective-permute-start.24) | collective-permute-done | bytes 524320 | tf_op jit(solution)/shard_map/ppermute | solution.py:30
  123.4 1.3 slice_select_fusion.1
  124.7 2.0 collective-permute-start.25
  126.7 2.2 collective-permute-start.26
  128.9 1.1 select_select_fusion.2
  130.9 1.9 collective-permute-start.8
  134.4 9.9 %collective-permute-done.8 = bf16[64,8,256]{2,1,0:T(8,128)(2,1)S(1)} collective-permute-done((bf16[64,8,256]{2,1,0:T(8,128)(2,1)}, bf16[64,8,256]{2,1,0:T(8,128)(2,1)S(1)}, u32[]{:S(2)}, u32[]{:S(2)}) %collective-permute-start.8) | collective-permute-done | bytes 262176 | tf_op jit(solution)/shard_map/ppermute | solution.py:28
  144.3 3.4 %collective-permute-start.16 = (bf16[128,8,256]{2,1,0:T(8,128)(2,1)S(1)}, bf16[128,8,256]{2,1,0:T(8,128)(2,1)S(1)}, u32[]{:S(2)}, u32[]{:S(2)}) collective-permute-start(bf16[128,8,256]{2,1,0:T(8,128)(2,1)S(1)} %get-tuple-element.9), channel_id=1, source_target_pairs={{0,96},{16,112},{32,0},{48,16},{64,32},{80,48},{96,64},{112,80},{1... | collective-permute-start | bytes 1572872 | tf_op jit(solution)/shard_map/ppermute | solution.py:28
  148.7 1.7 collective-permute-start.9
  152.1 1.3 collective-permute-start.27
  153.9 5.6 %collective-permute-done.16 = bf16[128,8,256]{2,1,0:T(8,128)(2,1)S(1)} collective-permute-done((bf16[128,8,256]{2,1,0:T(8,128)(2,1)S(1)}, bf16[128,8,256]{2,1,0:T(8,128)(2,1)S(1)}, u32[]{:S(2)}, u32[]{:S(2)}) %collective-permute-start.16) | collective-permute-done | bytes 524320 | tf_op jit(solution)/shard_map/ppermute | solution.py:28
  159.7 1.8 fusion.30
  161.9 12.0 %collective-permute-start.10 = (f32[8,64,256]{2,1,0:T(8,128)S(1)}, f32[8,64,256]{2,1,0:T(8,128)}, u32[]{:S(2)}, u32[]{:S(2)}) collective-permute-start(f32[8,64,256]{2,1,0:T(8,128)S(1)} %dynamic-slice_bitcast_fusion.2), channel_id=1, source_target_pairs={{0,1},{1,0},{2,3},{3,2},{4,5},{5,4},{6,7},{7,6},{8,9},{9,8},{10,11... | collective-permute-start | bytes 1572872 | tf_op jit(solution)/shard_map/ppermute | solution.py:52
  173.9 1.5 collective-permute-start.18
  176.0 1.2 maximum_select_fusion.5
  177.2 1.7 collective-permute-start.29
  178.9 3.5 %collective-permute-done.18 = bf16[64,8,256]{2,1,0:T(8,128)(2,1)} collective-permute-done((bf16[64,8,256]{2,1,0:T(8,128)(2,1)S(1)}, bf16[64,8,256]{2,1,0:T(8,128)(2,1)}, u32[]{:S(2)}, u32[]{:S(2)}) %collective-permute-start.18) | collective-permute-done | bytes 262176 | tf_op jit(solution)/shard_map/ppermute | solution.py:28
  182.3 2.3 collective-permute-done.17
  185.8 1.7 collective-permute-start.19
  188.6 17.0 %collective-permute-start.11 = (f32[4,64,256]{2,1,0:T(8,128)S(1)}, f32[4,64,256]{2,1,0:T(8,128)}, u32[]{:S(2)}, u32[]{:S(2)}) collective-permute-start(f32[4,64,256]{2,1,0:T(8,128)S(1)} %dynamic-slice_bitcast_fusion.5), channel_id=1, source_target_pairs={{0,2},{1,3},{2,0},{3,1},{4,6},{5,7},{6,4},{7,5},{8,10},{9,11},{10,... | collective-permute-start | bytes 786440 | tf_op jit(solution)/shard_map/ppermute | solution.py:52
  205.8 1.8 fusion.18
  208.8 1.9 maximum_select_fusion.1
  213.0 10.5 %collective-permute-start.12 = (f32[2,64,256]{2,1,0:T(8,128)}, f32[2,64,256]{2,1,0:T(8,128)S(1)}, u32[]{:S(2)}, u32[]{:S(2)}) collective-permute-start(f32[2,64,256]{2,1,0:T(8,128)} %dynamic-slice_bitcast_fusion.8), channel_id=1, source_target_pairs={{0,4},{1,5},{2,6},{3,7},{4,0},{5,1},{6,2},{7,3},{8,12},{9,13},{10,... | collective-permute-start | bytes 393224 | tf_op jit(solution)/shard_map/ppermute | solution.py:52
  223.4 1.8 fusion.24
  226.7 3.4 %collective-permute-start.13 = (f32[1,64,256]{2,1,0:T(8,128)S(1)}, f32[1,64,256]{2,1,0:T(8,128)S(1)}, u32[]{:S(2)}, u32[]{:S(2)}) collective-permute-start(f32[1,64,256]{2,1,0:T(8,128)S(1)} %constant_dynamic-slice_fusion.2), channel_id=1, source_target_pairs={{0,8},{1,9},{2,10},{3,11},{4,12},{5,13},{6,14},{7,15},{8,0},{9,1},... | collective-permute-start | bytes 196616 | tf_op jit(solution)/shard_map/ppermute | solution.py:52
  230.3 2.3 collective-permute-done.13
  232.6 1.1 bitcast_add_fusion
  233.7 8.1 %collective-permute-start.31 = (f32[4,64,256]{2,1,0:T(8,128)S(1)}, f32[4,64,256]{2,1,0:T(8,128)S(1)}, u32[]{:S(2)}, u32[]{:S(2)}) collective-permute-start(f32[4,64,256]{2,1,0:T(8,128)S(1)} %dynamic-slice_bitcast_fusion.3), channel_id=1, source_target_pairs={{0,2},{1,3},{2,0},{3,1},{4,6},{5,7},{6,4},{7,5},{8,10},{9,11},{10,... | collective-permute-start | bytes 786440 | tf_op jit(solution)/shard_map/ppermute | solution.py:52
  242.1 7.0 %collective-permute-done.31 = f32[4,64,256]{2,1,0:T(8,128)S(1)} collective-permute-done((f32[4,64,256]{2,1,0:T(8,128)S(1)}, f32[4,64,256]{2,1,0:T(8,128)S(1)}, u32[]{:S(2)}, u32[]{:S(2)}) %collective-permute-start.31) | collective-permute-done | bytes 262176 | tf_op jit(solution)/shard_map/ppermute | solution.py:52
  249.1 4.1 %collective-permute-start.32 = (f32[2,64,256]{2,1,0:T(8,128)S(1)}, f32[2,64,256]{2,1,0:T(8,128)S(1)}, u32[]{:S(2)}, u32[]{:S(2)}) collective-permute-start(f32[2,64,256]{2,1,0:T(8,128)S(1)} %dynamic-slice_bitcast_fusion.6), channel_id=1, source_target_pairs={{0,4},{1,5},{2,6},{3,7},{4,0},{5,1},{6,2},{7,3},{8,12},{9,13},{10,... | collective-permute-start | bytes 393224 | tf_op jit(solution)/shard_map/ppermute | solution.py:52
  253.3 4.7 %collective-permute-start.22 = (f32[2,64,256]{2,1,0:T(8,128)S(1)}, f32[2,64,256]{2,1,0:T(8,128)S(1)}, u32[]{:S(2)}, u32[]{:S(2)}) collective-permute-start(f32[2,64,256]{2,1,0:T(8,128)S(1)} %dynamic-slice_bitcast_fusion.7), channel_id=1, source_target_pairs={{0,4},{1,5},{2,6},{3,7},{4,0},{5,1},{6,2},{7,3},{8,12},{9,13},{10,... | collective-permute-start | bytes 393224 | tf_op jit(solution)/shard_map/ppermute | solution.py:52
  259.0 1.4 collective-permute-start.33
  261.0 1.8 collective-permute-start.23
  262.8 2.1 collective-permute-done.33
  264.9 2.0 collective-permute-done.23
  (96 shorter events, 18.7 us)
Async XLA Ops:
  0.6 9.3 %copy-start.6 = (f32[8]{0:T(128)S(1)}, f32[8]{0:T(128)}, u32[]{:S(2)}) copy-start(f32[8]{0:T(128)} %param.6) | copy-start | bytes 100
  0.6 9.3 %copy-start.4 = (s32[8,256]{1,0:T(8,128)S(1)}, s32[8,256]{1,0:T(8,128)}, u32[]{:S(2)}) copy-start(s32[8,256]{1,0:T(8,128)} %param.5) | copy-start | bytes 24580
  5.5 10.4 %collective-permute-start.3 = (bf16[1024,4,256]{2,1,0:T(4,128)(2,1)S(1)}, bf16[1024,4,256]{2,1,0:T(4,128)(2,1)S(1)}, u32[]{:S(2)}, u32[]{:S(2)}) collective-permute-start(bf16[1024,4,256]{2,1,0:T(4,128)(2,1)S(1)} %get-tuple-element.12), channel_id=1, source_target_pairs={{1,0},{2,1},{3,2},{4,3},{5,4},{6,5},{7,6},{8,7},{9,8},{10,9},{11,1... | collective-permute-start | bytes 6291464 | tf_op jit(solution)/shard_map/ppermute | solution.py:64
  6.8 9.1 %collective-permute-start.2 = (bf16[1024,4,256]{2,1,0:T(4,128)(2,1)S(1)}, bf16[1024,4,256]{2,1,0:T(4,128)(2,1)S(1)}, u32[]{:S(2)}, u32[]{:S(2)}) collective-permute-start(bf16[1024,4,256]{2,1,0:T(4,128)(2,1)S(1)} %get-tuple-element.11), channel_id=1, source_target_pairs={{0,1},{1,2},{2,3},{3,4},{4,5},{5,6},{6,7},{7,8},{8,9},{9,10},{10,1... | collective-permute-start | bytes 6291464 | tf_op jit(solution)/shard_map/ppermute | solution.py:63
  10.1 5.0 %collective-permute-start.1 = (f32[4,256]{1,0:T(4,128)S(1)}, f32[4,256]{1,0:T(4,128)S(1)}, u32[]{:S(2)}, u32[]{:S(2)}) collective-permute-start(f32[4,256]{1,0:T(4,128)S(1)} %get-tuple-element.20), channel_id=1, source_target_pairs={{1,0},{2,1},{3,2},{4,3},{5,4},{6,5},{7,6},{8,7},{9,8},{10,9},{11,1... | collective-permute-start | bytes 12296 | tf_op jit(solution)/shard_map/ppermute | solution.py:64
  11.4 4.4 %collective-permute-start = (f32[4,256]{1,0:T(4,128)S(1)}, f32[4,256]{1,0:T(4,128)S(1)}, u32[]{:S(2)}, u32[]{:S(2)}) collective-permute-start(f32[4,256]{1,0:T(4,128)S(1)} %get-tuple-element.19), channel_id=1, source_target_pairs={{0,1},{1,2},{2,3},{3,4},{4,5},{5,6},{6,7},{7,8},{8,9},{9,10},{10,1... | collective-permute-start | bytes 12296 | tf_op jit(solution)/shard_map/ppermute | solution.py:63
  15.9 3.6 %copy-start.3 = (f32[6,16,256]{2,1,0:T(8,128)}, f32[6,16,256]{2,1,0:T(8,128)S(1)}, u32[]{:S(2)}) copy-start(f32[6,16,256]{2,1,0:T(8,128)S(1)} %select_dynamic-update-slice_fusion.coef_ref) | copy-start | bytes 294916
  19.4 75.4 %copy-start.5 = (s32[8]{0:T(128)S(1)}, s32[8]{0:T(128)}, u32[]{:S(2)}) copy-start(s32[8]{0:T(128)} %param.7) | copy-start | bytes 100
  93.1 9.3 %collective-permute-start.4 = (bf16[128,8,256]{2,1,0:T(8,128)(2,1)S(1)}, bf16[128,8,256]{2,1,0:T(8,128)(2,1)S(1)}, u32[]{:S(2)}, u32[]{:S(2)}) collective-permute-start(bf16[128,8,256]{2,1,0:T(8,128)(2,1)S(1)} %slice.72), channel_id=1, source_target_pairs={{0,16},{16,0},{32,48},{48,32},{64,80},{80,64},{96,112},{112,96},{1... | collective-permute-start | bytes 1572872 | tf_op jit(solution)/shard_map/ppermute | solution.py:30
  103.9 10.7 %collective-permute-start.14 = (bf16[128,8,256]{2,1,0:T(8,128)(2,1)S(1)}, bf16[128,8,256]{2,1,0:T(8,128)(2,1)S(1)}, u32[]{:S(2)}, u32[]{:S(2)}) collective-permute-start(bf16[128,8,256]{2,1,0:T(8,128)(2,1)S(1)} %get-tuple-element.8), channel_id=1, source_target_pairs={{0,16},{16,0},{32,48},{48,32},{64,80},{80,64},{96,112},{112,96},{1... | collective-permute-start | bytes 1572872 | tf_op jit(solution)/shard_map/ppermute | solution.py:30
  105.5 17.9 %collective-permute-start.24 = (bf16[128,8,256]{2,1,0:T(8,128)(2,1)S(1)}, bf16[128,8,256]{2,1,0:T(8,128)(2,1)S(1)}, u32[]{:S(2)}, u32[]{:S(2)}) collective-permute-start(bf16[128,8,256]{2,1,0:T(8,128)(2,1)S(1)} %get-tuple-element.7), channel_id=1, source_target_pairs={{0,16},{16,0},{32,48},{48,32},{64,80},{80,64},{96,112},{112,96},{1... | collective-permute-start | bytes 1572872 | tf_op jit(solution)/shard_map/ppermute | solution.py:30
  106.0 22.9 %collective-permute-start.5 = (bf16[128,8,256]{2,1,0:T(8,128)(2,1)S(1)}, bf16[128,8,256]{2,1,0:T(8,128)(2,1)}, u32[]{:S(2)}, u32[]{:S(2)}) collective-permute-start(bf16[128,8,256]{2,1,0:T(8,128)(2,1)S(1)} %get-tuple-element.6), channel_id=1, source_target_pairs={{0,32},{16,48},{32,64},{48,80},{64,96},{80,112},{96,0},{112,16},{1... | collective-permute-start | bytes 1572872 | tf_op jit(solution)/shard_map/ppermute | solution.py:28
  107.9 21.0 %collective-permute-start.6 = (bf16[128,8,256]{2,1,0:T(8,128)(2,1)S(1)}, bf16[128,8,256]{2,1,0:T(8,128)(2,1)}, u32[]{:S(2)}, u32[]{:S(2)}) collective-permute-start(bf16[128,8,256]{2,1,0:T(8,128)(2,1)S(1)} %get-tuple-element.6), channel_id=1, source_target_pairs={{0,96},{16,112},{32,0},{48,16},{64,32},{80,48},{96,64},{112,80},{1... | collective-permute-start | bytes 1572872 | tf_op jit(solution)/shard_map/ppermute | solution.py:28
  124.7 25.7 %collective-permute-start.25 = (bf16[128,8,256]{2,1,0:T(8,128)(2,1)S(1)}, bf16[128,8,256]{2,1,0:T(8,128)(2,1)S(1)}, u32[]{:S(2)}, u32[]{:S(2)}) collective-permute-start(bf16[128,8,256]{2,1,0:T(8,128)(2,1)S(1)} %get-tuple-element.10), channel_id=1, source_target_pairs={{0,32},{16,48},{32,64},{48,80},{64,96},{80,112},{96,0},{112,16},{1... | collective-permute-start | bytes 1572872 | tf_op jit(solution)/shard_map/ppermute | solution.py:28
  126.7 23.7 %collective-permute-start.26 = (bf16[128,8,256]{2,1,0:T(8,128)(2,1)S(1)}, bf16[128,8,256]{2,1,0:T(8,128)(2,1)S(1)}, u32[]{:S(2)}, u32[]{:S(2)}) collective-permute-start(bf16[128,8,256]{2,1,0:T(8,128)(2,1)S(1)} %get-tuple-element.10), channel_id=1, source_target_pairs={{0,96},{16,112},{32,0},{48,16},{64,32},{80,48},{96,64},{112,80},{1... | collective-permute-start | bytes 1572872 | tf_op jit(solution)/shard_map/ppermute | solution.py:28
  130.9 13.4 %collective-permute-start.8 = (bf16[64,8,256]{2,1,0:T(8,128)(2,1)}, bf16[64,8,256]{2,1,0:T(8,128)(2,1)S(1)}, u32[]{:S(2)}, u32[]{:S(2)}) collective-permute-start(bf16[64,8,256]{2,1,0:T(8,128)(2,1)} %get-tuple-element.14), channel_id=1, source_target_pairs={{0,96},{16,112},{32,0},{48,16},{64,32},{80,48},{96,64},{112,80},{1... | collective-permute-start | bytes 786440 | tf_op jit(solution)/shard_map/ppermute | solution.py:28
  132.8 14.9 %collective-permute-start.7 = (bf16[64,8,256]{2,1,0:T(8,128)(2,1)}, bf16[64,8,256]{2,1,0:T(8,128)(2,1)}, u32[]{:S(2)}, u32[]{:S(2)}) collective-permute-start(bf16[64,8,256]{2,1,0:T(8,128)(2,1)} %get-tuple-element.13), channel_id=1, source_target_pairs={{0,32},{16,48},{32,64},{48,80},{64,96},{80,112},{96,0},{112,16},{1... | collective-permute-start | bytes 786440 | tf_op jit(solution)/shard_map/ppermute | solution.py:28
  134.3 25.5 %copy-start = (bf16[1024,8,256]{2,1,0:T(8,128)(2,1)S(1)}, bf16[1024,8,256]{2,1,0:T(8,128)(2,1)}, u32[]{:S(2)}) copy-start(bf16[1024,8,256]{2,1,0:T(8,128)(2,1)} %a_ref.1) | copy-start | bytes 12582916
  134.3 19.6 %collective-permute-start.15 = (bf16[128,8,256]{2,1,0:T(8,128)(2,1)S(1)}, bf16[128,8,256]{2,1,0:T(8,128)(2,1)S(1)}, u32[]{:S(2)}, u32[]{:S(2)}) collective-permute-start(bf16[128,8,256]{2,1,0:T(8,128)(2,1)S(1)} %get-tuple-element.9), channel_id=1, source_target_pairs={{0,32},{16,48},{32,64},{48,80},{64,96},{80,112},{96,0},{112,16},{1... | collective-permute-start | bytes 1572872 | tf_op jit(solution)/shard_map/ppermute | solution.py:28
  144.3 15.2 %collective-permute-start.16 = (bf16[128,8,256]{2,1,0:T(8,128)(2,1)S(1)}, bf16[128,8,256]{2,1,0:T(8,128)(2,1)S(1)}, u32[]{:S(2)}, u32[]{:S(2)}) collective-permute-start(bf16[128,8,256]{2,1,0:T(8,128)(2,1)S(1)} %get-tuple-element.9), channel_id=1, source_target_pairs={{0,96},{16,112},{32,0},{48,16},{64,32},{80,48},{96,64},{112,80},{1... | collective-permute-start | bytes 1572872 | tf_op jit(solution)/shard_map/ppermute | solution.py:28
  148.7 10.8 %collective-permute-start.9 = (bf16[128,8,256]{2,1,0:T(8,128)(2,1)S(1)}, bf16[128,8,256]{2,1,0:T(8,128)(2,1)S(1)}, u32[]{:S(2)}, u32[]{:S(2)}) collective-permute-start(bf16[128,8,256]{2,1,0:T(8,128)(2,1)S(1)} %maximum_select_fusion.3), channel_id=1, source_target_pairs={{0,16},{16,0},{32,48},{48,32},{64,80},{80,64},{96,112},{112,96},{1... | collective-permute-start | bytes 1572872 | tf_op jit(solution)/shard_map/ppermute | solution.py:37
  151.3 24.7 %collective-permute-start.28 = (bf16[64,8,256]{2,1,0:T(8,128)(2,1)}, bf16[64,8,256]{2,1,0:T(8,128)(2,1)S(1)}, u32[]{:S(2)}, u32[]{:S(2)}) collective-permute-start(bf16[64,8,256]{2,1,0:T(8,128)(2,1)} %get-tuple-element.18), channel_id=1, source_target_pairs={{0,96},{16,112},{32,0},{48,16},{64,32},{80,48},{96,64},{112,80},{1... | collective-permute-start | bytes 786440 | tf_op jit(solution)/shard_map/ppermute | solution.py:28
  152.1 24.0 %collective-permute-start.27 = (bf16[64,8,256]{2,1,0:T(8,128)(2,1)}, bf16[64,8,256]{2,1,0:T(8,128)(2,1)}, u32[]{:S(2)}, u32[]{:S(2)}) collective-permute-start(bf16[64,8,256]{2,1,0:T(8,128)(2,1)} %get-tuple-element.17), channel_id=1, source_target_pairs={{0,32},{16,48},{32,64},{48,80},{64,96},{80,112},{96,0},{112,16},{1... | collective-permute-start | bytes 786440 | tf_op jit(solution)/shard_map/ppermute | solution.py:28
  161.9 25.5 %collective-permute-start.10 = (f32[8,64,256]{2,1,0:T(8,128)S(1)}, f32[8,64,256]{2,1,0:T(8,128)}, u32[]{:S(2)}, u32[]{:S(2)}) collective-permute-start(f32[8,64,256]{2,1,0:T(8,128)S(1)} %dynamic-slice_bitcast_fusion.2), channel_id=1, source_target_pairs={{0,1},{1,0},{2,3},{3,2},{4,5},{5,4},{6,7},{7,6},{8,9},{9,8},{10,11... | collective-permute-start | bytes 1572872 | tf_op jit(solution)/shard_map/ppermute | solution.py:52
  173.9 8.4 %collective-permute-start.18 = (bf16[64,8,256]{2,1,0:T(8,128)(2,1)S(1)}, bf16[64,8,256]{2,1,0:T(8,128)(2,1)}, u32[]{:S(2)}, u32[]{:S(2)}) collective-permute-start(bf16[64,8,256]{2,1,0:T(8,128)(2,1)S(1)} %get-tuple-element.16), channel_id=1, source_target_pairs={{0,96},{16,112},{32,0},{48,16},{64,32},{80,48},{96,64},{112,80},{1... | collective-permute-start | bytes 786440 | tf_op jit(solution)/shard_map/ppermute | solution.py:28
  175.4 9.3 %collective-permute-start.17 = (bf16[64,8,256]{2,1,0:T(8,128)(2,1)S(1)}, bf16[64,8,256]{2,1,0:T(8,128)(2,1)}, u32[]{:S(2)}, u32[]{:S(2)}) collective-permute-start(bf16[64,8,256]{2,1,0:T(8,128)(2,1)S(1)} %get-tuple-element.15), channel_id=1, source_target_pairs={{0,32},{16,48},{32,64},{48,80},{64,96},{80,112},{96,0},{112,16},{1... | collective-permute-start | bytes 786440 | tf_op jit(solution)/shard_map/ppermute | solution.py:28
  176.0 29.7 %copy-start.1 = (bf16[1024,8,256]{2,1,0:T(8,128)(2,1)S(1)}, bf16[1024,8,256]{2,1,0:T(8,128)(2,1)}, u32[]{:S(2)}) copy-start(bf16[1024,8,256]{2,1,0:T(8,128)(2,1)} %a_ref.1) | copy-start | bytes 12582916
  177.2 28.4 %collective-permute-start.29 = (bf16[128,8,256]{2,1,0:T(8,128)(2,1)S(1)}, bf16[128,8,256]{2,1,0:T(8,128)(2,1)S(1)}, u32[]{:S(2)}, u32[]{:S(2)}) collective-permute-start(bf16[128,8,256]{2,1,0:T(8,128)(2,1)S(1)} %maximum_select_fusion.5), channel_id=1, source_target_pairs={{0,16},{16,0},{32,48},{48,32},{64,80},{80,64},{96,112},{112,96},{1... | collective-permute-start | bytes 1572872 | tf_op jit(solution)/shard_map/ppermute | solution.py:37
  185.8 23.0 %collective-permute-start.19 = (bf16[128,8,256]{2,1,0:T(8,128)(2,1)S(1)}, bf16[128,8,256]{2,1,0:T(8,128)(2,1)}, u32[]{:S(2)}, u32[]{:S(2)}) collective-permute-start(bf16[128,8,256]{2,1,0:T(8,128)(2,1)S(1)} %maximum_select_fusion.4), channel_id=1, source_target_pairs={{0,16},{16,0},{32,48},{48,32},{64,80},{80,64},{96,112},{112,96},{1... | collective-permute-start | bytes 1572872 | tf_op jit(solution)/shard_map/ppermute | solution.py:37
  188.6 22.7 %collective-permute-start.11 = (f32[4,64,256]{2,1,0:T(8,128)S(1)}, f32[4,64,256]{2,1,0:T(8,128)}, u32[]{:S(2)}, u32[]{:S(2)}) collective-permute-start(f32[4,64,256]{2,1,0:T(8,128)S(1)} %dynamic-slice_bitcast_fusion.5), channel_id=1, source_target_pairs={{0,2},{1,3},{2,0},{3,1},{4,6},{5,7},{6,4},{7,5},{8,10},{9,11},{10,... | collective-permute-start | bytes 786440 | tf_op jit(solution)/shard_map/ppermute | solution.py:52
  207.9 15.5 %copy-start.2 = (bf16[1024,8,256]{2,1,0:T(8,128)(2,1)S(1)}, bf16[1024,8,256]{2,1,0:T(8,128)(2,1)}, u32[]{:S(2)}) copy-start(bf16[1024,8,256]{2,1,0:T(8,128)(2,1)} %a_ref.1) | copy-start | bytes 12582916
  208.8 23.8 %collective-permute-start.30 = (f32[8,64,256]{2,1,0:T(8,128)}, f32[8,64,256]{2,1,0:T(8,128)}, u32[]{:S(2)}, u32[]{:S(2)}) collective-permute-start(f32[8,64,256]{2,1,0:T(8,128)} %dynamic-slice_bitcast_fusion), channel_id=1, source_target_pairs={{0,1},{1,0},{2,3},{3,2},{4,5},{5,4},{6,7},{7,6},{8,9},{9,8},{10,11... | collective-permute-start | bytes 1572872 | tf_op jit(solution)/shard_map/ppermute | solution.py:52
  213.0 13.7 %collective-permute-start.12 = (f32[2,64,256]{2,1,0:T(8,128)}, f32[2,64,256]{2,1,0:T(8,128)S(1)}, u32[]{:S(2)}, u32[]{:S(2)}) collective-permute-start(f32[2,64,256]{2,1,0:T(8,128)} %dynamic-slice_bitcast_fusion.8), channel_id=1, source_target_pairs={{0,4},{1,5},{2,6},{3,7},{4,0},{5,1},{6,2},{7,3},{8,12},{9,13},{10,... | collective-permute-start | bytes 393224 | tf_op jit(solution)/shard_map/ppermute | solution.py:52
  226.7 5.8 %collective-permute-start.13 = (f32[1,64,256]{2,1,0:T(8,128)S(1)}, f32[1,64,256]{2,1,0:T(8,128)S(1)}, u32[]{:S(2)}, u32[]{:S(2)}) collective-permute-start(f32[1,64,256]{2,1,0:T(8,128)S(1)} %constant_dynamic-slice_fusion.2), channel_id=1, source_target_pairs={{0,8},{1,9},{2,10},{3,11},{4,12},{5,13},{6,14},{7,15},{8,0},{9,1},... | collective-permute-start | bytes 196616 | tf_op jit(solution)/shard_map/ppermute | solution.py:52
  230.2 11.7 %collective-permute-start.20 = (f32[8,64,256]{2,1,0:T(8,128)S(1)}, f32[8,64,256]{2,1,0:T(8,128)S(1)}, u32[]{:S(2)}, u32[]{:S(2)}) collective-permute-start(f32[8,64,256]{2,1,0:T(8,128)S(1)} %dynamic-slice_bitcast_fusion.1), channel_id=1, source_target_pairs={{0,1},{1,0},{2,3},{3,2},{4,5},{5,4},{6,7},{7,6},{8,9},{9,8},{10,11... | collective-permute-start | bytes 1572872 | tf_op jit(solution)/shard_map/ppermute | solution.py:52
  233.7 15.3 %collective-permute-start.31 = (f32[4,64,256]{2,1,0:T(8,128)S(1)}, f32[4,64,256]{2,1,0:T(8,128)S(1)}, u32[]{:S(2)}, u32[]{:S(2)}) collective-permute-start(f32[4,64,256]{2,1,0:T(8,128)S(1)} %dynamic-slice_bitcast_fusion.3), channel_id=1, source_target_pairs={{0,2},{1,3},{2,0},{3,1},{4,6},{5,7},{6,4},{7,5},{8,10},{9,11},{10,... | collective-permute-start | bytes 786440 | tf_op jit(solution)/shard_map/ppermute | solution.py:52
  242.0 11.3 %collective-permute-start.21 = (f32[4,64,256]{2,1,0:T(8,128)S(1)}, f32[4,64,256]{2,1,0:T(8,128)S(1)}, u32[]{:S(2)}, u32[]{:S(2)}) collective-permute-start(f32[4,64,256]{2,1,0:T(8,128)S(1)} %dynamic-slice_bitcast_fusion.4), channel_id=1, source_target_pairs={{0,2},{1,3},{2,0},{3,1},{4,6},{5,7},{6,4},{7,5},{8,10},{9,11},{10,... | collective-permute-start | bytes 786440 | tf_op jit(solution)/shard_map/ppermute | solution.py:52
  249.1 9.8 %collective-permute-start.32 = (f32[2,64,256]{2,1,0:T(8,128)S(1)}, f32[2,64,256]{2,1,0:T(8,128)S(1)}, u32[]{:S(2)}, u32[]{:S(2)}) collective-permute-start(f32[2,64,256]{2,1,0:T(8,128)S(1)} %dynamic-slice_bitcast_fusion.6), channel_id=1, source_target_pairs={{0,4},{1,5},{2,6},{3,7},{4,0},{5,1},{6,2},{7,3},{8,12},{9,13},{10,... | collective-permute-start | bytes 393224 | tf_op jit(solution)/shard_map/ppermute | solution.py:52
  253.3 7.6 %collective-permute-start.22 = (f32[2,64,256]{2,1,0:T(8,128)S(1)}, f32[2,64,256]{2,1,0:T(8,128)S(1)}, u32[]{:S(2)}, u32[]{:S(2)}) collective-permute-start(f32[2,64,256]{2,1,0:T(8,128)S(1)} %dynamic-slice_bitcast_fusion.7), channel_id=1, source_target_pairs={{0,4},{1,5},{2,6},{3,7},{4,0},{5,1},{6,2},{7,3},{8,12},{9,13},{10,... | collective-permute-start | bytes 393224 | tf_op jit(solution)/shard_map/ppermute | solution.py:52
  259.0 5.8 %collective-permute-start.33 = (f32[1,64,256]{2,1,0:T(8,128)S(1)}, f32[1,64,256]{2,1,0:T(8,128)S(1)}, u32[]{:S(2)}, u32[]{:S(2)}) collective-permute-start(f32[1,64,256]{2,1,0:T(8,128)S(1)} %constant_dynamic-slice_fusion), channel_id=1, source_target_pairs={{0,8},{1,9},{2,10},{3,11},{4,12},{5,13},{6,14},{7,15},{8,0},{9,1},... | collective-permute-start | bytes 196616 | tf_op jit(solution)/shard_map/ppermute | solution.py:52
  261.0 5.8 %collective-permute-start.23 = (f32[1,64,256]{2,1,0:T(8,128)S(1)}, f32[1,64,256]{2,1,0:T(8,128)S(1)}, u32[]{:S(2)}, u32[]{:S(2)}) collective-permute-start(f32[1,64,256]{2,1,0:T(8,128)S(1)} %constant_dynamic-slice_fusion.1), channel_id=1, source_target_pairs={{0,8},{1,9},{2,10},{3,11},{4,12},{5,13},{6,14},{7,15},{8,0},{9,1},... | collective-permute-start | bytes 196616 | tf_op jit(solution)/shard_map/ppermute | solution.py:52

commit v12 on v8

--- a/solution.py
+++ b/solution.py
@@ -62,10 +62,10 @@
     bottom = lax.slice_in_dim(shard, 0, HALO, axis=dim)
     below = lax.ppermute(top, axis, up)
     above = lax.ppermute(bottom, axis, down)
-    return jnp.concatenate([below, above], axis=dim)
+    return below, above
 
 
-def smooth_kernel(coef_ref, a_ref, h_ref, o_ref, *, sub):
+def smooth_kernel(coef_ref, a_ref, lo_ref, hi_ref, o_ref, *, sub):
     depth, lat = a_ref.shape[1], a_ref.shape[2]
     half = lat // 2
     shape = (sub, depth, half)
@@ -80,7 +80,9 @@
     def body(i, carry):
         r = pl.multiple_of(i * sub, sub)
         own = a_ref[pl.ds(r, sub)].astype(jnp.float32)
-        hal = h_ref[pl.ds(r, sub)].astype(jnp.float32)
+        hal = jnp.concatenate(
+            [lo_ref[pl.ds(r, sub)].astype(jnp.float32), hi_ref[pl.ds(r, sub)].astype(jnp.float32)], axis=1
+        )
         own = [own[..., :half], own[..., half:]]
         hal = [hal[..., :half], hal[..., half:]]
         rot = [pltpu.roll(o, HALO, 1) for o in own]
@@ -138,7 +140,7 @@
     )
 
 
-def smooth(sensitivity, halo, coef, block=128, sub=16):
+def smooth(sensitivity, below, above, coef, block=128, sub=16):
     rows, depth, lat = sensitivity.shape
     kernel = functools.partial(smooth_kernel, sub=sub)
     return pl.pallas_call(
@@ -147,11 +149,12 @@
         in_specs=[
             pl.BlockSpec(coef.shape, lambda i: (0, 0, 0)),
             pl.BlockSpec((block, depth, lat), lambda i: (i, 0, 0)),
-            pl.BlockSpec((block, depth, lat), lambda i: (i, 0, 0)),
+            pl.BlockSpec((block, HALO, lat), lambda i: (i, 0, 0)),
+            pl.BlockSpec((block, HALO, lat), lambda i: (i, 0, 0)),
         ],
         out_specs=pl.BlockSpec((block, depth, lat), lambda i: (i, 0, 0)),
         out_shape=jax.ShapeDtypeStruct((rows, depth, lat), jnp.float32),
-    )(coef, sensitivity, halo)
+    )(coef, sensitivity, below, above)
 
 
 def body(sensitivity, cell_class, class_rate, panel_owner):
@@ -160,10 +163,9 @@
         jnp.float32
     )
     kappa = jnp.sum(onehot * class_rate[None, None, :], axis=-1)
-    halo = halo_of(sensitivity, "slab", 1)
-    kappa_halo = halo_of(kappa, "slab", 0)
-    kappa_col = jnp.concatenate([kappa_halo[:HALO], kappa, kappa_halo[HALO:]], axis=0)
-    field = smooth(sensitivity, halo, coefficients(kappa_col, lat))
+    below, above = halo_of(sensitivity, "slab", 1)
+    kappa_col = jnp.concatenate([halo_of(kappa, "slab", 0)[0], kappa, halo_of(kappa, "slab", 0)[1]], axis=0)
+    field = smooth(sensitivity, below, above, coefficients(kappa_col, lat))
     cells = depth * lat * lax.axis_size("slab")
     flat = sensitivity.reshape(rows, depth * lat)
     partials = []

time: 262 us -> 261 us (level)
    slice x0 -> x1, local copies, waits for them, and re-layouts: none -> 4.8 us  [halo_of(): bottom = lax.slice_in_dim(shard, 0, HALO, axis=dim)]
    slice x2 -> x1, local copies, waits for them, and re-layouts: 4.8 us -> 0.01 us  [halo_of(): top = lax.slice_in_dim(shard, length - HALO, length, axis=dim)]
    concatenate x1 -> x0, other arithmetic: 3.45 us -> none  [halo_of(): return jnp.concatenate([below, above], axis=dim)]
    unnamed x19 -> x21, local copies, waits for them, and re-layouts: 7.13 us -> 8.47 us
where the time goes in v12:
time: 261 us
  starting transfers between devices  109 us (42%)
  Pallas kernels  73 us (28%)
  waiting for transfers between devices  31.9 us (12%)
  local copies, waits for them, and re-layouts  18.4 us (7%)
  matrix products  10.5 us (4%)
  other arithmetic  9.73 us (4%)
  between operations  8.93 us (3%)
    pallas_call x1, Pallas kernels, smooth(): pl.pallas_call(kernel, grid=(rows // block,), in_specs=[pl.BlockSpec(coef...  73 us
    ppermute x12, starting transfers between devices, reduce_scatter_slab(): part = keep + lax.ppermute(send, axis, [(i, i ^ bit) for i in range(size)])  72.7 us
    ppermute x12, starting transfers between devices, shift(): return lax.ppermute(v, axis, [(i, (i + step) % size) for i in range(size)])  18.2 us
    ppermute x12, waiting for transfers between devices, shift(): return lax.ppermute(v, axis, [(i, (i + step) % size) for i in range(size)])  13.4 us
    ppermute x12, waiting for transfers between devices, reduce_scatter_slab(): part = keep + lax.ppermute(send, axis, [(i, i ^ bit) for i in range(size)])  12.8 us
    dot_general x3, matrix products, body(): lax.dot_general(flat, received, (((1,), (1,)), ((), ())), preferred_eleme...  10.5 us
    unnamed x21, local copies, waits for them, and re-layouts  8.47 us
    ppermute x2, starting transfers between devices, halo_of(): below = lax.ppermute(top, axis, up)  6.13 us
  transfers between devices with their start and end apart: 34, of which 15 were waited for; matrix products, arithmetic and copies ran while one was open for 10% of the time, Pallas kernels for 0%

profile of v12, /device:TPU:0, one launch (start us, length us, event | category | flops | bytes accessed | tf_op | source)
XLA Modules:
  0.0 261.3 jit_solution(13577846561709630566)
XLA Ops:
  0.6 4.8 %fusion.26 = (bf16[1024,4,256]{2,1,0:T(4,128)(2,1)S(1)}, bf16[1024,4,256]{2,1,0:T(4,128)(2,1)S(1)}) fusion(bf16[1024,8,256]{2,1,0:T(8,128)(2,1)} %a_ref.1), kind=kLoop, calls=%fused_computation.80 | loop fusion | bytes 8388608 | tf_op jit(solution)/shard_map/slice | solution.py:62
  5.5 1.4 collective-permute-start.2
  6.9 1.3 collective-permute-start.3
  8.3 4.7 %collective-permute-start = (f32[4,256]{1,0:T(4,128)S(1)}, f32[4,256]{1,0:T(4,128)S(1)}, u32[]{:S(2)}, u32[]{:S(2)}) collective-permute-start(f32[4,256]{1,0:T(4,128)S(1)} %get-tuple-element.16), channel_id=1, source_target_pairs={{0,1},{1,2},{2,3},{3,4},{4,5},{5,6},{6,7},{7,8},{8,9},{9,10},{10,1... | collective-permute-start | bytes 12296 | tf_op jit(solution)/shard_map/ppermute | solution.py:63
  13.0 1.3 collective-permute-start.1
  14.4 2.9 %collective-permute-done.1 = f32[4,256]{1,0:T(4,128)S(1)} collective-permute-done((f32[4,256]{1,0:T(4,128)S(1)}, f32[4,256]{1,0:T(4,128)S(1)}, u32[]{:S(2)}, u32[]{:S(2)}) %collective-permute-start.1) | collective-permute-done | bytes 4128 | tf_op jit(solution)/shard_map/ppermute | solution.py:64
  18.8 73.0 %shard_map.59 = f32[1024,8,256]{2,1,0:T(8,128)} custom-call(f32[6,16,256]{2,1,0:T(8,128)} %copy-done.3, bf16[1024,8,256]{2,1,0:T(8,128)(2,1)} %a_ref.1, bf16[1024,4,256]{2,1,0:T(4,128)(2,1)} %copy-done.1, bf16[1024,4,256]{2,1,0:T(4,128)(2,1)} %collective-permute-done.3.hi_ref), custom_call_target="tpu_custom_call" | custom-call | tf_op jit(solution)/shard_map/pallas_call | solution.py:146
  91.9 3.8 %convert.5 = bf16[1024,8,256]{2,1,0:T(8,128)(2,1)S(1)} convert(f32[1024,8,256]{2,1,0:T(8,128)} %shard_map.59) | non-fusion elementwise | flops 2097152 | bytes 12582912 | tf_op jit(solution)/shard_map/convert.2
  96.8 1.6 collective-permute-start.4
  107.4 5.6 %copy.17 = bf16[128,8,8,256]{3,1,2,0:T(8,128)(2,1)} copy(bf16[128,8,8,256]{3,2,1,0:T(8,128)(2,1)} %bitcast.84) | data formatting | bytes 8388608
  113.4 1.7 collective-permute-start.24
  116.3 2.0 collective-permute-start.5
  118.3 2.2 collective-permute-start.6
  120.6 3.2 %collective-permute-start.16 = (bf16[128,2048]{1,0:T(8,128)(2,1)S(1)}, bf16[128,2048]{1,0:T(8,128)(2,1)S(1)}, u32[]{:S(2)}, u32[]{:S(2)}) collective-permute-start(bf16[128,2048]{1,0:T(8,128)(2,1)S(1)} %broadcast_select_fusion.1), channel_id=1, source_target_pairs={{0,96},{16,112},{32,0},{48,16},{64,32},{80,48},{96,64},{112,80},{1... | collective-permute-start | bytes 1572872 | tf_op jit(solution)/shard_map/ppermute | solution.py:28
  123.8 2.6 %collective-permute-done.24 = bf16[128,2048]{1,0:T(8,128)(2,1)S(1)} collective-permute-done((bf16[128,2048]{1,0:T(8,128)(2,1)S(1)}, bf16[128,2048]{1,0:T(8,128)(2,1)S(1)}, u32[]{:S(2)}, u32[]{:S(2)}) %collective-permute-start.24) | collective-permute-done | bytes 524320 | tf_op jit(solution)/shard_map/ppermute | solution.py:30
  126.5 2.0 collective-permute-start.25
  128.5 2.2 collective-permute-start.26
  130.9 2.2 collective-permute-done.15
  133.2 2.0 collective-permute-start.8
  135.4 3.4 %collective-permute-done.25 = bf16[128,2048]{1,0:T(8,128)(2,1)S(1)} collective-permute-done((bf16[128,2048]{1,0:T(8,128)(2,1)S(1)}, bf16[128,2048]{1,0:T(8,128)(2,1)S(1)}, u32[]{:S(2)}, u32[]{:S(2)}) %collective-permute-start.25) | collective-permute-done | bytes 524320 | tf_op jit(solution)/shard_map/ppermute | solution.py:28
  138.8 2.0 collective-permute-start.18
  141.0 2.5 collective-permute-done.7
  143.5 2.3 collective-permute-start.28
  146.0 1.8 collective-permute-start.9
  147.8 1.4 collective-permute-done.17
  149.6 1.8 collective-permute-start.19
  151.4 3.4 %collective-permute-done.27 = bf16[64,2048]{1,0:T(8,128)(2,1)S(1)} collective-permute-done((bf16[64,2048]{1,0:T(8,128)(2,1)S(1)}, bf16[64,2048]{1,0:T(8,128)(2,1)S(1)}, u32[]{:S(2)}, u32[]{:S(2)}) %collective-permute-start.27) | collective-permute-done | bytes 262176 | tf_op jit(solution)/shard_map/ppermute | solution.py:28
  156.0 1.7 collective-permute-start.29
  157.7 1.3 fusion.2
  160.2 19.5 %collective-permute-start.10 = (f32[8,64,256]{2,1,0:T(8,128)}, f32[8,64,256]{2,1,0:T(8,128)}, u32[]{:S(2)}, u32[]{:S(2)}) collective-permute-start(f32[8,64,256]{2,1,0:T(8,128)} %dynamic-slice_bitcast_fusion.2), channel_id=1, source_target_pairs={{0,1},{1,0},{2,3},{3,2},{4,5},{5,4},{6,7},{7,6},{8,9},{9,8},{10,11... | collective-permute-start | bytes 1572872 | tf_op jit(solution)/shard_map/ppermute | solution.py:52
  179.7 4.1 %fusion.1 = f32[1024,256]{0,1:T(8,128)S(1)} fusion(bf16[1024,2048]{1,0:T(8,128)(2,1)} %bitcast.85, bf16[128,2048]{1,0:T(8,128)(2,1)} %collective-permute-done.19, bf16[128,2048]{1,0:T(8,128)(2,1)} %copy-done.2, pred[]{:T(512)S(6)} %eq.83), kind=kOutput, calls=%fused_computation.3 | convolution fusion | flops 1078722560 | bytes 6291457 | tf_op jit(solution)/shard_map/dot_general | solution.py:176
  185.0 3.2 %collective-permute-start.20 = (f32[8,64,256]{2,1,0:T(8,128)}, f32[8,64,256]{2,1,0:T(8,128)}, u32[]{:S(2)}, u32[]{:S(2)}) collective-permute-start(f32[8,64,256]{2,1,0:T(8,128)} %dynamic-slice_bitcast_fusion.1), channel_id=1, source_target_pairs={{0,1},{1,0},{2,3},{3,2},{4,5},{5,4},{6,7},{7,6},{8,9},{9,8},{10,11... | collective-permute-start | bytes 1572872 | tf_op jit(solution)/shard_map/ppermute | solution.py:52
  188.3 5.1 %fusion = f32[1024,256]{0,1:T(8,128)} fusion(bf16[1024,2048]{1,0:T(8,128)(2,1)} %bitcast.86, bf16[128,2048]{1,0:T(8,128)(2,1)} %collective-permute-done.29, bf16[128,2048]{1,0:T(8,128)(2,1)} %maximum_select_fusion.8, pred[]{:T(512)S(6)} %eq.87), kind=kOutput, calls=%fused_computation.1 | convolution fusion | flops 1078722560 | bytes 6291457 | tf_op jit(solution)/shard_map/dot_general | solution.py:176
  193.4 1.6 copy.14
  195.3 1.1 bitcast_add_fusion.2
  196.5 30.2 %collective-permute-start.11 = (f32[4,64,256]{2,1,0:T(8,128)S(1)}, f32[4,64,256]{2,1,0:T(8,128)S(1)}, u32[]{:S(2)}, u32[]{:S(2)}) collective-permute-start(f32[4,64,256]{2,1,0:T(8,128)S(1)} %dynamic-slice_bitcast_fusion.5), channel_id=1, source_target_pairs={{0,2},{1,3},{2,0},{3,1},{4,6},{5,7},{6,4},{7,5},{8,10},{9,11},{10,... | collective-permute-start | bytes 786440 | tf_op jit(solution)/shard_map/ppermute | solution.py:52
  226.7 1.1 bitcast_add_fusion.1
  228.1 2.1 collective-permute-start.31
  230.1 3.7 %collective-permute-done.11 = f32[4,64,256]{2,1,0:T(8,128)S(1)} collective-permute-done((f32[4,64,256]{2,1,0:T(8,128)S(1)}, f32[4,64,256]{2,1,0:T(8,128)S(1)}, u32[]{:S(2)}, u32[]{:S(2)}) %collective-permute-start.11) | collective-permute-done | bytes 262176 | tf_op jit(solution)/shard_map/ppermute | solution.py:52
  233.9 3.0 %collective-permute-start.12 = (f32[2,64,256]{2,1,0:T(8,128)S(1)}, f32[2,64,256]{2,1,0:T(8,128)S(1)}, u32[]{:S(2)}, u32[]{:S(2)}) collective-permute-start(f32[2,64,256]{2,1,0:T(8,128)S(1)} %dynamic-slice_bitcast_fusion.8), channel_id=1, source_target_pairs={{0,4},{1,5},{2,6},{3,7},{4,0},{5,1},{6,2},{7,3},{8,12},{9,13},{10,... | collective-permute-start | bytes 393224 | tf_op jit(solution)/shard_map/ppermute | solution.py:52
  236.9 2.6 collective-permute-done.21
  239.5 3.0 %collective-permute-start.22 = (f32[2,64,256]{2,1,0:T(8,128)S(1)}, f32[2,64,256]{2,1,0:T(8,128)S(1)}, u32[]{:S(2)}, u32[]{:S(2)}) collective-permute-start(f32[2,64,256]{2,1,0:T(8,128)S(1)} %dynamic-slice_bitcast_fusion.7), channel_id=1, source_target_pairs={{0,4},{1,5},{2,6},{3,7},{4,0},{5,1},{6,2},{7,3},{8,12},{9,13},{10,... | collective-permute-start | bytes 393224 | tf_op jit(solution)/shard_map/ppermute | solution.py:52
  242.5 2.6 collective-permute-done.31
  245.2 3.0 %collective-permute-start.32 = (f32[2,64,256]{2,1,0:T(8,128)S(1)}, f32[2,64,256]{2,1,0:T(8,128)S(1)}, u32[]{:S(2)}, u32[]{:S(2)}) collective-permute-start(f32[2,64,256]{2,1,0:T(8,128)S(1)} %dynamic-slice_bitcast_fusion.6), channel_id=1, source_target_pairs={{0,4},{1,5},{2,6},{3,7},{4,0},{5,1},{6,2},{7,3},{8,12},{9,13},{10,... | collective-permute-start | bytes 393224 | tf_op jit(solution)/shard_map/ppermute | solution.py:52
  248.9 3.0 %collective-permute-start.13 = (f32[1,64,256]{2,1,0:T(8,128)S(1)}, f32[1,64,256]{2,1,0:T(8,128)S(1)}, u32[]{:S(2)}, u32[]{:S(2)}) collective-permute-start(f32[1,64,256]{2,1,0:T(8,128)S(1)} %constant_dynamic-slice_fusion.2), channel_id=1, source_target_pairs={{0,8},{1,9},{2,10},{3,11},{4,12},{5,13},{6,14},{7,15},{8,0},{9,1},... | collective-permute-start | bytes 196616 | tf_op jit(solution)/shard_map/ppermute | solution.py:52
  251.9 2.8 %collective-permute-start.23 = (f32[1,64,256]{2,1,0:T(8,128)S(1)}, f32[1,64,256]{2,1,0:T(8,128)S(1)}, u32[]{:S(2)}, u32[]{:S(2)}) collective-permute-start(f32[1,64,256]{2,1,0:T(8,128)S(1)} %constant_dynamic-slice_fusion.1), channel_id=1, source_target_pairs={{0,8},{1,9},{2,10},{3,11},{4,12},{5,13},{6,14},{7,15},{8,0},{9,1},... | collective-permute-start | bytes 196616 | tf_op jit(solution)/shard_map/ppermute | solution.py:52
  254.7 2.6 collective-permute-start.33
  257.8 2.8 %collective-permute-done.33 = f32[1,64,256]{2,1,0:T(8,128)S(1)} collective-permute-done((f32[1,64,256]{2,1,0:T(8,128)S(1)}, f32[1,64,256]{2,1,0:T(8,128)S(1)}, u32[]{:S(2)}, u32[]{:S(2)}) %collective-permute-start.33) | collective-permute-done | bytes 65568 | tf_op jit(solution)/shard_map/ppermute | solution.py:52
  (101 shorter events, 13.2 us)
Async XLA Ops:
  0.6 7.6 %copy-start.4 = (s32[8,256]{1,0:T(8,128)S(1)}, s32[8,256]{1,0:T(8,128)}, u32[]{:S(2)}) copy-start(s32[8,256]{1,0:T(8,128)} %param.5) | copy-start | bytes 24580
  0.6 7.6 %copy-start.6 = (f32[8]{0:T(128)S(1)}, f32[8]{0:T(128)}, u32[]{:S(2)}) copy-start(f32[8]{0:T(128)} %param.6) | copy-start | bytes 100
  5.5 12.0 %collective-permute-start.2 = (bf16[1024,4,256]{2,1,0:T(4,128)(2,1)S(1)}, bf16[1024,4,256]{2,1,0:T(4,128)(2,1)S(1)}, u32[]{:S(2)}, u32[]{:S(2)}) collective-permute-start(bf16[1024,4,256]{2,1,0:T(4,128)(2,1)S(1)} %get-tuple-element.9), channel_id=1, source_target_pairs={{0,1},{1,2},{2,3},{3,4},{4,5},{5,6},{6,7},{7,8},{8,9},{9,10},{10,1... | collective-permute-start | bytes 6291464 | tf_op jit(solution)/shard_map/ppermute | solution.py:63
  6.9 10.6 %collective-permute-start.3 = (bf16[1024,4,256]{2,1,0:T(4,128)(2,1)S(1)}, bf16[1024,4,256]{2,1,0:T(4,128)(2,1)}, u32[]{:S(2)}, u32[]{:S(2)}) collective-permute-start(bf16[1024,4,256]{2,1,0:T(4,128)(2,1)S(1)} %get-tuple-element.8), channel_id=1, source_target_pairs={{1,0},{2,1},{3,2},{4,3},{5,4},{6,5},{7,6},{8,7},{9,8},{10,9},{11,1... | collective-permute-start | bytes 6291464 | tf_op jit(solution)/shard_map/ppermute | solution.py:64
  8.3 6.1 %collective-permute-start = (f32[4,256]{1,0:T(4,128)S(1)}, f32[4,256]{1,0:T(4,128)S(1)}, u32[]{:S(2)}, u32[]{:S(2)}) collective-permute-start(f32[4,256]{1,0:T(4,128)S(1)} %get-tuple-element.16), channel_id=1, source_target_pairs={{0,1},{1,2},{2,3},{3,4},{4,5},{5,6},{6,7},{7,8},{8,9},{9,10},{10,1... | collective-permute-start | bytes 12296 | tf_op jit(solution)/shard_map/ppermute | solution.py:63
  13.0 4.3 %collective-permute-start.1 = (f32[4,256]{1,0:T(4,128)S(1)}, f32[4,256]{1,0:T(4,128)S(1)}, u32[]{:S(2)}, u32[]{:S(2)}) collective-permute-start(f32[4,256]{1,0:T(4,128)S(1)} %get-tuple-element.17), channel_id=1, source_target_pairs={{1,0},{2,1},{3,2},{4,3},{5,4},{6,5},{7,6},{8,7},{9,8},{10,9},{11,1... | collective-permute-start | bytes 12296 | tf_op jit(solution)/shard_map/ppermute | solution.py:64
  17.4 0.6 copy-start.3
  17.4 1.4 copy-start.1
  95.9 3.1 %copy-start.5 = (s32[8]{0:T(128)S(1)}, s32[8]{0:T(128)}, u32[]{:S(2)}) copy-start(s32[8]{0:T(128)} %param.7) | copy-start | bytes 100
  96.8 18.4 %collective-permute-start.4 = (bf16[128,2048]{1,0:T(8,128)(2,1)}, bf16[128,2048]{1,0:T(8,128)(2,1)}, u32[]{:S(2)}, u32[]{:S(2)}) collective-permute-start(bf16[128,2048]{1,0:T(8,128)(2,1)} %bitcast.43), channel_id=1, source_target_pairs={{0,16},{16,0},{32,48},{48,32},{64,80},{80,64},{96,112},{112,96},{1... | collective-permute-start | bytes 1572872 | tf_op jit(solution)/shard_map/ppermute | solution.py:30
  98.5 22.0 %collective-permute-start.14 = (bf16[128,2048]{1,0:T(8,128)(2,1)S(1)}, bf16[128,2048]{1,0:T(8,128)(2,1)S(1)}, u32[]{:S(2)}, u32[]{:S(2)}) collective-permute-start(bf16[128,2048]{1,0:T(8,128)(2,1)S(1)} %bitcast.115), channel_id=1, source_target_pairs={{0,16},{16,0},{32,48},{48,32},{64,80},{80,64},{96,112},{112,96},{1... | collective-permute-start | bytes 1572872 | tf_op jit(solution)/shard_map/ppermute | solution.py:30
  113.4 13.1 %collective-permute-start.24 = (bf16[128,2048]{1,0:T(8,128)(2,1)S(1)}, bf16[128,2048]{1,0:T(8,128)(2,1)S(1)}, u32[]{:S(2)}, u32[]{:S(2)}) collective-permute-start(bf16[128,2048]{1,0:T(8,128)(2,1)S(1)} %bitcast.116), channel_id=1, source_target_pairs={{0,16},{16,0},{32,48},{48,32},{64,80},{80,64},{96,112},{112,96},{1... | collective-permute-start | bytes 1572872 | tf_op jit(solution)/shard_map/ppermute | solution.py:30
  116.3 12.2 %collective-permute-start.5 = (bf16[128,2048]{1,0:T(8,128)(2,1)S(1)}, bf16[128,2048]{1,0:T(8,128)(2,1)S(1)}, u32[]{:S(2)}, u32[]{:S(2)}) collective-permute-start(bf16[128,2048]{1,0:T(8,128)(2,1)S(1)} %broadcast_select_fusion.2), channel_id=1, source_target_pairs={{0,32},{16,48},{32,64},{48,80},{64,96},{80,112},{96,0},{112,16},{1... | collective-permute-start | bytes 1572872 | tf_op jit(solution)/shard_map/ppermute | solution.py:28
  118.3 12.4 %collective-permute-start.6 = (bf16[128,2048]{1,0:T(8,128)(2,1)S(1)}, bf16[128,2048]{1,0:T(8,128)(2,1)S(1)}, u32[]{:S(2)}, u32[]{:S(2)}) collective-permute-start(bf16[128,2048]{1,0:T(8,128)(2,1)S(1)} %broadcast_select_fusion.2), channel_id=1, source_target_pairs={{0,96},{16,112},{32,0},{48,16},{64,32},{80,48},{96,64},{112,80},{1... | collective-permute-start | bytes 1572872 | tf_op jit(solution)/shard_map/ppermute | solution.py:28
  120.5 12.6 %collective-permute-start.15 = (bf16[128,2048]{1,0:T(8,128)(2,1)S(1)}, bf16[128,2048]{1,0:T(8,128)(2,1)S(1)}, u32[]{:S(2)}, u32[]{:S(2)}) collective-permute-start(bf16[128,2048]{1,0:T(8,128)(2,1)S(1)} %broadcast_select_fusion.1), channel_id=1, source_target_pairs={{0,32},{16,48},{32,64},{48,80},{64,96},{80,112},{96,0},{112,16},{1... | collective-permute-start | bytes 1572872 | tf_op jit(solution)/shard_map/ppermute | solution.py:28
  120.6 14.6 %collective-permute-start.16 = (bf16[128,2048]{1,0:T(8,128)(2,1)S(1)}, bf16[128,2048]{1,0:T(8,128)(2,1)S(1)}, u32[]{:S(2)}, u32[]{:S(2)}) collective-permute-start(bf16[128,2048]{1,0:T(8,128)(2,1)S(1)} %broadcast_select_fusion.1), channel_id=1, source_target_pairs={{0,96},{16,112},{32,0},{48,16},{64,32},{80,48},{96,64},{112,80},{1... | collective-permute-start | bytes 1572872 | tf_op jit(solution)/shard_map/ppermute | solution.py:28
  126.5 12.3 %collective-permute-start.25 = (bf16[128,2048]{1,0:T(8,128)(2,1)S(1)}, bf16[128,2048]{1,0:T(8,128)(2,1)S(1)}, u32[]{:S(2)}, u32[]{:S(2)}) collective-permute-start(bf16[128,2048]{1,0:T(8,128)(2,1)S(1)} %broadcast_select_fusion), channel_id=1, source_target_pairs={{0,32},{16,48},{32,64},{48,80},{64,96},{80,112},{96,0},{112,16},{1... | collective-permute-start | bytes 1572872 | tf_op jit(solution)/shard_map/ppermute | solution.py:28
  128.5 12.3 %collective-permute-start.26 = (bf16[128,2048]{1,0:T(8,128)(2,1)S(1)}, bf16[128,2048]{1,0:T(8,128)(2,1)S(1)}, u32[]{:S(2)}, u32[]{:S(2)}) collective-permute-start(bf16[128,2048]{1,0:T(8,128)(2,1)S(1)} %broadcast_select_fusion), channel_id=1, source_target_pairs={{0,96},{16,112},{32,0},{48,16},{64,32},{80,48},{96,64},{112,80},{1... | collective-permute-start | bytes 1572872 | tf_op jit(solution)/shard_map/ppermute | solution.py:28
  130.8 12.7 %collective-permute-start.7 = (bf16[64,2048]{1,0:T(8,128)(2,1)S(1)}, bf16[64,2048]{1,0:T(8,128)(2,1)S(1)}, u32[]{:S(2)}, u32[]{:S(2)}) collective-permute-start(bf16[64,2048]{1,0:T(8,128)(2,1)S(1)} %get-tuple-element.10), channel_id=1, source_target_pairs={{0,32},{16,48},{32,64},{48,80},{64,96},{80,112},{96,0},{112,16},{1... | collective-permute-start | bytes 786440 | tf_op jit(solution)/shard_map/ppermute | solution.py:28
  133.2 12.7 %collective-permute-start.8 = (bf16[64,2048]{1,0:T(8,128)(2,1)S(1)}, bf16[64,2048]{1,0:T(8,128)(2,1)S(1)}, u32[]{:S(2)}, u32[]{:S(2)}) collective-permute-start(bf16[64,2048]{1,0:T(8,128)(2,1)S(1)} %get-tuple-element.11), channel_id=1, source_target_pairs={{0,96},{16,112},{32,0},{48,16},{64,32},{80,48},{96,64},{112,80},{1... | collective-permute-start | bytes 786440 | tf_op jit(solution)/shard_map/ppermute | solution.py:28
  135.3 13.8 %collective-permute-start.17 = (bf16[64,2048]{1,0:T(8,128)(2,1)S(1)}, bf16[64,2048]{1,0:T(8,128)(2,1)S(1)}, u32[]{:S(2)}, u32[]{:S(2)}) collective-permute-start(bf16[64,2048]{1,0:T(8,128)(2,1)S(1)} %get-tuple-element.12), channel_id=1, source_target_pairs={{0,32},{16,48},{32,64},{48,80},{64,96},{80,112},{96,0},{112,16},{1... | collective-permute-start | bytes 786440 | tf_op jit(solution)/shard_map/ppermute | solution.py:28
  138.8 10.6 %collective-permute-start.18 = (bf16[64,2048]{1,0:T(8,128)(2,1)S(1)}, bf16[64,2048]{1,0:T(8,128)(2,1)S(1)}, u32[]{:S(2)}, u32[]{:S(2)}) collective-permute-start(bf16[64,2048]{1,0:T(8,128)(2,1)S(1)} %get-tuple-element.13), channel_id=1, source_target_pairs={{0,96},{16,112},{32,0},{48,16},{64,32},{80,48},{96,64},{112,80},{1... | collective-permute-start | bytes 786440 | tf_op jit(solution)/shard_map/ppermute | solution.py:28
  140.9 13.8 %collective-permute-start.27 = (bf16[64,2048]{1,0:T(8,128)(2,1)S(1)}, bf16[64,2048]{1,0:T(8,128)(2,1)S(1)}, u32[]{:S(2)}, u32[]{:S(2)}) collective-permute-start(bf16[64,2048]{1,0:T(8,128)(2,1)S(1)} %get-tuple-element.14), channel_id=1, source_target_pairs={{0,32},{16,48},{32,64},{48,80},{64,96},{80,112},{96,0},{112,16},{1... | collective-permute-start | bytes 786440 | tf_op jit(solution)/shard_map/ppermute | solution.py:28
  143.5 14.2 %copy-start = (bf16[128,8,8,256]{3,1,2,0:T(8,128)(2,1)S(1)}, bf16[128,8,8,256]{3,1,2,0:T(8,128)(2,1)}, u32[]{:S(2)}) copy-start(bf16[128,8,8,256]{3,1,2,0:T(8,128)(2,1)} %copy.17) | copy-start | bytes 12582916
  143.5 11.5 %collective-permute-start.28 = (bf16[64,2048]{1,0:T(8,128)(2,1)S(1)}, bf16[64,2048]{1,0:T(8,128)(2,1)S(1)}, u32[]{:S(2)}, u32[]{:S(2)}) collective-permute-start(bf16[64,2048]{1,0:T(8,128)(2,1)S(1)} %get-tuple-element.15), channel_id=1, source_target_pairs={{0,96},{16,112},{32,0},{48,16},{64,32},{80,48},{96,64},{112,80},{1... | collective-permute-start | bytes 786440 | tf_op jit(solution)/shard_map/ppermute | solution.py:28
  146.0 11.7 %collective-permute-start.9 = (bf16[128,2048]{1,0:T(8,128)(2,1)S(1)}, bf16[128,2048]{1,0:T(8,128)(2,1)S(1)}, u32[]{:S(2)}, u32[]{:S(2)}) collective-permute-start(bf16[128,2048]{1,0:T(8,128)(2,1)S(1)} %maximum_select_fusion.6), channel_id=1, source_target_pairs={{0,16},{16,0},{32,48},{48,32},{64,80},{80,64},{96,112},{112,96},{1... | collective-permute-start | bytes 1572872 | tf_op jit(solution)/shard_map/ppermute | solution.py:37
  149.6 9.8 %copy-start.2 = (bf16[128,2048]{1,0:T(8,128)(2,1)}, bf16[128,2048]{1,0:T(8,128)(2,1)S(1)}, u32[]{:S(2)}) copy-start(bf16[128,2048]{1,0:T(8,128)(2,1)S(1)} %maximum_select_fusion.7) | copy-start | bytes 1572868
  149.6 30.1 %collective-permute-start.19 = (bf16[128,2048]{1,0:T(8,128)(2,1)S(1)}, bf16[128,2048]{1,0:T(8,128)(2,1)}, u32[]{:S(2)}, u32[]{:S(2)}) collective-permute-start(bf16[128,2048]{1,0:T(8,128)(2,1)S(1)} %maximum_select_fusion.7), channel_id=1, source_target_pairs={{0,16},{16,0},{32,48},{48,32},{64,80},{80,64},{96,112},{112,96},{1... | collective-permute-start | bytes 1572872 | tf_op jit(solution)/shard_map/ppermute | solution.py:37
  156.0 32.3 %collective-permute-start.29 = (bf16[128,2048]{1,0:T(8,128)(2,1)}, bf16[128,2048]{1,0:T(8,128)(2,1)}, u32[]{:S(2)}, u32[]{:S(2)}) collective-permute-start(bf16[128,2048]{1,0:T(8,128)(2,1)} %maximum_select_fusion.8), channel_id=1, source_target_pairs={{0,16},{16,0},{32,48},{48,32},{64,80},{80,64},{96,112},{112,96},{1... | collective-permute-start | bytes 1572872 | tf_op jit(solution)/shard_map/ppermute | solution.py:37
  160.2 35.1 %collective-permute-start.10 = (f32[8,64,256]{2,1,0:T(8,128)}, f32[8,64,256]{2,1,0:T(8,128)}, u32[]{:S(2)}, u32[]{:S(2)}) collective-permute-start(f32[8,64,256]{2,1,0:T(8,128)} %dynamic-slice_bitcast_fusion.2), channel_id=1, source_target_pairs={{0,1},{1,0},{2,3},{3,2},{4,5},{5,4},{6,7},{7,6},{8,9},{9,8},{10,11... | collective-permute-start | bytes 1572872 | tf_op jit(solution)/shard_map/ppermute | solution.py:52
  185.0 41.7 %collective-permute-start.20 = (f32[8,64,256]{2,1,0:T(8,128)}, f32[8,64,256]{2,1,0:T(8,128)}, u32[]{:S(2)}, u32[]{:S(2)}) collective-permute-start(f32[8,64,256]{2,1,0:T(8,128)} %dynamic-slice_bitcast_fusion.1), channel_id=1, source_target_pairs={{0,1},{1,0},{2,3},{3,2},{4,5},{5,4},{6,7},{7,6},{8,9},{9,8},{10,11... | collective-permute-start | bytes 1572872 | tf_op jit(solution)/shard_map/ppermute | solution.py:52
  195.0 32.9 %collective-permute-start.30 = (f32[8,64,256]{2,1,0:T(8,128)S(1)}, f32[8,64,256]{2,1,0:T(8,128)S(1)}, u32[]{:S(2)}, u32[]{:S(2)}) collective-permute-start(f32[8,64,256]{2,1,0:T(8,128)S(1)} %dynamic-slice_bitcast_fusion), channel_id=1, source_target_pairs={{0,1},{1,0},{2,3},{3,2},{4,5},{5,4},{6,7},{7,6},{8,9},{9,8},{10,11... | collective-permute-start | bytes 1572872 | tf_op jit(solution)/shard_map/ppermute | solution.py:52
  196.5 37.4 %collective-permute-start.11 = (f32[4,64,256]{2,1,0:T(8,128)S(1)}, f32[4,64,256]{2,1,0:T(8,128)S(1)}, u32[]{:S(2)}, u32[]{:S(2)}) collective-permute-start(f32[4,64,256]{2,1,0:T(8,128)S(1)} %dynamic-slice_bitcast_fusion.5), channel_id=1, source_target_pairs={{0,2},{1,3},{2,0},{3,1},{4,6},{5,7},{6,4},{7,5},{8,10},{9,11},{10,... | collective-permute-start | bytes 786440 | tf_op jit(solution)/shard_map/ppermute | solution.py:52
  227.8 11.6 %collective-permute-start.21 = (f32[4,64,256]{2,1,0:T(8,128)S(1)}, f32[4,64,256]{2,1,0:T(8,128)S(1)}, u32[]{:S(2)}, u32[]{:S(2)}) collective-permute-start(f32[4,64,256]{2,1,0:T(8,128)S(1)} %dynamic-slice_bitcast_fusion.4), channel_id=1, source_target_pairs={{0,2},{1,3},{2,0},{3,1},{4,6},{5,7},{6,4},{7,5},{8,10},{9,11},{10,... | collective-permute-start | bytes 786440 | tf_op jit(solution)/shard_map/ppermute | solution.py:52
  228.1 17.0 %collective-permute-start.31 = (f32[4,64,256]{2,1,0:T(8,128)S(1)}, f32[4,64,256]{2,1,0:T(8,128)S(1)}, u32[]{:S(2)}, u32[]{:S(2)}) collective-permute-start(f32[4,64,256]{2,1,0:T(8,128)S(1)} %dynamic-slice_bitcast_fusion.3), channel_id=1, source_target_pairs={{0,2},{1,3},{2,0},{3,1},{4,6},{5,7},{6,4},{7,5},{8,10},{9,11},{10,... | collective-permute-start | bytes 786440 | tf_op jit(solution)/shard_map/ppermute | solution.py:52
  233.9 14.9 %collective-permute-start.12 = (f32[2,64,256]{2,1,0:T(8,128)S(1)}, f32[2,64,256]{2,1,0:T(8,128)S(1)}, u32[]{:S(2)}, u32[]{:S(2)}) collective-permute-start(f32[2,64,256]{2,1,0:T(8,128)S(1)} %dynamic-slice_bitcast_fusion.8), channel_id=1, source_target_pairs={{0,4},{1,5},{2,6},{3,7},{4,0},{5,1},{6,2},{7,3},{8,12},{9,13},{10,... | collective-permute-start | bytes 393224 | tf_op jit(solution)/shard_map/ppermute | solution.py:52
  239.5 12.4 %collective-permute-start.22 = (f32[2,64,256]{2,1,0:T(8,128)S(1)}, f32[2,64,256]{2,1,0:T(8,128)S(1)}, u32[]{:S(2)}, u32[]{:S(2)}) collective-permute-start(f32[2,64,256]{2,1,0:T(8,128)S(1)} %dynamic-slice_bitcast_fusion.7), channel_id=1, source_target_pairs={{0,4},{1,5},{2,6},{3,7},{4,0},{5,1},{6,2},{7,3},{8,12},{9,13},{10,... | collective-permute-start | bytes 393224 | tf_op jit(solution)/shard_map/ppermute | solution.py:52
  245.2 9.5 %collective-permute-start.32 = (f32[2,64,256]{2,1,0:T(8,128)S(1)}, f32[2,64,256]{2,1,0:T(8,128)S(1)}, u32[]{:S(2)}, u32[]{:S(2)}) collective-permute-start(f32[2,64,256]{2,1,0:T(8,128)S(1)} %dynamic-slice_bitcast_fusion.6), channel_id=1, source_target_pairs={{0,4},{1,5},{2,6},{3,7},{4,0},{5,1},{6,2},{7,3},{8,12},{9,13},{10,... | collective-permute-start | bytes 393224 | tf_op jit(solution)/shard_map/ppermute | solution.py:52
  248.9 8.4 %collective-permute-start.13 = (f32[1,64,256]{2,1,0:T(8,128)S(1)}, f32[1,64,256]{2,1,0:T(8,128)S(1)}, u32[]{:S(2)}, u32[]{:S(2)}) collective-permute-start(f32[1,64,256]{2,1,0:T(8,128)S(1)} %constant_dynamic-slice_fusion.2), channel_id=1, source_target_pairs={{0,8},{1,9},{2,10},{3,11},{4,12},{5,13},{6,14},{7,15},{8,0},{9,1},... | collective-permute-start | bytes 196616 | tf_op jit(solution)/shard_map/ppermute | solution.py:52
  251.9 5.8 %collective-permute-start.23 = (f32[1,64,256]{2,1,0:T(8,128)S(1)}, f32[1,64,256]{2,1,0:T(8,128)S(1)}, u32[]{:S(2)}, u32[]{:S(2)}) collective-permute-start(f32[1,64,256]{2,1,0:T(8,128)S(1)} %constant_dynamic-slice_fusion.1), channel_id=1, source_target_pairs={{0,8},{1,9},{2,10},{3,11},{4,12},{5,13},{6,14},{7,15},{8,0},{9,1},... | collective-permute-start | bytes 196616 | tf_op jit(solution)/shard_map/ppermute | solution.py:52
  254.7 5.8 %collective-permute-start.33 = (f32[1,64,256]{2,1,0:T(8,128)S(1)}, f32[1,64,256]{2,1,0:T(8,128)S(1)}, u32[]{:S(2)}, u32[]{:S(2)}) collective-permute-start(f32[1,64,256]{2,1,0:T(8,128)S(1)} %constant_dynamic-slice_fusion), channel_id=1, source_target_pairs={{0,8},{1,9},{2,10},{3,11},{4,12},{5,13},{6,14},{7,15},{8,0},{9,1},... | collective-permute-start | bytes 196616 | tf_op jit(solution)/shard_map/ppermute | solution.py:52

commit v13 on v12

--- a/solution.py
+++ b/solution.py
@@ -65,7 +65,8 @@
     return below, above
 
 
-def smooth_kernel(coef_ref, a_ref, lo_ref, hi_ref, o_ref, *, sub):
+def smooth_kernel(coef_ref, a_ref, lo_ref, hi_ref, *refs, sub, aliased):
+    o_ref = refs[-1]
     depth, lat = a_ref.shape[1], a_ref.shape[2]
     half = lat // 2
     shape = (sub, depth, half)
@@ -140,21 +141,28 @@
     )
 
 
-def smooth(sensitivity, below, above, coef, block=128, sub=16):
+def smooth(sensitivity, below, above, coef, field, first, count, block=128, sub=16):
     rows, depth, lat = sensitivity.shape
-    kernel = functools.partial(smooth_kernel, sub=sub)
+    aliased = field is not None
+    kernel = functools.partial(smooth_kernel, sub=sub, aliased=aliased)
+    in_specs = [
+        pl.BlockSpec(coef.shape, lambda i: (0, 0, 0)),
+        pl.BlockSpec((block, depth, lat), lambda i: (i + first, 0, 0)),
+        pl.BlockSpec((block, HALO, lat), lambda i: (i + first, 0, 0)),
+        pl.BlockSpec((block, HALO, lat), lambda i: (i + first, 0, 0)),
+    ]
+    args = [coef, sensitivity, below, above]
+    if aliased:
+        in_specs.append(pl.BlockSpec(memory_space=pl.ANY))
+        args.append(field)
     return pl.pallas_call(
         kernel,
-        grid=(rows // block,),
-        in_specs=[
-            pl.BlockSpec(coef.shape, lambda i: (0, 0, 0)),
-            pl.BlockSpec((block, depth, lat), lambda i: (i, 0, 0)),
-            pl.BlockSpec((block, HALO, lat), lambda i: (i, 0, 0)),
-            pl.BlockSpec((block, HALO, lat), lambda i: (i, 0, 0)),
-        ],
-        out_specs=pl.BlockSpec((block, depth, lat), lambda i: (i, 0, 0)),
+        grid=(count,),
+        in_specs=in_specs,
+        out_specs=pl.BlockSpec((block, depth, lat), lambda i: (i + first, 0, 0)),
         out_shape=jax.ShapeDtypeStruct((rows, depth, lat), jnp.float32),
-    )(coef, sensitivity, below, above)
+        input_output_aliases={4: 0} if aliased else {},
+    )(*args)
 
 
 def body(sensitivity, cell_class, class_rate, panel_owner):
@@ -165,12 +173,16 @@
     kappa = jnp.sum(onehot * class_rate[None, None, :], axis=-1)
     below, above = halo_of(sensitivity, "slab", 1)
     kappa_col = jnp.concatenate([halo_of(kappa, "slab", 0)[0], kappa, halo_of(kappa, "slab", 0)[1]], axis=0)
-    field = smooth(sensitivity, below, above, coefficients(kappa_col, lat))
+    coef = coefficients(kappa_col, lat)
+    block = 128
+    head = PANELS * PANEL // block
+    early = smooth(sensitivity, below, above, coef, None, 0, head, block)
+    field = smooth(sensitivity, below, above, coef, early, head, rows // block - head, block)
     cells = depth * lat * lax.axis_size("slab")
     flat = sensitivity.reshape(rows, depth * lat)
     partials = []
     for p in range(PANELS):
-        piece = field[p * PANEL : (p + 1) * PANEL].reshape(PANEL, depth * lat).astype(jnp.bfloat16)
+        piece = early[p * PANEL : (p + 1) * PANEL].reshape(PANEL, depth * lat).astype(jnp.bfloat16)
         received = broadcast_dp(piece, panel_owner[p], "dp")
         term = (
             lax.dot_general(

time: 261 us -> 264 us (1.011)
  starting transfers between devices: 109 us -> 103 us
  waiting for transfers between devices: 31.9 us -> 36.2 us
    ppermute x12, waiting for transfers between devices: 13.4 us -> 20.4 us  [shift(): return lax.ppermute(v, axis, [(i, (i + step) % size) for i in range(size)])]
    ppermute x3, starting transfers between devices: 5.38 us -> 0.17 us  [broadcast_dp(): other = lax.ppermute(val, axis, [(i, i ^ 1) for i in range(size)])]
    pallas_call x1 -> x2, Pallas kernels: 73 us -> 75.3 us  [smooth(): pl.pallas_call(kernel, grid=(count,), in_specs=in_specs, out_specs=pl.Blo...]
  transfers between devices with their start and end apart: 34 -> 34, of which waited for: 15 -> 15; matrix products, arithmetic and copies ran while one was open for 10% -> 11% of each run, Pallas kernels for 0% -> 8%
where the time goes in v13:
time: 264 us
  starting transfers between devices  103 us (39%)
  Pallas kernels  75.3 us (29%)
  waiting for transfers between devices  36.2 us (14%)
  local copies, waits for them, and re-layouts  18.5 us (7%)
  other arithmetic  10.8 us (4%)
  matrix products  10.6 us (4%)
  between operations  8.88 us (3%)
    pallas_call x2, Pallas kernels, smooth(): pl.pallas_call(kernel, grid=(count,), in_specs=in_specs, out_specs=pl.Blo...  75.3 us
    ppermute x12, starting transfers between devices, reduce_scatter_slab(): part = keep + lax.ppermute(send, axis, [(i, i ^ bit) for i in range(size)])  74.4 us
    ppermute x12, waiting for transfers between devices, shift(): return lax.ppermute(v, axis, [(i, (i + step) % size) for i in range(size)])  20.4 us
    ppermute x12, starting transfers between devices, shift(): return lax.ppermute(v, axis, [(i, (i + step) % size) for i in range(size)])  16.3 us
    ppermute x12, waiting for transfers between devices, reduce_scatter_slab(): part = keep + lax.ppermute(send, axis, [(i, i ^ bit) for i in range(size)])  12.8 us
    dot_general x3, matrix products, body(): lax.dot_general(flat, received, (((1,), (1,)), ((), ())), preferred_eleme...  10.6 us
    unnamed x21, local copies, waits for them, and re-layouts  8.5 us
    ppermute x2, starting transfers between devices, halo_of(): below = lax.ppermute(top, axis, up)  6.13 us
  transfers between devices with their start and end apart: 34, of which 15 were waited for; matrix products, arithmetic and copies ran while one was open for 11% of the time, Pallas kernels for 8%

profile of v13, /device:TPU:0, one launch (start us, length us, event | category | flops | bytes accessed | tf_op | source)
XLA Modules:
  0.0 263.5 jit_solution(15707331430057864031)
XLA Ops:
  0.6 4.8 %fusion.26 = (bf16[1024,4,256]{2,1,0:T(4,128)(2,1)S(1)}, bf16[1024,4,256]{2,1,0:T(4,128)(2,1)S(1)}) fusion(bf16[1024,8,256]{2,1,0:T(8,128)(2,1)} %a_ref.3), kind=kLoop, calls=%fused_computation.80 | loop fusion | bytes 8388608 | tf_op jit(solution)/shard_map/slice | solution.py:62
  5.5 1.4 collective-permute-start.2
  6.9 1.3 collective-permute-start.3
  8.3 4.7 %collective-permute-start = (f32[4,256]{1,0:T(4,128)S(1)}, f32[4,256]{1,0:T(4,128)S(1)}, u32[]{:S(2)}, u32[]{:S(2)}) collective-permute-start(f32[4,256]{1,0:T(4,128)S(1)} %get-tuple-element.16), channel_id=1, source_target_pairs={{0,1},{1,2},{2,3},{3,4},{4,5},{5,6},{6,7},{7,8},{8,9},{9,10},{10,1... | collective-permute-start | bytes 12296 | tf_op jit(solution)/shard_map/ppermute | solution.py:63
  13.0 1.3 collective-permute-start.1
  14.4 2.9 %collective-permute-done.1 = f32[4,256]{1,0:T(4,128)S(1)} collective-permute-done((f32[4,256]{1,0:T(4,128)S(1)}, f32[4,256]{1,0:T(4,128)S(1)}, u32[]{:S(2)}, u32[]{:S(2)}) %collective-permute-start.1) | collective-permute-done | bytes 4128 | tf_op jit(solution)/shard_map/ppermute | solution.py:64
  18.8 55.3 %shard_map.59.refs_0_ = f32[1024,8,256]{2,1,0:T(8,128)} custom-call(f32[6,16,256]{2,1,0:T(8,128)} %copy-done.3, bf16[1024,8,256]{2,1,0:T(8,128)(2,1)} %a_ref.3, bf16[1024,4,256]{2,1,0:T(4,128)(2,1)} %copy-done, bf16[1024,4,256]{2,1,0:T(4,128)(2,1)} %collective-permute-done.3.hi_ref), custom_call_target="tpu_custom_call" | custom-call | tf_op jit(solution)/shard_map/pallas_call | solution.py:158
  74.2 3.8 %convert.5 = bf16[1024,8,256]{2,1,0:T(8,128)(2,1)S(1)} convert(f32[1024,8,256]{2,1,0:T(8,128)} %shard_map.59.refs_0_) | non-fusion elementwise | flops 2097152 | bytes 12582912 | tf_op jit(solution)/shard_map/convert.2
  78.2 0.9 copy.17
  79.1 1.6 collective-permute-start.4
  89.7 5.6 %copy.18 = bf16[128,8,8,256]{3,1,2,0:T(8,128)(2,1)} copy(bf16[128,8,8,256]{3,2,1,0:T(8,128)(2,1)} %bitcast.84) | data formatting | bytes 8388608
  95.7 1.7 collective-permute-start.24
  97.4 20.0 %shard_map.60 = f32[1024,8,256]{2,1,0:T(8,128)} custom-call(f32[6,16,256]{2,1,0:T(8,128)} %copy-done.3, bf16[1024,8,256]{2,1,0:T(8,128)(2,1)} %a_ref.3, bf16[1024,4,256]{2,1,0:T(4,128)(2,1)} %copy-done, bf16[1024,4,256]{2,1,0:T(4,128)(2,1)} %collective-permute-done.3.hi_ref, f32[1024,8,256]{2,1,0:T(8,128)} %shard_map.59.refs_0_), custom_call_target="tpu_custom_call", output_to_operand_aliasing={{}: (4, {})} | custom-call | tf_op jit(solution)/shard_map/pallas_call | solution.py:158
  117.4 1.1 broadcast_select_fusion.2
  118.5 2.0 collective-permute-start.5
  120.5 2.2 collective-permute-start.6
  122.8 3.2 %collective-permute-start.16 = (bf16[128,2048]{1,0:T(8,128)(2,1)S(1)}, bf16[128,2048]{1,0:T(8,128)(2,1)S(1)}, u32[]{:S(2)}, u32[]{:S(2)}) collective-permute-start(bf16[128,2048]{1,0:T(8,128)(2,1)S(1)} %broadcast_select_fusion.1), channel_id=1, source_target_pairs={{0,96},{16,112},{32,0},{48,16},{64,32},{80,48},{96,64},{112,80},{1... | collective-permute-start | bytes 1572872 | tf_op jit(solution)/shard_map/ppermute | solution.py:28
  126.1 1.1 broadcast_select_fusion
  127.3 2.5 collective-permute-done.5
  129.8 2.0 collective-permute-start.26
  132.0 3.4 %collective-permute-done.15 = bf16[128,2048]{1,0:T(8,128)(2,1)S(1)} collective-permute-done((bf16[128,2048]{1,0:T(8,128)(2,1)S(1)}, bf16[128,2048]{1,0:T(8,128)(2,1)S(1)}, u32[]{:S(2)}, u32[]{:S(2)}) %collective-permute-start.15) | collective-permute-done | bytes 524320 | tf_op jit(solution)/shard_map/ppermute | solution.py:28
  135.4 2.0 collective-permute-start.8
  137.8 3.2 %collective-permute-done.25 = bf16[128,2048]{1,0:T(8,128)(2,1)S(1)} collective-permute-done((bf16[128,2048]{1,0:T(8,128)(2,1)S(1)}, bf16[128,2048]{1,0:T(8,128)(2,1)S(1)}, u32[]{:S(2)}, u32[]{:S(2)}) %collective-permute-start.25) | collective-permute-done | bytes 524320 | tf_op jit(solution)/shard_map/ppermute | solution.py:28
  141.0 2.0 collective-permute-start.18
  143.2 2.5 collective-permute-done.7
  145.8 2.3 collective-permute-start.28
  148.3 3.1 %collective-permute-done.17 = bf16[64,2048]{1,0:T(8,128)(2,1)S(1)} collective-permute-done((bf16[64,2048]{1,0:T(8,128)(2,1)S(1)}, bf16[64,2048]{1,0:T(8,128)(2,1)S(1)}, u32[]{:S(2)}, u32[]{:S(2)}) %collective-permute-start.17) | collective-permute-done | bytes 262176 | tf_op jit(solution)/shard_map/ppermute | solution.py:28
  151.9 5.1 %collective-permute-done.27 = bf16[64,2048]{1,0:T(8,128)(2,1)S(1)} collective-permute-done((bf16[64,2048]{1,0:T(8,128)(2,1)S(1)}, bf16[64,2048]{1,0:T(8,128)(2,1)S(1)}, u32[]{:S(2)}, u32[]{:S(2)}) %collective-permute-start.27) | collective-permute-done | bytes 262176 | tf_op jit(solution)/shard_map/ppermute | solution.py:28
  158.2 1.3 fusion.2
  160.7 21.2 %collective-permute-start.10 = (f32[8,64,256]{2,1,0:T(8,128)}, f32[8,64,256]{2,1,0:T(8,128)}, u32[]{:S(2)}, u32[]{:S(2)}) collective-permute-start(f32[8,64,256]{2,1,0:T(8,128)} %dynamic-slice_bitcast_fusion.2), channel_id=1, source_target_pairs={{0,1},{1,0},{2,3},{3,2},{4,5},{5,4},{6,7},{7,6},{8,9},{9,8},{10,11... | collective-permute-start | bytes 1572872 | tf_op jit(solution)/shard_map/ppermute | solution.py:52
  181.9 4.1 %fusion.1 = f32[1024,256]{0,1:T(8,128)S(1)} fusion(bf16[1024,2048]{1,0:T(8,128)(2,1)} %bitcast.85, bf16[128,2048]{1,0:T(8,128)(2,1)} %collective-permute-done.19, bf16[128,2048]{1,0:T(8,128)(2,1)} %copy-done.2, pred[]{:T(512)S(6)} %eq.83), kind=kOutput, calls=%fused_computation.3 | convolution fusion | flops 1078722560 | bytes 6291457 | tf_op jit(solution)/shard_map/dot_general | solution.py:188
  187.3 3.2 %collective-permute-start.20 = (f32[8,64,256]{2,1,0:T(8,128)}, f32[8,64,256]{2,1,0:T(8,128)}, u32[]{:S(2)}, u32[]{:S(2)}) collective-permute-start(f32[8,64,256]{2,1,0:T(8,128)} %dynamic-slice_bitcast_fusion.1), channel_id=1, source_target_pairs={{0,1},{1,0},{2,3},{3,2},{4,5},{5,4},{6,7},{7,6},{8,9},{9,8},{10,11... | collective-permute-start | bytes 1572872 | tf_op jit(solution)/shard_map/ppermute | solution.py:52
  190.5 5.1 %fusion = f32[1024,256]{0,1:T(8,128)} fusion(bf16[1024,2048]{1,0:T(8,128)(2,1)} %bitcast.86, bf16[128,2048]{1,0:T(8,128)(2,1)} %collective-permute-done.29, bf16[128,2048]{1,0:T(8,128)(2,1)} %maximum_select_fusion.8, pred[]{:T(512)S(6)} %eq.87), kind=kOutput, calls=%fused_computation.1 | convolution fusion | flops 1078722560 | bytes 6291457 | tf_op jit(solution)/shard_map/dot_general | solution.py:188
  195.6 1.6 copy.15
  197.5 1.1 bitcast_add_fusion.2
  198.7 30.2 %collective-permute-start.11 = (f32[4,64,256]{2,1,0:T(8,128)S(1)}, f32[4,64,256]{2,1,0:T(8,128)S(1)}, u32[]{:S(2)}, u32[]{:S(2)}) collective-permute-start(f32[4,64,256]{2,1,0:T(8,128)S(1)} %dynamic-slice_bitcast_fusion.5), channel_id=1, source_target_pairs={{0,2},{1,3},{2,0},{3,1},{4,6},{5,7},{6,4},{7,5},{8,10},{9,11},{10,... | collective-permute-start | bytes 786440 | tf_op jit(solution)/shard_map/ppermute | solution.py:52
  228.9 1.1 bitcast_add_fusion.1
  230.3 2.1 collective-permute-start.31
  232.4 3.7 %collective-permute-done.11 = f32[4,64,256]{2,1,0:T(8,128)S(1)} collective-permute-done((f32[4,64,256]{2,1,0:T(8,128)S(1)}, f32[4,64,256]{2,1,0:T(8,128)S(1)}, u32[]{:S(2)}, u32[]{:S(2)}) %collective-permute-start.11) | collective-permute-done | bytes 262176 | tf_op jit(solution)/shard_map/ppermute | solution.py:52
  236.1 3.0 %collective-permute-start.12 = (f32[2,64,256]{2,1,0:T(8,128)S(1)}, f32[2,64,256]{2,1,0:T(8,128)S(1)}, u32[]{:S(2)}, u32[]{:S(2)}) collective-permute-start(f32[2,64,256]{2,1,0:T(8,128)S(1)} %dynamic-slice_bitcast_fusion.8), channel_id=1, source_target_pairs={{0,4},{1,5},{2,6},{3,7},{4,0},{5,1},{6,2},{7,3},{8,12},{9,13},{10,... | collective-permute-start | bytes 393224 | tf_op jit(solution)/shard_map/ppermute | solution.py:52
  239.1 2.6 collective-permute-done.21
  241.8 3.0 %collective-permute-start.22 = (f32[2,64,256]{2,1,0:T(8,128)S(1)}, f32[2,64,256]{2,1,0:T(8,128)S(1)}, u32[]{:S(2)}, u32[]{:S(2)}) collective-permute-start(f32[2,64,256]{2,1,0:T(8,128)S(1)} %dynamic-slice_bitcast_fusion.7), channel_id=1, source_target_pairs={{0,4},{1,5},{2,6},{3,7},{4,0},{5,1},{6,2},{7,3},{8,12},{9,13},{10,... | collective-permute-start | bytes 393224 | tf_op jit(solution)/shard_map/ppermute | solution.py:52
  244.7 2.6 collective-permute-done.31
  247.4 3.0 %collective-permute-start.32 = (f32[2,64,256]{2,1,0:T(8,128)S(1)}, f32[2,64,256]{2,1,0:T(8,128)S(1)}, u32[]{:S(2)}, u32[]{:S(2)}) collective-permute-start(f32[2,64,256]{2,1,0:T(8,128)S(1)} %dynamic-slice_bitcast_fusion.6), channel_id=1, source_target_pairs={{0,4},{1,5},{2,6},{3,7},{4,0},{5,1},{6,2},{7,3},{8,12},{9,13},{10,... | collective-permute-start | bytes 393224 | tf_op jit(solution)/shard_map/ppermute | solution.py:52
  251.1 3.0 %collective-permute-start.13 = (f32[1,64,256]{2,1,0:T(8,128)S(1)}, f32[1,64,256]{2,1,0:T(8,128)S(1)}, u32[]{:S(2)}, u32[]{:S(2)}) collective-permute-start(f32[1,64,256]{2,1,0:T(8,128)S(1)} %constant_dynamic-slice_fusion.2), channel_id=1, source_target_pairs={{0,8},{1,9},{2,10},{3,11},{4,12},{5,13},{6,14},{7,15},{8,0},{9,1},... | collective-permute-start | bytes 196616 | tf_op jit(solution)/shard_map/ppermute | solution.py:52
  254.1 2.8 %collective-permute-start.23 = (f32[1,64,256]{2,1,0:T(8,128)S(1)}, f32[1,64,256]{2,1,0:T(8,128)S(1)}, u32[]{:S(2)}, u32[]{:S(2)}) collective-permute-start(f32[1,64,256]{2,1,0:T(8,128)S(1)} %constant_dynamic-slice_fusion.1), channel_id=1, source_target_pairs={{0,8},{1,9},{2,10},{3,11},{4,12},{5,13},{6,14},{7,15},{8,0},{9,1},... | collective-permute-start | bytes 196616 | tf_op jit(solution)/shard_map/ppermute | solution.py:52
  257.0 2.6 collective-permute-start.33
  260.0 2.8 %collective-permute-done.33 = f32[1,64,256]{2,1,0:T(8,128)S(1)} collective-permute-done((f32[1,64,256]{2,1,0:T(8,128)S(1)}, f32[1,64,256]{2,1,0:T(8,128)S(1)}, u32[]{:S(2)}, u32[]{:S(2)}) %collective-permute-start.33) | collective-permute-done | bytes 65568 | tf_op jit(solution)/shard_map/ppermute | solution.py:52
  (102 shorter events, 11.6 us)
Async XLA Ops:
  0.6 7.6 %copy-start.4 = (s32[8,256]{1,0:T(8,128)S(1)}, s32[8,256]{1,0:T(8,128)}, u32[]{:S(2)}) copy-start(s32[8,256]{1,0:T(8,128)} %param.5) | copy-start | bytes 24580
  0.6 7.6 %copy-start.6 = (f32[8]{0:T(128)S(1)}, f32[8]{0:T(128)}, u32[]{:S(2)}) copy-start(f32[8]{0:T(128)} %param.6) | copy-start | bytes 100
  5.5 12.0 %collective-permute-start.2 = (bf16[1024,4,256]{2,1,0:T(4,128)(2,1)S(1)}, bf16[1024,4,256]{2,1,0:T(4,128)(2,1)S(1)}, u32[]{:S(2)}, u32[]{:S(2)}) collective-permute-start(bf16[1024,4,256]{2,1,0:T(4,128)(2,1)S(1)} %get-tuple-element.9), channel_id=1, source_target_pairs={{0,1},{1,2},{2,3},{3,4},{4,5},{5,6},{6,7},{7,8},{8,9},{9,10},{10,1... | collective-permute-start | bytes 6291464 | tf_op jit(solution)/shard_map/ppermute | solution.py:63
  6.9 10.6 %collective-permute-start.3 = (bf16[1024,4,256]{2,1,0:T(4,128)(2,1)S(1)}, bf16[1024,4,256]{2,1,0:T(4,128)(2,1)}, u32[]{:S(2)}, u32[]{:S(2)}) collective-permute-start(bf16[1024,4,256]{2,1,0:T(4,128)(2,1)S(1)} %get-tuple-element.8), channel_id=1, source_target_pairs={{1,0},{2,1},{3,2},{4,3},{5,4},{6,5},{7,6},{8,7},{9,8},{10,9},{11,1... | collective-permute-start | bytes 6291464 | tf_op jit(solution)/shard_map/ppermute | solution.py:64
  8.3 6.1 %collective-permute-start = (f32[4,256]{1,0:T(4,128)S(1)}, f32[4,256]{1,0:T(4,128)S(1)}, u32[]{:S(2)}, u32[]{:S(2)}) collective-permute-start(f32[4,256]{1,0:T(4,128)S(1)} %get-tuple-element.16), channel_id=1, source_target_pairs={{0,1},{1,2},{2,3},{3,4},{4,5},{5,6},{6,7},{7,8},{8,9},{9,10},{10,1... | collective-permute-start | bytes 12296 | tf_op jit(solution)/shard_map/ppermute | solution.py:63
  13.0 4.3 %collective-permute-start.1 = (f32[4,256]{1,0:T(4,128)S(1)}, f32[4,256]{1,0:T(4,128)S(1)}, u32[]{:S(2)}, u32[]{:S(2)}) collective-permute-start(f32[4,256]{1,0:T(4,128)S(1)} %get-tuple-element.17), channel_id=1, source_target_pairs={{1,0},{2,1},{3,2},{4,3},{5,4},{6,5},{7,6},{8,7},{9,8},{10,9},{11,1... | collective-permute-start | bytes 12296 | tf_op jit(solution)/shard_map/ppermute | solution.py:64
  17.4 0.6 copy-start.3
  17.4 1.4 copy-start
  78.2 3.2 %copy-start.5 = (s32[8]{0:T(128)S(1)}, s32[8]{0:T(128)}, u32[]{:S(2)}) copy-start(s32[8]{0:T(128)} %param.7) | copy-start | bytes 100
  79.1 38.3 %collective-permute-start.4 = (bf16[128,2048]{1,0:T(8,128)(2,1)}, bf16[128,2048]{1,0:T(8,128)(2,1)}, u32[]{:S(2)}, u32[]{:S(2)}) collective-permute-start(bf16[128,2048]{1,0:T(8,128)(2,1)} %bitcast.43), channel_id=1, source_target_pairs={{0,16},{16,0},{32,48},{48,32},{64,80},{80,64},{96,112},{112,96},{1... | collective-permute-start | bytes 1572872 | tf_op jit(solution)/shard_map/ppermute | solution.py:30
  80.8 41.9 %collective-permute-start.14 = (bf16[128,2048]{1,0:T(8,128)(2,1)S(1)}, bf16[128,2048]{1,0:T(8,128)(2,1)}, u32[]{:S(2)}, u32[]{:S(2)}) collective-permute-start(bf16[128,2048]{1,0:T(8,128)(2,1)S(1)} %bitcast.115), channel_id=1, source_target_pairs={{0,16},{16,0},{32,48},{48,32},{64,80},{80,64},{96,112},{112,96},{1... | collective-permute-start | bytes 1572872 | tf_op jit(solution)/shard_map/ppermute | solution.py:30
  95.7 30.4 %collective-permute-start.24 = (bf16[128,2048]{1,0:T(8,128)(2,1)S(1)}, bf16[128,2048]{1,0:T(8,128)(2,1)}, u32[]{:S(2)}, u32[]{:S(2)}) collective-permute-start(bf16[128,2048]{1,0:T(8,128)(2,1)S(1)} %bitcast.116), channel_id=1, source_target_pairs={{0,16},{16,0},{32,48},{48,32},{64,80},{80,64},{96,112},{112,96},{1... | collective-permute-start | bytes 1572872 | tf_op jit(solution)/shard_map/ppermute | solution.py:30
  118.5 11.3 %collective-permute-start.5 = (bf16[128,2048]{1,0:T(8,128)(2,1)S(1)}, bf16[128,2048]{1,0:T(8,128)(2,1)S(1)}, u32[]{:S(2)}, u32[]{:S(2)}) collective-permute-start(bf16[128,2048]{1,0:T(8,128)(2,1)S(1)} %broadcast_select_fusion.2), channel_id=1, source_target_pairs={{0,32},{16,48},{32,64},{48,80},{64,96},{80,112},{96,0},{112,16},{1... | collective-permute-start | bytes 1572872 | tf_op jit(solution)/shard_map/ppermute | solution.py:28
  120.5 11.3 %collective-permute-start.6 = (bf16[128,2048]{1,0:T(8,128)(2,1)S(1)}, bf16[128,2048]{1,0:T(8,128)(2,1)S(1)}, u32[]{:S(2)}, u32[]{:S(2)}) collective-permute-start(bf16[128,2048]{1,0:T(8,128)(2,1)S(1)} %broadcast_select_fusion.2), channel_id=1, source_target_pairs={{0,96},{16,112},{32,0},{48,16},{64,32},{80,48},{96,64},{112,80},{1... | collective-permute-start | bytes 1572872 | tf_op jit(solution)/shard_map/ppermute | solution.py:28
  122.8 12.6 %collective-permute-start.15 = (bf16[128,2048]{1,0:T(8,128)(2,1)S(1)}, bf16[128,2048]{1,0:T(8,128)(2,1)S(1)}, u32[]{:S(2)}, u32[]{:S(2)}) collective-permute-start(bf16[128,2048]{1,0:T(8,128)(2,1)S(1)} %broadcast_select_fusion.1), channel_id=1, source_target_pairs={{0,32},{16,48},{32,64},{48,80},{64,96},{80,112},{96,0},{112,16},{1... | collective-permute-start | bytes 1572872 | tf_op jit(solution)/shard_map/ppermute | solution.py:28
  122.8 14.6 %collective-permute-start.16 = (bf16[128,2048]{1,0:T(8,128)(2,1)S(1)}, bf16[128,2048]{1,0:T(8,128)(2,1)S(1)}, u32[]{:S(2)}, u32[]{:S(2)}) collective-permute-start(bf16[128,2048]{1,0:T(8,128)(2,1)S(1)} %broadcast_select_fusion.1), channel_id=1, source_target_pairs={{0,96},{16,112},{32,0},{48,16},{64,32},{80,48},{96,64},{112,80},{1... | collective-permute-start | bytes 1572872 | tf_op jit(solution)/shard_map/ppermute | solution.py:28
  127.2 13.8 %collective-permute-start.25 = (bf16[128,2048]{1,0:T(8,128)(2,1)S(1)}, bf16[128,2048]{1,0:T(8,128)(2,1)S(1)}, u32[]{:S(2)}, u32[]{:S(2)}) collective-permute-start(bf16[128,2048]{1,0:T(8,128)(2,1)S(1)} %broadcast_select_fusion), channel_id=1, source_target_pairs={{0,32},{16,48},{32,64},{48,80},{64,96},{80,112},{96,0},{112,16},{1... | collective-permute-start | bytes 1572872 | tf_op jit(solution)/shard_map/ppermute | solution.py:28
  129.8 13.3 %collective-permute-start.26 = (bf16[128,2048]{1,0:T(8,128)(2,1)S(1)}, bf16[128,2048]{1,0:T(8,128)(2,1)S(1)}, u32[]{:S(2)}, u32[]{:S(2)}) collective-permute-start(bf16[128,2048]{1,0:T(8,128)(2,1)S(1)} %broadcast_select_fusion), channel_id=1, source_target_pairs={{0,96},{16,112},{32,0},{48,16},{64,32},{80,48},{96,64},{112,80},{1... | collective-permute-start | bytes 1572872 | tf_op jit(solution)/shard_map/ppermute | solution.py:28
  131.9 13.8 %collective-permute-start.7 = (bf16[64,2048]{1,0:T(8,128)(2,1)S(1)}, bf16[64,2048]{1,0:T(8,128)(2,1)S(1)}, u32[]{:S(2)}, u32[]{:S(2)}) collective-permute-start(bf16[64,2048]{1,0:T(8,128)(2,1)S(1)} %get-tuple-element.10), channel_id=1, source_target_pairs={{0,32},{16,48},{32,64},{48,80},{64,96},{80,112},{96,0},{112,16},{1... | collective-permute-start | bytes 786440 | tf_op jit(solution)/shard_map/ppermute | solution.py:28
  135.4 12.7 %collective-permute-start.8 = (bf16[64,2048]{1,0:T(8,128)(2,1)S(1)}, bf16[64,2048]{1,0:T(8,128)(2,1)S(1)}, u32[]{:S(2)}, u32[]{:S(2)}) collective-permute-start(bf16[64,2048]{1,0:T(8,128)(2,1)S(1)} %get-tuple-element.11), channel_id=1, source_target_pairs={{0,96},{16,112},{32,0},{48,16},{64,32},{80,48},{96,64},{112,80},{1... | collective-permute-start | bytes 786440 | tf_op jit(solution)/shard_map/ppermute | solution.py:28
  137.5 13.8 %collective-permute-start.17 = (bf16[64,2048]{1,0:T(8,128)(2,1)S(1)}, bf16[64,2048]{1,0:T(8,128)(2,1)S(1)}, u32[]{:S(2)}, u32[]{:S(2)}) collective-permute-start(bf16[64,2048]{1,0:T(8,128)(2,1)S(1)} %get-tuple-element.12), channel_id=1, source_target_pairs={{0,32},{16,48},{32,64},{48,80},{64,96},{80,112},{96,0},{112,16},{1... | collective-permute-start | bytes 786440 | tf_op jit(solution)/shard_map/ppermute | solution.py:28
  141.0 10.6 %collective-permute-start.18 = (bf16[64,2048]{1,0:T(8,128)(2,1)S(1)}, bf16[64,2048]{1,0:T(8,128)(2,1)S(1)}, u32[]{:S(2)}, u32[]{:S(2)}) collective-permute-start(bf16[64,2048]{1,0:T(8,128)(2,1)S(1)} %get-tuple-element.13), channel_id=1, source_target_pairs={{0,96},{16,112},{32,0},{48,16},{64,32},{80,48},{96,64},{112,80},{1... | collective-permute-start | bytes 786440 | tf_op jit(solution)/shard_map/ppermute | solution.py:28
  143.2 13.8 %collective-permute-start.27 = (bf16[64,2048]{1,0:T(8,128)(2,1)S(1)}, bf16[64,2048]{1,0:T(8,128)(2,1)S(1)}, u32[]{:S(2)}, u32[]{:S(2)}) collective-permute-start(bf16[64,2048]{1,0:T(8,128)(2,1)S(1)} %get-tuple-element.14), channel_id=1, source_target_pairs={{0,32},{16,48},{32,64},{48,80},{64,96},{80,112},{96,0},{112,16},{1... | collective-permute-start | bytes 786440 | tf_op jit(solution)/shard_map/ppermute | solution.py:28
  145.7 12.4 %copy-start.1 = (bf16[128,8,8,256]{3,1,2,0:T(8,128)(2,1)S(1)}, bf16[128,8,8,256]{3,1,2,0:T(8,128)(2,1)}, u32[]{:S(2)}) copy-start(bf16[128,8,8,256]{3,1,2,0:T(8,128)(2,1)} %copy.18) | copy-start | bytes 12582916
  145.8 11.5 %collective-permute-start.28 = (bf16[64,2048]{1,0:T(8,128)(2,1)S(1)}, bf16[64,2048]{1,0:T(8,128)(2,1)S(1)}, u32[]{:S(2)}, u32[]{:S(2)}) collective-permute-start(bf16[64,2048]{1,0:T(8,128)(2,1)S(1)} %get-tuple-element.15), channel_id=1, source_target_pairs={{0,96},{16,112},{32,0},{48,16},{64,32},{80,48},{96,64},{112,80},{1... | collective-permute-start | bytes 786440 | tf_op jit(solution)/shard_map/ppermute | solution.py:28
  148.2 10.0 %collective-permute-start.9 = (bf16[128,2048]{1,0:T(8,128)(2,1)S(1)}, bf16[128,2048]{1,0:T(8,128)(2,1)S(1)}, u32[]{:S(2)}, u32[]{:S(2)}) collective-permute-start(bf16[128,2048]{1,0:T(8,128)(2,1)S(1)} %maximum_select_fusion.6), channel_id=1, source_target_pairs={{0,16},{16,0},{32,48},{48,32},{64,80},{80,64},{96,112},{112,96},{1... | collective-permute-start | bytes 1572872 | tf_op jit(solution)/shard_map/ppermute | solution.py:37
  151.8 8.0 %copy-start.2 = (bf16[128,2048]{1,0:T(8,128)(2,1)}, bf16[128,2048]{1,0:T(8,128)(2,1)S(1)}, u32[]{:S(2)}) copy-start(bf16[128,2048]{1,0:T(8,128)(2,1)S(1)} %maximum_select_fusion.7) | copy-start | bytes 1572868
  151.8 30.1 %collective-permute-start.19 = (bf16[128,2048]{1,0:T(8,128)(2,1)S(1)}, bf16[128,2048]{1,0:T(8,128)(2,1)}, u32[]{:S(2)}, u32[]{:S(2)}) collective-permute-start(bf16[128,2048]{1,0:T(8,128)(2,1)S(1)} %maximum_select_fusion.7), channel_id=1, source_target_pairs={{0,16},{16,0},{32,48},{48,32},{64,80},{80,64},{96,112},{112,96},{1... | collective-permute-start | bytes 1572872 | tf_op jit(solution)/shard_map/ppermute | solution.py:37
  158.2 32.3 %collective-permute-start.29 = (bf16[128,2048]{1,0:T(8,128)(2,1)}, bf16[128,2048]{1,0:T(8,128)(2,1)}, u32[]{:S(2)}, u32[]{:S(2)}) collective-permute-start(bf16[128,2048]{1,0:T(8,128)(2,1)} %maximum_select_fusion.8), channel_id=1, source_target_pairs={{0,16},{16,0},{32,48},{48,32},{64,80},{80,64},{96,112},{112,96},{1... | collective-permute-start | bytes 1572872 | tf_op jit(solution)/shard_map/ppermute | solution.py:37
  160.7 36.9 %collective-permute-start.10 = (f32[8,64,256]{2,1,0:T(8,128)}, f32[8,64,256]{2,1,0:T(8,128)}, u32[]{:S(2)}, u32[]{:S(2)}) collective-permute-start(f32[8,64,256]{2,1,0:T(8,128)} %dynamic-slice_bitcast_fusion.2), channel_id=1, source_target_pairs={{0,1},{1,0},{2,3},{3,2},{4,5},{5,4},{6,7},{7,6},{8,9},{9,8},{10,11... | collective-permute-start | bytes 1572872 | tf_op jit(solution)/shard_map/ppermute | solution.py:52
  187.3 41.7 %collective-permute-start.20 = (f32[8,64,256]{2,1,0:T(8,128)}, f32[8,64,256]{2,1,0:T(8,128)}, u32[]{:S(2)}, u32[]{:S(2)}) collective-permute-start(f32[8,64,256]{2,1,0:T(8,128)} %dynamic-slice_bitcast_fusion.1), channel_id=1, source_target_pairs={{0,1},{1,0},{2,3},{3,2},{4,5},{5,4},{6,7},{7,6},{8,9},{9,8},{10,11... | collective-permute-start | bytes 1572872 | tf_op jit(solution)/shard_map/ppermute | solution.py:52
  197.2 33.0 %collective-permute-start.30 = (f32[8,64,256]{2,1,0:T(8,128)S(1)}, f32[8,64,256]{2,1,0:T(8,128)S(1)}, u32[]{:S(2)}, u32[]{:S(2)}) collective-permute-start(f32[8,64,256]{2,1,0:T(8,128)S(1)} %dynamic-slice_bitcast_fusion), channel_id=1, source_target_pairs={{0,1},{1,0},{2,3},{3,2},{4,5},{5,4},{6,7},{7,6},{8,9},{9,8},{10,11... | collective-permute-start | bytes 1572872 | tf_op jit(solution)/shard_map/ppermute | solution.py:52
  198.7 37.4 %collective-permute-start.11 = (f32[4,64,256]{2,1,0:T(8,128)S(1)}, f32[4,64,256]{2,1,0:T(8,128)S(1)}, u32[]{:S(2)}, u32[]{:S(2)}) collective-permute-start(f32[4,64,256]{2,1,0:T(8,128)S(1)} %dynamic-slice_bitcast_fusion.5), channel_id=1, source_target_pairs={{0,2},{1,3},{2,0},{3,1},{4,6},{5,7},{6,4},{7,5},{8,10},{9,11},{10,... | collective-permute-start | bytes 786440 | tf_op jit(solution)/shard_map/ppermute | solution.py:52
  230.1 11.6 %collective-permute-start.21 = (f32[4,64,256]{2,1,0:T(8,128)S(1)}, f32[4,64,256]{2,1,0:T(8,128)S(1)}, u32[]{:S(2)}, u32[]{:S(2)}) collective-permute-start(f32[4,64,256]{2,1,0:T(8,128)S(1)} %dynamic-slice_bitcast_fusion.4), channel_id=1, source_target_pairs={{0,2},{1,3},{2,0},{3,1},{4,6},{5,7},{6,4},{7,5},{8,10},{9,11},{10,... | collective-permute-start | bytes 786440 | tf_op jit(solution)/shard_map/ppermute | solution.py:52
  230.3 17.0 %collective-permute-start.31 = (f32[4,64,256]{2,1,0:T(8,128)S(1)}, f32[4,64,256]{2,1,0:T(8,128)S(1)}, u32[]{:S(2)}, u32[]{:S(2)}) collective-permute-start(f32[4,64,256]{2,1,0:T(8,128)S(1)} %dynamic-slice_bitcast_fusion.3), channel_id=1, source_target_pairs={{0,2},{1,3},{2,0},{3,1},{4,6},{5,7},{6,4},{7,5},{8,10},{9,11},{10,... | collective-permute-start | bytes 786440 | tf_op jit(solution)/shard_map/ppermute | solution.py:52
  236.1 14.9 %collective-permute-start.12 = (f32[2,64,256]{2,1,0:T(8,128)S(1)}, f32[2,64,256]{2,1,0:T(8,128)S(1)}, u32[]{:S(2)}, u32[]{:S(2)}) collective-permute-start(f32[2,64,256]{2,1,0:T(8,128)S(1)} %dynamic-slice_bitcast_fusion.8), channel_id=1, source_target_pairs={{0,4},{1,5},{2,6},{3,7},{4,0},{5,1},{6,2},{7,3},{8,12},{9,13},{10,... | collective-permute-start | bytes 393224 | tf_op jit(solution)/shard_map/ppermute | solution.py:52
  241.8 12.4 %collective-permute-start.22 = (f32[2,64,256]{2,1,0:T(8,128)S(1)}, f32[2,64,256]{2,1,0:T(8,128)S(1)}, u32[]{:S(2)}, u32[]{:S(2)}) collective-permute-start(f32[2,64,256]{2,1,0:T(8,128)S(1)} %dynamic-slice_bitcast_fusion.7), channel_id=1, source_target_pairs={{0,4},{1,5},{2,6},{3,7},{4,0},{5,1},{6,2},{7,3},{8,12},{9,13},{10,... | collective-permute-start | bytes 393224 | tf_op jit(solution)/shard_map/ppermute | solution.py:52
  247.4 9.5 %collective-permute-start.32 = (f32[2,64,256]{2,1,0:T(8,128)S(1)}, f32[2,64,256]{2,1,0:T(8,128)S(1)}, u32[]{:S(2)}, u32[]{:S(2)}) collective-permute-start(f32[2,64,256]{2,1,0:T(8,128)S(1)} %dynamic-slice_bitcast_fusion.6), channel_id=1, source_target_pairs={{0,4},{1,5},{2,6},{3,7},{4,0},{5,1},{6,2},{7,3},{8,12},{9,13},{10,... | collective-permute-start | bytes 393224 | tf_op jit(solution)/shard_map/ppermute | solution.py:52
  251.1 8.4 %collective-permute-start.13 = (f32[1,64,256]{2,1,0:T(8,128)S(1)}, f32[1,64,256]{2,1,0:T(8,128)S(1)}, u32[]{:S(2)}, u32[]{:S(2)}) collective-permute-start(f32[1,64,256]{2,1,0:T(8,128)S(1)} %constant_dynamic-slice_fusion.2), channel_id=1, source_target_pairs={{0,8},{1,9},{2,10},{3,11},{4,12},{5,13},{6,14},{7,15},{8,0},{9,1},... | collective-permute-start | bytes 196616 | tf_op jit(solution)/shard_map/ppermute | solution.py:52
  254.1 5.8 %collective-permute-start.23 = (f32[1,64,256]{2,1,0:T(8,128)S(1)}, f32[1,64,256]{2,1,0:T(8,128)S(1)}, u32[]{:S(2)}, u32[]{:S(2)}) collective-permute-start(f32[1,64,256]{2,1,0:T(8,128)S(1)} %constant_dynamic-slice_fusion.1), channel_id=1, source_target_pairs={{0,8},{1,9},{2,10},{3,11},{4,12},{5,13},{6,14},{7,15},{8,0},{9,1},... | collective-permute-start | bytes 196616 | tf_op jit(solution)/shard_map/ppermute | solution.py:52
  257.0 5.8 %collective-permute-start.33 = (f32[1,64,256]{2,1,0:T(8,128)S(1)}, f32[1,64,256]{2,1,0:T(8,128)S(1)}, u32[]{:S(2)}, u32[]{:S(2)}) collective-permute-start(f32[1,64,256]{2,1,0:T(8,128)S(1)} %constant_dynamic-slice_fusion), channel_id=1, source_target_pairs={{0,8},{1,9},{2,10},{3,11},{4,12},{5,13},{6,14},{7,15},{8,0},{9,1},... | collective-permute-start | bytes 196616 | tf_op jit(solution)/shard_map/ppermute | solution.py:52

commit v14 on v12

--- a/solution.py
+++ b/solution.py
@@ -38,19 +38,21 @@
     return jnp.where(mine, jnp.concatenate([val, other]), jnp.concatenate([other, val]))
 
 
-def reduce_scatter_slab(term, axis):
+def reduce_scatter_slab(term, axis, order=(2, 4, 8, 1)):
     size = lax.axis_size(axis)
     me = lax.axis_index(axis)
     rows = term.shape[0] // size
     part = term.reshape((size, rows) + term.shape[1:])
-    bit = 1
-    while bit < size:
+    left = sorted(b for b in order if b < size)
+    for bit in [b for b in order if b < size]:
+        lo = 2 ** left.index(bit)
         mine = (me // bit) % 2
-        halves = part.reshape((part.shape[0] // 2, 2) + part.shape[1:])
-        keep = lax.dynamic_index_in_dim(halves, mine, axis=1, keepdims=False)
-        send = lax.dynamic_index_in_dim(halves, 1 - mine, axis=1, keepdims=False)
-        part = keep + lax.ppermute(send, axis, [(i, i ^ bit) for i in range(size)])
-        bit *= 2
+        split = part.reshape((part.shape[0] // (2 * lo), 2, lo) + part.shape[1:])
+        keep = lax.dynamic_index_in_dim(split, mine, axis=1, keepdims=False)
+        send = lax.dynamic_index_in_dim(split, 1 - mine, axis=1, keepdims=False)
+        got = lax.ppermute(send, axis, [(i, i ^ bit) for i in range(size)])
+        part = (keep + got).reshape((part.shape[0] // 2,) + part.shape[1:])
+        left.remove(bit)
     return part.reshape((rows,) + term.shape[1:])
 
 

time: 261 us -> 267 us (1.023)
  waiting for transfers between devices: 31.9 us -> 41.6 us
  starting transfers between devices: 109 us -> 103 us
    ppermute x12, waiting for transfers between devices: 12.8 us -> 22.4 us  [reduce_scatter_slab(): got = lax.ppermute(send, axis, [(i, i ^ bit) for i in range(size)])]
    ppermute x12, starting transfers between devices: 72.7 us -> 67.6 us  [reduce_scatter_slab(): got = lax.ppermute(send, axis, [(i, i ^ bit) for i in range(size)])]
  transfers between devices with their start and end apart: 34 -> 34, of which waited for: 15 -> 16; matrix products, arithmetic and copies ran while one was open for 10% -> 10% of each run, Pallas kernels for 0% -> 0%
where the time goes in v14:
time: 267 us; the launch traced here: 265 us
  starting transfers between devices  103 us (39%)
  Pallas kernels  73 us (27%)
  waiting for transfers between devices  41.6 us (16%)
  local copies, waits for them, and re-layouts  18.4 us (7%)
  matrix products  10.5 us (4%)
  between operations  8.96 us (3%)
  other arithmetic  8.7 us (3%)
    pallas_call x1, Pallas kernels, smooth(): pl.pallas_call(kernel, grid=(rows // block,), in_specs=[pl.BlockSpec(coef...  73 us
    ppermute x12, starting transfers between devices, reduce_scatter_slab(): got = lax.ppermute(send, axis, [(i, i ^ bit) for i in range(size)])  67.6 us
    ppermute x12, waiting for transfers between devices, reduce_scatter_slab(): got = lax.ppermute(send, axis, [(i, i ^ bit) for i in range(size)])  22.4 us
    ppermute x12, starting transfers between devices, shift(): return lax.ppermute(v, axis, [(i, (i + step) % size) for i in range(size)])  18.2 us
    ppermute x12, waiting for transfers between devices, shift(): return lax.ppermute(v, axis, [(i, (i + step) % size) for i in range(size)])  12.6 us
    dot_general x3, matrix products, body(): lax.dot_general(flat, received, (((1,), (1,)), ((), ())), preferred_eleme...  10.5 us
    unnamed x21, local copies, waits for them, and re-layouts  8.47 us
    ppermute x2, starting transfers between devices, halo_of(): below = lax.ppermute(top, axis, up)  6.13 us
  transfers between devices with their start and end apart: 34, of which 16 were waited for; matrix products, arithmetic and copies ran while one was open for 10% of the time, Pallas kernels for 0%

profile of v14, /device:TPU:0, one launch (start us, length us, event | category | flops | bytes accessed | tf_op | source)
XLA Modules:
  0.0 264.7 jit_solution(7971260809620714867)
XLA Ops:
  0.6 4.8 %fusion.26 = (bf16[1024,4,256]{2,1,0:T(4,128)(2,1)S(1)}, bf16[1024,4,256]{2,1,0:T(4,128)(2,1)S(1)}) fusion(bf16[1024,8,256]{2,1,0:T(8,128)(2,1)} %a_ref.1), kind=kLoop, calls=%fused_computation.80 | loop fusion | bytes 8388608 | tf_op jit(solution)/shard_map/slice | solution.py:64
  5.5 1.4 collective-permute-start.2
  6.9 1.3 collective-permute-start.3
  8.3 4.7 %collective-permute-start = (f32[4,256]{1,0:T(4,128)S(1)}, f32[4,256]{1,0:T(4,128)S(1)}, u32[]{:S(2)}, u32[]{:S(2)}) collective-permute-start(f32[4,256]{1,0:T(4,128)S(1)} %get-tuple-element.16), channel_id=1, source_target_pairs={{0,1},{1,2},{2,3},{3,4},{4,5},{5,6},{6,7},{7,8},{8,9},{9,10},{10,1... | collective-permute-start | bytes 12296 | tf_op jit(solution)/shard_map/ppermute | solution.py:65
  13.0 1.3 collective-permute-start.1
  14.4 2.9 %collective-permute-done.1 = f32[4,256]{1,0:T(4,128)S(1)} collective-permute-done((f32[4,256]{1,0:T(4,128)S(1)}, f32[4,256]{1,0:T(4,128)S(1)}, u32[]{:S(2)}, u32[]{:S(2)}) %collective-permute-start.1) | collective-permute-done | bytes 4128 | tf_op jit(solution)/shard_map/ppermute | solution.py:66
  18.8 73.0 %shard_map.59 = f32[1024,8,256]{2,1,0:T(8,128)} custom-call(f32[6,16,256]{2,1,0:T(8,128)} %copy-done.3, bf16[1024,8,256]{2,1,0:T(8,128)(2,1)} %a_ref.1, bf16[1024,4,256]{2,1,0:T(4,128)(2,1)} %copy-done.1, bf16[1024,4,256]{2,1,0:T(4,128)(2,1)} %collective-permute-done.3.hi_ref), custom_call_target="tpu_custom_call" | custom-call | tf_op jit(solution)/shard_map/pallas_call | solution.py:148
  91.9 3.8 %convert.5 = bf16[1024,8,256]{2,1,0:T(8,128)(2,1)S(1)} convert(f32[1024,8,256]{2,1,0:T(8,128)} %shard_map.59) | non-fusion elementwise | flops 2097152 | bytes 12582912 | tf_op jit(solution)/shard_map/convert.2
  96.8 1.6 collective-permute-start.4
  107.4 5.6 %copy.14 = bf16[128,8,8,256]{3,1,2,0:T(8,128)(2,1)} copy(bf16[128,8,8,256]{3,2,1,0:T(8,128)(2,1)} %bitcast.69) | data formatting | bytes 8388608
  113.4 1.7 collective-permute-start.24
  115.3 2.0 collective-permute-start.5
  117.2 2.2 collective-permute-start.6
  119.6 3.2 %collective-permute-start.16 = (bf16[128,2048]{1,0:T(8,128)(2,1)S(1)}, bf16[128,2048]{1,0:T(8,128)(2,1)S(1)}, u32[]{:S(2)}, u32[]{:S(2)}) collective-permute-start(bf16[128,2048]{1,0:T(8,128)(2,1)S(1)} %broadcast_select_fusion.1), channel_id=1, source_target_pairs={{0,96},{16,112},{32,0},{48,16},{64,32},{80,48},{96,64},{112,80},{1... | collective-permute-start | bytes 1572872 | tf_op jit(solution)/shard_map/ppermute | solution.py:28
  122.8 3.6 %collective-permute-done.24 = bf16[128,2048]{1,0:T(8,128)(2,1)S(1)} collective-permute-done((bf16[128,2048]{1,0:T(8,128)(2,1)S(1)}, bf16[128,2048]{1,0:T(8,128)(2,1)S(1)}, u32[]{:S(2)}, u32[]{:S(2)}) %collective-permute-start.24) | collective-permute-done | bytes 524320 | tf_op jit(solution)/shard_map/ppermute | solution.py:30
  126.5 2.0 collective-permute-start.25
  128.5 2.2 collective-permute-start.26
  130.9 1.2 collective-permute-done.15
  132.1 2.0 collective-permute-start.8
  134.4 3.4 %collective-permute-done.25 = bf16[128,2048]{1,0:T(8,128)(2,1)S(1)} collective-permute-done((bf16[128,2048]{1,0:T(8,128)(2,1)S(1)}, bf16[128,2048]{1,0:T(8,128)(2,1)S(1)}, u32[]{:S(2)}, u32[]{:S(2)}) %collective-permute-start.25) | collective-permute-done | bytes 524320 | tf_op jit(solution)/shard_map/ppermute | solution.py:28
  137.8 2.0 collective-permute-start.18
  140.0 2.5 collective-permute-done.7
  142.6 2.3 collective-permute-start.28
  145.0 1.7 collective-permute-start.9
  146.7 1.4 collective-permute-done.17
  148.6 1.7 collective-permute-start.19
  150.3 3.4 %collective-permute-done.27 = bf16[64,2048]{1,0:T(8,128)(2,1)S(1)} collective-permute-done((bf16[64,2048]{1,0:T(8,128)(2,1)S(1)}, bf16[64,2048]{1,0:T(8,128)(2,1)S(1)}, u32[]{:S(2)}, u32[]{:S(2)}) %collective-permute-start.27) | collective-permute-done | bytes 262176 | tf_op jit(solution)/shard_map/ppermute | solution.py:28
  155.0 1.7 collective-permute-start.29
  156.7 1.3 fusion.2
  159.2 39.5 %collective-permute-start.10 = (f32[4,2,64,256]{3,2,1,0:T(8,128)}, f32[4,2,64,256]{3,2,1,0:T(8,128)}, u32[]{:S(2)}, u32[]{:S(2)}) collective-permute-start(f32[4,2,64,256]{3,2,1,0:T(8,128)} %dynamic-slice_bitcast_fusion.2), channel_id=1, source_target_pairs={{0,2},{1,3},{2,0},{3,1},{4,6},{5,7},{6,4},{7,5},{8,10},{9,11},{10,... | collective-permute-start | bytes 1572872 | tf_op jit(solution)/shard_map/ppermute | solution.py:53
  198.6 4.1 %fusion.1 = f32[1024,256]{0,1:T(8,128)S(1)} fusion(bf16[1024,2048]{1,0:T(8,128)(2,1)} %bitcast.70, bf16[128,2048]{1,0:T(8,128)(2,1)} %collective-permute-done.19, bf16[128,2048]{1,0:T(8,128)(2,1)} %copy-done.2, pred[]{:T(512)S(6)} %eq.83), kind=kOutput, calls=%fused_computation.3 | convolution fusion | flops 1078722560 | bytes 6291457 | tf_op jit(solution)/shard_map/dot_general | solution.py:178
  204.0 8.8 %collective-permute-start.20 = (f32[4,2,64,256]{3,2,1,0:T(8,128)}, f32[4,2,64,256]{3,2,1,0:T(8,128)}, u32[]{:S(2)}, u32[]{:S(2)}) collective-permute-start(f32[4,2,64,256]{3,2,1,0:T(8,128)} %dynamic-slice_bitcast_fusion.1), channel_id=1, source_target_pairs={{0,2},{1,3},{2,0},{3,1},{4,6},{5,7},{6,4},{7,5},{8,10},{9,11},{10,... | collective-permute-start | bytes 1572872 | tf_op jit(solution)/shard_map/ppermute | solution.py:53
  212.8 5.1 %fusion = f32[1024,256]{0,1:T(8,128)} fusion(bf16[1024,2048]{1,0:T(8,128)(2,1)} %bitcast.71, bf16[128,2048]{1,0:T(8,128)(2,1)} %collective-permute-done.29, bf16[128,2048]{1,0:T(8,128)(2,1)} %maximum_select_fusion.8, pred[]{:T(512)S(6)} %eq.87), kind=kOutput, calls=%fused_computation.1 | convolution fusion | flops 1078722560 | bytes 6291457 | tf_op jit(solution)/shard_map/dot_general | solution.py:178
  218.0 1.6 copy.11
  219.6 4.8 %collective-permute-start.30 = (f32[4,2,64,256]{3,2,1,0:T(8,128)S(1)}, f32[4,2,64,256]{3,2,1,0:T(8,128)S(1)}, u32[]{:S(2)}, u32[]{:S(2)}) collective-permute-start(f32[4,2,64,256]{3,2,1,0:T(8,128)S(1)} %dynamic-slice_bitcast_fusion), channel_id=1, source_target_pairs={{0,2},{1,3},{2,0},{3,1},{4,6},{5,7},{6,4},{7,5},{8,10},{9,11},{10,... | collective-permute-start | bytes 1572872 | tf_op jit(solution)/shard_map/ppermute | solution.py:53
  224.4 1.1 bitcast_add_fusion.2
  226.6 1.1 bitcast_add_fusion.1
  227.8 2.9 %collective-permute-start.21 = (f32[2,2,64,256]{3,2,1,0:T(8,128)S(1)}, f32[2,2,64,256]{3,2,1,0:T(8,128)S(1)}, u32[]{:S(2)}, u32[]{:S(2)}) collective-permute-start(f32[2,2,64,256]{3,2,1,0:T(8,128)S(1)} %dynamic-slice_bitcast_fusion.4), channel_id=1, source_target_pairs={{0,4},{1,5},{2,6},{3,7},{4,0},{5,1},{6,2},{7,3},{8,12},{9,13},{10,... | collective-permute-start | bytes 786440 | tf_op jit(solution)/shard_map/ppermute | solution.py:53
  230.7 6.6 %collective-permute-done.30 = f32[4,2,64,256]{3,2,1,0:T(8,128)S(1)} collective-permute-done((f32[4,2,64,256]{3,2,1,0:T(8,128)S(1)}, f32[4,2,64,256]{3,2,1,0:T(8,128)S(1)}, u32[]{:S(2)}, u32[]{:S(2)}) %collective-permute-start.30) | collective-permute-done | bytes 524320 | tf_op jit(solution)/shard_map/ppermute | solution.py:53
  237.3 3.4 %collective-permute-start.31 = (f32[2,2,64,256]{3,2,1,0:T(8,128)S(1)}, f32[2,2,64,256]{3,2,1,0:T(8,128)S(1)}, u32[]{:S(2)}, u32[]{:S(2)}) collective-permute-start(f32[2,2,64,256]{3,2,1,0:T(8,128)S(1)} %dynamic-slice_bitcast_fusion.3), channel_id=1, source_target_pairs={{0,4},{1,5},{2,6},{3,7},{4,0},{5,1},{6,2},{7,3},{8,12},{9,13},{10,... | collective-permute-start | bytes 786440 | tf_op jit(solution)/shard_map/ppermute | solution.py:53
  240.8 3.0 %collective-permute-done.11 = f32[2,2,64,256]{3,2,1,0:T(8,128)S(1)} collective-permute-done((f32[2,2,64,256]{3,2,1,0:T(8,128)S(1)}, f32[2,2,64,256]{3,2,1,0:T(8,128)S(1)}, u32[]{:S(2)}, u32[]{:S(2)}) %collective-permute-start.11) | collective-permute-done | bytes 262176 | tf_op jit(solution)/shard_map/ppermute | solution.py:53
  243.9 3.0 %collective-permute-start.12 = (f32[1,2,64,256]{3,2,1,0:T(8,128)S(1)}, f32[1,2,64,256]{3,2,1,0:T(8,128)S(1)}, u32[]{:S(2)}, u32[]{:S(2)}) collective-permute-start(f32[1,2,64,256]{3,2,1,0:T(8,128)S(1)} %constant_dynamic-slice_fusion.5), channel_id=1, source_target_pairs={{0,8},{1,9},{2,10},{3,11},{4,12},{5,13},{6,14},{7,15},{8,0},{9,1},... | collective-permute-start | bytes 393224 | tf_op jit(solution)/shard_map/ppermute | solution.py:53
  246.9 2.5 collective-permute-done.21
  249.5 3.0 %collective-permute-start.22 = (f32[1,2,64,256]{3,2,1,0:T(8,128)S(1)}, f32[1,2,64,256]{3,2,1,0:T(8,128)S(1)}, u32[]{:S(2)}, u32[]{:S(2)}) collective-permute-start(f32[1,2,64,256]{3,2,1,0:T(8,128)S(1)} %constant_dynamic-slice_fusion.3), channel_id=1, source_target_pairs={{0,8},{1,9},{2,10},{3,11},{4,12},{5,13},{6,14},{7,15},{8,0},{9,1},... | collective-permute-start | bytes 393224 | tf_op jit(solution)/shard_map/ppermute | solution.py:53
  252.5 2.5 collective-permute-done.31
  255.9 1.5 collective-permute-done.22
  257.7 5.0 %collective-permute-done.32 = f32[1,2,64,256]{3,2,1,0:T(8,128)S(1)} collective-permute-done((f32[1,2,64,256]{3,2,1,0:T(8,128)S(1)}, f32[1,2,64,256]{3,2,1,0:T(8,128)S(1)}, u32[]{:S(2)}, u32[]{:S(2)}) %collective-permute-start.32) | collective-permute-done | bytes 131104 | tf_op jit(solution)/shard_map/ppermute | solution.py:53
  262.9 1.2 collective-permute-done.33
  (101 shorter events, 12.7 us)
Async XLA Ops:
  0.6 7.6 %copy-start.4 = (s32[8,256]{1,0:T(8,128)S(1)}, s32[8,256]{1,0:T(8,128)}, u32[]{:S(2)}) copy-start(s32[8,256]{1,0:T(8,128)} %param.5) | copy-start | bytes 24580
  0.6 7.6 %copy-start.6 = (f32[8]{0:T(128)S(1)}, f32[8]{0:T(128)}, u32[]{:S(2)}) copy-start(f32[8]{0:T(128)} %param.6) | copy-start | bytes 100
  5.5 12.0 %collective-permute-start.2 = (bf16[1024,4,256]{2,1,0:T(4,128)(2,1)S(1)}, bf16[1024,4,256]{2,1,0:T(4,128)(2,1)S(1)}, u32[]{:S(2)}, u32[]{:S(2)}) collective-permute-start(bf16[1024,4,256]{2,1,0:T(4,128)(2,1)S(1)} %get-tuple-element.9), channel_id=1, source_target_pairs={{0,1},{1,2},{2,3},{3,4},{4,5},{5,6},{6,7},{7,8},{8,9},{9,10},{10,1... | collective-permute-start | bytes 6291464 | tf_op jit(solution)/shard_map/ppermute | solution.py:65
  6.9 10.6 %collective-permute-start.3 = (bf16[1024,4,256]{2,1,0:T(4,128)(2,1)S(1)}, bf16[1024,4,256]{2,1,0:T(4,128)(2,1)}, u32[]{:S(2)}, u32[]{:S(2)}) collective-permute-start(bf16[1024,4,256]{2,1,0:T(4,128)(2,1)S(1)} %get-tuple-element.8), channel_id=1, source_target_pairs={{1,0},{2,1},{3,2},{4,3},{5,4},{6,5},{7,6},{8,7},{9,8},{10,9},{11,1... | collective-permute-start | bytes 6291464 | tf_op jit(solution)/shard_map/ppermute | solution.py:66
  8.3 6.1 %collective-permute-start = (f32[4,256]{1,0:T(4,128)S(1)}, f32[4,256]{1,0:T(4,128)S(1)}, u32[]{:S(2)}, u32[]{:S(2)}) collective-permute-start(f32[4,256]{1,0:T(4,128)S(1)} %get-tuple-element.16), channel_id=1, source_target_pairs={{0,1},{1,2},{2,3},{3,4},{4,5},{5,6},{6,7},{7,8},{8,9},{9,10},{10,1... | collective-permute-start | bytes 12296 | tf_op jit(solution)/shard_map/ppermute | solution.py:65
  13.0 4.3 %collective-permute-start.1 = (f32[4,256]{1,0:T(4,128)S(1)}, f32[4,256]{1,0:T(4,128)S(1)}, u32[]{:S(2)}, u32[]{:S(2)}) collective-permute-start(f32[4,256]{1,0:T(4,128)S(1)} %get-tuple-element.17), channel_id=1, source_target_pairs={{1,0},{2,1},{3,2},{4,3},{5,4},{6,5},{7,6},{8,7},{9,8},{10,9},{11,1... | collective-permute-start | bytes 12296 | tf_op jit(solution)/shard_map/ppermute | solution.py:66
  17.4 0.6 copy-start.3
  17.4 1.4 copy-start.1
  95.9 3.1 %copy-start.5 = (s32[8]{0:T(128)S(1)}, s32[8]{0:T(128)}, u32[]{:S(2)}) copy-start(s32[8]{0:T(128)} %param.7) | copy-start | bytes 100
  96.8 18.4 %collective-permute-start.4 = (bf16[128,2048]{1,0:T(8,128)(2,1)}, bf16[128,2048]{1,0:T(8,128)(2,1)}, u32[]{:S(2)}, u32[]{:S(2)}) collective-permute-start(bf16[128,2048]{1,0:T(8,128)(2,1)} %bitcast.34), channel_id=1, source_target_pairs={{0,16},{16,0},{32,48},{48,32},{64,80},{80,64},{96,112},{112,96},{1... | collective-permute-start | bytes 1572872 | tf_op jit(solution)/shard_map/ppermute | solution.py:30
  98.5 21.0 %collective-permute-start.14 = (bf16[128,2048]{1,0:T(8,128)(2,1)S(1)}, bf16[128,2048]{1,0:T(8,128)(2,1)S(1)}, u32[]{:S(2)}, u32[]{:S(2)}) collective-permute-start(bf16[128,2048]{1,0:T(8,128)(2,1)S(1)} %bitcast.94), channel_id=1, source_target_pairs={{0,16},{16,0},{32,48},{48,32},{64,80},{80,64},{96,112},{112,96},{1... | collective-permute-start | bytes 1572872 | tf_op jit(solution)/shard_map/ppermute | solution.py:30
  113.4 13.1 %collective-permute-start.24 = (bf16[128,2048]{1,0:T(8,128)(2,1)S(1)}, bf16[128,2048]{1,0:T(8,128)(2,1)S(1)}, u32[]{:S(2)}, u32[]{:S(2)}) collective-permute-start(bf16[128,2048]{1,0:T(8,128)(2,1)S(1)} %bitcast.95), channel_id=1, source_target_pairs={{0,16},{16,0},{32,48},{48,32},{64,80},{80,64},{96,112},{112,96},{1... | collective-permute-start | bytes 1572872 | tf_op jit(solution)/shard_map/ppermute | solution.py:30
  115.3 13.3 %collective-permute-start.5 = (bf16[128,2048]{1,0:T(8,128)(2,1)S(1)}, bf16[128,2048]{1,0:T(8,128)(2,1)S(1)}, u32[]{:S(2)}, u32[]{:S(2)}) collective-permute-start(bf16[128,2048]{1,0:T(8,128)(2,1)S(1)} %broadcast_select_fusion.2), channel_id=1, source_target_pairs={{0,32},{16,48},{32,64},{48,80},{64,96},{80,112},{96,0},{112,16},{1... | collective-permute-start | bytes 1572872 | tf_op jit(solution)/shard_map/ppermute | solution.py:28
  117.2 13.5 %collective-permute-start.6 = (bf16[128,2048]{1,0:T(8,128)(2,1)S(1)}, bf16[128,2048]{1,0:T(8,128)(2,1)S(1)}, u32[]{:S(2)}, u32[]{:S(2)}) collective-permute-start(bf16[128,2048]{1,0:T(8,128)(2,1)S(1)} %broadcast_select_fusion.2), channel_id=1, source_target_pairs={{0,96},{16,112},{32,0},{48,16},{64,32},{80,48},{96,64},{112,80},{1... | collective-permute-start | bytes 1572872 | tf_op jit(solution)/shard_map/ppermute | solution.py:28
  119.5 12.6 %collective-permute-start.15 = (bf16[128,2048]{1,0:T(8,128)(2,1)S(1)}, bf16[128,2048]{1,0:T(8,128)(2,1)S(1)}, u32[]{:S(2)}, u32[]{:S(2)}) collective-permute-start(bf16[128,2048]{1,0:T(8,128)(2,1)S(1)} %broadcast_select_fusion.1), channel_id=1, source_target_pairs={{0,32},{16,48},{32,64},{48,80},{64,96},{80,112},{96,0},{112,16},{1... | collective-permute-start | bytes 1572872 | tf_op jit(solution)/shard_map/ppermute | solution.py:28
  119.6 14.6 %collective-permute-start.16 = (bf16[128,2048]{1,0:T(8,128)(2,1)S(1)}, bf16[128,2048]{1,0:T(8,128)(2,1)S(1)}, u32[]{:S(2)}, u32[]{:S(2)}) collective-permute-start(bf16[128,2048]{1,0:T(8,128)(2,1)S(1)} %broadcast_select_fusion.1), channel_id=1, source_target_pairs={{0,96},{16,112},{32,0},{48,16},{64,32},{80,48},{96,64},{112,80},{1... | collective-permute-start | bytes 1572872 | tf_op jit(solution)/shard_map/ppermute | solution.py:28
  126.5 11.3 %collective-permute-start.25 = (bf16[128,2048]{1,0:T(8,128)(2,1)S(1)}, bf16[128,2048]{1,0:T(8,128)(2,1)S(1)}, u32[]{:S(2)}, u32[]{:S(2)}) collective-permute-start(bf16[128,2048]{1,0:T(8,128)(2,1)S(1)} %broadcast_select_fusion), channel_id=1, source_target_pairs={{0,32},{16,48},{32,64},{48,80},{64,96},{80,112},{96,0},{112,16},{1... | collective-permute-start | bytes 1572872 | tf_op jit(solution)/shard_map/ppermute | solution.py:28
  128.5 11.3 %collective-permute-start.26 = (bf16[128,2048]{1,0:T(8,128)(2,1)S(1)}, bf16[128,2048]{1,0:T(8,128)(2,1)S(1)}, u32[]{:S(2)}, u32[]{:S(2)}) collective-permute-start(bf16[128,2048]{1,0:T(8,128)(2,1)S(1)} %broadcast_select_fusion), channel_id=1, source_target_pairs={{0,96},{16,112},{32,0},{48,16},{64,32},{80,48},{96,64},{112,80},{1... | collective-permute-start | bytes 1572872 | tf_op jit(solution)/shard_map/ppermute | solution.py:28
  130.8 11.7 %collective-permute-start.7 = (bf16[64,2048]{1,0:T(8,128)(2,1)S(1)}, bf16[64,2048]{1,0:T(8,128)(2,1)S(1)}, u32[]{:S(2)}, u32[]{:S(2)}) collective-permute-start(bf16[64,2048]{1,0:T(8,128)(2,1)S(1)} %get-tuple-element.10), channel_id=1, source_target_pairs={{0,32},{16,48},{32,64},{48,80},{64,96},{80,112},{96,0},{112,16},{1... | collective-permute-start | bytes 786440 | tf_op jit(solution)/shard_map/ppermute | solution.py:28
  132.1 12.7 %collective-permute-start.8 = (bf16[64,2048]{1,0:T(8,128)(2,1)S(1)}, bf16[64,2048]{1,0:T(8,128)(2,1)S(1)}, u32[]{:S(2)}, u32[]{:S(2)}) collective-permute-start(bf16[64,2048]{1,0:T(8,128)(2,1)S(1)} %get-tuple-element.11), channel_id=1, source_target_pairs={{0,96},{16,112},{32,0},{48,16},{64,32},{80,48},{96,64},{112,80},{1... | collective-permute-start | bytes 786440 | tf_op jit(solution)/shard_map/ppermute | solution.py:28
  134.3 13.9 %collective-permute-start.17 = (bf16[64,2048]{1,0:T(8,128)(2,1)S(1)}, bf16[64,2048]{1,0:T(8,128)(2,1)S(1)}, u32[]{:S(2)}, u32[]{:S(2)}) collective-permute-start(bf16[64,2048]{1,0:T(8,128)(2,1)S(1)} %get-tuple-element.12), channel_id=1, source_target_pairs={{0,32},{16,48},{32,64},{48,80},{64,96},{80,112},{96,0},{112,16},{1... | collective-permute-start | bytes 786440 | tf_op jit(solution)/shard_map/ppermute | solution.py:28
  137.8 10.7 %collective-permute-start.18 = (bf16[64,2048]{1,0:T(8,128)(2,1)S(1)}, bf16[64,2048]{1,0:T(8,128)(2,1)S(1)}, u32[]{:S(2)}, u32[]{:S(2)}) collective-permute-start(bf16[64,2048]{1,0:T(8,128)(2,1)S(1)} %get-tuple-element.13), channel_id=1, source_target_pairs={{0,96},{16,112},{32,0},{48,16},{64,32},{80,48},{96,64},{112,80},{1... | collective-permute-start | bytes 786440 | tf_op jit(solution)/shard_map/ppermute | solution.py:28
  139.9 13.9 %collective-permute-start.27 = (bf16[64,2048]{1,0:T(8,128)(2,1)S(1)}, bf16[64,2048]{1,0:T(8,128)(2,1)S(1)}, u32[]{:S(2)}, u32[]{:S(2)}) collective-permute-start(bf16[64,2048]{1,0:T(8,128)(2,1)S(1)} %get-tuple-element.14), channel_id=1, source_target_pairs={{0,32},{16,48},{32,64},{48,80},{64,96},{80,112},{96,0},{112,16},{1... | collective-permute-start | bytes 786440 | tf_op jit(solution)/shard_map/ppermute | solution.py:28
  142.5 14.1 %copy-start = (bf16[128,8,8,256]{3,1,2,0:T(8,128)(2,1)S(1)}, bf16[128,8,8,256]{3,1,2,0:T(8,128)(2,1)}, u32[]{:S(2)}) copy-start(bf16[128,8,8,256]{3,1,2,0:T(8,128)(2,1)} %copy.14) | copy-start | bytes 12582916
  142.6 11.5 %collective-permute-start.28 = (bf16[64,2048]{1,0:T(8,128)(2,1)S(1)}, bf16[64,2048]{1,0:T(8,128)(2,1)S(1)}, u32[]{:S(2)}, u32[]{:S(2)}) collective-permute-start(bf16[64,2048]{1,0:T(8,128)(2,1)S(1)} %get-tuple-element.15), channel_id=1, source_target_pairs={{0,96},{16,112},{32,0},{48,16},{64,32},{80,48},{96,64},{112,80},{1... | collective-permute-start | bytes 786440 | tf_op jit(solution)/shard_map/ppermute | solution.py:28
  145.0 11.7 %collective-permute-start.9 = (bf16[128,2048]{1,0:T(8,128)(2,1)S(1)}, bf16[128,2048]{1,0:T(8,128)(2,1)S(1)}, u32[]{:S(2)}, u32[]{:S(2)}) collective-permute-start(bf16[128,2048]{1,0:T(8,128)(2,1)S(1)} %maximum_select_fusion.6), channel_id=1, source_target_pairs={{0,16},{16,0},{32,48},{48,32},{64,80},{80,64},{96,112},{112,96},{1... | collective-permute-start | bytes 1572872 | tf_op jit(solution)/shard_map/ppermute | solution.py:37
  148.6 9.7 %copy-start.2 = (bf16[128,2048]{1,0:T(8,128)(2,1)}, bf16[128,2048]{1,0:T(8,128)(2,1)S(1)}, u32[]{:S(2)}) copy-start(bf16[128,2048]{1,0:T(8,128)(2,1)S(1)} %maximum_select_fusion.7) | copy-start | bytes 1572868
  148.6 50.0 %collective-permute-start.19 = (bf16[128,2048]{1,0:T(8,128)(2,1)S(1)}, bf16[128,2048]{1,0:T(8,128)(2,1)}, u32[]{:S(2)}, u32[]{:S(2)}) collective-permute-start(bf16[128,2048]{1,0:T(8,128)(2,1)S(1)} %maximum_select_fusion.7), channel_id=1, source_target_pairs={{0,16},{16,0},{32,48},{48,32},{64,80},{80,64},{96,112},{112,96},{1... | collective-permute-start | bytes 1572872 | tf_op jit(solution)/shard_map/ppermute | solution.py:37
  155.0 57.8 %collective-permute-start.29 = (bf16[128,2048]{1,0:T(8,128)(2,1)}, bf16[128,2048]{1,0:T(8,128)(2,1)}, u32[]{:S(2)}, u32[]{:S(2)}) collective-permute-start(bf16[128,2048]{1,0:T(8,128)(2,1)} %maximum_select_fusion.8), channel_id=1, source_target_pairs={{0,16},{16,0},{32,48},{48,32},{64,80},{80,64},{96,112},{112,96},{1... | collective-permute-start | bytes 1572872 | tf_op jit(solution)/shard_map/ppermute | solution.py:37
  159.2 65.2 %collective-permute-start.10 = (f32[4,2,64,256]{3,2,1,0:T(8,128)}, f32[4,2,64,256]{3,2,1,0:T(8,128)}, u32[]{:S(2)}, u32[]{:S(2)}) collective-permute-start(f32[4,2,64,256]{3,2,1,0:T(8,128)} %dynamic-slice_bitcast_fusion.2), channel_id=1, source_target_pairs={{0,2},{1,3},{2,0},{3,1},{4,6},{5,7},{6,4},{7,5},{8,10},{9,11},{10,... | collective-permute-start | bytes 1572872 | tf_op jit(solution)/shard_map/ppermute | solution.py:53
  204.0 22.6 %collective-permute-start.20 = (f32[4,2,64,256]{3,2,1,0:T(8,128)}, f32[4,2,64,256]{3,2,1,0:T(8,128)}, u32[]{:S(2)}, u32[]{:S(2)}) collective-permute-start(f32[4,2,64,256]{3,2,1,0:T(8,128)} %dynamic-slice_bitcast_fusion.1), channel_id=1, source_target_pairs={{0,2},{1,3},{2,0},{3,1},{4,6},{5,7},{6,4},{7,5},{8,10},{9,11},{10,... | collective-permute-start | bytes 1572872 | tf_op jit(solution)/shard_map/ppermute | solution.py:53
  219.6 17.7 %collective-permute-start.30 = (f32[4,2,64,256]{3,2,1,0:T(8,128)S(1)}, f32[4,2,64,256]{3,2,1,0:T(8,128)S(1)}, u32[]{:S(2)}, u32[]{:S(2)}) collective-permute-start(f32[4,2,64,256]{3,2,1,0:T(8,128)S(1)} %dynamic-slice_bitcast_fusion), channel_id=1, source_target_pairs={{0,2},{1,3},{2,0},{3,1},{4,6},{5,7},{6,4},{7,5},{8,10},{9,11},{10,... | collective-permute-start | bytes 1572872 | tf_op jit(solution)/shard_map/ppermute | solution.py:53
  225.6 18.3 %collective-permute-start.11 = (f32[2,2,64,256]{3,2,1,0:T(8,128)S(1)}, f32[2,2,64,256]{3,2,1,0:T(8,128)S(1)}, u32[]{:S(2)}, u32[]{:S(2)}) collective-permute-start(f32[2,2,64,256]{3,2,1,0:T(8,128)S(1)} %dynamic-slice_bitcast_fusion.5), channel_id=1, source_target_pairs={{0,4},{1,5},{2,6},{3,7},{4,0},{5,1},{6,2},{7,3},{8,12},{9,13},{10,... | collective-permute-start | bytes 786440 | tf_op jit(solution)/shard_map/ppermute | solution.py:53
  227.8 21.7 %collective-permute-start.21 = (f32[2,2,64,256]{3,2,1,0:T(8,128)S(1)}, f32[2,2,64,256]{3,2,1,0:T(8,128)S(1)}, u32[]{:S(2)}, u32[]{:S(2)}) collective-permute-start(f32[2,2,64,256]{3,2,1,0:T(8,128)S(1)} %dynamic-slice_bitcast_fusion.4), channel_id=1, source_target_pairs={{0,4},{1,5},{2,6},{3,7},{4,0},{5,1},{6,2},{7,3},{8,12},{9,13},{10,... | collective-permute-start | bytes 786440 | tf_op jit(solution)/shard_map/ppermute | solution.py:53
  237.3 17.7 %collective-permute-start.31 = (f32[2,2,64,256]{3,2,1,0:T(8,128)S(1)}, f32[2,2,64,256]{3,2,1,0:T(8,128)S(1)}, u32[]{:S(2)}, u32[]{:S(2)}) collective-permute-start(f32[2,2,64,256]{3,2,1,0:T(8,128)S(1)} %dynamic-slice_bitcast_fusion.3), channel_id=1, source_target_pairs={{0,4},{1,5},{2,6},{3,7},{4,0},{5,1},{6,2},{7,3},{8,12},{9,13},{10,... | collective-permute-start | bytes 786440 | tf_op jit(solution)/shard_map/ppermute | solution.py:53
  243.9 11.9 %collective-permute-start.12 = (f32[1,2,64,256]{3,2,1,0:T(8,128)S(1)}, f32[1,2,64,256]{3,2,1,0:T(8,128)S(1)}, u32[]{:S(2)}, u32[]{:S(2)}) collective-permute-start(f32[1,2,64,256]{3,2,1,0:T(8,128)S(1)} %constant_dynamic-slice_fusion.5), channel_id=1, source_target_pairs={{0,8},{1,9},{2,10},{3,11},{4,12},{5,13},{6,14},{7,15},{8,0},{9,1},... | collective-permute-start | bytes 393224 | tf_op jit(solution)/shard_map/ppermute | solution.py:53
  249.5 7.9 %collective-permute-start.22 = (f32[1,2,64,256]{3,2,1,0:T(8,128)S(1)}, f32[1,2,64,256]{3,2,1,0:T(8,128)S(1)}, u32[]{:S(2)}, u32[]{:S(2)}) collective-permute-start(f32[1,2,64,256]{3,2,1,0:T(8,128)S(1)} %constant_dynamic-slice_fusion.3), channel_id=1, source_target_pairs={{0,8},{1,9},{2,10},{3,11},{4,12},{5,13},{6,14},{7,15},{8,0},{9,1},... | collective-permute-start | bytes 393224 | tf_op jit(solution)/shard_map/ppermute | solution.py:53
  255.1 7.5 %collective-permute-start.32 = (f32[1,2,64,256]{3,2,1,0:T(8,128)S(1)}, f32[1,2,64,256]{3,2,1,0:T(8,128)S(1)}, u32[]{:S(2)}, u32[]{:S(2)}) collective-permute-start(f32[1,2,64,256]{3,2,1,0:T(8,128)S(1)} %constant_dynamic-slice_fusion.1), channel_id=1, source_target_pairs={{0,8},{1,9},{2,10},{3,11},{4,12},{5,13},{6,14},{7,15},{8,0},{9,1},... | collective-permute-start | bytes 393224 | tf_op jit(solution)/shard_map/ppermute | solution.py:53
  255.8 7.0 %collective-permute-start.13 = (f32[1,1,64,256]{3,2,1,0:T(8,128)S(1)}, f32[1,1,64,256]{3,2,1,0:T(8,128)S(1)}, u32[]{:S(2)}, u32[]{:S(2)}) collective-permute-start(f32[1,1,64,256]{3,2,1,0:T(8,128)S(1)} %constant_dynamic-slice_fusion.4), channel_id=1, source_target_pairs={{0,1},{1,0},{2,3},{3,2},{4,5},{5,4},{6,7},{7,6},{8,9},{9,8},{10,11... | collective-permute-start | bytes 196616 | tf_op jit(solution)/shard_map/ppermute | solution.py:53
  257.5 5.3 %collective-permute-start.23 = (f32[1,1,64,256]{3,2,1,0:T(8,128)S(1)}, f32[1,1,64,256]{3,2,1,0:T(8,128)S(1)}, u32[]{:S(2)}, u32[]{:S(2)}) collective-permute-start(f32[1,1,64,256]{3,2,1,0:T(8,128)S(1)} %constant_dynamic-slice_fusion.2), channel_id=1, source_target_pairs={{0,1},{1,0},{2,3},{3,2},{4,5},{5,4},{6,7},{7,6},{8,9},{9,8},{10,11... | collective-permute-start | bytes 196616 | tf_op jit(solution)/shard_map/ppermute | solution.py:53
  262.7 1.3 collective-permute-start.33

commit v15 on v12

--- a/solution.py
+++ b/solution.py
@@ -140,7 +140,7 @@
     )
 
 
-def smooth(sensitivity, below, above, coef, block=128, sub=16):
+def smooth(sensitivity, below, above, coef, block=256, sub=16):
     rows, depth, lat = sensitivity.shape
     kernel = functools.partial(smooth_kernel, sub=sub)
     return pl.pallas_call(

time: 261 us -> 262 us (level)
  no operation moved by 1% of the time
where the time goes in v15:
time: 262 us; the launch traced here: 261 us
  starting transfers between devices  109 us (42%)
  Pallas kernels  73.6 us (28%)
  waiting for transfers between devices  32.1 us (12%)
  local copies, waits for them, and re-layouts  18.4 us (7%)
  matrix products  10.5 us (4%)
  between operations  8.93 us (3%)
  other arithmetic  8.69 us (3%)
    pallas_call x1, Pallas kernels, smooth(): pl.pallas_call(kernel, grid=(rows // block,), in_specs=[pl.BlockSpec(coef...  73.6 us
    ppermute x12, starting transfers between devices, reduce_scatter_slab(): part = keep + lax.ppermute(send, axis, [(i, i ^ bit) for i in range(size)])  72.7 us
    ppermute x12, starting transfers between devices, shift(): return lax.ppermute(v, axis, [(i, (i + step) % size) for i in range(size)])  18.2 us
    ppermute x12, waiting for transfers between devices, reduce_scatter_slab(): part = keep + lax.ppermute(send, axis, [(i, i ^ bit) for i in range(size)])  12.8 us
    ppermute x12, waiting for transfers between devices, shift(): return lax.ppermute(v, axis, [(i, (i + step) % size) for i in range(size)])  12.6 us
    dot_general x3, matrix products, body(): lax.dot_general(flat, received, (((1,), (1,)), ((), ())), preferred_eleme...  10.5 us
    unnamed x21, local copies, waits for them, and re-layouts  8.47 us
    ppermute x2, starting transfers between devices, halo_of(): below = lax.ppermute(top, axis, up)  6.13 us
  transfers between devices with their start and end apart: 34, of which 15 were waited for; matrix products, arithmetic and copies ran while one was open for 10% of the time, Pallas kernels for 0%

profile of v15, /device:TPU:0, one launch (start us, length us, event | category | flops | bytes accessed | tf_op | source)
XLA Modules:
  0.0 260.9 jit_solution(9412128910269563091)
XLA Ops:
  0.6 4.8 %fusion.26 = (bf16[1024,4,256]{2,1,0:T(4,128)(2,1)S(1)}, bf16[1024,4,256]{2,1,0:T(4,128)(2,1)S(1)}) fusion(bf16[1024,8,256]{2,1,0:T(8,128)(2,1)} %a_ref.1), kind=kLoop, calls=%fused_computation.80 | loop fusion | bytes 8388608 | tf_op jit(solution)/shard_map/slice | solution.py:62
  5.5 1.4 collective-permute-start.2
  6.9 1.3 collective-permute-start.3
  8.3 4.7 %collective-permute-start = (f32[4,256]{1,0:T(4,128)S(1)}, f32[4,256]{1,0:T(4,128)S(1)}, u32[]{:S(2)}, u32[]{:S(2)}) collective-permute-start(f32[4,256]{1,0:T(4,128)S(1)} %get-tuple-element.16), channel_id=1, source_target_pairs={{0,1},{1,2},{2,3},{3,4},{4,5},{5,6},{6,7},{7,8},{8,9},{9,10},{10,1... | collective-permute-start | bytes 12296 | tf_op jit(solution)/shard_map/ppermute | solution.py:63
  13.0 1.3 collective-permute-start.1
  14.4 2.9 %collective-permute-done.1 = f32[4,256]{1,0:T(4,128)S(1)} collective-permute-done((f32[4,256]{1,0:T(4,128)S(1)}, f32[4,256]{1,0:T(4,128)S(1)}, u32[]{:S(2)}, u32[]{:S(2)}) %collective-permute-start.1) | collective-permute-done | bytes 4128 | tf_op jit(solution)/shard_map/ppermute | solution.py:64
  18.8 73.6 %shard_map.59 = f32[1024,8,256]{2,1,0:T(8,128)} custom-call(f32[6,16,256]{2,1,0:T(8,128)} %copy-done.3, bf16[1024,8,256]{2,1,0:T(8,128)(2,1)} %a_ref.1, bf16[1024,4,256]{2,1,0:T(4,128)(2,1)} %copy-done.1, bf16[1024,4,256]{2,1,0:T(4,128)(2,1)} %collective-permute-done.3.hi_ref), custom_call_target="tpu_custom_call" | custom-call | tf_op jit(solution)/shard_map/pallas_call | solution.py:146
  92.5 3.8 %convert.5 = bf16[1024,8,256]{2,1,0:T(8,128)(2,1)S(1)} convert(f32[1024,8,256]{2,1,0:T(8,128)} %shard_map.59) | non-fusion elementwise | flops 2097152 | bytes 12582912 | tf_op jit(solution)/shard_map/convert.2
  97.4 1.6 collective-permute-start.4
  108.0 5.6 %copy.17 = bf16[128,8,8,256]{3,1,2,0:T(8,128)(2,1)} copy(bf16[128,8,8,256]{3,2,1,0:T(8,128)(2,1)} %bitcast.84) | data formatting | bytes 8388608
  114.0 1.7 collective-permute-start.24
  115.9 2.0 collective-permute-start.5
  117.8 2.2 collective-permute-start.6
  120.2 3.2 %collective-permute-start.16 = (bf16[128,2048]{1,0:T(8,128)(2,1)S(1)}, bf16[128,2048]{1,0:T(8,128)(2,1)S(1)}, u32[]{:S(2)}, u32[]{:S(2)}) collective-permute-start(bf16[128,2048]{1,0:T(8,128)(2,1)S(1)} %broadcast_select_fusion.1), channel_id=1, source_target_pairs={{0,96},{16,112},{32,0},{48,16},{64,32},{80,48},{96,64},{112,80},{1... | collective-permute-start | bytes 1572872 | tf_op jit(solution)/shard_map/ppermute | solution.py:28
  123.4 3.7 %collective-permute-done.24 = bf16[128,2048]{1,0:T(8,128)(2,1)S(1)} collective-permute-done((bf16[128,2048]{1,0:T(8,128)(2,1)S(1)}, bf16[128,2048]{1,0:T(8,128)(2,1)S(1)}, u32[]{:S(2)}, u32[]{:S(2)}) %collective-permute-start.24) | collective-permute-done | bytes 524320 | tf_op jit(solution)/shard_map/ppermute | solution.py:30
  127.1 2.0 collective-permute-start.25
  129.1 2.2 collective-permute-start.26
  131.5 1.2 collective-permute-done.15
  132.7 2.0 collective-permute-start.8
  135.0 3.4 %collective-permute-done.25 = bf16[128,2048]{1,0:T(8,128)(2,1)S(1)} collective-permute-done((bf16[128,2048]{1,0:T(8,128)(2,1)S(1)}, bf16[128,2048]{1,0:T(8,128)(2,1)S(1)}, u32[]{:S(2)}, u32[]{:S(2)}) %collective-permute-start.25) | collective-permute-done | bytes 524320 | tf_op jit(solution)/shard_map/ppermute | solution.py:28
  138.4 2.0 collective-permute-start.18
  140.6 2.5 collective-permute-done.7
  143.2 2.3 collective-permute-start.28
  145.6 1.7 collective-permute-start.9
  147.4 1.4 collective-permute-done.17
  149.2 1.7 collective-permute-start.19
  151.0 3.4 %collective-permute-done.27 = bf16[64,2048]{1,0:T(8,128)(2,1)S(1)} collective-permute-done((bf16[64,2048]{1,0:T(8,128)(2,1)S(1)}, bf16[64,2048]{1,0:T(8,128)(2,1)S(1)}, u32[]{:S(2)}, u32[]{:S(2)}) %collective-permute-start.27) | collective-permute-done | bytes 262176 | tf_op jit(solution)/shard_map/ppermute | solution.py:28
  155.6 1.7 collective-permute-start.29
  157.3 1.3 fusion.2
  159.8 19.5 %collective-permute-start.10 = (f32[8,64,256]{2,1,0:T(8,128)}, f32[8,64,256]{2,1,0:T(8,128)}, u32[]{:S(2)}, u32[]{:S(2)}) collective-permute-start(f32[8,64,256]{2,1,0:T(8,128)} %dynamic-slice_bitcast_fusion.2), channel_id=1, source_target_pairs={{0,1},{1,0},{2,3},{3,2},{4,5},{5,4},{6,7},{7,6},{8,9},{9,8},{10,11... | collective-permute-start | bytes 1572872 | tf_op jit(solution)/shard_map/ppermute | solution.py:52
  179.3 4.1 %fusion.1 = f32[1024,256]{0,1:T(8,128)S(1)} fusion(bf16[1024,2048]{1,0:T(8,128)(2,1)} %bitcast.85, bf16[128,2048]{1,0:T(8,128)(2,1)} %collective-permute-done.19, bf16[128,2048]{1,0:T(8,128)(2,1)} %copy-done.2, pred[]{:T(512)S(6)} %eq.83), kind=kOutput, calls=%fused_computation.3 | convolution fusion | flops 1078722560 | bytes 6291457 | tf_op jit(solution)/shard_map/dot_general | solution.py:176
  184.6 3.2 %collective-permute-start.20 = (f32[8,64,256]{2,1,0:T(8,128)}, f32[8,64,256]{2,1,0:T(8,128)}, u32[]{:S(2)}, u32[]{:S(2)}) collective-permute-start(f32[8,64,256]{2,1,0:T(8,128)} %dynamic-slice_bitcast_fusion.1), channel_id=1, source_target_pairs={{0,1},{1,0},{2,3},{3,2},{4,5},{5,4},{6,7},{7,6},{8,9},{9,8},{10,11... | collective-permute-start | bytes 1572872 | tf_op jit(solution)/shard_map/ppermute | solution.py:52
  187.9 5.1 %fusion = f32[1024,256]{0,1:T(8,128)} fusion(bf16[1024,2048]{1,0:T(8,128)(2,1)} %bitcast.86, bf16[128,2048]{1,0:T(8,128)(2,1)} %collective-permute-done.29, bf16[128,2048]{1,0:T(8,128)(2,1)} %maximum_select_fusion.8, pred[]{:T(512)S(6)} %eq.87), kind=kOutput, calls=%fused_computation.1 | convolution fusion | flops 1078722560 | bytes 6291457 | tf_op jit(solution)/shard_map/dot_general | solution.py:176
  193.0 1.6 copy.14
  194.9 1.1 bitcast_add_fusion.2
  196.1 30.2 %collective-permute-start.11 = (f32[4,64,256]{2,1,0:T(8,128)S(1)}, f32[4,64,256]{2,1,0:T(8,128)S(1)}, u32[]{:S(2)}, u32[]{:S(2)}) collective-permute-start(f32[4,64,256]{2,1,0:T(8,128)S(1)} %dynamic-slice_bitcast_fusion.5), channel_id=1, source_target_pairs={{0,2},{1,3},{2,0},{3,1},{4,6},{5,7},{6,4},{7,5},{8,10},{9,11},{10,... | collective-permute-start | bytes 786440 | tf_op jit(solution)/shard_map/ppermute | solution.py:52
  226.3 1.1 bitcast_add_fusion.1
  227.6 2.1 collective-permute-start.31
  229.7 3.7 %collective-permute-done.11 = f32[4,64,256]{2,1,0:T(8,128)S(1)} collective-permute-done((f32[4,64,256]{2,1,0:T(8,128)S(1)}, f32[4,64,256]{2,1,0:T(8,128)S(1)}, u32[]{:S(2)}, u32[]{:S(2)}) %collective-permute-start.11) | collective-permute-done | bytes 262176 | tf_op jit(solution)/shard_map/ppermute | solution.py:52
  233.5 3.0 %collective-permute-start.12 = (f32[2,64,256]{2,1,0:T(8,128)S(1)}, f32[2,64,256]{2,1,0:T(8,128)S(1)}, u32[]{:S(2)}, u32[]{:S(2)}) collective-permute-start(f32[2,64,256]{2,1,0:T(8,128)S(1)} %dynamic-slice_bitcast_fusion.8), channel_id=1, source_target_pairs={{0,4},{1,5},{2,6},{3,7},{4,0},{5,1},{6,2},{7,3},{8,12},{9,13},{10,... | collective-permute-start | bytes 393224 | tf_op jit(solution)/shard_map/ppermute | solution.py:52
  236.5 2.6 collective-permute-done.21
  239.1 3.0 %collective-permute-start.22 = (f32[2,64,256]{2,1,0:T(8,128)S(1)}, f32[2,64,256]{2,1,0:T(8,128)S(1)}, u32[]{:S(2)}, u32[]{:S(2)}) collective-permute-start(f32[2,64,256]{2,1,0:T(8,128)S(1)} %dynamic-slice_bitcast_fusion.7), channel_id=1, source_target_pairs={{0,4},{1,5},{2,6},{3,7},{4,0},{5,1},{6,2},{7,3},{8,12},{9,13},{10,... | collective-permute-start | bytes 393224 | tf_op jit(solution)/shard_map/ppermute | solution.py:52
  242.1 2.6 collective-permute-done.31
  244.7 3.0 %collective-permute-start.32 = (f32[2,64,256]{2,1,0:T(8,128)S(1)}, f32[2,64,256]{2,1,0:T(8,128)S(1)}, u32[]{:S(2)}, u32[]{:S(2)}) collective-permute-start(f32[2,64,256]{2,1,0:T(8,128)S(1)} %dynamic-slice_bitcast_fusion.6), channel_id=1, source_target_pairs={{0,4},{1,5},{2,6},{3,7},{4,0},{5,1},{6,2},{7,3},{8,12},{9,13},{10,... | collective-permute-start | bytes 393224 | tf_op jit(solution)/shard_map/ppermute | solution.py:52
  248.5 3.0 %collective-permute-start.13 = (f32[1,64,256]{2,1,0:T(8,128)S(1)}, f32[1,64,256]{2,1,0:T(8,128)S(1)}, u32[]{:S(2)}, u32[]{:S(2)}) collective-permute-start(f32[1,64,256]{2,1,0:T(8,128)S(1)} %constant_dynamic-slice_fusion.2), channel_id=1, source_target_pairs={{0,8},{1,9},{2,10},{3,11},{4,12},{5,13},{6,14},{7,15},{8,0},{9,1},... | collective-permute-start | bytes 196616 | tf_op jit(solution)/shard_map/ppermute | solution.py:52
  251.5 2.8 %collective-permute-start.23 = (f32[1,64,256]{2,1,0:T(8,128)S(1)}, f32[1,64,256]{2,1,0:T(8,128)S(1)}, u32[]{:S(2)}, u32[]{:S(2)}) collective-permute-start(f32[1,64,256]{2,1,0:T(8,128)S(1)} %constant_dynamic-slice_fusion.1), channel_id=1, source_target_pairs={{0,8},{1,9},{2,10},{3,11},{4,12},{5,13},{6,14},{7,15},{8,0},{9,1},... | collective-permute-start | bytes 196616 | tf_op jit(solution)/shard_map/ppermute | solution.py:52
  254.3 2.6 collective-permute-start.33
  257.4 2.8 %collective-permute-done.33 = f32[1,64,256]{2,1,0:T(8,128)S(1)} collective-permute-done((f32[1,64,256]{2,1,0:T(8,128)S(1)}, f32[1,64,256]{2,1,0:T(8,128)S(1)}, u32[]{:S(2)}, u32[]{:S(2)}) %collective-permute-start.33) | collective-permute-done | bytes 65568 | tf_op jit(solution)/shard_map/ppermute | solution.py:52
  (101 shorter events, 12.2 us)
Async XLA Ops:
  0.6 7.6 %copy-start.4 = (s32[8,256]{1,0:T(8,128)S(1)}, s32[8,256]{1,0:T(8,128)}, u32[]{:S(2)}) copy-start(s32[8,256]{1,0:T(8,128)} %param.5) | copy-start | bytes 24580
  0.6 7.6 %copy-start.6 = (f32[8]{0:T(128)S(1)}, f32[8]{0:T(128)}, u32[]{:S(2)}) copy-start(f32[8]{0:T(128)} %param.6) | copy-start | bytes 100
  5.5 12.0 %collective-permute-start.2 = (bf16[1024,4,256]{2,1,0:T(4,128)(2,1)S(1)}, bf16[1024,4,256]{2,1,0:T(4,128)(2,1)S(1)}, u32[]{:S(2)}, u32[]{:S(2)}) collective-permute-start(bf16[1024,4,256]{2,1,0:T(4,128)(2,1)S(1)} %get-tuple-element.9), channel_id=1, source_target_pairs={{0,1},{1,2},{2,3},{3,4},{4,5},{5,6},{6,7},{7,8},{8,9},{9,10},{10,1... | collective-permute-start | bytes 6291464 | tf_op jit(solution)/shard_map/ppermute | solution.py:63
  6.9 10.6 %collective-permute-start.3 = (bf16[1024,4,256]{2,1,0:T(4,128)(2,1)S(1)}, bf16[1024,4,256]{2,1,0:T(4,128)(2,1)}, u32[]{:S(2)}, u32[]{:S(2)}) collective-permute-start(bf16[1024,4,256]{2,1,0:T(4,128)(2,1)S(1)} %get-tuple-element.8), channel_id=1, source_target_pairs={{1,0},{2,1},{3,2},{4,3},{5,4},{6,5},{7,6},{8,7},{9,8},{10,9},{11,1... | collective-permute-start | bytes 6291464 | tf_op jit(solution)/shard_map/ppermute | solution.py:64
  8.3 6.1 %collective-permute-start = (f32[4,256]{1,0:T(4,128)S(1)}, f32[4,256]{1,0:T(4,128)S(1)}, u32[]{:S(2)}, u32[]{:S(2)}) collective-permute-start(f32[4,256]{1,0:T(4,128)S(1)} %get-tuple-element.16), channel_id=1, source_target_pairs={{0,1},{1,2},{2,3},{3,4},{4,5},{5,6},{6,7},{7,8},{8,9},{9,10},{10,1... | collective-permute-start | bytes 12296 | tf_op jit(solution)/shard_map/ppermute | solution.py:63
  13.0 4.3 %collective-permute-start.1 = (f32[4,256]{1,0:T(4,128)S(1)}, f32[4,256]{1,0:T(4,128)S(1)}, u32[]{:S(2)}, u32[]{:S(2)}) collective-permute-start(f32[4,256]{1,0:T(4,128)S(1)} %get-tuple-element.17), channel_id=1, source_target_pairs={{1,0},{2,1},{3,2},{4,3},{5,4},{6,5},{7,6},{8,7},{9,8},{10,9},{11,1... | collective-permute-start | bytes 12296 | tf_op jit(solution)/shard_map/ppermute | solution.py:64
  17.4 0.6 copy-start.3
  17.4 1.4 copy-start.1
  96.5 3.1 %copy-start.5 = (s32[8]{0:T(128)S(1)}, s32[8]{0:T(128)}, u32[]{:S(2)}) copy-start(s32[8]{0:T(128)} %param.7) | copy-start | bytes 100
  97.4 18.4 %collective-permute-start.4 = (bf16[128,2048]{1,0:T(8,128)(2,1)}, bf16[128,2048]{1,0:T(8,128)(2,1)}, u32[]{:S(2)}, u32[]{:S(2)}) collective-permute-start(bf16[128,2048]{1,0:T(8,128)(2,1)} %bitcast.43), channel_id=1, source_target_pairs={{0,16},{16,0},{32,48},{48,32},{64,80},{80,64},{96,112},{112,96},{1... | collective-permute-start | bytes 1572872 | tf_op jit(solution)/shard_map/ppermute | solution.py:30
  99.1 21.0 %collective-permute-start.14 = (bf16[128,2048]{1,0:T(8,128)(2,1)S(1)}, bf16[128,2048]{1,0:T(8,128)(2,1)S(1)}, u32[]{:S(2)}, u32[]{:S(2)}) collective-permute-start(bf16[128,2048]{1,0:T(8,128)(2,1)S(1)} %bitcast.115), channel_id=1, source_target_pairs={{0,16},{16,0},{32,48},{48,32},{64,80},{80,64},{96,112},{112,96},{1... | collective-permute-start | bytes 1572872 | tf_op jit(solution)/shard_map/ppermute | solution.py:30
  114.0 13.1 %collective-permute-start.24 = (bf16[128,2048]{1,0:T(8,128)(2,1)S(1)}, bf16[128,2048]{1,0:T(8,128)(2,1)S(1)}, u32[]{:S(2)}, u32[]{:S(2)}) collective-permute-start(bf16[128,2048]{1,0:T(8,128)(2,1)S(1)} %bitcast.116), channel_id=1, source_target_pairs={{0,16},{16,0},{32,48},{48,32},{64,80},{80,64},{96,112},{112,96},{1... | collective-permute-start | bytes 1572872 | tf_op jit(solution)/shard_map/ppermute | solution.py:30
  115.9 13.3 %collective-permute-start.5 = (bf16[128,2048]{1,0:T(8,128)(2,1)S(1)}, bf16[128,2048]{1,0:T(8,128)(2,1)S(1)}, u32[]{:S(2)}, u32[]{:S(2)}) collective-permute-start(bf16[128,2048]{1,0:T(8,128)(2,1)S(1)} %broadcast_select_fusion.2), channel_id=1, source_target_pairs={{0,32},{16,48},{32,64},{48,80},{64,96},{80,112},{96,0},{112,16},{1... | collective-permute-start | bytes 1572872 | tf_op jit(solution)/shard_map/ppermute | solution.py:28
  117.8 13.5 %collective-permute-start.6 = (bf16[128,2048]{1,0:T(8,128)(2,1)S(1)}, bf16[128,2048]{1,0:T(8,128)(2,1)S(1)}, u32[]{:S(2)}, u32[]{:S(2)}) collective-permute-start(bf16[128,2048]{1,0:T(8,128)(2,1)S(1)} %broadcast_select_fusion.2), channel_id=1, source_target_pairs={{0,96},{16,112},{32,0},{48,16},{64,32},{80,48},{96,64},{112,80},{1... | collective-permute-start | bytes 1572872 | tf_op jit(solution)/shard_map/ppermute | solution.py:28
  120.1 12.6 %collective-permute-start.15 = (bf16[128,2048]{1,0:T(8,128)(2,1)S(1)}, bf16[128,2048]{1,0:T(8,128)(2,1)S(1)}, u32[]{:S(2)}, u32[]{:S(2)}) collective-permute-start(bf16[128,2048]{1,0:T(8,128)(2,1)S(1)} %broadcast_select_fusion.1), channel_id=1, source_target_pairs={{0,32},{16,48},{32,64},{48,80},{64,96},{80,112},{96,0},{112,16},{1... | collective-permute-start | bytes 1572872 | tf_op jit(solution)/shard_map/ppermute | solution.py:28
  120.2 14.6 %collective-permute-start.16 = (bf16[128,2048]{1,0:T(8,128)(2,1)S(1)}, bf16[128,2048]{1,0:T(8,128)(2,1)S(1)}, u32[]{:S(2)}, u32[]{:S(2)}) collective-permute-start(bf16[128,2048]{1,0:T(8,128)(2,1)S(1)} %broadcast_select_fusion.1), channel_id=1, source_target_pairs={{0,96},{16,112},{32,0},{48,16},{64,32},{80,48},{96,64},{112,80},{1... | collective-permute-start | bytes 1572872 | tf_op jit(solution)/shard_map/ppermute | solution.py:28
  127.1 11.3 %collective-permute-start.25 = (bf16[128,2048]{1,0:T(8,128)(2,1)S(1)}, bf16[128,2048]{1,0:T(8,128)(2,1)S(1)}, u32[]{:S(2)}, u32[]{:S(2)}) collective-permute-start(bf16[128,2048]{1,0:T(8,128)(2,1)S(1)} %broadcast_select_fusion), channel_id=1, source_target_pairs={{0,32},{16,48},{32,64},{48,80},{64,96},{80,112},{96,0},{112,16},{1... | collective-permute-start | bytes 1572872 | tf_op jit(solution)/shard_map/ppermute | solution.py:28
  129.1 11.3 %collective-permute-start.26 = (bf16[128,2048]{1,0:T(8,128)(2,1)S(1)}, bf16[128,2048]{1,0:T(8,128)(2,1)S(1)}, u32[]{:S(2)}, u32[]{:S(2)}) collective-permute-start(bf16[128,2048]{1,0:T(8,128)(2,1)S(1)} %broadcast_select_fusion), channel_id=1, source_target_pairs={{0,96},{16,112},{32,0},{48,16},{64,32},{80,48},{96,64},{112,80},{1... | collective-permute-start | bytes 1572872 | tf_op jit(solution)/shard_map/ppermute | solution.py:28
  131.5 11.7 %collective-permute-start.7 = (bf16[64,2048]{1,0:T(8,128)(2,1)S(1)}, bf16[64,2048]{1,0:T(8,128)(2,1)S(1)}, u32[]{:S(2)}, u32[]{:S(2)}) collective-permute-start(bf16[64,2048]{1,0:T(8,128)(2,1)S(1)} %get-tuple-element.10), channel_id=1, source_target_pairs={{0,32},{16,48},{32,64},{48,80},{64,96},{80,112},{96,0},{112,16},{1... | collective-permute-start | bytes 786440 | tf_op jit(solution)/shard_map/ppermute | solution.py:28
  132.7 12.7 %collective-permute-start.8 = (bf16[64,2048]{1,0:T(8,128)(2,1)S(1)}, bf16[64,2048]{1,0:T(8,128)(2,1)S(1)}, u32[]{:S(2)}, u32[]{:S(2)}) collective-permute-start(bf16[64,2048]{1,0:T(8,128)(2,1)S(1)} %get-tuple-element.11), channel_id=1, source_target_pairs={{0,96},{16,112},{32,0},{48,16},{64,32},{80,48},{96,64},{112,80},{1... | collective-permute-start | bytes 786440 | tf_op jit(solution)/shard_map/ppermute | solution.py:28
  134.9 13.9 %collective-permute-start.17 = (bf16[64,2048]{1,0:T(8,128)(2,1)S(1)}, bf16[64,2048]{1,0:T(8,128)(2,1)S(1)}, u32[]{:S(2)}, u32[]{:S(2)}) collective-permute-start(bf16[64,2048]{1,0:T(8,128)(2,1)S(1)} %get-tuple-element.12), channel_id=1, source_target_pairs={{0,32},{16,48},{32,64},{48,80},{64,96},{80,112},{96,0},{112,16},{1... | collective-permute-start | bytes 786440 | tf_op jit(solution)/shard_map/ppermute | solution.py:28
  138.4 10.7 %collective-permute-start.18 = (bf16[64,2048]{1,0:T(8,128)(2,1)S(1)}, bf16[64,2048]{1,0:T(8,128)(2,1)S(1)}, u32[]{:S(2)}, u32[]{:S(2)}) collective-permute-start(bf16[64,2048]{1,0:T(8,128)(2,1)S(1)} %get-tuple-element.13), channel_id=1, source_target_pairs={{0,96},{16,112},{32,0},{48,16},{64,32},{80,48},{96,64},{112,80},{1... | collective-permute-start | bytes 786440 | tf_op jit(solution)/shard_map/ppermute | solution.py:28
  140.5 13.9 %collective-permute-start.27 = (bf16[64,2048]{1,0:T(8,128)(2,1)S(1)}, bf16[64,2048]{1,0:T(8,128)(2,1)S(1)}, u32[]{:S(2)}, u32[]{:S(2)}) collective-permute-start(bf16[64,2048]{1,0:T(8,128)(2,1)S(1)} %get-tuple-element.14), channel_id=1, source_target_pairs={{0,32},{16,48},{32,64},{48,80},{64,96},{80,112},{96,0},{112,16},{1... | collective-permute-start | bytes 786440 | tf_op jit(solution)/shard_map/ppermute | solution.py:28
  143.2 14.1 %copy-start = (bf16[128,8,8,256]{3,1,2,0:T(8,128)(2,1)S(1)}, bf16[128,8,8,256]{3,1,2,0:T(8,128)(2,1)}, u32[]{:S(2)}) copy-start(bf16[128,8,8,256]{3,1,2,0:T(8,128)(2,1)} %copy.17) | copy-start | bytes 12582916
  143.2 11.5 %collective-permute-start.28 = (bf16[64,2048]{1,0:T(8,128)(2,1)S(1)}, bf16[64,2048]{1,0:T(8,128)(2,1)S(1)}, u32[]{:S(2)}, u32[]{:S(2)}) collective-permute-start(bf16[64,2048]{1,0:T(8,128)(2,1)S(1)} %get-tuple-element.15), channel_id=1, source_target_pairs={{0,96},{16,112},{32,0},{48,16},{64,32},{80,48},{96,64},{112,80},{1... | collective-permute-start | bytes 786440 | tf_op jit(solution)/shard_map/ppermute | solution.py:28
  145.6 11.7 %collective-permute-start.9 = (bf16[128,2048]{1,0:T(8,128)(2,1)S(1)}, bf16[128,2048]{1,0:T(8,128)(2,1)S(1)}, u32[]{:S(2)}, u32[]{:S(2)}) collective-permute-start(bf16[128,2048]{1,0:T(8,128)(2,1)S(1)} %maximum_select_fusion.6), channel_id=1, source_target_pairs={{0,16},{16,0},{32,48},{48,32},{64,80},{80,64},{96,112},{112,96},{1... | collective-permute-start | bytes 1572872 | tf_op jit(solution)/shard_map/ppermute | solution.py:37
  149.2 9.7 %copy-start.2 = (bf16[128,2048]{1,0:T(8,128)(2,1)}, bf16[128,2048]{1,0:T(8,128)(2,1)S(1)}, u32[]{:S(2)}) copy-start(bf16[128,2048]{1,0:T(8,128)(2,1)S(1)} %maximum_select_fusion.7) | copy-start | bytes 1572868
  149.2 30.0 %collective-permute-start.19 = (bf16[128,2048]{1,0:T(8,128)(2,1)S(1)}, bf16[128,2048]{1,0:T(8,128)(2,1)}, u32[]{:S(2)}, u32[]{:S(2)}) collective-permute-start(bf16[128,2048]{1,0:T(8,128)(2,1)S(1)} %maximum_select_fusion.7), channel_id=1, source_target_pairs={{0,16},{16,0},{32,48},{48,32},{64,80},{80,64},{96,112},{112,96},{1... | collective-permute-start | bytes 1572872 | tf_op jit(solution)/shard_map/ppermute | solution.py:37
  155.6 32.2 %collective-permute-start.29 = (bf16[128,2048]{1,0:T(8,128)(2,1)}, bf16[128,2048]{1,0:T(8,128)(2,1)}, u32[]{:S(2)}, u32[]{:S(2)}) collective-permute-start(bf16[128,2048]{1,0:T(8,128)(2,1)} %maximum_select_fusion.8), channel_id=1, source_target_pairs={{0,16},{16,0},{32,48},{48,32},{64,80},{80,64},{96,112},{112,96},{1... | collective-permute-start | bytes 1572872 | tf_op jit(solution)/shard_map/ppermute | solution.py:37
  159.8 35.2 %collective-permute-start.10 = (f32[8,64,256]{2,1,0:T(8,128)}, f32[8,64,256]{2,1,0:T(8,128)}, u32[]{:S(2)}, u32[]{:S(2)}) collective-permute-start(f32[8,64,256]{2,1,0:T(8,128)} %dynamic-slice_bitcast_fusion.2), channel_id=1, source_target_pairs={{0,1},{1,0},{2,3},{3,2},{4,5},{5,4},{6,7},{7,6},{8,9},{9,8},{10,11... | collective-permute-start | bytes 1572872 | tf_op jit(solution)/shard_map/ppermute | solution.py:52
  184.6 41.6 %collective-permute-start.20 = (f32[8,64,256]{2,1,0:T(8,128)}, f32[8,64,256]{2,1,0:T(8,128)}, u32[]{:S(2)}, u32[]{:S(2)}) collective-permute-start(f32[8,64,256]{2,1,0:T(8,128)} %dynamic-slice_bitcast_fusion.1), channel_id=1, source_target_pairs={{0,1},{1,0},{2,3},{3,2},{4,5},{5,4},{6,7},{7,6},{8,9},{9,8},{10,11... | collective-permute-start | bytes 1572872 | tf_op jit(solution)/shard_map/ppermute | solution.py:52
  194.6 32.9 %collective-permute-start.30 = (f32[8,64,256]{2,1,0:T(8,128)S(1)}, f32[8,64,256]{2,1,0:T(8,128)S(1)}, u32[]{:S(2)}, u32[]{:S(2)}) collective-permute-start(f32[8,64,256]{2,1,0:T(8,128)S(1)} %dynamic-slice_bitcast_fusion), channel_id=1, source_target_pairs={{0,1},{1,0},{2,3},{3,2},{4,5},{5,4},{6,7},{7,6},{8,9},{9,8},{10,11... | collective-permute-start | bytes 1572872 | tf_op jit(solution)/shard_map/ppermute | solution.py:52
  196.1 37.3 %collective-permute-start.11 = (f32[4,64,256]{2,1,0:T(8,128)S(1)}, f32[4,64,256]{2,1,0:T(8,128)S(1)}, u32[]{:S(2)}, u32[]{:S(2)}) collective-permute-start(f32[4,64,256]{2,1,0:T(8,128)S(1)} %dynamic-slice_bitcast_fusion.5), channel_id=1, source_target_pairs={{0,2},{1,3},{2,0},{3,1},{4,6},{5,7},{6,4},{7,5},{8,10},{9,11},{10,... | collective-permute-start | bytes 786440 | tf_op jit(solution)/shard_map/ppermute | solution.py:52
  227.4 11.6 %collective-permute-start.21 = (f32[4,64,256]{2,1,0:T(8,128)S(1)}, f32[4,64,256]{2,1,0:T(8,128)S(1)}, u32[]{:S(2)}, u32[]{:S(2)}) collective-permute-start(f32[4,64,256]{2,1,0:T(8,128)S(1)} %dynamic-slice_bitcast_fusion.4), channel_id=1, source_target_pairs={{0,2},{1,3},{2,0},{3,1},{4,6},{5,7},{6,4},{7,5},{8,10},{9,11},{10,... | collective-permute-start | bytes 786440 | tf_op jit(solution)/shard_map/ppermute | solution.py:52
  227.6 17.0 %collective-permute-start.31 = (f32[4,64,256]{2,1,0:T(8,128)S(1)}, f32[4,64,256]{2,1,0:T(8,128)S(1)}, u32[]{:S(2)}, u32[]{:S(2)}) collective-permute-start(f32[4,64,256]{2,1,0:T(8,128)S(1)} %dynamic-slice_bitcast_fusion.3), channel_id=1, source_target_pairs={{0,2},{1,3},{2,0},{3,1},{4,6},{5,7},{6,4},{7,5},{8,10},{9,11},{10,... | collective-permute-start | bytes 786440 | tf_op jit(solution)/shard_map/ppermute | solution.py:52
  233.5 14.9 %collective-permute-start.12 = (f32[2,64,256]{2,1,0:T(8,128)S(1)}, f32[2,64,256]{2,1,0:T(8,128)S(1)}, u32[]{:S(2)}, u32[]{:S(2)}) collective-permute-start(f32[2,64,256]{2,1,0:T(8,128)S(1)} %dynamic-slice_bitcast_fusion.8), channel_id=1, source_target_pairs={{0,4},{1,5},{2,6},{3,7},{4,0},{5,1},{6,2},{7,3},{8,12},{9,13},{10,... | collective-permute-start | bytes 393224 | tf_op jit(solution)/shard_map/ppermute | solution.py:52
  239.1 12.4 %collective-permute-start.22 = (f32[2,64,256]{2,1,0:T(8,128)S(1)}, f32[2,64,256]{2,1,0:T(8,128)S(1)}, u32[]{:S(2)}, u32[]{:S(2)}) collective-permute-start(f32[2,64,256]{2,1,0:T(8,128)S(1)} %dynamic-slice_bitcast_fusion.7), channel_id=1, source_target_pairs={{0,4},{1,5},{2,6},{3,7},{4,0},{5,1},{6,2},{7,3},{8,12},{9,13},{10,... | collective-permute-start | bytes 393224 | tf_op jit(solution)/shard_map/ppermute | solution.py:52
  244.7 9.6 %collective-permute-start.32 = (f32[2,64,256]{2,1,0:T(8,128)S(1)}, f32[2,64,256]{2,1,0:T(8,128)S(1)}, u32[]{:S(2)}, u32[]{:S(2)}) collective-permute-start(f32[2,64,256]{2,1,0:T(8,128)S(1)} %dynamic-slice_bitcast_fusion.6), channel_id=1, source_target_pairs={{0,4},{1,5},{2,6},{3,7},{4,0},{5,1},{6,2},{7,3},{8,12},{9,13},{10,... | collective-permute-start | bytes 393224 | tf_op jit(solution)/shard_map/ppermute | solution.py:52
  248.5 8.4 %collective-permute-start.13 = (f32[1,64,256]{2,1,0:T(8,128)S(1)}, f32[1,64,256]{2,1,0:T(8,128)S(1)}, u32[]{:S(2)}, u32[]{:S(2)}) collective-permute-start(f32[1,64,256]{2,1,0:T(8,128)S(1)} %constant_dynamic-slice_fusion.2), channel_id=1, source_target_pairs={{0,8},{1,9},{2,10},{3,11},{4,12},{5,13},{6,14},{7,15},{8,0},{9,1},... | collective-permute-start | bytes 196616 | tf_op jit(solution)/shard_map/ppermute | solution.py:52
  251.5 5.8 %collective-permute-start.23 = (f32[1,64,256]{2,1,0:T(8,128)S(1)}, f32[1,64,256]{2,1,0:T(8,128)S(1)}, u32[]{:S(2)}, u32[]{:S(2)}) collective-permute-start(f32[1,64,256]{2,1,0:T(8,128)S(1)} %constant_dynamic-slice_fusion.1), channel_id=1, source_target_pairs={{0,8},{1,9},{2,10},{3,11},{4,12},{5,13},{6,14},{7,15},{8,0},{9,1},... | collective-permute-start | bytes 196616 | tf_op jit(solution)/shard_map/ppermute | solution.py:52
  254.3 5.8 %collective-permute-start.33 = (f32[1,64,256]{2,1,0:T(8,128)S(1)}, f32[1,64,256]{2,1,0:T(8,128)S(1)}, u32[]{:S(2)}, u32[]{:S(2)}) collective-permute-start(f32[1,64,256]{2,1,0:T(8,128)S(1)} %constant_dynamic-slice_fusion), channel_id=1, source_target_pairs={{0,8},{1,9},{2,10},{3,11},{4,12},{5,13},{6,14},{7,15},{8,0},{9,1},... | collective-permute-start | bytes 196616 | tf_op jit(solution)/shard_map/ppermute | solution.py:52

commit v16 on v12

--- a/solution.py
+++ b/solution.py
@@ -35,7 +35,7 @@
     last = jnp.concatenate([shift(val[:quarter], 2), shift(val[quarter:], -2)])
     val = jnp.where(z == (oz + 2) % ring, last, val)
     other = lax.ppermute(val, axis, [(i, i ^ 1) for i in range(size)])
-    return jnp.where(mine, jnp.concatenate([val, other]), jnp.concatenate([other, val]))
+    return jnp.concatenate([jnp.where(mine, val, other), jnp.where(mine, other, val)])
 
 
 def reduce_scatter_slab(term, axis):

time: 261 us -> 260 us (level)
  starting transfers between devices: 109 us -> 103 us
    ppermute x12, starting transfers between devices: 72.7 us -> 67.5 us  [reduce_scatter_slab(): part = keep + lax.ppermute(send, axis, [(i, i ^ bit) for i in range(size)])]
    unnamed x21 -> x19, local copies, waits for them, and re-layouts: 8.47 us -> 8.46 us
  transfers between devices with their start and end apart: 34 -> 34, of which waited for: 15 -> 16; matrix products, arithmetic and copies ran while one was open for 10% -> 11% of each run, Pallas kernels for 0% -> 0%
where the time goes in v16:
time: 260 us; the launch traced here: 259 us
  starting transfers between devices  103 us (40%)
  Pallas kernels  73 us (28%)
  waiting for transfers between devices  33.5 us (13%)
  local copies, waits for them, and re-layouts  20.8 us (8%)
  matrix products  11.2 us (4%)
  other arithmetic  9.17 us (4%)
  between operations  8.78 us (3%)
    pallas_call x1, Pallas kernels, smooth(): pl.pallas_call(kernel, grid=(rows // block,), in_specs=[pl.BlockSpec(coef...  73 us
    ppermute x12, starting transfers between devices, reduce_scatter_slab(): part = keep + lax.ppermute(send, axis, [(i, i ^ bit) for i in range(size)])  67.5 us
    ppermute x12, starting transfers between devices, shift(): return lax.ppermute(v, axis, [(i, (i + step) % size) for i in range(size)])  18.2 us
    ppermute x12, waiting for transfers between devices, reduce_scatter_slab(): part = keep + lax.ppermute(send, axis, [(i, i ^ bit) for i in range(size)])  14 us
    ppermute x12, waiting for transfers between devices, shift(): return lax.ppermute(v, axis, [(i, (i + step) % size) for i in range(size)])  13.1 us
    dot_general x3, matrix products, body(): lax.dot_general(flat, received, (((1,), (1,)), ((), ())), preferred_eleme...  11.2 us
    unnamed x19, local copies, waits for them, and re-layouts  8.46 us
    ppermute x2, starting transfers between devices, halo_of(): below = lax.ppermute(top, axis, up)  6.13 us
  transfers between devices with their start and end apart: 34, of which 16 were waited for; matrix products, arithmetic and copies ran while one was open for 11% of the time, Pallas kernels for 0%

profile of v16, /device:TPU:0, one launch (start us, length us, event | category | flops | bytes accessed | tf_op | source)
XLA Modules:
  0.0 259.5 jit_solution(9437945058867082938)
XLA Ops:
  0.6 4.8 %fusion.17 = (bf16[1024,4,256]{2,1,0:T(4,128)(2,1)S(1)}, bf16[1024,4,256]{2,1,0:T(4,128)(2,1)S(1)}) fusion(bf16[1024,8,256]{2,1,0:T(8,128)(2,1)} %a_ref.1), kind=kLoop, calls=%fused_computation.74 | loop fusion | bytes 8388608 | tf_op jit(solution)/shard_map/slice | solution.py:62
  5.5 1.4 collective-permute-start.2
  6.9 1.3 collective-permute-start.3
  8.3 4.7 %collective-permute-start = (f32[4,256]{1,0:T(4,128)S(1)}, f32[4,256]{1,0:T(4,128)S(1)}, u32[]{:S(2)}, u32[]{:S(2)}) collective-permute-start(f32[4,256]{1,0:T(4,128)S(1)} %get-tuple-element.22), channel_id=1, source_target_pairs={{0,1},{1,2},{2,3},{3,4},{4,5},{5,6},{6,7},{7,8},{8,9},{9,10},{10,1... | collective-permute-start | bytes 12296 | tf_op jit(solution)/shard_map/ppermute | solution.py:63
  13.0 1.3 collective-permute-start.1
  14.4 2.9 %collective-permute-done.1 = f32[4,256]{1,0:T(4,128)S(1)} collective-permute-done((f32[4,256]{1,0:T(4,128)S(1)}, f32[4,256]{1,0:T(4,128)S(1)}, u32[]{:S(2)}, u32[]{:S(2)}) %collective-permute-start.1) | collective-permute-done | bytes 4128 | tf_op jit(solution)/shard_map/ppermute | solution.py:64
  18.8 73.0 %shard_map.59 = f32[1024,8,256]{2,1,0:T(8,128)} custom-call(f32[6,16,256]{2,1,0:T(8,128)} %copy-done.2, bf16[1024,8,256]{2,1,0:T(8,128)(2,1)} %a_ref.1, bf16[1024,4,256]{2,1,0:T(4,128)(2,1)} %copy-done.1, bf16[1024,4,256]{2,1,0:T(4,128)(2,1)} %collective-permute-done.3.hi_ref), custom_call_target="tpu_custom_call" | custom-call | tf_op jit(solution)/shard_map/pallas_call | solution.py:146
  91.8 3.8 %convert.5 = bf16[1024,8,256]{2,1,0:T(8,128)(2,1)S(1)} convert(f32[1024,8,256]{2,1,0:T(8,128)} %shard_map.59) | non-fusion elementwise | flops 2097152 | bytes 12582912 | tf_op jit(solution)/shard_map/convert.2
  96.8 1.6 collective-permute-start.4
  107.2 5.6 %copy.17 = bf16[128,8,8,256]{3,1,2,0:T(8,128)(2,1)} copy(bf16[128,8,8,256]{3,2,1,0:T(8,128)(2,1)} %bitcast.84) | data formatting | bytes 8388608
  113.2 1.7 collective-permute-start.24
  115.1 2.0 collective-permute-start.5
  117.1 2.2 collective-permute-start.6
  119.4 3.2 %collective-permute-start.16 = (bf16[128,2048]{1,0:T(8,128)(2,1)S(1)}, bf16[128,2048]{1,0:T(8,128)(2,1)S(1)}, u32[]{:S(2)}, u32[]{:S(2)}) collective-permute-start(bf16[128,2048]{1,0:T(8,128)(2,1)S(1)} %broadcast_select_fusion.5), channel_id=1, source_target_pairs={{0,96},{16,112},{32,0},{48,16},{64,32},{80,48},{96,64},{112,80},{1... | collective-permute-start | bytes 1572872 | tf_op jit(solution)/shard_map/ppermute | solution.py:28
  122.6 3.5 %collective-permute-done.24 = bf16[128,2048]{1,0:T(8,128)(2,1)S(1)} collective-permute-done((bf16[128,2048]{1,0:T(8,128)(2,1)S(1)}, bf16[128,2048]{1,0:T(8,128)(2,1)S(1)}, u32[]{:S(2)}, u32[]{:S(2)}) %collective-permute-start.24) | collective-permute-done | bytes 524320 | tf_op jit(solution)/shard_map/ppermute | solution.py:30
  126.2 2.0 collective-permute-start.25
  128.2 2.2 collective-permute-start.26
  130.6 1.4 collective-permute-done.15
  132.0 2.0 collective-permute-start.8
  134.2 3.4 %collective-permute-done.25 = bf16[128,2048]{1,0:T(8,128)(2,1)S(1)} collective-permute-done((bf16[128,2048]{1,0:T(8,128)(2,1)S(1)}, bf16[128,2048]{1,0:T(8,128)(2,1)S(1)}, u32[]{:S(2)}, u32[]{:S(2)}) %collective-permute-start.25) | collective-permute-done | bytes 524320 | tf_op jit(solution)/shard_map/ppermute | solution.py:28
  137.6 2.0 collective-permute-start.18
  139.8 2.5 collective-permute-done.7
  142.3 2.3 collective-permute-start.28
  144.8 1.6 collective-permute-start.9
  146.3 1.6 collective-permute-done.17
  148.4 1.6 collective-permute-start.19
  149.9 3.6 %collective-permute-done.27 = bf16[64,2048]{1,0:T(8,128)(2,1)S(1)} collective-permute-done((bf16[64,2048]{1,0:T(8,128)(2,1)S(1)}, bf16[64,2048]{1,0:T(8,128)(2,1)S(1)}, u32[]{:S(2)}, u32[]{:S(2)}) %collective-permute-start.27) | collective-permute-done | bytes 262176 | tf_op jit(solution)/shard_map/ppermute | solution.py:28
  154.0 1.6 collective-permute-start.29
  155.6 2.3 fusion.2
  157.9 1.6 copy.12
  160.3 20.3 %collective-permute-start.10 = (f32[8,64,256]{2,1,0:T(8,128)}, f32[8,64,256]{2,1,0:T(8,128)}, u32[]{:S(2)}, u32[]{:S(2)}) collective-permute-start(f32[8,64,256]{2,1,0:T(8,128)} %dynamic-slice_bitcast_fusion.2), channel_id=1, source_target_pairs={{0,1},{1,0},{2,3},{3,2},{4,5},{5,4},{6,7},{7,6},{8,9},{9,8},{10,11... | collective-permute-start | bytes 1572872 | tf_op jit(solution)/shard_map/ppermute | solution.py:52
  181.8 4.5 %fusion.1 = f32[1024,256]{0,1:T(8,128)} fusion(bf16[1024,2048]{1,0:T(8,128)(2,1)} %bitcast.85, bf16[128,2048]{1,0:T(8,128)(2,1)S(1)} %get-tuple-element.13, bf16[128,2048]{1,0:T(8,128)(2,1)S(1)} %get-tuple-element.12), kind=kOutput, calls=%fused_computation.3 | convolution fusion | flops 1076101120 | bytes 6291456 | tf_op jit(solution)/shard_map/dot_general | solution.py:176
  186.3 1.6 copy.13
  189.7 4.5 %fusion = f32[1024,256]{0,1:T(8,128)} fusion(bf16[1024,2048]{1,0:T(8,128)(2,1)} %bitcast.86, bf16[128,2048]{1,0:T(8,128)(2,1)S(1)} %get-tuple-element.15, bf16[128,2048]{1,0:T(8,128)(2,1)S(1)} %get-tuple-element.14), kind=kOutput, calls=%fused_computation.1 | convolution fusion | flops 1076101120 | bytes 6291456 | tf_op jit(solution)/shard_map/dot_general | solution.py:176
  194.1 1.6 copy.14
  197.0 27.8 %collective-permute-start.11 = (f32[4,64,256]{2,1,0:T(8,128)S(1)}, f32[4,64,256]{2,1,0:T(8,128)S(1)}, u32[]{:S(2)}, u32[]{:S(2)}) collective-permute-start(f32[4,64,256]{2,1,0:T(8,128)S(1)} %dynamic-slice_bitcast_fusion.5), channel_id=1, source_target_pairs={{0,2},{1,3},{2,0},{3,1},{4,6},{5,7},{6,4},{7,5},{8,10},{9,11},{10,... | collective-permute-start | bytes 786440 | tf_op jit(solution)/shard_map/ppermute | solution.py:52
  226.2 2.1 collective-permute-start.31
  228.3 3.7 %collective-permute-done.11 = f32[4,64,256]{2,1,0:T(8,128)S(1)} collective-permute-done((f32[4,64,256]{2,1,0:T(8,128)S(1)}, f32[4,64,256]{2,1,0:T(8,128)S(1)}, u32[]{:S(2)}, u32[]{:S(2)}) %collective-permute-start.11) | collective-permute-done | bytes 262176 | tf_op jit(solution)/shard_map/ppermute | solution.py:52
  232.0 3.0 %collective-permute-start.12 = (f32[2,64,256]{2,1,0:T(8,128)S(1)}, f32[2,64,256]{2,1,0:T(8,128)S(1)}, u32[]{:S(2)}, u32[]{:S(2)}) collective-permute-start(f32[2,64,256]{2,1,0:T(8,128)S(1)} %dynamic-slice_bitcast_fusion.8), channel_id=1, source_target_pairs={{0,4},{1,5},{2,6},{3,7},{4,0},{5,1},{6,2},{7,3},{8,12},{9,13},{10,... | collective-permute-start | bytes 393224 | tf_op jit(solution)/shard_map/ppermute | solution.py:52
  235.0 2.6 collective-permute-done.21
  237.6 3.0 %collective-permute-start.22 = (f32[2,64,256]{2,1,0:T(8,128)S(1)}, f32[2,64,256]{2,1,0:T(8,128)S(1)}, u32[]{:S(2)}, u32[]{:S(2)}) collective-permute-start(f32[2,64,256]{2,1,0:T(8,128)S(1)} %dynamic-slice_bitcast_fusion.7), channel_id=1, source_target_pairs={{0,4},{1,5},{2,6},{3,7},{4,0},{5,1},{6,2},{7,3},{8,12},{9,13},{10,... | collective-permute-start | bytes 393224 | tf_op jit(solution)/shard_map/ppermute | solution.py:52
  240.6 2.6 collective-permute-done.31
  243.3 3.0 %collective-permute-start.32 = (f32[2,64,256]{2,1,0:T(8,128)S(1)}, f32[2,64,256]{2,1,0:T(8,128)S(1)}, u32[]{:S(2)}, u32[]{:S(2)}) collective-permute-start(f32[2,64,256]{2,1,0:T(8,128)S(1)} %dynamic-slice_bitcast_fusion.6), channel_id=1, source_target_pairs={{0,4},{1,5},{2,6},{3,7},{4,0},{5,1},{6,2},{7,3},{8,12},{9,13},{10,... | collective-permute-start | bytes 393224 | tf_op jit(solution)/shard_map/ppermute | solution.py:52
  246.3 1.4 collective-permute-done.12
  247.7 2.3 collective-permute-start.13
  250.5 2.3 collective-permute-start.23
  252.9 2.5 collective-permute-start.33
  256.4 2.4 collective-permute-done.33
  (102 shorter events, 15.1 us)
Async XLA Ops:
  0.6 7.6 %copy-start.3 = (s32[8,256]{1,0:T(8,128)S(1)}, s32[8,256]{1,0:T(8,128)}, u32[]{:S(2)}) copy-start(s32[8,256]{1,0:T(8,128)} %param.5) | copy-start | bytes 24580
  0.6 7.6 %copy-start.5 = (f32[8]{0:T(128)S(1)}, f32[8]{0:T(128)}, u32[]{:S(2)}) copy-start(f32[8]{0:T(128)} %param.6) | copy-start | bytes 100
  5.5 12.0 %collective-permute-start.2 = (bf16[1024,4,256]{2,1,0:T(4,128)(2,1)S(1)}, bf16[1024,4,256]{2,1,0:T(4,128)(2,1)S(1)}, u32[]{:S(2)}, u32[]{:S(2)}) collective-permute-start(bf16[1024,4,256]{2,1,0:T(4,128)(2,1)S(1)} %get-tuple-element.9), channel_id=1, source_target_pairs={{0,1},{1,2},{2,3},{3,4},{4,5},{5,6},{6,7},{7,8},{8,9},{9,10},{10,1... | collective-permute-start | bytes 6291464 | tf_op jit(solution)/shard_map/ppermute | solution.py:63
  6.9 10.6 %collective-permute-start.3 = (bf16[1024,4,256]{2,1,0:T(4,128)(2,1)S(1)}, bf16[1024,4,256]{2,1,0:T(4,128)(2,1)}, u32[]{:S(2)}, u32[]{:S(2)}) collective-permute-start(bf16[1024,4,256]{2,1,0:T(4,128)(2,1)S(1)} %get-tuple-element.8), channel_id=1, source_target_pairs={{1,0},{2,1},{3,2},{4,3},{5,4},{6,5},{7,6},{8,7},{9,8},{10,9},{11,1... | collective-permute-start | bytes 6291464 | tf_op jit(solution)/shard_map/ppermute | solution.py:64
  8.3 6.1 %collective-permute-start = (f32[4,256]{1,0:T(4,128)S(1)}, f32[4,256]{1,0:T(4,128)S(1)}, u32[]{:S(2)}, u32[]{:S(2)}) collective-permute-start(f32[4,256]{1,0:T(4,128)S(1)} %get-tuple-element.22), channel_id=1, source_target_pairs={{0,1},{1,2},{2,3},{3,4},{4,5},{5,6},{6,7},{7,8},{8,9},{9,10},{10,1... | collective-permute-start | bytes 12296 | tf_op jit(solution)/shard_map/ppermute | solution.py:63
  13.0 4.3 %collective-permute-start.1 = (f32[4,256]{1,0:T(4,128)S(1)}, f32[4,256]{1,0:T(4,128)S(1)}, u32[]{:S(2)}, u32[]{:S(2)}) collective-permute-start(f32[4,256]{1,0:T(4,128)S(1)} %get-tuple-element.23), channel_id=1, source_target_pairs={{1,0},{2,1},{3,2},{4,3},{5,4},{6,5},{7,6},{8,7},{9,8},{10,9},{11,1... | collective-permute-start | bytes 12296 | tf_op jit(solution)/shard_map/ppermute | solution.py:64
  17.4 0.6 copy-start.2
  17.4 1.4 copy-start.1
  95.6 3.4 %copy-start.4 = (s32[8]{0:T(128)S(1)}, s32[8]{0:T(128)}, u32[]{:S(2)}) copy-start(s32[8]{0:T(128)} %param.7) | copy-start | bytes 100
  96.8 18.2 %collective-permute-start.4 = (bf16[128,2048]{1,0:T(8,128)(2,1)}, bf16[128,2048]{1,0:T(8,128)(2,1)}, u32[]{:S(2)}, u32[]{:S(2)}) collective-permute-start(bf16[128,2048]{1,0:T(8,128)(2,1)} %bitcast.43), channel_id=1, source_target_pairs={{0,16},{16,0},{32,48},{48,32},{64,80},{80,64},{96,112},{112,96},{1... | collective-permute-start | bytes 1572872 | tf_op jit(solution)/shard_map/ppermute | solution.py:30
  98.5 20.8 %collective-permute-start.14 = (bf16[128,2048]{1,0:T(8,128)(2,1)S(1)}, bf16[128,2048]{1,0:T(8,128)(2,1)S(1)}, u32[]{:S(2)}, u32[]{:S(2)}) collective-permute-start(bf16[128,2048]{1,0:T(8,128)(2,1)S(1)} %bitcast.115), channel_id=1, source_target_pairs={{0,16},{16,0},{32,48},{48,32},{64,80},{80,64},{96,112},{112,96},{1... | collective-permute-start | bytes 1572872 | tf_op jit(solution)/shard_map/ppermute | solution.py:30
  113.2 12.9 %collective-permute-start.24 = (bf16[128,2048]{1,0:T(8,128)(2,1)S(1)}, bf16[128,2048]{1,0:T(8,128)(2,1)S(1)}, u32[]{:S(2)}, u32[]{:S(2)}) collective-permute-start(bf16[128,2048]{1,0:T(8,128)(2,1)S(1)} %bitcast.116), channel_id=1, source_target_pairs={{0,16},{16,0},{32,48},{48,32},{64,80},{80,64},{96,112},{112,96},{1... | collective-permute-start | bytes 1572872 | tf_op jit(solution)/shard_map/ppermute | solution.py:30
  115.1 13.1 %collective-permute-start.5 = (bf16[128,2048]{1,0:T(8,128)(2,1)S(1)}, bf16[128,2048]{1,0:T(8,128)(2,1)S(1)}, u32[]{:S(2)}, u32[]{:S(2)}) collective-permute-start(bf16[128,2048]{1,0:T(8,128)(2,1)S(1)} %broadcast_select_fusion.8), channel_id=1, source_target_pairs={{0,32},{16,48},{32,64},{48,80},{64,96},{80,112},{96,0},{112,16},{1... | collective-permute-start | bytes 1572872 | tf_op jit(solution)/shard_map/ppermute | solution.py:28
  117.1 13.3 %collective-permute-start.6 = (bf16[128,2048]{1,0:T(8,128)(2,1)S(1)}, bf16[128,2048]{1,0:T(8,128)(2,1)S(1)}, u32[]{:S(2)}, u32[]{:S(2)}) collective-permute-start(bf16[128,2048]{1,0:T(8,128)(2,1)S(1)} %broadcast_select_fusion.8), channel_id=1, source_target_pairs={{0,96},{16,112},{32,0},{48,16},{64,32},{80,48},{96,64},{112,80},{1... | collective-permute-start | bytes 1572872 | tf_op jit(solution)/shard_map/ppermute | solution.py:28
  119.3 12.6 %collective-permute-start.15 = (bf16[128,2048]{1,0:T(8,128)(2,1)S(1)}, bf16[128,2048]{1,0:T(8,128)(2,1)S(1)}, u32[]{:S(2)}, u32[]{:S(2)}) collective-permute-start(bf16[128,2048]{1,0:T(8,128)(2,1)S(1)} %broadcast_select_fusion.5), channel_id=1, source_target_pairs={{0,32},{16,48},{32,64},{48,80},{64,96},{80,112},{96,0},{112,16},{1... | collective-permute-start | bytes 1572872 | tf_op jit(solution)/shard_map/ppermute | solution.py:28
  119.4 14.6 %collective-permute-start.16 = (bf16[128,2048]{1,0:T(8,128)(2,1)S(1)}, bf16[128,2048]{1,0:T(8,128)(2,1)S(1)}, u32[]{:S(2)}, u32[]{:S(2)}) collective-permute-start(bf16[128,2048]{1,0:T(8,128)(2,1)S(1)} %broadcast_select_fusion.5), channel_id=1, source_target_pairs={{0,96},{16,112},{32,0},{48,16},{64,32},{80,48},{96,64},{112,80},{1... | collective-permute-start | bytes 1572872 | tf_op jit(solution)/shard_map/ppermute | solution.py:28
  126.2 11.4 %collective-permute-start.25 = (bf16[128,2048]{1,0:T(8,128)(2,1)S(1)}, bf16[128,2048]{1,0:T(8,128)(2,1)S(1)}, u32[]{:S(2)}, u32[]{:S(2)}) collective-permute-start(bf16[128,2048]{1,0:T(8,128)(2,1)S(1)} %broadcast_select_fusion.2), channel_id=1, source_target_pairs={{0,32},{16,48},{32,64},{48,80},{64,96},{80,112},{96,0},{112,16},{1... | collective-permute-start | bytes 1572872 | tf_op jit(solution)/shard_map/ppermute | solution.py:28
  128.2 11.4 %collective-permute-start.26 = (bf16[128,2048]{1,0:T(8,128)(2,1)S(1)}, bf16[128,2048]{1,0:T(8,128)(2,1)S(1)}, u32[]{:S(2)}, u32[]{:S(2)}) collective-permute-start(bf16[128,2048]{1,0:T(8,128)(2,1)S(1)} %broadcast_select_fusion.2), channel_id=1, source_target_pairs={{0,96},{16,112},{32,0},{48,16},{64,32},{80,48},{96,64},{112,80},{1... | collective-permute-start | bytes 1572872 | tf_op jit(solution)/shard_map/ppermute | solution.py:28
  130.5 11.8 %collective-permute-start.7 = (bf16[64,2048]{1,0:T(8,128)(2,1)S(1)}, bf16[64,2048]{1,0:T(8,128)(2,1)S(1)}, u32[]{:S(2)}, u32[]{:S(2)}) collective-permute-start(bf16[64,2048]{1,0:T(8,128)(2,1)S(1)} %get-tuple-element.16), channel_id=1, source_target_pairs={{0,32},{16,48},{32,64},{48,80},{64,96},{80,112},{96,0},{112,16},{1... | collective-permute-start | bytes 786440 | tf_op jit(solution)/shard_map/ppermute | solution.py:28
  132.0 12.7 %collective-permute-start.8 = (bf16[64,2048]{1,0:T(8,128)(2,1)S(1)}, bf16[64,2048]{1,0:T(8,128)(2,1)S(1)}, u32[]{:S(2)}, u32[]{:S(2)}) collective-permute-start(bf16[64,2048]{1,0:T(8,128)(2,1)S(1)} %get-tuple-element.17), channel_id=1, source_target_pairs={{0,96},{16,112},{32,0},{48,16},{64,32},{80,48},{96,64},{112,80},{1... | collective-permute-start | bytes 786440 | tf_op jit(solution)/shard_map/ppermute | solution.py:28
  134.1 13.8 %collective-permute-start.17 = (bf16[64,2048]{1,0:T(8,128)(2,1)S(1)}, bf16[64,2048]{1,0:T(8,128)(2,1)S(1)}, u32[]{:S(2)}, u32[]{:S(2)}) collective-permute-start(bf16[64,2048]{1,0:T(8,128)(2,1)S(1)} %get-tuple-element.18), channel_id=1, source_target_pairs={{0,32},{16,48},{32,64},{48,80},{64,96},{80,112},{96,0},{112,16},{1... | collective-permute-start | bytes 786440 | tf_op jit(solution)/shard_map/ppermute | solution.py:28
  137.6 10.6 %collective-permute-start.18 = (bf16[64,2048]{1,0:T(8,128)(2,1)S(1)}, bf16[64,2048]{1,0:T(8,128)(2,1)S(1)}, u32[]{:S(2)}, u32[]{:S(2)}) collective-permute-start(bf16[64,2048]{1,0:T(8,128)(2,1)S(1)} %get-tuple-element.19), channel_id=1, source_target_pairs={{0,96},{16,112},{32,0},{48,16},{64,32},{80,48},{96,64},{112,80},{1... | collective-permute-start | bytes 786440 | tf_op jit(solution)/shard_map/ppermute | solution.py:28
  139.7 15.9 %copy-start = (bf16[128,8,8,256]{3,1,2,0:T(8,128)(2,1)S(1)}, bf16[128,8,8,256]{3,1,2,0:T(8,128)(2,1)}, u32[]{:S(2)}) copy-start(bf16[128,8,8,256]{3,1,2,0:T(8,128)(2,1)} %copy.17) | copy-start | bytes 12582916
  139.8 13.8 %collective-permute-start.27 = (bf16[64,2048]{1,0:T(8,128)(2,1)S(1)}, bf16[64,2048]{1,0:T(8,128)(2,1)S(1)}, u32[]{:S(2)}, u32[]{:S(2)}) collective-permute-start(bf16[64,2048]{1,0:T(8,128)(2,1)S(1)} %get-tuple-element.20), channel_id=1, source_target_pairs={{0,32},{16,48},{32,64},{48,80},{64,96},{80,112},{96,0},{112,16},{1... | collective-permute-start | bytes 786440 | tf_op jit(solution)/shard_map/ppermute | solution.py:28
  142.3 11.5 %collective-permute-start.28 = (bf16[64,2048]{1,0:T(8,128)(2,1)S(1)}, bf16[64,2048]{1,0:T(8,128)(2,1)S(1)}, u32[]{:S(2)}, u32[]{:S(2)}) collective-permute-start(bf16[64,2048]{1,0:T(8,128)(2,1)S(1)} %get-tuple-element.21), channel_id=1, source_target_pairs={{0,96},{16,112},{32,0},{48,16},{64,32},{80,48},{96,64},{112,80},{1... | collective-permute-start | bytes 786440 | tf_op jit(solution)/shard_map/ppermute | solution.py:28
  144.8 10.8 %collective-permute-start.9 = (bf16[128,2048]{1,0:T(8,128)(2,1)S(1)}, bf16[128,2048]{1,0:T(8,128)(2,1)S(1)}, u32[]{:S(2)}, u32[]{:S(2)}) collective-permute-start(bf16[128,2048]{1,0:T(8,128)(2,1)S(1)} %maximum_select_fusion), channel_id=1, source_target_pairs={{0,16},{16,0},{32,48},{48,32},{64,80},{80,64},{96,112},{112,96},{1... | collective-permute-start | bytes 1572872 | tf_op jit(solution)/shard_map/ppermute | solution.py:37
  148.4 32.3 %collective-permute-start.19 = (bf16[128,2048]{1,0:T(8,128)(2,1)S(1)}, bf16[128,2048]{1,0:T(8,128)(2,1)}, u32[]{:S(2)}, u32[]{:S(2)}) collective-permute-start(bf16[128,2048]{1,0:T(8,128)(2,1)S(1)} %maximum_select_fusion.1), channel_id=1, source_target_pairs={{0,16},{16,0},{32,48},{48,32},{64,80},{80,64},{96,112},{112,96},{1... | collective-permute-start | bytes 1572872 | tf_op jit(solution)/shard_map/ppermute | solution.py:37
  154.0 35.6 %collective-permute-start.29 = (bf16[128,2048]{1,0:T(8,128)(2,1)S(1)}, bf16[128,2048]{1,0:T(8,128)(2,1)S(1)}, u32[]{:S(2)}, u32[]{:S(2)}) collective-permute-start(bf16[128,2048]{1,0:T(8,128)(2,1)S(1)} %maximum_select_fusion.2), channel_id=1, source_target_pairs={{0,16},{16,0},{32,48},{48,32},{64,80},{80,64},{96,112},{112,96},{1... | collective-permute-start | bytes 1572872 | tf_op jit(solution)/shard_map/ppermute | solution.py:37
  160.3 35.5 %collective-permute-start.10 = (f32[8,64,256]{2,1,0:T(8,128)}, f32[8,64,256]{2,1,0:T(8,128)}, u32[]{:S(2)}, u32[]{:S(2)}) collective-permute-start(f32[8,64,256]{2,1,0:T(8,128)} %dynamic-slice_bitcast_fusion.2), channel_id=1, source_target_pairs={{0,1},{1,0},{2,3},{3,2},{4,5},{5,4},{6,7},{7,6},{8,9},{9,8},{10,11... | collective-permute-start | bytes 1572872 | tf_op jit(solution)/shard_map/ppermute | solution.py:52
  188.7 36.1 %collective-permute-start.20 = (f32[8,64,256]{2,1,0:T(8,128)}, f32[8,64,256]{2,1,0:T(8,128)}, u32[]{:S(2)}, u32[]{:S(2)}) collective-permute-start(f32[8,64,256]{2,1,0:T(8,128)} %dynamic-slice_bitcast_fusion.1), channel_id=1, source_target_pairs={{0,1},{1,0},{2,3},{3,2},{4,5},{5,4},{6,7},{7,6},{8,9},{9,8},{10,11... | collective-permute-start | bytes 1572872 | tf_op jit(solution)/shard_map/ppermute | solution.py:52
  195.8 30.3 %collective-permute-start.30 = (f32[8,64,256]{2,1,0:T(8,128)S(1)}, f32[8,64,256]{2,1,0:T(8,128)S(1)}, u32[]{:S(2)}, u32[]{:S(2)}) collective-permute-start(f32[8,64,256]{2,1,0:T(8,128)S(1)} %dynamic-slice_bitcast_fusion), channel_id=1, source_target_pairs={{0,1},{1,0},{2,3},{3,2},{4,5},{5,4},{6,7},{7,6},{8,9},{9,8},{10,11... | collective-permute-start | bytes 1572872 | tf_op jit(solution)/shard_map/ppermute | solution.py:52
  197.0 34.9 %collective-permute-start.11 = (f32[4,64,256]{2,1,0:T(8,128)S(1)}, f32[4,64,256]{2,1,0:T(8,128)S(1)}, u32[]{:S(2)}, u32[]{:S(2)}) collective-permute-start(f32[4,64,256]{2,1,0:T(8,128)S(1)} %dynamic-slice_bitcast_fusion.5), channel_id=1, source_target_pairs={{0,2},{1,3},{2,0},{3,1},{4,6},{5,7},{6,4},{7,5},{8,10},{9,11},{10,... | collective-permute-start | bytes 786440 | tf_op jit(solution)/shard_map/ppermute | solution.py:52
  226.0 11.6 %collective-permute-start.21 = (f32[4,64,256]{2,1,0:T(8,128)S(1)}, f32[4,64,256]{2,1,0:T(8,128)S(1)}, u32[]{:S(2)}, u32[]{:S(2)}) collective-permute-start(f32[4,64,256]{2,1,0:T(8,128)S(1)} %dynamic-slice_bitcast_fusion.4), channel_id=1, source_target_pairs={{0,2},{1,3},{2,0},{3,1},{4,6},{5,7},{6,4},{7,5},{8,10},{9,11},{10,... | collective-permute-start | bytes 786440 | tf_op jit(solution)/shard_map/ppermute | solution.py:52
  226.2 17.0 %collective-permute-start.31 = (f32[4,64,256]{2,1,0:T(8,128)S(1)}, f32[4,64,256]{2,1,0:T(8,128)S(1)}, u32[]{:S(2)}, u32[]{:S(2)}) collective-permute-start(f32[4,64,256]{2,1,0:T(8,128)S(1)} %dynamic-slice_bitcast_fusion.3), channel_id=1, source_target_pairs={{0,2},{1,3},{2,0},{3,1},{4,6},{5,7},{6,4},{7,5},{8,10},{9,11},{10,... | collective-permute-start | bytes 786440 | tf_op jit(solution)/shard_map/ppermute | solution.py:52
  232.0 15.6 %collective-permute-start.12 = (f32[2,64,256]{2,1,0:T(8,128)S(1)}, f32[2,64,256]{2,1,0:T(8,128)S(1)}, u32[]{:S(2)}, u32[]{:S(2)}) collective-permute-start(f32[2,64,256]{2,1,0:T(8,128)S(1)} %dynamic-slice_bitcast_fusion.8), channel_id=1, source_target_pairs={{0,4},{1,5},{2,6},{3,7},{4,0},{5,1},{6,2},{7,3},{8,12},{9,13},{10,... | collective-permute-start | bytes 393224 | tf_op jit(solution)/shard_map/ppermute | solution.py:52
  237.6 12.8 %collective-permute-start.22 = (f32[2,64,256]{2,1,0:T(8,128)S(1)}, f32[2,64,256]{2,1,0:T(8,128)S(1)}, u32[]{:S(2)}, u32[]{:S(2)}) collective-permute-start(f32[2,64,256]{2,1,0:T(8,128)S(1)} %dynamic-slice_bitcast_fusion.7), channel_id=1, source_target_pairs={{0,4},{1,5},{2,6},{3,7},{4,0},{5,1},{6,2},{7,3},{8,12},{9,13},{10,... | collective-permute-start | bytes 393224 | tf_op jit(solution)/shard_map/ppermute | solution.py:52
  243.3 9.6 %collective-permute-start.32 = (f32[2,64,256]{2,1,0:T(8,128)S(1)}, f32[2,64,256]{2,1,0:T(8,128)S(1)}, u32[]{:S(2)}, u32[]{:S(2)}) collective-permute-start(f32[2,64,256]{2,1,0:T(8,128)S(1)} %dynamic-slice_bitcast_fusion.6), channel_id=1, source_target_pairs={{0,4},{1,5},{2,6},{3,7},{4,0},{5,1},{6,2},{7,3},{8,12},{9,13},{10,... | collective-permute-start | bytes 393224 | tf_op jit(solution)/shard_map/ppermute | solution.py:52
  247.7 7.7 %collective-permute-start.13 = (f32[1,64,256]{2,1,0:T(8,128)S(1)}, f32[1,64,256]{2,1,0:T(8,128)S(1)}, u32[]{:S(2)}, u32[]{:S(2)}) collective-permute-start(f32[1,64,256]{2,1,0:T(8,128)S(1)} %constant_dynamic-slice_fusion.2), channel_id=1, source_target_pairs={{0,8},{1,9},{2,10},{3,11},{4,12},{5,13},{6,14},{7,15},{8,0},{9,1},... | collective-permute-start | bytes 196616 | tf_op jit(solution)/shard_map/ppermute | solution.py:52
  250.5 5.8 %collective-permute-start.23 = (f32[1,64,256]{2,1,0:T(8,128)S(1)}, f32[1,64,256]{2,1,0:T(8,128)S(1)}, u32[]{:S(2)}, u32[]{:S(2)}) collective-permute-start(f32[1,64,256]{2,1,0:T(8,128)S(1)} %constant_dynamic-slice_fusion.1), channel_id=1, source_target_pairs={{0,8},{1,9},{2,10},{3,11},{4,12},{5,13},{6,14},{7,15},{8,0},{9,1},... | collective-permute-start | bytes 196616 | tf_op jit(solution)/shard_map/ppermute | solution.py:52
  252.9 5.8 %collective-permute-start.33 = (f32[1,64,256]{2,1,0:T(8,128)S(1)}, f32[1,64,256]{2,1,0:T(8,128)S(1)}, u32[]{:S(2)}, u32[]{:S(2)}) collective-permute-start(f32[1,64,256]{2,1,0:T(8,128)S(1)} %constant_dynamic-slice_fusion), channel_id=1, source_target_pairs={{0,8},{1,9},{2,10},{3,11},{4,12},{5,13},{6,14},{7,15},{8,0},{9,1},... | collective-permute-start | bytes 196616 | tf_op jit(solution)/shard_map/ppermute | solution.py:52

commit v17 on v16

--- a/solution.py
+++ b/solution.py
@@ -32,8 +32,13 @@
     from_below, from_above = shift(val, 2), shift(val, -2)
     val = jnp.where(z == oz, val, jnp.where(z == (oz + 1) % ring, from_below, from_above))
     quarter = half // 2
-    last = jnp.concatenate([shift(val[:quarter], 2), shift(val[quarter:], -2)])
-    val = jnp.where(z == (oz + 2) % ring, last, val)
+    far = z == (oz + 2) % ring
+    val = jnp.concatenate(
+        [
+            jnp.where(far, shift(val[:quarter], 2), val[:quarter]),
+            jnp.where(far, shift(val[quarter:], -2), val[quarter:]),
+        ]
+    )
     other = lax.ppermute(val, axis, [(i, i ^ 1) for i in range(size)])
     return jnp.concatenate([jnp.where(mine, val, other), jnp.where(mine, other, val)])
 

time: 260 us -> 272 us (1.046)
  starting transfers between devices: 103 us -> 109 us
  waiting for transfers between devices: 33.5 us -> 37.1 us
    ppermute x12, waiting for transfers between devices: 13.1 us -> 17.8 us  [shift(): return lax.ppermute(v, axis, [(i, (i + step) % size) for i in range(size)])]
    ppermute x12, starting transfers between devices: 18.2 us -> 22.8 us  [shift(): return lax.ppermute(v, axis, [(i, (i + step) % size) for i in range(size)])]
  transfers between devices with their start and end apart: 34 -> 34, of which waited for: 16 -> 14; matrix products, arithmetic and copies ran while one was open for 11% -> 12% of each run, Pallas kernels for 0% -> 0%
where the time goes in v17:
time: 272 us; the launch traced here: 271 us
  starting transfers between devices  109 us (40%)
  Pallas kernels  73 us (27%)
  waiting for transfers between devices  37.1 us (14%)
  local copies, waits for them, and re-layouts  20.8 us (8%)
  other arithmetic  11.2 us (4%)
  matrix products  11.2 us (4%)
  between operations  8.79 us (3%)
    pallas_call x1, Pallas kernels, smooth(): pl.pallas_call(kernel, grid=(rows // block,), in_specs=[pl.BlockSpec(coef...  73 us
    ppermute x12, starting transfers between devices, reduce_scatter_slab(): part = keep + lax.ppermute(send, axis, [(i, i ^ bit) for i in range(size)])  69.9 us
    ppermute x12, starting transfers between devices, shift(): return lax.ppermute(v, axis, [(i, (i + step) % size) for i in range(size)])  22.8 us
    ppermute x12, waiting for transfers between devices, shift(): return lax.ppermute(v, axis, [(i, (i + step) % size) for i in range(size)])  17.8 us
    ppermute x12, waiting for transfers between devices, reduce_scatter_slab(): part = keep + lax.ppermute(send, axis, [(i, i ^ bit) for i in range(size)])  12.8 us
    dot_general x3, matrix products, body(): lax.dot_general(flat, received, (((1,), (1,)), ((), ())), preferred_eleme...  11.2 us
    unnamed x19, local copies, waits for them, and re-layouts  8.46 us
    ppermute x2, starting transfers between devices, halo_of(): below = lax.ppermute(top, axis, up)  6.13 us
  transfers between devices with their start and end apart: 34, of which 14 were waited for; matrix products, arithmetic and copies ran while one was open for 12% of the time, Pallas kernels for 0%

profile of v17, /device:TPU:0, one launch (start us, length us, event | category | flops | bytes accessed | tf_op | source)
XLA Modules:
  0.0 271.1 jit_solution(2612710986323072511)
XLA Ops:
  0.6 4.8 %fusion.17 = (bf16[1024,4,256]{2,1,0:T(4,128)(2,1)S(1)}, bf16[1024,4,256]{2,1,0:T(4,128)(2,1)S(1)}) fusion(bf16[1024,8,256]{2,1,0:T(8,128)(2,1)} %a_ref.1), kind=kLoop, calls=%fused_computation.80 | loop fusion | bytes 8388608 | tf_op jit(solution)/shard_map/slice | solution.py:67
  5.5 1.4 collective-permute-start.2
  6.9 1.3 collective-permute-start.3
  8.3 4.7 %collective-permute-start = (f32[4,256]{1,0:T(4,128)S(1)}, f32[4,256]{1,0:T(4,128)S(1)}, u32[]{:S(2)}, u32[]{:S(2)}) collective-permute-start(f32[4,256]{1,0:T(4,128)S(1)} %get-tuple-element.22), channel_id=1, source_target_pairs={{0,1},{1,2},{2,3},{3,4},{4,5},{5,6},{6,7},{7,8},{8,9},{9,10},{10,1... | collective-permute-start | bytes 12296 | tf_op jit(solution)/shard_map/ppermute | solution.py:68
  14.4 2.9 %collective-permute-done.1 = f32[4,256]{1,0:T(4,128)S(1)} collective-permute-done((f32[4,256]{1,0:T(4,128)S(1)}, f32[4,256]{1,0:T(4,128)S(1)}, u32[]{:S(2)}, u32[]{:S(2)}) %collective-permute-start.1) | collective-permute-done | bytes 4128 | tf_op jit(solution)/shard_map/ppermute | solution.py:69
  18.8 73.0 %shard_map.59 = f32[1024,8,256]{2,1,0:T(8,128)} custom-call(f32[6,16,256]{2,1,0:T(8,128)} %copy-done.2, bf16[1024,8,256]{2,1,0:T(8,128)(2,1)} %a_ref.1, bf16[1024,4,256]{2,1,0:T(4,128)(2,1)} %copy-done.1, bf16[1024,4,256]{2,1,0:T(4,128)(2,1)} %collective-permute-done.3.hi_ref), custom_call_target="tpu_custom_call" | custom-call | tf_op jit(solution)/shard_map/pallas_call | solution.py:151
  91.8 3.8 %convert.5 = bf16[1024,8,256]{2,1,0:T(8,128)(2,1)S(1)} convert(f32[1024,8,256]{2,1,0:T(8,128)} %shard_map.59) | non-fusion elementwise | flops 2097152 | bytes 12582912 | tf_op jit(solution)/shard_map/convert.2
  96.8 1.6 collective-permute-start.4
  107.2 5.6 %copy.17 = bf16[128,8,8,256]{3,1,2,0:T(8,128)(2,1)} copy(bf16[128,8,8,256]{3,2,1,0:T(8,128)(2,1)} %bitcast.84) | data formatting | bytes 8388608
  113.2 1.7 collective-permute-start.24
  115.1 2.0 collective-permute-start.5
  117.1 2.2 collective-permute-start.6
  119.4 3.2 %collective-permute-start.16 = (bf16[128,2048]{1,0:T(8,128)(2,1)S(1)}, bf16[128,2048]{1,0:T(8,128)(2,1)S(1)}, u32[]{:S(2)}, u32[]{:S(2)}) collective-permute-start(bf16[128,2048]{1,0:T(8,128)(2,1)S(1)} %broadcast_select_fusion.5), channel_id=1, source_target_pairs={{0,96},{16,112},{32,0},{48,16},{64,32},{80,48},{96,64},{112,80},{1... | collective-permute-start | bytes 1572872 | tf_op jit(solution)/shard_map/ppermute | solution.py:28
  122.6 3.5 %collective-permute-done.24 = bf16[128,2048]{1,0:T(8,128)(2,1)S(1)} collective-permute-done((bf16[128,2048]{1,0:T(8,128)(2,1)S(1)}, bf16[128,2048]{1,0:T(8,128)(2,1)S(1)}, u32[]{:S(2)}, u32[]{:S(2)}) %collective-permute-start.24) | collective-permute-done | bytes 524320 | tf_op jit(solution)/shard_map/ppermute | solution.py:30
  126.2 2.0 collective-permute-start.25
  128.2 2.2 collective-permute-start.26
  130.6 1.4 collective-permute-done.15
  132.1 1.9 collective-permute-start.17
  134.0 3.6 %collective-permute-done.25 = bf16[128,2048]{1,0:T(8,128)(2,1)S(1)} collective-permute-done((bf16[128,2048]{1,0:T(8,128)(2,1)S(1)}, bf16[128,2048]{1,0:T(8,128)(2,1)S(1)}, u32[]{:S(2)}, u32[]{:S(2)}) %collective-permute-start.25) | collective-permute-done | bytes 524320 | tf_op jit(solution)/shard_map/ppermute | solution.py:28
  137.7 1.9 collective-permute-start.27
  139.6 2.7 %collective-permute-done.7 = bf16[64,2048]{1,0:T(8,128)(2,1)S(1)} collective-permute-done((bf16[64,2048]{1,0:T(8,128)(2,1)S(1)}, bf16[64,2048]{1,0:T(8,128)(2,1)S(1)}, u32[]{:S(2)}, u32[]{:S(2)}) %collective-permute-start.7) | collective-permute-done | bytes 262176 | tf_op jit(solution)/shard_map/ppermute | solution.py:28
  142.4 2.4 collective-permute-start.8
  144.8 3.2 %collective-permute-done.17 = bf16[64,2048]{1,0:T(8,128)(2,1)S(1)} collective-permute-done((bf16[64,2048]{1,0:T(8,128)(2,1)S(1)}, bf16[64,2048]{1,0:T(8,128)(2,1)S(1)}, u32[]{:S(2)}, u32[]{:S(2)}) %collective-permute-start.17) | collective-permute-done | bytes 262176 | tf_op jit(solution)/shard_map/ppermute | solution.py:28
  148.0 2.4 collective-permute-start.18
  150.4 3.2 %collective-permute-done.27 = bf16[64,2048]{1,0:T(8,128)(2,1)S(1)} collective-permute-done((bf16[64,2048]{1,0:T(8,128)(2,1)S(1)}, bf16[64,2048]{1,0:T(8,128)(2,1)S(1)}, u32[]{:S(2)}, u32[]{:S(2)}) %collective-permute-start.27) | collective-permute-done | bytes 262176 | tf_op jit(solution)/shard_map/ppermute | solution.py:28
  153.6 2.5 collective-permute-start.28
  156.2 1.6 collective-permute-start.9
  159.5 3.6 %collective-permute-done.28 = bf16[64,2048]{1,0:T(8,128)(2,1)S(1)} collective-permute-done((bf16[64,2048]{1,0:T(8,128)(2,1)S(1)}, bf16[64,2048]{1,0:T(8,128)(2,1)S(1)}, u32[]{:S(2)}, u32[]{:S(2)}) %collective-permute-start.28) | collective-permute-done | bytes 262176 | tf_op jit(solution)/shard_map/ppermute | solution.py:28
  164.0 1.5 collective-permute-start.29
  165.8 2.3 fusion.2
  168.0 1.6 copy.12
  170.5 16.7 %collective-permute-start.10 = (f32[8,64,256]{2,1,0:T(8,128)}, f32[8,64,256]{2,1,0:T(8,128)}, u32[]{:S(2)}, u32[]{:S(2)}) collective-permute-start(f32[8,64,256]{2,1,0:T(8,128)} %dynamic-slice_bitcast_fusion.2), channel_id=1, source_target_pairs={{0,1},{1,0},{2,3},{3,2},{4,5},{5,4},{6,7},{7,6},{8,9},{9,8},{10,11... | collective-permute-start | bytes 1572872 | tf_op jit(solution)/shard_map/ppermute | solution.py:57
  188.4 4.5 %fusion.1 = f32[1024,256]{0,1:T(8,128)} fusion(bf16[1024,2048]{1,0:T(8,128)(2,1)} %bitcast.85, bf16[128,2048]{1,0:T(8,128)(2,1)S(1)} %get-tuple-element.13, bf16[128,2048]{1,0:T(8,128)(2,1)S(1)} %get-tuple-element.12), kind=kOutput, calls=%fused_computation.3 | convolution fusion | flops 1076101120 | bytes 6291456 | tf_op jit(solution)/shard_map/dot_general | solution.py:181
  192.9 1.6 copy.13
  196.3 4.5 %fusion = f32[1024,256]{0,1:T(8,128)} fusion(bf16[1024,2048]{1,0:T(8,128)(2,1)} %bitcast.86, bf16[128,2048]{1,0:T(8,128)(2,1)S(1)} %get-tuple-element.15, bf16[128,2048]{1,0:T(8,128)(2,1)S(1)} %get-tuple-element.14), kind=kOutput, calls=%fused_computation.1 | convolution fusion | flops 1076101120 | bytes 6291456 | tf_op jit(solution)/shard_map/dot_general | solution.py:181
  200.8 1.6 copy.14
  203.7 32.8 %collective-permute-start.11 = (f32[4,64,256]{2,1,0:T(8,128)S(1)}, f32[4,64,256]{2,1,0:T(8,128)S(1)}, u32[]{:S(2)}, u32[]{:S(2)}) collective-permute-start(f32[4,64,256]{2,1,0:T(8,128)S(1)} %dynamic-slice_bitcast_fusion.5), channel_id=1, source_target_pairs={{0,2},{1,3},{2,0},{3,1},{4,6},{5,7},{6,4},{7,5},{8,10},{9,11},{10,... | collective-permute-start | bytes 786440 | tf_op jit(solution)/shard_map/ppermute | solution.py:57
  237.8 2.1 collective-permute-start.31
  239.9 3.7 %collective-permute-done.11 = f32[4,64,256]{2,1,0:T(8,128)S(1)} collective-permute-done((f32[4,64,256]{2,1,0:T(8,128)S(1)}, f32[4,64,256]{2,1,0:T(8,128)S(1)}, u32[]{:S(2)}, u32[]{:S(2)}) %collective-permute-start.11) | collective-permute-done | bytes 262176 | tf_op jit(solution)/shard_map/ppermute | solution.py:57
  243.6 3.0 %collective-permute-start.12 = (f32[2,64,256]{2,1,0:T(8,128)S(1)}, f32[2,64,256]{2,1,0:T(8,128)S(1)}, u32[]{:S(2)}, u32[]{:S(2)}) collective-permute-start(f32[2,64,256]{2,1,0:T(8,128)S(1)} %dynamic-slice_bitcast_fusion.8), channel_id=1, source_target_pairs={{0,4},{1,5},{2,6},{3,7},{4,0},{5,1},{6,2},{7,3},{8,12},{9,13},{10,... | collective-permute-start | bytes 393224 | tf_op jit(solution)/shard_map/ppermute | solution.py:57
  246.7 2.5 collective-permute-done.21
  249.3 3.0 %collective-permute-start.22 = (f32[2,64,256]{2,1,0:T(8,128)S(1)}, f32[2,64,256]{2,1,0:T(8,128)S(1)}, u32[]{:S(2)}, u32[]{:S(2)}) collective-permute-start(f32[2,64,256]{2,1,0:T(8,128)S(1)} %dynamic-slice_bitcast_fusion.7), channel_id=1, source_target_pairs={{0,4},{1,5},{2,6},{3,7},{4,0},{5,1},{6,2},{7,3},{8,12},{9,13},{10,... | collective-permute-start | bytes 393224 | tf_op jit(solution)/shard_map/ppermute | solution.py:57
  252.3 2.5 collective-permute-done.31
  254.9 3.0 %collective-permute-start.32 = (f32[2,64,256]{2,1,0:T(8,128)S(1)}, f32[2,64,256]{2,1,0:T(8,128)S(1)}, u32[]{:S(2)}, u32[]{:S(2)}) collective-permute-start(f32[2,64,256]{2,1,0:T(8,128)S(1)} %dynamic-slice_bitcast_fusion.6), channel_id=1, source_target_pairs={{0,4},{1,5},{2,6},{3,7},{4,0},{5,1},{6,2},{7,3},{8,12},{9,13},{10,... | collective-permute-start | bytes 393224 | tf_op jit(solution)/shard_map/ppermute | solution.py:57
  258.7 3.0 %collective-permute-start.13 = (f32[1,64,256]{2,1,0:T(8,128)S(1)}, f32[1,64,256]{2,1,0:T(8,128)S(1)}, u32[]{:S(2)}, u32[]{:S(2)}) collective-permute-start(f32[1,64,256]{2,1,0:T(8,128)S(1)} %constant_dynamic-slice_fusion.2), channel_id=1, source_target_pairs={{0,8},{1,9},{2,10},{3,11},{4,12},{5,13},{6,14},{7,15},{8,0},{9,1},... | collective-permute-start | bytes 196616 | tf_op jit(solution)/shard_map/ppermute | solution.py:57
  261.7 2.8 %collective-permute-start.23 = (f32[1,64,256]{2,1,0:T(8,128)S(1)}, f32[1,64,256]{2,1,0:T(8,128)S(1)}, u32[]{:S(2)}, u32[]{:S(2)}) collective-permute-start(f32[1,64,256]{2,1,0:T(8,128)S(1)} %constant_dynamic-slice_fusion.1), channel_id=1, source_target_pairs={{0,8},{1,9},{2,10},{3,11},{4,12},{5,13},{6,14},{7,15},{8,0},{9,1},... | collective-permute-start | bytes 196616 | tf_op jit(solution)/shard_map/ppermute | solution.py:57
  264.5 2.6 collective-permute-start.33
  267.6 2.8 %collective-permute-done.33 = f32[1,64,256]{2,1,0:T(8,128)S(1)} collective-permute-done((f32[1,64,256]{2,1,0:T(8,128)S(1)}, f32[1,64,256]{2,1,0:T(8,128)S(1)}, u32[]{:S(2)}, u32[]{:S(2)}) %collective-permute-start.33) | collective-permute-done | bytes 65568 | tf_op jit(solution)/shard_map/ppermute | solution.py:57
  (108 shorter events, 18.1 us)
Async XLA Ops:
  0.6 7.6 %copy-start.3 = (s32[8,256]{1,0:T(8,128)S(1)}, s32[8,256]{1,0:T(8,128)}, u32[]{:S(2)}) copy-start(s32[8,256]{1,0:T(8,128)} %param.5) | copy-start | bytes 24580
  0.6 7.6 %copy-start.5 = (f32[8]{0:T(128)S(1)}, f32[8]{0:T(128)}, u32[]{:S(2)}) copy-start(f32[8]{0:T(128)} %param.6) | copy-start | bytes 100
  5.5 12.0 %collective-permute-start.2 = (bf16[1024,4,256]{2,1,0:T(4,128)(2,1)S(1)}, bf16[1024,4,256]{2,1,0:T(4,128)(2,1)S(1)}, u32[]{:S(2)}, u32[]{:S(2)}) collective-permute-start(bf16[1024,4,256]{2,1,0:T(4,128)(2,1)S(1)} %get-tuple-element.9), channel_id=1, source_target_pairs={{0,1},{1,2},{2,3},{3,4},{4,5},{5,6},{6,7},{7,8},{8,9},{9,10},{10,1... | collective-permute-start | bytes 6291464 | tf_op jit(solution)/shard_map/ppermute | solution.py:68
  6.9 10.6 %collective-permute-start.3 = (bf16[1024,4,256]{2,1,0:T(4,128)(2,1)S(1)}, bf16[1024,4,256]{2,1,0:T(4,128)(2,1)}, u32[]{:S(2)}, u32[]{:S(2)}) collective-permute-start(bf16[1024,4,256]{2,1,0:T(4,128)(2,1)S(1)} %get-tuple-element.8), channel_id=1, source_target_pairs={{1,0},{2,1},{3,2},{4,3},{5,4},{6,5},{7,6},{8,7},{9,8},{10,9},{11,1... | collective-permute-start | bytes 6291464 | tf_op jit(solution)/shard_map/ppermute | solution.py:69
  8.3 6.1 %collective-permute-start = (f32[4,256]{1,0:T(4,128)S(1)}, f32[4,256]{1,0:T(4,128)S(1)}, u32[]{:S(2)}, u32[]{:S(2)}) collective-permute-start(f32[4,256]{1,0:T(4,128)S(1)} %get-tuple-element.22), channel_id=1, source_target_pairs={{0,1},{1,2},{2,3},{3,4},{4,5},{5,6},{6,7},{7,8},{8,9},{9,10},{10,1... | collective-permute-start | bytes 12296 | tf_op jit(solution)/shard_map/ppermute | solution.py:68
  13.0 4.3 %collective-permute-start.1 = (f32[4,256]{1,0:T(4,128)S(1)}, f32[4,256]{1,0:T(4,128)S(1)}, u32[]{:S(2)}, u32[]{:S(2)}) collective-permute-start(f32[4,256]{1,0:T(4,128)S(1)} %get-tuple-element.23), channel_id=1, source_target_pairs={{1,0},{2,1},{3,2},{4,3},{5,4},{6,5},{7,6},{8,7},{9,8},{10,9},{11,1... | collective-permute-start | bytes 12296 | tf_op jit(solution)/shard_map/ppermute | solution.py:69
  17.4 0.6 copy-start.2
  17.4 1.4 copy-start.1
  95.6 3.4 %copy-start.4 = (s32[8]{0:T(128)S(1)}, s32[8]{0:T(128)}, u32[]{:S(2)}) copy-start(s32[8]{0:T(128)} %param.7) | copy-start | bytes 100
  96.8 18.2 %collective-permute-start.4 = (bf16[128,2048]{1,0:T(8,128)(2,1)}, bf16[128,2048]{1,0:T(8,128)(2,1)}, u32[]{:S(2)}, u32[]{:S(2)}) collective-permute-start(bf16[128,2048]{1,0:T(8,128)(2,1)} %bitcast.43), channel_id=1, source_target_pairs={{0,16},{16,0},{32,48},{48,32},{64,80},{80,64},{96,112},{112,96},{1... | collective-permute-start | bytes 1572872 | tf_op jit(solution)/shard_map/ppermute | solution.py:30
  98.5 20.8 %collective-permute-start.14 = (bf16[128,2048]{1,0:T(8,128)(2,1)S(1)}, bf16[128,2048]{1,0:T(8,128)(2,1)S(1)}, u32[]{:S(2)}, u32[]{:S(2)}) collective-permute-start(bf16[128,2048]{1,0:T(8,128)(2,1)S(1)} %bitcast.115), channel_id=1, source_target_pairs={{0,16},{16,0},{32,48},{48,32},{64,80},{80,64},{96,112},{112,96},{1... | collective-permute-start | bytes 1572872 | tf_op jit(solution)/shard_map/ppermute | solution.py:30
  113.2 12.9 %collective-permute-start.24 = (bf16[128,2048]{1,0:T(8,128)(2,1)S(1)}, bf16[128,2048]{1,0:T(8,128)(2,1)S(1)}, u32[]{:S(2)}, u32[]{:S(2)}) collective-permute-start(bf16[128,2048]{1,0:T(8,128)(2,1)S(1)} %bitcast.116), channel_id=1, source_target_pairs={{0,16},{16,0},{32,48},{48,32},{64,80},{80,64},{96,112},{112,96},{1... | collective-permute-start | bytes 1572872 | tf_op jit(solution)/shard_map/ppermute | solution.py:30
  115.1 13.1 %collective-permute-start.5 = (bf16[128,2048]{1,0:T(8,128)(2,1)S(1)}, bf16[128,2048]{1,0:T(8,128)(2,1)S(1)}, u32[]{:S(2)}, u32[]{:S(2)}) collective-permute-start(bf16[128,2048]{1,0:T(8,128)(2,1)S(1)} %broadcast_select_fusion.8), channel_id=1, source_target_pairs={{0,32},{16,48},{32,64},{48,80},{64,96},{80,112},{96,0},{112,16},{1... | collective-permute-start | bytes 1572872 | tf_op jit(solution)/shard_map/ppermute | solution.py:28
  117.1 13.3 %collective-permute-start.6 = (bf16[128,2048]{1,0:T(8,128)(2,1)S(1)}, bf16[128,2048]{1,0:T(8,128)(2,1)S(1)}, u32[]{:S(2)}, u32[]{:S(2)}) collective-permute-start(bf16[128,2048]{1,0:T(8,128)(2,1)S(1)} %broadcast_select_fusion.8), channel_id=1, source_target_pairs={{0,96},{16,112},{32,0},{48,16},{64,32},{80,48},{96,64},{112,80},{1... | collective-permute-start | bytes 1572872 | tf_op jit(solution)/shard_map/ppermute | solution.py:28
  119.3 12.6 %collective-permute-start.15 = (bf16[128,2048]{1,0:T(8,128)(2,1)S(1)}, bf16[128,2048]{1,0:T(8,128)(2,1)S(1)}, u32[]{:S(2)}, u32[]{:S(2)}) collective-permute-start(bf16[128,2048]{1,0:T(8,128)(2,1)S(1)} %broadcast_select_fusion.5), channel_id=1, source_target_pairs={{0,32},{16,48},{32,64},{48,80},{64,96},{80,112},{96,0},{112,16},{1... | collective-permute-start | bytes 1572872 | tf_op jit(solution)/shard_map/ppermute | solution.py:28
  119.4 12.6 %collective-permute-start.16 = (bf16[128,2048]{1,0:T(8,128)(2,1)S(1)}, bf16[128,2048]{1,0:T(8,128)(2,1)S(1)}, u32[]{:S(2)}, u32[]{:S(2)}) collective-permute-start(bf16[128,2048]{1,0:T(8,128)(2,1)S(1)} %broadcast_select_fusion.5), channel_id=1, source_target_pairs={{0,96},{16,112},{32,0},{48,16},{64,32},{80,48},{96,64},{112,80},{1... | collective-permute-start | bytes 1572872 | tf_op jit(solution)/shard_map/ppermute | solution.py:28
  126.2 11.4 %collective-permute-start.25 = (bf16[128,2048]{1,0:T(8,128)(2,1)S(1)}, bf16[128,2048]{1,0:T(8,128)(2,1)S(1)}, u32[]{:S(2)}, u32[]{:S(2)}) collective-permute-start(bf16[128,2048]{1,0:T(8,128)(2,1)S(1)} %broadcast_select_fusion.2), channel_id=1, source_target_pairs={{0,32},{16,48},{32,64},{48,80},{64,96},{80,112},{96,0},{112,16},{1... | collective-permute-start | bytes 1572872 | tf_op jit(solution)/shard_map/ppermute | solution.py:28
  128.2 9.4 %collective-permute-start.26 = (bf16[128,2048]{1,0:T(8,128)(2,1)S(1)}, bf16[128,2048]{1,0:T(8,128)(2,1)S(1)}, u32[]{:S(2)}, u32[]{:S(2)}) collective-permute-start(bf16[128,2048]{1,0:T(8,128)(2,1)S(1)} %broadcast_select_fusion.2), channel_id=1, source_target_pairs={{0,96},{16,112},{32,0},{48,16},{64,32},{80,48},{96,64},{112,80},{1... | collective-permute-start | bytes 1572872 | tf_op jit(solution)/shard_map/ppermute | solution.py:28
  130.5 11.8 %collective-permute-start.7 = (bf16[64,2048]{1,0:T(8,128)(2,1)S(1)}, bf16[64,2048]{1,0:T(8,128)(2,1)S(1)}, u32[]{:S(2)}, u32[]{:S(2)}) collective-permute-start(bf16[64,2048]{1,0:T(8,128)(2,1)S(1)} %slice.122), channel_id=1, source_target_pairs={{0,32},{16,48},{32,64},{48,80},{64,96},{80,112},{96,0},{112,16},{1... | collective-permute-start | bytes 786440 | tf_op jit(solution)/shard_map/ppermute | solution.py:28
  132.1 15.9 %collective-permute-start.17 = (bf16[64,2048]{1,0:T(8,128)(2,1)S(1)}, bf16[64,2048]{1,0:T(8,128)(2,1)S(1)}, u32[]{:S(2)}, u32[]{:S(2)}) collective-permute-start(bf16[64,2048]{1,0:T(8,128)(2,1)S(1)} %slice.126), channel_id=1, source_target_pairs={{0,32},{16,48},{32,64},{48,80},{64,96},{80,112},{96,0},{112,16},{1... | collective-permute-start | bytes 786440 | tf_op jit(solution)/shard_map/ppermute | solution.py:28
  137.7 15.9 %collective-permute-start.27 = (bf16[64,2048]{1,0:T(8,128)(2,1)S(1)}, bf16[64,2048]{1,0:T(8,128)(2,1)S(1)}, u32[]{:S(2)}, u32[]{:S(2)}) collective-permute-start(bf16[64,2048]{1,0:T(8,128)(2,1)S(1)} %slice.130), channel_id=1, source_target_pairs={{0,32},{16,48},{32,64},{48,80},{64,96},{80,112},{96,0},{112,16},{1... | collective-permute-start | bytes 786440 | tf_op jit(solution)/shard_map/ppermute | solution.py:28
  142.4 13.8 %collective-permute-start.8 = (bf16[64,2048]{1,0:T(8,128)(2,1)S(1)}, bf16[64,2048]{1,0:T(8,128)(2,1)S(1)}, u32[]{:S(2)}, u32[]{:S(2)}) collective-permute-start(bf16[64,2048]{1,0:T(8,128)(2,1)S(1)} %get-tuple-element.17), channel_id=1, source_target_pairs={{0,96},{16,112},{32,0},{48,16},{64,32},{80,48},{96,64},{112,80},{1... | collective-permute-start | bytes 786440 | tf_op jit(solution)/shard_map/ppermute | solution.py:28
  148.0 17.7 %copy-start = (bf16[128,8,8,256]{3,1,2,0:T(8,128)(2,1)S(1)}, bf16[128,8,8,256]{3,1,2,0:T(8,128)(2,1)}, u32[]{:S(2)}) copy-start(bf16[128,8,8,256]{3,1,2,0:T(8,128)(2,1)} %copy.17) | copy-start | bytes 12582916
  148.0 9.8 %collective-permute-start.18 = (bf16[64,2048]{1,0:T(8,128)(2,1)S(1)}, bf16[64,2048]{1,0:T(8,128)(2,1)S(1)}, u32[]{:S(2)}, u32[]{:S(2)}) collective-permute-start(bf16[64,2048]{1,0:T(8,128)(2,1)S(1)} %get-tuple-element.19), channel_id=1, source_target_pairs={{0,96},{16,112},{32,0},{48,16},{64,32},{80,48},{96,64},{112,80},{1... | collective-permute-start | bytes 786440 | tf_op jit(solution)/shard_map/ppermute | solution.py:28
  153.6 9.5 %collective-permute-start.28 = (bf16[64,2048]{1,0:T(8,128)(2,1)S(1)}, bf16[64,2048]{1,0:T(8,128)(2,1)S(1)}, u32[]{:S(2)}, u32[]{:S(2)}) collective-permute-start(bf16[64,2048]{1,0:T(8,128)(2,1)S(1)} %get-tuple-element.21), channel_id=1, source_target_pairs={{0,96},{16,112},{32,0},{48,16},{64,32},{80,48},{96,64},{112,80},{1... | collective-permute-start | bytes 786440 | tf_op jit(solution)/shard_map/ppermute | solution.py:28
  156.2 9.3 %collective-permute-start.9 = (bf16[128,2048]{1,0:T(8,128)(2,1)S(1)}, bf16[128,2048]{1,0:T(8,128)(2,1)S(1)}, u32[]{:S(2)}, u32[]{:S(2)}) collective-permute-start(bf16[128,2048]{1,0:T(8,128)(2,1)S(1)} %pad_maximum_fusion), channel_id=1, source_target_pairs={{0,16},{16,0},{32,48},{48,32},{64,80},{80,64},{96,112},{112,96},{1... | collective-permute-start | bytes 1572872 | tf_op jit(solution)/shard_map/ppermute | solution.py:42
  158.7 28.5 %collective-permute-start.19 = (bf16[128,2048]{1,0:T(8,128)(2,1)}, bf16[128,2048]{1,0:T(8,128)(2,1)}, u32[]{:S(2)}, u32[]{:S(2)}) collective-permute-start(bf16[128,2048]{1,0:T(8,128)(2,1)} %pad_maximum_fusion.1), channel_id=1, source_target_pairs={{0,16},{16,0},{32,48},{48,32},{64,80},{80,64},{96,112},{112,96},{1... | collective-permute-start | bytes 1572872 | tf_op jit(solution)/shard_map/ppermute | solution.py:42
  164.0 32.1 %collective-permute-start.29 = (bf16[128,2048]{1,0:T(8,128)(2,1)}, bf16[128,2048]{1,0:T(8,128)(2,1)S(1)}, u32[]{:S(2)}, u32[]{:S(2)}) collective-permute-start(bf16[128,2048]{1,0:T(8,128)(2,1)} %pad_maximum_fusion.2), channel_id=1, source_target_pairs={{0,16},{16,0},{32,48},{48,32},{64,80},{80,64},{96,112},{112,96},{1... | collective-permute-start | bytes 1572872 | tf_op jit(solution)/shard_map/ppermute | solution.py:42
  170.5 32.0 %collective-permute-start.10 = (f32[8,64,256]{2,1,0:T(8,128)}, f32[8,64,256]{2,1,0:T(8,128)}, u32[]{:S(2)}, u32[]{:S(2)}) collective-permute-start(f32[8,64,256]{2,1,0:T(8,128)} %dynamic-slice_bitcast_fusion.2), channel_id=1, source_target_pairs={{0,1},{1,0},{2,3},{3,2},{4,5},{5,4},{6,7},{7,6},{8,9},{9,8},{10,11... | collective-permute-start | bytes 1572872 | tf_op jit(solution)/shard_map/ppermute | solution.py:57
  195.3 41.1 %collective-permute-start.20 = (f32[8,64,256]{2,1,0:T(8,128)}, f32[8,64,256]{2,1,0:T(8,128)}, u32[]{:S(2)}, u32[]{:S(2)}) collective-permute-start(f32[8,64,256]{2,1,0:T(8,128)} %dynamic-slice_bitcast_fusion.1), channel_id=1, source_target_pairs={{0,1},{1,0},{2,3},{3,2},{4,5},{5,4},{6,7},{7,6},{8,9},{9,8},{10,11... | collective-permute-start | bytes 1572872 | tf_op jit(solution)/shard_map/ppermute | solution.py:57
  202.4 35.3 %collective-permute-start.30 = (f32[8,64,256]{2,1,0:T(8,128)S(1)}, f32[8,64,256]{2,1,0:T(8,128)S(1)}, u32[]{:S(2)}, u32[]{:S(2)}) collective-permute-start(f32[8,64,256]{2,1,0:T(8,128)S(1)} %dynamic-slice_bitcast_fusion), channel_id=1, source_target_pairs={{0,1},{1,0},{2,3},{3,2},{4,5},{5,4},{6,7},{7,6},{8,9},{9,8},{10,11... | collective-permute-start | bytes 1572872 | tf_op jit(solution)/shard_map/ppermute | solution.py:57
  203.7 39.9 %collective-permute-start.11 = (f32[4,64,256]{2,1,0:T(8,128)S(1)}, f32[4,64,256]{2,1,0:T(8,128)S(1)}, u32[]{:S(2)}, u32[]{:S(2)}) collective-permute-start(f32[4,64,256]{2,1,0:T(8,128)S(1)} %dynamic-slice_bitcast_fusion.5), channel_id=1, source_target_pairs={{0,2},{1,3},{2,0},{3,1},{4,6},{5,7},{6,4},{7,5},{8,10},{9,11},{10,... | collective-permute-start | bytes 786440 | tf_op jit(solution)/shard_map/ppermute | solution.py:57
  237.6 11.6 %collective-permute-start.21 = (f32[4,64,256]{2,1,0:T(8,128)S(1)}, f32[4,64,256]{2,1,0:T(8,128)S(1)}, u32[]{:S(2)}, u32[]{:S(2)}) collective-permute-start(f32[4,64,256]{2,1,0:T(8,128)S(1)} %dynamic-slice_bitcast_fusion.4), channel_id=1, source_target_pairs={{0,2},{1,3},{2,0},{3,1},{4,6},{5,7},{6,4},{7,5},{8,10},{9,11},{10,... | collective-permute-start | bytes 786440 | tf_op jit(solution)/shard_map/ppermute | solution.py:57
  237.8 17.0 %collective-permute-start.31 = (f32[4,64,256]{2,1,0:T(8,128)S(1)}, f32[4,64,256]{2,1,0:T(8,128)S(1)}, u32[]{:S(2)}, u32[]{:S(2)}) collective-permute-start(f32[4,64,256]{2,1,0:T(8,128)S(1)} %dynamic-slice_bitcast_fusion.3), channel_id=1, source_target_pairs={{0,2},{1,3},{2,0},{3,1},{4,6},{5,7},{6,4},{7,5},{8,10},{9,11},{10,... | collective-permute-start | bytes 786440 | tf_op jit(solution)/shard_map/ppermute | solution.py:57
  243.6 15.0 %collective-permute-start.12 = (f32[2,64,256]{2,1,0:T(8,128)S(1)}, f32[2,64,256]{2,1,0:T(8,128)S(1)}, u32[]{:S(2)}, u32[]{:S(2)}) collective-permute-start(f32[2,64,256]{2,1,0:T(8,128)S(1)} %dynamic-slice_bitcast_fusion.8), channel_id=1, source_target_pairs={{0,4},{1,5},{2,6},{3,7},{4,0},{5,1},{6,2},{7,3},{8,12},{9,13},{10,... | collective-permute-start | bytes 393224 | tf_op jit(solution)/shard_map/ppermute | solution.py:57
  249.3 12.4 %collective-permute-start.22 = (f32[2,64,256]{2,1,0:T(8,128)S(1)}, f32[2,64,256]{2,1,0:T(8,128)S(1)}, u32[]{:S(2)}, u32[]{:S(2)}) collective-permute-start(f32[2,64,256]{2,1,0:T(8,128)S(1)} %dynamic-slice_bitcast_fusion.7), channel_id=1, source_target_pairs={{0,4},{1,5},{2,6},{3,7},{4,0},{5,1},{6,2},{7,3},{8,12},{9,13},{10,... | collective-permute-start | bytes 393224 | tf_op jit(solution)/shard_map/ppermute | solution.py:57
  254.9 9.6 %collective-permute-start.32 = (f32[2,64,256]{2,1,0:T(8,128)S(1)}, f32[2,64,256]{2,1,0:T(8,128)S(1)}, u32[]{:S(2)}, u32[]{:S(2)}) collective-permute-start(f32[2,64,256]{2,1,0:T(8,128)S(1)} %dynamic-slice_bitcast_fusion.6), channel_id=1, source_target_pairs={{0,4},{1,5},{2,6},{3,7},{4,0},{5,1},{6,2},{7,3},{8,12},{9,13},{10,... | collective-permute-start | bytes 393224 | tf_op jit(solution)/shard_map/ppermute | solution.py:57
  258.7 8.4 %collective-permute-start.13 = (f32[1,64,256]{2,1,0:T(8,128)S(1)}, f32[1,64,256]{2,1,0:T(8,128)S(1)}, u32[]{:S(2)}, u32[]{:S(2)}) collective-permute-start(f32[1,64,256]{2,1,0:T(8,128)S(1)} %constant_dynamic-slice_fusion.2), channel_id=1, source_target_pairs={{0,8},{1,9},{2,10},{3,11},{4,12},{5,13},{6,14},{7,15},{8,0},{9,1},... | collective-permute-start | bytes 196616 | tf_op jit(solution)/shard_map/ppermute | solution.py:57
  261.7 5.8 %collective-permute-start.23 = (f32[1,64,256]{2,1,0:T(8,128)S(1)}, f32[1,64,256]{2,1,0:T(8,128)S(1)}, u32[]{:S(2)}, u32[]{:S(2)}) collective-permute-start(f32[1,64,256]{2,1,0:T(8,128)S(1)} %constant_dynamic-slice_fusion.1), channel_id=1, source_target_pairs={{0,8},{1,9},{2,10},{3,11},{4,12},{5,13},{6,14},{7,15},{8,0},{9,1},... | collective-permute-start | bytes 196616 | tf_op jit(solution)/shard_map/ppermute | solution.py:57
  264.5 5.8 %collective-permute-start.33 = (f32[1,64,256]{2,1,0:T(8,128)S(1)}, f32[1,64,256]{2,1,0:T(8,128)S(1)}, u32[]{:S(2)}, u32[]{:S(2)}) collective-permute-start(f32[1,64,256]{2,1,0:T(8,128)S(1)} %constant_dynamic-slice_fusion), channel_id=1, source_target_pairs={{0,8},{1,9},{2,10},{3,11},{4,12},{5,13},{6,14},{7,15},{8,0},{9,1},... | collective-permute-start | bytes 196616 | tf_op jit(solution)/shard_map/ppermute | solution.py:57
